TPU v7x, 128 devices: a whole 4x4x4 slice. The times are simulated.
128 devices in a mesh: dp: 16 (over x, z), fsdp: 8 (over y, core).
Axes of the slice: x: 4, y: 4, z: 4, core: 2. Of those that a mesh axis runs over, the one named last changes fastest.
Arguments:
- tokens: bfloat16 [2048, 4096], P('dp', 'fsdp'), may hold values from -6 to 6
- expert_ids: int32 [2048, 2], P('dp'), may hold values from 0 to 7, all different within a row; in each aligned block of 128 rows (0 to 127, 128 to 255, ...) at most 40 rows name the same one
- route_probs: float32 [2048, 2], P('dp'), may hold values from 0.1 to 0.9
- w_gate: bfloat16 [4096, 65536], P(None, ('dp', 'fsdp')), may hold values from -0.09375 to 0.09375
- w_up: bfloat16 [4096, 65536], P(None, ('dp', 'fsdp')), may hold values from -0.09375 to 0.09375
- w_down: bfloat16 [65536, 4096], P(('dp', 'fsdp')), may hold values from -0.0625 to 0.0625
- out_grad: bfloat16 [2048, 4096], P('dp', 'fsdp'), may hold values from -0.59765625 to 0.59765625
Outputs:
- mixed: bfloat16 [2048, 4096], P('dp', 'fsdp')
- token_grad: bfloat16 [2048, 4096], P('dp', 'fsdp')
- prob_grad: float32 [2048, 2], P('dp')
- gate_weight_grad: bfloat16 [4096, 65536], P(None, ('dp', 'fsdp'))
- up_weight_grad: bfloat16 [4096, 65536], P(None, ('dp', 'fsdp'))
- down_weight_grad: bfloat16 [65536, 4096], P(('dp', 'fsdp'))
Inputs may be any that keep to these rules, and one draw needn't show every extreme that they name: `expert_ids`: each token names two different experts. Within the 128 tokens of one dp index (aligned blocks of rows) no expert is named more than 40 times, and in some block one expert is named exactly 40 times.
All inputs are finite; a program needn't handle non-finite values.
Results may differ from a plain program's by a relative error of at most 0.019.
Values may be sent and summed in bfloat16 or wider, within the bound.
No kernel may reach another device: no remote copies, remote signals or barrier semaphores. Data moves between devices by JAX's collectives and lax.ppermute only.
A program may use at most 128 MiB of HBM per device.

v0:
```python
import jax
import jax.numpy as jnp
from jax import lax
from jax.sharding import PartitionSpec as P

E = 8
CAP = 40


def local(tokens, expert_ids, route_probs, w_gate, w_up, w_down, out_grad):
    dp_count = lax.axis_size("dp")
    groups = dp_count // E
    token_count = tokens.shape[0]
    slot_total = E * CAP
    routing = expert_ids.reshape(-1)
    onehot = (routing[:, None] == jnp.arange(E, dtype=jnp.int32)[None, :]).astype(jnp.int32)
    position = jnp.sum((jnp.cumsum(onehot, axis=0) - onehot) * onehot, axis=1)
    slot_of = (routing * CAP + position).reshape(token_count, 2)
    slot_index = jnp.arange(slot_total, dtype=jnp.int32)
    select_first = slot_of[:, 0:1] == slot_index[None, :]
    select_second = slot_of[:, 1:2] == slot_index[None, :]
    picker = jnp.logical_or(select_first, select_second)
    picker_bf = picker.astype(jnp.bfloat16)
    weighted = jnp.where(select_first, route_probs[:, 0:1], 0.0) + jnp.where(
        select_second, route_probs[:, 1:2], 0.0
    )
    contract_rows = (((0,), (0,)), ((), ()))
    back_dims = (((1,), (1,)), ((), ()))

    def place_rows(source, scaled):
        if scaled:
            placed = lax.dot_general(
                weighted,
                source.astype(jnp.float32),
                contract_rows,
                precision=lax.Precision.HIGHEST,
                preferred_element_type=jnp.float32,
            )
        else:
            placed = lax.dot_general(
                picker_bf, source, contract_rows, preferred_element_type=jnp.float32
            )
        placed = placed.astype(jnp.bfloat16).reshape(E, CAP, source.shape[1])
        return jnp.repeat(placed, groups, axis=0)

    def to_expert_layout(source, scaled):
        joined = lax.all_gather(source, "fsdp", axis=1, tiled=True)
        arrived = lax.all_to_all(
            place_rows(joined, scaled), "dp", split_axis=0, concat_axis=0, tiled=True
        )
        return arrived.reshape(dp_count * CAP, arrived.shape[2])

    def to_token_layout(partial_value):
        shares = lax.psum_scatter(
            partial_value.astype(jnp.bfloat16), "fsdp", scatter_dimension=1, tiled=True
        ).astype(jnp.float32)
        returned = lax.all_to_all(
            shares.reshape(dp_count, CAP, shares.shape[1]).astype(jnp.bfloat16),
            "dp",
            split_axis=0,
            concat_axis=0,
            tiled=True,
        ).astype(jnp.float32)
        return jnp.sum(returned.reshape(E, groups, CAP, returned.shape[2]), axis=1).reshape(
            slot_total, returned.shape[2]
        )

    expert_rows = to_expert_layout(tokens, False)
    gate_proj = jnp.dot(expert_rows, w_gate, preferred_element_type=jnp.float32)
    up_proj = jnp.dot(expert_rows, w_up, preferred_element_type=jnp.float32)
    sigmoid_gate = jax.nn.sigmoid(gate_proj)
    activated = gate_proj * sigmoid_gate
    hidden = (activated * up_proj).astype(jnp.bfloat16)
    out_partial = jnp.dot(hidden, w_down, preferred_element_type=jnp.float32)
    out_slots = to_token_layout(out_partial)
    first_pair = jnp.dot(
        select_first.astype(jnp.float32),
        out_slots,
        precision=lax.Precision.HIGHEST,
        preferred_element_type=jnp.float32,
    )
    second_pair = jnp.dot(
        select_second.astype(jnp.float32),
        out_slots,
        precision=lax.Precision.HIGHEST,
        preferred_element_type=jnp.float32,
    )
    mixed = (route_probs[:, 0:1] * first_pair + route_probs[:, 1:2] * second_pair).astype(
        jnp.bfloat16
    )
    grad_local = out_grad.astype(jnp.float32)
    prob_terms = jnp.stack(
        [jnp.sum(first_pair * grad_local, axis=1), jnp.sum(second_pair * grad_local, axis=1)],
        axis=1,
    )
    prob_grad = lax.psum(prob_terms, "fsdp")
    grad_rows = to_expert_layout(out_grad, True)
    hidden_grad = lax.dot_general(grad_rows, w_down, back_dims, preferred_element_type=jnp.float32)
    gate_grad = (
        hidden_grad * up_proj * sigmoid_gate * (1.0 + gate_proj * (1.0 - sigmoid_gate))
    ).astype(jnp.bfloat16)
    up_grad = (hidden_grad * activated).astype(jnp.bfloat16)
    gate_weight_grad = lax.dot_general(
        expert_rows, gate_grad, contract_rows, preferred_element_type=jnp.float32
    ).astype(jnp.bfloat16)
    up_weight_grad = lax.dot_general(
        expert_rows, up_grad, contract_rows, preferred_element_type=jnp.float32
    ).astype(jnp.bfloat16)
    down_weight_grad = lax.dot_general(
        hidden, grad_rows, contract_rows, preferred_element_type=jnp.float32
    ).astype(jnp.bfloat16)
    input_partial = lax.dot_general(
        gate_grad, w_gate, back_dims, preferred_element_type=jnp.float32
    )
    input_partial = input_partial + lax.dot_general(
        up_grad, w_up, back_dims, preferred_element_type=jnp.float32
    )
    input_slots = to_token_layout(input_partial)
    token_grad = jnp.dot(
        picker.astype(jnp.float32),
        input_slots,
        precision=lax.Precision.HIGHEST,
        preferred_element_type=jnp.float32,
    ).astype(jnp.bfloat16)
    return (mixed, token_grad, prob_grad, gate_weight_grad, up_weight_grad, down_weight_grad)


def solution(mesh):
    placed = (
        P("dp", "fsdp"),
        P("dp", None),
        P("dp", None),
        P(None, ("dp", "fsdp")),
        P(None, ("dp", "fsdp")),
        P(("dp", "fsdp"), None),
        P("dp", "fsdp"),
    )
    return jax.shard_map(
        local,
        mesh=mesh,
        in_specs=placed,
        out_specs=(
            P("dp", "fsdp"),
            P("dp", "fsdp"),
            P("dp", None),
            P(None, ("dp", "fsdp")),
            P(None, ("dp", "fsdp")),
            P(("dp", "fsdp"), None),
        ),
        check_vma=False,
    )
```

profile of v0, /device:TPU:0, one launch (start us, length us, event | category | flops | bytes accessed | tf_op | source)
XLA Modules:
  0.0 347.3 jit_solution(6366988755404527250)
XLA Ops:
  7.2 0.7 all-gather.3.cloned.1.call-update
  7.9 0.8 copy.21
  9.0 0.6 reduce-window.6
  10.1 0.7 multiply_add_fusion
  10.8 24.7 %all-gather.3.cloned.1.call-done = bf16[128,4096]{1,0:T(8,128)(2,1)} async-done(((bf16[128,512]{1,0:T(8,128)(2,1)}), bf16[128,4096]{1,0:T(8,128)(2,1)}) %all-gather.3.cloned.1.call-update) | async-done | bytes 1048592 | tf_op jit(solution)/shard_map/all_gather | solution.py:47
  35.6 2.2 convolution_convert_fusion.5
  37.8 3.0 broadcast_in_dim.27
  40.7 7.1 %all-to-all-start = ((bf16[16,40,4096]{2,1,0:T(8,128)(2,1)}), bf16[16,40,4096]{2,1,0:T(8,128)(2,1)}, u32[]{:S(2)}, u32[]{:S(2)}) async-start(bf16[16,40,4096]{2,1,0:T(8,128)(2,1)} %bitcast.57), calls=%async_computation | async-start | bytes 10485760 | tf_op jit(solution)/shard_map/all_to_all | solution.py:48
  47.9 0.7 all-gather.5.cloned.1.call-update
  48.6 25.2 %all-gather.5.cloned.1.call-done = bf16[128,4096]{1,0:T(8,128)(2,1)} async-done(((bf16[128,512]{1,0:T(8,128)(2,1)}), bf16[128,4096]{1,0:T(8,128)(2,1)}) %all-gather.5.cloned.1.call-update) | async-done | bytes 1048592 | tf_op jit(solution)/shard_map/all_gather | solution.py:47
  73.9 3.6 %convolution_convert_fusion.4 = bf16[320,4096]{1,0:T(8,128)(2,1)S(1)} fusion(bf16[128,4096]{1,0:T(8,128)(2,1)} %all-gather.5.cloned.1.call-done, f32[128]{0:T(128)S(1)} %get-tuple-element.13, f32[128]{0:T(128)S(1)} %get-tuple-element.12, s32[128]{0:T(128)S(1)} %get-tuple-element.15, s32[128]{0:T(128)S(1)} %get-tuple-element.14), kind=kOutput, calls=%fused_computation.5 | convolution fusion | flops 2014781440 | bytes 3672064 | tf_op jit(solution)/shard_map/dot_general | solution.py:32
  77.5 47.5 %all-to-all-done = bf16[16,40,4096]{2,1,0:T(8,128)(2,1)} async-done(((bf16[16,40,4096]{2,1,0:T(8,128)(2,1)}), bf16[16,40,4096]{2,1,0:T(8,128)(2,1)}, u32[]{:S(2)}, u32[]{:S(2)}) %all-to-all-start) | async-done | bytes 5242912 | tf_op jit(solution)/shard_map/all_to_all | solution.py:48
  125.0 3.0 broadcast_in_dim.31
  128.0 14.4 %all-to-all-start.2 = ((bf16[16,40,4096]{2,1,0:T(8,128)(2,1)}), bf16[16,40,4096]{2,1,0:T(8,128)(2,1)}, u32[]{:S(2)}, u32[]{:S(2)}) async-start(bf16[16,40,4096]{2,1,0:T(8,128)(2,1)} %bitcast.58), calls=%async_computation.3 | async-start | bytes 10485760 | tf_op jit(solution)/shard_map/all_to_all | solution.py:48
  142.7 7.8 %fusion.26 = f32[640,512]{1,0:T(8,128)} fusion(bf16[640,4096]{1,0:T(8,128)(2,1)} %bitcast.7, bf16[4096,512]{1,0:T(8,128)(2,1)} %param.10), kind=kOutput, calls=%fused_computation.53 | convolution fusion | flops 2684354560 | bytes 10747904 | tf_op jit(solution)/shard_map/dot_general | solution.py:69
  150.5 6.4 %fusion.27 = f32[640,512]{1,0:T(8,128)} fusion(bf16[640,4096]{1,0:T(8,128)(2,1)} %bitcast.7, bf16[4096,512]{1,0:T(8,128)(2,1)S(1)} %copy-done.3), kind=kOutput, calls=%fused_computation.54 | convolution fusion | flops 2684354560 | bytes 10747904 | tf_op jit(solution)/shard_map/dot_general | solution.py:70
  156.9 64.3 %all-to-all-done.2 = bf16[16,40,4096]{2,1,0:T(8,128)(2,1)} async-done(((bf16[16,40,4096]{2,1,0:T(8,128)(2,1)}), bf16[16,40,4096]{2,1,0:T(8,128)(2,1)}, u32[]{:S(2)}, u32[]{:S(2)}) %all-to-all-start.2) | async-done | bytes 5242912 | tf_op jit(solution)/shard_map/all_to_all | solution.py:48
  221.2 8.0 %multiply_convert_fusion = (bf16[640,512]{1,0:T(8,128)(2,1)S(1)}, bf16[640,512]{1,0:T(8,128)(2,1)S(1)}, bf16[640,512]{1,0:T(8,128)(2,1)S(1)}) fusion(f32[640,512]{1,0:T(8,128)} %fusion.26, f32[640,512]{1,0:T(8,128)} %fusion.27, bf16[640,4096]{1,0:T(8,128)(2,1)} %bitcast.14, bf16[512,4096]{1,0:T(8,128)(2,1)} %param.12), kind=kOutput, calls=%fused_computation.9 | convolution fusion | flops 2689269760 | bytes 14024704 | tf_op jit(solution)/shard_map/dot_general | solution.py:98
  229.2 4.7 %convolution_convert_fusion = bf16[640,4096]{1,0:T(8,128)(2,1)} fusion(bf16[640,512]{1,0:T(8,128)(2,1)S(1)} %get-tuple-element.10, bf16[512,4096]{1,0:T(8,128)(2,1)S(1)} %copy-done.2), kind=kOutput, calls=%fused_computation.1 | convolution fusion | flops 2686976000 | bytes 10092544 | tf_op jit(solution)/shard_map/dot_general | solution.py:74
  234.2 4.9 %fusion.28 = f32[640,4096]{1,0:T(8,128)S(1)} fusion(bf16[640,512]{1,0:T(8,128)(2,1)S(1)} %get-tuple-element.9, bf16[4096,512]{1,0:T(8,128)(2,1)} %param.10), kind=kOutput, calls=%fused_computation.55 | convolution fusion | flops 2684354560 | bytes 15335424 | tf_op jit(solution)/shard_map/dot_general | solution.py:112
  239.1 4.8 %add_convert_fusion = bf16[640,4096]{1,0:T(8,128)(2,1)} fusion(f32[640,4096]{1,0:T(8,128)S(1)} %fusion.28, bf16[640,512]{1,0:T(8,128)(2,1)S(1)} %get-tuple-element.8, bf16[4096,512]{1,0:T(8,128)(2,1)S(1)} %copy-done.4), kind=kOutput, calls=%fused_computation | convolution fusion | flops 2689597440 | bytes 20578304 | tf_op jit(solution)/shard_map/dot_general | solution.py:115
  243.9 7.5 %convolution_convert_fusion.1 = bf16[512,4096]{1,0:T(8,128)(2,1)} fusion(bf16[640,512]{1,0:T(8,128)(2,1)S(1)} %get-tuple-element.10, bf16[640,4096]{1,0:T(8,128)(2,1)} %bitcast.14), kind=kOutput, calls=%fused_computation.2 | convolution fusion | flops 2686451712 | bytes 10092544 | tf_op jit(solution)/shard_map/dot_general | solution.py:109
  251.4 7.7 %convolution_convert_fusion.2 = bf16[4096,512]{1,0:T(8,128)(2,1)} fusion(bf16[640,4096]{1,0:T(8,128)(2,1)} %bitcast.7, bf16[640,512]{1,0:T(8,128)(2,1)S(1)} %get-tuple-element.8), kind=kOutput, calls=%fused_computation.3 | convolution fusion | flops 2686451712 | bytes 10092544 | tf_op jit(solution)/shard_map/dot_general | solution.py:106
  259.1 15.8 %reduce-scatter.3.cloned.1.call-done = bf16[640,512]{1,0:T(8,128)(2,1)} async-done(((bf16[640,4096]{1,0:T(8,128)(2,1)}), bf16[640,512]{1,0:T(8,128)(2,1)}) %reduce-scatter.3.cloned.1.call-update) | async-done | bytes 655376 | tf_op jit(solution)/shard_map/reduce_scatter | solution.py:54
  274.9 7.0 %all-to-all-start.1 = ((bf16[16,40,512]{2,1,0:T(8,128)(2,1)}), bf16[16,40,512]{2,1,0:T(8,128)(2,1)S(1)}, u32[]{:S(2)}, u32[]{:S(2)}) async-start(bf16[16,40,512]{2,1,0:T(8,128)(2,1)} %bitcast.65), calls=%async_computation.2 | async-start | bytes 1310720 | tf_op jit(solution)/shard_map/all_to_all | solution.py:57
  281.9 7.6 %convolution_convert_fusion.3 = bf16[4096,512]{1,0:T(8,128)(2,1)} fusion(bf16[640,4096]{1,0:T(8,128)(2,1)} %bitcast.7, bf16[640,512]{1,0:T(8,128)(2,1)S(1)} %get-tuple-element.9), kind=kOutput, calls=%fused_computation.4 | convolution fusion | flops 2686451712 | bytes 10092544 | tf_op jit(solution)/shard_map/dot_general | solution.py:103
  289.5 27.1 %reduce-scatter.5.cloned.1.call-done = bf16[640,512]{1,0:T(8,128)(2,1)} async-done(((bf16[640,4096]{1,0:T(8,128)(2,1)}), bf16[640,512]{1,0:T(8,128)(2,1)}) %reduce-scatter.5.cloned.1.call-update) | async-done | bytes 655376 | tf_op jit(solution)/shard_map/reduce_scatter | solution.py:54
  316.6 7.0 %all-to-all-start.3 = ((bf16[16,40,512]{2,1,0:T(8,128)(2,1)}), bf16[16,40,512]{2,1,0:T(8,128)(2,1)S(1)}, u32[]{:S(2)}, u32[]{:S(2)}) async-start(bf16[16,40,512]{2,1,0:T(8,128)(2,1)} %bitcast.64), calls=%async_computation.5 | async-start | bytes 1310720 | tf_op jit(solution)/shard_map/all_to_all | solution.py:57
  323.7 0.5 fusion.6
  324.2 1.1 fusion.1
  325.4 14.2 %psum.7 = f32[128,2]{0,1:T(2,128)} all-reduce(f32[128,2]{0,1:T(2,128)S(1)} %pad_maximum_fusion), channel_id=1, replica_groups=mesh['dp'=16,'fsdp'=8] {'fsdp'}, use_global_device_ids=true, to_apply=%region_9.10 | all-reduce | flops 256 | bytes 2048 | tf_op jit(solution)/shard_map/psum | solution.py:96
  339.6 1.1 convolution_convert_fusion.6
  (32 shorter events, 1.7 us)
Async XLA Ops:
  7.2 28.4 %all-gather.3.cloned.1.call-start = ((), (), s32[]{:S(2)}) async-start(), calls=%async_computation.6 | async-start | bytes 1179648 | tf_op jit(solution)/shard_map/all_gather | solution.py:47
  40.7 7.9 %copy-start.1 = (f32[128,2]{0,1:T(2,128)S(1)}, f32[128,2]{0,1:T(2,128)}, u32[]{:S(2)}) copy-start(f32[128,2]{0,1:T(2,128)} %param.9) | copy-start | bytes 3076
  40.7 84.3 %all-to-all-start = ((bf16[16,40,4096]{2,1,0:T(8,128)(2,1)}), bf16[16,40,4096]{2,1,0:T(8,128)(2,1)}, u32[]{:S(2)}, u32[]{:S(2)}) async-start(bf16[16,40,4096]{2,1,0:T(8,128)(2,1)} %bitcast.57), calls=%async_computation | async-start | bytes 10485760 | tf_op jit(solution)/shard_map/all_to_all | solution.py:48
  47.9 26.0 %all-gather.5.cloned.1.call-start = ((), (), s32[]{:S(2)}) async-start(), calls=%async_computation.8 | async-start | bytes 1179648 | tf_op jit(solution)/shard_map/all_gather | solution.py:47
  128.0 93.2 %all-to-all-start.2 = ((bf16[16,40,4096]{2,1,0:T(8,128)(2,1)}), bf16[16,40,4096]{2,1,0:T(8,128)(2,1)}, u32[]{:S(2)}, u32[]{:S(2)}) async-start(bf16[16,40,4096]{2,1,0:T(8,128)(2,1)} %bitcast.58), calls=%async_computation.3 | async-start | bytes 10485760 | tf_op jit(solution)/shard_map/all_to_all | solution.py:48
  142.4 132.5 %reduce-scatter.3.cloned.1.call-start = ((), (), s32[]{:S(2)}) async-start(), calls=%async_computation.7 | async-start | bytes 5898240 | tf_op jit(solution)/shard_map/reduce_scatter | solution.py:54
  142.6 7.8 %copy-start.3 = (bf16[4096,512]{1,0:T(8,128)(2,1)S(1)}, bf16[4096,512]{1,0:T(8,128)(2,1)}, u32[]{:S(2)}) copy-start(bf16[4096,512]{1,0:T(8,128)(2,1)} %param.11) | copy-start | bytes 12582916
  221.2 8.0 %copy-start.2 = (bf16[512,4096]{1,0:T(8,128)(2,1)S(1)}, bf16[512,4096]{1,0:T(8,128)(2,1)}, u32[]{:S(2)}) copy-start(bf16[512,4096]{1,0:T(8,128)(2,1)} %param.12) | copy-start | bytes 12582916
  233.9 82.7 %reduce-scatter.5.cloned.1.call-start = ((), (), s32[]{:S(2)}) async-start(), calls=%async_computation.9 | async-start | bytes 5898240 | tf_op jit(solution)/shard_map/reduce_scatter | solution.py:54
  234.2 4.9 %copy-start.4 = (bf16[4096,512]{1,0:T(8,128)(2,1)S(1)}, bf16[4096,512]{1,0:T(8,128)(2,1)}, u32[]{:S(2)}) copy-start(bf16[4096,512]{1,0:T(8,128)(2,1)} %param.11) | copy-start | bytes 12582916
  274.9 41.7 %all-to-all-start.1 = ((bf16[16,40,512]{2,1,0:T(8,128)(2,1)}), bf16[16,40,512]{2,1,0:T(8,128)(2,1)S(1)}, u32[]{:S(2)}, u32[]{:S(2)}) async-start(bf16[16,40,512]{2,1,0:T(8,128)(2,1)} %bitcast.65), calls=%async_computation.2 | async-start | bytes 1310720 | tf_op jit(solution)/shard_map/all_to_all | solution.py:57
  281.9 42.3 %copy-start = (bf16[128,512]{1,0:T(8,128)(2,1)S(1)}, bf16[128,512]{1,0:T(8,128)(2,1)}, u32[]{:S(2)}) copy-start(bf16[128,512]{1,0:T(8,128)(2,1)} %param.13) | copy-start | bytes 393220
  316.6 22.9 %all-to-all-start.3 = ((bf16[16,40,512]{2,1,0:T(8,128)(2,1)}), bf16[16,40,512]{2,1,0:T(8,128)(2,1)S(1)}, u32[]{:S(2)}, u32[]{:S(2)}) async-start(bf16[16,40,512]{2,1,0:T(8,128)(2,1)} %bitcast.64), calls=%async_computation.5 | async-start | bytes 1310720 | tf_op jit(solution)/shard_map/all_to_all | solution.py:57
Sparse Core Ops, SparseCore 0:
  9.7 25.8 all-gather.2
  50.4 23.4 all-gather.4
  234.0 40.8 reduce-scatter.2
  277.1 39.4 reduce-scatter.4
where the time goes:
time: 348 us; the launch traced here: 347 us
  waiting for transfers between devices  206 us (59%)
  matrix products  67.8 us (19%)
  starting transfers between devices  36.1 us (10%)
  blocking collectives  14.2 us (4%)
  between operations  13.9 us (4%)
  local copies, waits for them, and re-layouts  7.52 us (2%)
    all_to_all x2, waiting for transfers between devices, to_expert_layout(): lax.all_to_all(place_rows(joined, scaled), 'dp', split_axis=0, concat_axi...  112 us
    all_gather x2, waiting for transfers between devices, to_expert_layout(): joined = lax.all_gather(source, 'fsdp', axis=1, tiled=True)  50 us
    reduce_scatter x2, waiting for transfers between devices, to_token_layout(): lax.psum_scatter(partial_value.astype(jnp.bfloat16), 'fsdp', scatter_dime...  42.9 us
    all_to_all x2, starting transfers between devices, to_expert_layout(): lax.all_to_all(place_rows(joined, scaled), 'dp', split_axis=0, concat_axi...  21.5 us
    psum x1, blocking collectives, local(): prob_grad = lax.psum(prob_terms, 'fsdp')  14.2 us
    all_to_all x2, starting transfers between devices, to_token_layout(): lax.all_to_all(shares.reshape(dp_count, CAP, shares.shape[1]).astype(jnp....  14 us
    dot_general x1, matrix products, local(): lax.dot_general(grad_rows, w_down, back_dims, preferred_element_type=jnp....  7.96 us
    dot_general x1, matrix products, local(): gate_proj = jnp.dot(expert_rows, w_gate, preferred_element_type=jnp.float32)  7.81 us
  transfers between devices with their start and end apart: 8, of which 6 were waited for; matrix products, arithmetic and copies ran while one was open for 16% of the time, Pallas kernels for 0%

commit v1 on v0

--- a/solution.py
+++ b/solution.py
@@ -9,9 +9,14 @@
 
 def local(tokens, expert_ids, route_probs, w_gate, w_up, w_down, out_grad):
     dp_count = lax.axis_size("dp")
+    fsdp_count = lax.axis_size("fsdp")
     groups = dp_count // E
     token_count = tokens.shape[0]
+    feat = tokens.shape[1]
+    model = w_down.shape[1]
+    hid = w_gate.shape[1]
     slot_total = E * CAP
+    rows = dp_count * CAP
     routing = expert_ids.reshape(-1)
     onehot = (routing[:, None] == jnp.arange(E, dtype=jnp.int32)[None, :]).astype(jnp.int32)
     position = jnp.sum((jnp.cumsum(onehot, axis=0) - onehot) * onehot, axis=1)
@@ -44,34 +49,39 @@
         return jnp.repeat(placed, groups, axis=0)
 
     def to_expert_layout(source, scaled):
-        joined = lax.all_gather(source, "fsdp", axis=1, tiled=True)
         arrived = lax.all_to_all(
-            place_rows(joined, scaled), "dp", split_axis=0, concat_axis=0, tiled=True
+            place_rows(source, scaled), "dp", split_axis=0, concat_axis=0, tiled=True
         )
-        return arrived.reshape(dp_count * CAP, arrived.shape[2])
+        joined = lax.all_gather(arrived.reshape(rows, feat), "fsdp", axis=0, tiled=False)
+        return joined
 
     def to_token_layout(partial_value):
         shares = lax.psum_scatter(
-            partial_value.astype(jnp.bfloat16), "fsdp", scatter_dimension=1, tiled=True
-        ).astype(jnp.float32)
+            partial_value.astype(jnp.bfloat16), "fsdp", scatter_dimension=0, tiled=False
+        )
         returned = lax.all_to_all(
-            shares.reshape(dp_count, CAP, shares.shape[1]).astype(jnp.bfloat16),
+            shares.reshape(dp_count, CAP, feat),
             "dp",
             split_axis=0,
             concat_axis=0,
             tiled=True,
         ).astype(jnp.float32)
-        return jnp.sum(returned.reshape(E, groups, CAP, returned.shape[2]), axis=1).reshape(
-            slot_total, returned.shape[2]
-        )
+        return jnp.sum(returned.reshape(E, groups, CAP, feat), axis=1).reshape(slot_total, feat)
+
+    gate_w3 = w_gate.reshape(fsdp_count, feat, hid)
+    up_w3 = w_up.reshape(fsdp_count, feat, hid)
+    down_w3 = w_down.reshape(hid, fsdp_count, feat)
+    in_dims = (((0, 2), (0, 1)), ((), ()))
 
     expert_rows = to_expert_layout(tokens, False)
-    gate_proj = jnp.dot(expert_rows, w_gate, preferred_element_type=jnp.float32)
-    up_proj = jnp.dot(expert_rows, w_up, preferred_element_type=jnp.float32)
+    gate_proj = lax.dot_general(expert_rows, gate_w3, in_dims, preferred_element_type=jnp.float32)
+    up_proj = lax.dot_general(expert_rows, up_w3, in_dims, preferred_element_type=jnp.float32)
     sigmoid_gate = jax.nn.sigmoid(gate_proj)
     activated = gate_proj * sigmoid_gate
     hidden = (activated * up_proj).astype(jnp.bfloat16)
-    out_partial = jnp.dot(hidden, w_down, preferred_element_type=jnp.float32)
+    out_partial = jnp.einsum(
+        "rh,hfd->frd", hidden, down_w3, preferred_element_type=jnp.float32
+    )
     out_slots = to_token_layout(out_partial)
     first_pair = jnp.dot(
         select_first.astype(jnp.float32),
@@ -93,27 +103,29 @@
         [jnp.sum(first_pair * grad_local, axis=1), jnp.sum(second_pair * grad_local, axis=1)],
         axis=1,
     )
-    prob_grad = lax.psum(prob_terms, "fsdp")
+    prob_grad = jnp.sum(lax.all_gather(prob_terms, "fsdp", axis=0, tiled=False), axis=0)
     grad_rows = to_expert_layout(out_grad, True)
-    hidden_grad = lax.dot_general(grad_rows, w_down, back_dims, preferred_element_type=jnp.float32)
+    hidden_grad = lax.dot_general(grad_rows, down_w3, (((0, 2), (1, 2)), ((), ())),
+                                  preferred_element_type=jnp.float32)
     gate_grad = (
         hidden_grad * up_proj * sigmoid_gate * (1.0 + gate_proj * (1.0 - sigmoid_gate))
     ).astype(jnp.bfloat16)
     up_grad = (hidden_grad * activated).astype(jnp.bfloat16)
+    w_grad_dims = (((1,), (0,)), ((), ()))
     gate_weight_grad = lax.dot_general(
-        expert_rows, gate_grad, contract_rows, preferred_element_type=jnp.float32
-    ).astype(jnp.bfloat16)
+        expert_rows, gate_grad, w_grad_dims, preferred_element_type=jnp.float32
+    ).astype(jnp.bfloat16).reshape(fsdp_count * feat, hid)
     up_weight_grad = lax.dot_general(
-        expert_rows, up_grad, contract_rows, preferred_element_type=jnp.float32
-    ).astype(jnp.bfloat16)
-    down_weight_grad = lax.dot_general(
-        hidden, grad_rows, contract_rows, preferred_element_type=jnp.float32
-    ).astype(jnp.bfloat16)
-    input_partial = lax.dot_general(
-        gate_grad, w_gate, back_dims, preferred_element_type=jnp.float32
+        expert_rows, up_grad, w_grad_dims, preferred_element_type=jnp.float32
+    ).astype(jnp.bfloat16).reshape(fsdp_count * feat, hid)
+    down_weight_grad = jnp.einsum(
+        "rh,frd->hfd", hidden, grad_rows, preferred_element_type=jnp.float32
+    ).astype(jnp.bfloat16).reshape(hid, model)
+    input_partial = jnp.einsum(
+        "rh,fdh->frd", gate_grad, gate_w3, preferred_element_type=jnp.float32
     )
-    input_partial = input_partial + lax.dot_general(
-        up_grad, w_up, back_dims, preferred_element_type=jnp.float32
+    input_partial = input_partial + jnp.einsum(
+        "rh,fdh->frd", up_grad, up_w3, preferred_element_type=jnp.float32
     )
     input_slots = to_token_layout(input_partial)
     token_grad = jnp.dot(

time: 348 us -> 247 us (0.71)
  waiting for transfers between devices: 206 us -> 101 us
  blocking collectives: 14.2 us -> 43.6 us
  starting transfers between devices: 36.1 us -> 14.1 us
  matrix products: 67.8 us -> 60.4 us
    all_to_all x4 -> x2, waiting for transfers between devices: 112 us -> 0.01 us  [to_token_layout(): lax.all_to_all(shares.reshape(dp_count, CAP, feat), 'dp', split_axis=0, c...]
    all_to_all x0 -> x2, blocking collectives: none -> 35.7 us  [to_expert_layout(): lax.all_to_all(place_rows(source, scaled), 'dp', split_axis=0, concat_axi...]
    all_to_all x4 -> x2, starting transfers between devices: 35.5 us -> 13.8 us  [to_token_layout(): lax.all_to_all(shares.reshape(dp_count, CAP, feat), 'dp', split_axis=0, c...]
    psum x1 -> x0, blocking collectives: 14.2 us -> none  [local(): prob_grad = lax.psum(prob_terms, 'fsdp')]
    reduce_scatter x2, waiting for transfers between devices: 42.9 us -> 51.4 us  [to_token_layout(): lax.psum_scatter(partial_value.astype(jnp.bfloat16), 'fsdp', scatter_dime...]
    all_gather x0 -> x1, blocking collectives: none -> 7.84 us  [local(): lax.all_gather(prob_terms, 'fsdp', axis=0, tiled=False)]
    unnamed x11 -> x16, local copies, waits for them, and re-layouts: 0.81 us -> 7.79 us
    broadcast_in_dim x2, local copies, waits for them, and re-layouts: 6 us -> 0.09 us  [place_rows(): return jnp.repeat(placed, groups, axis=0)]
  transfers between devices with their start and end apart: 8 -> 6, of which waited for: 6 -> 4; matrix products, arithmetic and copies ran while one was open for 16% -> 19% of each run, Pallas kernels for 0% -> 0%
where the time goes in v1:
time: 247 us; the launch traced here: 245 us
  waiting for transfers between devices  101 us (41%)
  matrix products  60.4 us (24%)
  blocking collectives  43.6 us (18%)
  starting transfers between devices  14.1 us (6%)
  between operations  13.9 us (6%)
  local copies, waits for them, and re-layouts  9.35 us (4%)
    reduce_scatter x2, waiting for transfers between devices, to_token_layout(): lax.psum_scatter(partial_value.astype(jnp.bfloat16), 'fsdp', scatter_dime...  51.4 us
    all_gather x2, waiting for transfers between devices, to_expert_layout(): lax.all_gather(arrived.reshape(rows, feat), 'fsdp', axis=0, tiled=False)  49.7 us
    all_to_all x2, blocking collectives, to_expert_layout(): lax.all_to_all(place_rows(source, scaled), 'dp', split_axis=0, concat_axi...  35.7 us
    all_to_all x2, starting transfers between devices, to_token_layout(): lax.all_to_all(shares.reshape(dp_count, CAP, feat), 'dp', split_axis=0, c...  13.8 us
    dot_general x1, matrix products, local(): jnp.einsum('rh,frd->hfd', hidden, grad_rows, preferred_element_type=jnp.f...  8.94 us
    all_gather x1, blocking collectives, local(): lax.all_gather(prob_terms, 'fsdp', axis=0, tiled=False)  7.84 us
    unnamed x16, local copies, waits for them, and re-layouts  7.79 us
    dot_general x1, matrix products, local(): lax.dot_general(grad_rows, down_w3, (((0, 2), (1, 2)), ((), ())), preferr...  7.72 us
  transfers between devices with their start and end apart: 6, of which 4 were waited for; matrix products, arithmetic and copies ran while one was open for 19% of the time, Pallas kernels for 0%

profile of v1, /device:TPU:0, one launch (start us, length us, event | category | flops | bytes accessed | tf_op | source)
XLA Modules:
  0.0 244.7 jit_solution(17944123879494629458)
XLA Ops:
  7.2 0.8 copy.49
  8.3 0.6 reduce-window.6
  9.5 0.7 multiply_add_fusion
  10.2 0.8 slice_bitcast_fusion.3
  11.0 1.5 convolution_convert_fusion.3
  12.5 20.6 %all_to_all.20 = bf16[16,40,512]{2,1,0:T(8,128)(2,1)} all-to-all(bf16[16,40,512]{2,1,0:T(8,128)(2,1)S(1)} %bitcast.103), channel_id=1, replica_groups=mesh['dp'=16,'fsdp'=8] {'dp'}, dimensions={0} | all-to-all | bytes 1310720 | tf_op jit(solution)/shard_map/all_to_all | solution.py:52
  33.2 0.4 convolution_convert_fusion.4
  33.6 15.1 %all_to_all.21 = bf16[16,40,512]{2,1,0:T(8,128)(2,1)} all-to-all(bf16[16,40,512]{2,1,0:T(8,128)(2,1)S(1)} %bitcast.104), channel_id=1, replica_groups=mesh['dp'=16,'fsdp'=8] {'dp'}, dimensions={0} | all-to-all | bytes 1310720 | tf_op jit(solution)/shard_map/all_to_all | solution.py:52
  48.8 19.2 %all-gather.6.cloned.1.call-done = bf16[8,640,512]{2,1,0:T(8,128)(2,1)} async-done(((bf16[1,640,512]{2,1,0:T(8,128)(2,1)}), bf16[8,640,512]{2,1,0:T(8,128)(2,1)}) %all-gather.6.cloned.1.call-update) | async-done | bytes 5242896 | tf_op jit(solution)/shard_map/all_gather | solution.py:55
  68.0 7.7 %fusion.9 = f32[640,512]{1,0:T(8,128)} fusion(bf16[8,640,512]{2,1,0:T(8,128)(2,1)} %all-gather.6.cloned.1.call-done, bf16[64,8,8,512]{3,2,1,0:T(8,128)(2,1)} %bitcast.113), kind=kOutput, calls=%fused_computation.12 | convolution fusion | flops 2684354560 | bytes 10747904 | tf_op jit(solution)/shard_map/dot_general | solution.py:108
  75.7 30.5 %all-gather.4.cloned.1.call-done = bf16[8,640,512]{2,1,0:T(8,128)(2,1)} async-done(((bf16[1,640,512]{2,1,0:T(8,128)(2,1)}), bf16[8,640,512]{2,1,0:T(8,128)(2,1)}) %all-gather.4.cloned.1.call-update) | async-done | bytes 5242896 | tf_op jit(solution)/shard_map/all_gather | solution.py:55
  106.2 6.2 %convolution_bitcast_fusion = f32[640,512]{1,0:T(8,128)S(1)} fusion(bf16[8,640,512]{2,1,0:T(8,128)(2,1)} %all-gather.4.cloned.1.call-done, bf16[8,512,512]{2,1,0:T(8,128)(2,1)} %bitcast.98), kind=kOutput, calls=%fused_computation.13 | convolution fusion | flops 2684354560 | bytes 10747904 | tf_op jit(solution)/shard_map/dot_general | solution.py:78
  112.4 0.3 copy-done.5
  112.7 0.3 copy-done.6
  113.0 3.4 %fusion.14 = (bf16[640,512,1]{1,0,2:T(8,128)(2,1)S(1)}, bf16[640,512]{1,0:T(8,128)(2,1)S(1)}, bf16[640,512,1]{1,0,2:T(8,128)(2,1)S(1)}) fusion(f32[640,512]{1,0:T(8,128)S(1)} %copy-done.6, f32[640,512]{1,0:T(8,128)S(1)} %convolution_bitcast_fusion, bf16[8,640,512]{2,1,0:T(8,128)(2,1)S(1)} %copy-done.5, bf16[8,512,512]{2,1,0:T(8,128)(2,1)S(1)} %bitcast.94), kind=kOutput, calls=%fused_computation.26 | convolution fusion | flops 2689269760 | bytes 14024704 | tf_op jit(solution)/shard_map/dot_general | solution.py:77
  116.5 2.9 %fusion.16 = f32[640,8,512]{2,0,1:T(8,128)S(1)} fusion(bf16[8,512,512]{2,1,0:T(8,128)(2,1)S(1)} %bitcast.95, bf16[640,512]{1,0:T(8,128)(2,1)S(1)} %get-tuple-element.39), kind=kOutput, calls=%fused_computation.28 | convolution fusion | flops 2684354560 | bytes 15335424 | tf_op jit(solution)/shard_map/rh,fdh->frd/dot_general | solution.py:124
  119.4 4.8 %fusion = bf16[8,640,512]{2,1,0:T(8,128)(2,1)} fusion(f32[640,8,512]{2,0,1:T(8,128)S(1)} %fusion.16, bf16[640,512,1]{1,0,2:T(8,128)(2,1)S(1)} %get-tuple-element.38, bf16[8,512,512]{2,1,0:T(8,128)(2,1)S(1)} %bitcast.99), kind=kOutput, calls=%fused_computation.1 | convolution fusion | flops 2689597440 | bytes 20578304 | tf_op jit(solution)/shard_map/rh,fdh->frd/dot_general | solution.py:127
  124.2 0.2 reduce-scatter.3.cloned.1.call-start
  124.4 6.8 %convert_bitcast_fusion = bf16[8,640,512]{2,1,0:T(8,128)(2,1)} fusion(bf16[640,512,1]{1,0,2:T(8,128)(2,1)S(1)} %get-tuple-element.40, bf16[64,8,8,512]{3,2,1,0:T(8,128)(2,1)} %bitcast.114), kind=kOutput, calls=%fused_computation.2 | convolution fusion | flops 2686976000 | bytes 10092544 | tf_op jit(solution)/shard_map/rh,hfd->frd/dot_general | solution.py:82
  131.3 8.9 %convolution_convert_fusion = bf16[512,8,512]{0,2,1:T(8,128)(2,1)} fusion(bf16[640,512,1]{1,0,2:T(8,128)(2,1)S(1)} %get-tuple-element.40, bf16[8,640,512]{2,1,0:T(8,128)(2,1)} %all-gather.6.cloned.1.call-done), kind=kOutput, calls=%fused_computation.9 | convolution fusion | flops 2686451712 | bytes 10092544 | tf_op jit(solution)/shard_map/rh,frd->hfd/dot_general | solution.py:121
  140.2 24.1 %reduce-scatter.5.cloned.1.call-done = bf16[1,640,512]{2,1,0:T(8,128)(2,1)} async-done(((bf16[8,640,512]{2,1,0:T(8,128)(2,1)}), bf16[1,640,512]{2,1,0:T(8,128)(2,1)}) %reduce-scatter.5.cloned.1.call-update) | async-done | bytes 655376 | tf_op jit(solution)/shard_map/reduce_scatter | solution.py:59
  164.3 6.9 %all-to-all-start.3 = ((bf16[16,40,512]{2,1,0:T(8,128)(2,1)}), bf16[16,40,512]{2,1,0:T(8,128)(2,1)S(1)}, u32[]{:S(2)}, u32[]{:S(2)}) async-start(bf16[16,40,512]{2,1,0:T(8,128)(2,1)} %bitcast.108), calls=%async_computation.5 | async-start | bytes 1310720 | tf_op jit(solution)/shard_map/all_to_all | solution.py:62
  171.2 7.5 %convolution_convert_fusion.2 = bf16[8,512,512]{2,1,0:T(8,128)(2,1)} fusion(bf16[8,640,512]{2,1,0:T(8,128)(2,1)} %all-gather.4.cloned.1.call-done, bf16[640,512]{1,0:T(8,128)(2,1)S(1)} %get-tuple-element.39), kind=kOutput, calls=%fused_computation.11 | convolution fusion | flops 2686451712 | bytes 10092544 | tf_op jit(solution)/shard_map/dot_general | solution.py:115
  178.8 27.2 %reduce-scatter.3.cloned.1.call-done = bf16[1,640,512]{2,1,0:T(8,128)(2,1)} async-done(((bf16[8,640,512]{2,1,0:T(8,128)(2,1)}), bf16[1,640,512]{2,1,0:T(8,128)(2,1)}) %reduce-scatter.3.cloned.1.call-update) | async-done | bytes 655376 | tf_op jit(solution)/shard_map/reduce_scatter | solution.py:59
  206.0 6.9 %all-to-all-start.1 = ((bf16[16,40,512]{2,1,0:T(8,128)(2,1)}), bf16[16,40,512]{2,1,0:T(8,128)(2,1)S(1)}, u32[]{:S(2)}, u32[]{:S(2)}) async-start(bf16[16,40,512]{2,1,0:T(8,128)(2,1)} %bitcast.107), calls=%async_computation.2 | async-start | bytes 1310720 | tf_op jit(solution)/shard_map/all_to_all | solution.py:62
  212.9 7.5 %convolution_convert_fusion.1 = bf16[8,512,512]{2,1,0:T(8,128)(2,1)} fusion(bf16[8,640,512]{2,1,0:T(8,128)(2,1)} %all-gather.4.cloned.1.call-done, bf16[640,512,1]{1,0,2:T(8,128)(2,1)S(1)} %get-tuple-element.38), kind=kOutput, calls=%fused_computation.10 | convolution fusion | flops 2686451712 | bytes 10092544 | tf_op jit(solution)/shard_map/dot_general | solution.py:118
  220.4 6.4 %copy.57 = bf16[512,4096]{1,0:T(8,128)(2,1)} copy(bf16[512,4096]{0,1:T(8,128)(2,1)} %bitcast.100) | data formatting | bytes 8388608
  226.9 1.1 convolution_convert_fusion.5
  228.1 0.5 fusion.23
  228.6 1.1 fusion.18
  229.8 7.8 %all-gather = f32[1024,2]{0,1:T(2,128)S(1)} all-gather(f32[128,2]{0,1:T(2,128)S(1)} %pad_maximum_fusion), channel_id=2, replica_groups=mesh['dp'=16,'fsdp'=8] {'fsdp'}, dimensions={0}, use_global_device_ids=true | all-gather | bytes 9216 | tf_op jit(solution)/shard_map/all_gather | solution.py:106
  237.6 0.6 bitcast_reduce_fusion
  (36 shorter events, 1.4 us)
Async XLA Ops:
  7.2 26.0 %copy-start = (bf16[128,512]{1,0:T(8,128)(2,1)S(1)}, bf16[128,512]{1,0:T(8,128)(2,1)}, u32[]{:S(2)}) copy-start(bf16[128,512]{1,0:T(8,128)(2,1)} %param.7) | copy-start | bytes 393220
  7.2 60.8 %all-gather.6.cloned.1.call-start = ((), (), s32[]{:S(2)}) async-start(), calls=%async_computation.8 | async-start | bytes 5898240 | tf_op jit(solution)/shard_map/all_gather | solution.py:55
  33.1 73.1 %all-gather.4.cloned.1.call-start = ((), (), s32[]{:S(2)}) async-start(), calls=%async_computation.6 | async-start | bytes 5898240 | tf_op jit(solution)/shard_map/all_gather | solution.py:55
  48.7 115.6 %reduce-scatter.5.cloned.1.call-start = ((), (), s32[]{:S(2)}) async-start(), calls=%async_computation.9 | async-start | bytes 5898240 | tf_op jit(solution)/shard_map/reduce_scatter | solution.py:59
  106.2 6.2 %copy-start.2 = (bf16[4096,512]{1,0:T(8,128)(2,1)S(1)}, bf16[4096,512]{1,0:T(8,128)(2,1)}, u32[]{:S(2)}) copy-start(bf16[4096,512]{1,0:T(8,128)(2,1)} %param.10) | copy-start | bytes 12582916
  106.2 6.5 %copy-start.5 = (bf16[8,640,512]{2,1,0:T(8,128)(2,1)S(1)}, bf16[8,640,512]{2,1,0:T(8,128)(2,1)}, u32[]{:S(2)}) copy-start(bf16[8,640,512]{2,1,0:T(8,128)(2,1)} %all-gather.4.cloned.1.call-done) | copy-start | bytes 15728644
  106.2 6.8 %copy-start.6 = (f32[640,512]{1,0:T(8,128)S(1)}, f32[640,512]{1,0:T(8,128)}, u32[]{:S(2)}) copy-start(f32[640,512]{1,0:T(8,128)} %fusion.9) | copy-start | bytes 3932164
  116.4 2.9 %copy-start.3 = (bf16[4096,512]{1,0:T(8,128)(2,1)S(1)}, bf16[4096,512]{1,0:T(8,128)(2,1)}, u32[]{:S(2)}) copy-start(bf16[4096,512]{1,0:T(8,128)(2,1)} %param.11) | copy-start | bytes 12582916
  124.2 81.8 %reduce-scatter.3.cloned.1.call-start = ((), (), s32[]{:S(2)}) async-start(), calls=%async_computation.7 | async-start | bytes 5898240 | tf_op jit(solution)/shard_map/reduce_scatter | solution.py:59
  164.3 41.7 %all-to-all-start.3 = ((bf16[16,40,512]{2,1,0:T(8,128)(2,1)}), bf16[16,40,512]{2,1,0:T(8,128)(2,1)S(1)}, u32[]{:S(2)}, u32[]{:S(2)}) async-start(bf16[16,40,512]{2,1,0:T(8,128)(2,1)} %bitcast.108), calls=%async_computation.5 | async-start | bytes 1310720 | tf_op jit(solution)/shard_map/all_to_all | solution.py:62
  206.0 22.0 %all-to-all-start.1 = ((bf16[16,40,512]{2,1,0:T(8,128)(2,1)}), bf16[16,40,512]{2,1,0:T(8,128)(2,1)S(1)}, u32[]{:S(2)}, u32[]{:S(2)}) async-start(bf16[16,40,512]{2,1,0:T(8,128)(2,1)} %bitcast.107), calls=%async_computation.2 | async-start | bytes 1310720 | tf_op jit(solution)/shard_map/all_to_all | solution.py:62
  220.4 17.7 %copy-start.1 = (bf16[128,512]{1,0:T(8,128)(2,1)S(1)}, bf16[128,512]{1,0:T(8,128)(2,1)}, u32[]{:S(2)}) copy-start(bf16[128,512]{1,0:T(8,128)(2,1)} %param.7) | copy-start | bytes 393220
  226.8 1.8 copy-start.4
Sparse Core Ops, SparseCore 0:
  33.3 34.6 all-gather.5
  69.6 36.5 all-gather.3
  124.3 39.9 reduce-scatter.4
  166.6 39.3 reduce-scatter.2

commit v2 on v1

--- a/solution.py
+++ b/solution.py
@@ -1,7 +1,7 @@
 import jax
 import jax.numpy as jnp
 from jax import lax
-from jax.sharding import PartitionSpec as P
+from jax.sharding import Mesh, PartitionSpec as P
 
 E = 8
 CAP = 40
@@ -9,7 +9,9 @@
 
 def local(tokens, expert_ids, route_probs, w_gate, w_up, w_down, out_grad):
     dp_count = lax.axis_size("dp")
-    fsdp_count = lax.axis_size("fsdp")
+    chips = lax.axis_size("fy")
+    cores = lax.axis_size("fc")
+    fsdp_count = chips * cores
     groups = dp_count // E
     token_count = tokens.shape[0]
     feat = tokens.shape[1]
@@ -17,6 +19,8 @@
     hid = w_gate.shape[1]
     slot_total = E * CAP
     rows = dp_count * CAP
+    core = lax.axis_index("fc")
+    swap = [(0, 1), (1, 0)]
     routing = expert_ids.reshape(-1)
     onehot = (routing[:, None] == jnp.arange(E, dtype=jnp.int32)[None, :]).astype(jnp.int32)
     position = jnp.sum((jnp.cumsum(onehot, axis=0) - onehot) * onehot, axis=1)
@@ -52,13 +56,18 @@
         arrived = lax.all_to_all(
             place_rows(source, scaled), "dp", split_axis=0, concat_axis=0, tiled=True
         )
-        joined = lax.all_gather(arrived.reshape(rows, feat), "fsdp", axis=0, tiled=False)
-        return joined
+        across = lax.all_gather(arrived.reshape(rows, feat), "fy", axis=0, tiled=False)
+        other = lax.ppermute(across, "fc", swap)
+        joined = jnp.where(core == 0, jnp.stack([across, other], axis=1),
+                           jnp.stack([other, across], axis=1))
+        return joined.reshape(fsdp_count, rows, feat)
 
     def to_token_layout(partial_value):
-        shares = lax.psum_scatter(
-            partial_value.astype(jnp.bfloat16), "fsdp", scatter_dimension=0, tiled=False
-        )
+        blocks = partial_value.astype(jnp.bfloat16).reshape(chips, cores, rows, feat)
+        kept = lax.dynamic_index_in_dim(blocks, core, axis=1, keepdims=False)
+        sent = lax.dynamic_index_in_dim(blocks, 1 - core, axis=1, keepdims=False)
+        within = kept.astype(jnp.float32) + lax.ppermute(sent, "fc", swap).astype(jnp.float32)
+        shares = lax.psum_scatter(within.astype(jnp.bfloat16), "fy", scatter_dimension=0, tiled=False)
         returned = lax.all_to_all(
             shares.reshape(dp_count, CAP, feat),
             "dp",
@@ -103,7 +112,7 @@
         [jnp.sum(first_pair * grad_local, axis=1), jnp.sum(second_pair * grad_local, axis=1)],
         axis=1,
     )
-    prob_grad = jnp.sum(lax.all_gather(prob_terms, "fsdp", axis=0, tiled=False), axis=0)
+    prob_grad = jnp.sum(lax.all_gather(prob_terms, ("fy", "fc"), axis=0, tiled=False), axis=0)
     grad_rows = to_expert_layout(out_grad, True)
     hidden_grad = lax.dot_general(grad_rows, down_w3, (((0, 2), (1, 2)), ((), ())),
                                   preferred_element_type=jnp.float32)
@@ -111,12 +120,11 @@
         hidden_grad * up_proj * sigmoid_gate * (1.0 + gate_proj * (1.0 - sigmoid_gate))
     ).astype(jnp.bfloat16)
     up_grad = (hidden_grad * activated).astype(jnp.bfloat16)
-    w_grad_dims = (((1,), (0,)), ((), ()))
-    gate_weight_grad = lax.dot_general(
-        expert_rows, gate_grad, w_grad_dims, preferred_element_type=jnp.float32
+    gate_weight_grad = jnp.einsum(
+        "frd,rh->fdh", expert_rows, gate_grad, preferred_element_type=jnp.float32
     ).astype(jnp.bfloat16).reshape(fsdp_count * feat, hid)
-    up_weight_grad = lax.dot_general(
-        expert_rows, up_grad, w_grad_dims, preferred_element_type=jnp.float32
+    up_weight_grad = jnp.einsum(
+        "frd,rh->fdh", expert_rows, up_grad, preferred_element_type=jnp.float32
     ).astype(jnp.bfloat16).reshape(fsdp_count * feat, hid)
     down_weight_grad = jnp.einsum(
         "rh,frd->hfd", hidden, grad_rows, preferred_element_type=jnp.float32
@@ -138,26 +146,30 @@
 
 
 def solution(mesh):
+    dp_size, fsdp_size = mesh.devices.shape
+    cores = 2
+    split = Mesh(mesh.devices.reshape(dp_size, fsdp_size // cores, cores), ("dp", "fy", "fc"))
+    fs = ("fy", "fc")
     placed = (
-        P("dp", "fsdp"),
+        P("dp", fs),
         P("dp", None),
         P("dp", None),
-        P(None, ("dp", "fsdp")),
-        P(None, ("dp", "fsdp")),
-        P(("dp", "fsdp"), None),
-        P("dp", "fsdp"),
+        P(None, ("dp",) + fs),
+        P(None, ("dp",) + fs),
+        P(("dp",) + fs, None),
+        P("dp", fs),
     )
     return jax.shard_map(
         local,
-        mesh=mesh,
+        mesh=split,
         in_specs=placed,
         out_specs=(
-            P("dp", "fsdp"),
-            P("dp", "fsdp"),
+            P("dp", fs),
+            P("dp", fs),
             P("dp", None),
-            P(None, ("dp", "fsdp")),
-            P(None, ("dp", "fsdp")),
-            P(("dp", "fsdp"), None),
+            P(None, ("dp",) + fs),
+            P(None, ("dp",) + fs),
+            P(("dp",) + fs, None),
         ),
         check_vma=False,
     )

time: 247 us -> 243 us (0.984)
  waiting for transfers between devices: 101 us -> 86.6 us
  other arithmetic: 2.22 us -> 15.1 us
  matrix products: 60.4 us -> 52 us
  local copies, waits for them, and re-layouts: 9.35 us -> 15.7 us
    reduce_scatter x2, waiting for transfers between devices: 51.4 us -> 14.6 us  [to_token_layout(): lax.psum_scatter(within.astype(jnp.bfloat16), 'fy', scatter_dimension=0,...]
    ppermute x0 -> x4, waiting for transfers between devices: none -> 15 us  [the longest x2 9.76 us: to_token_layout(): lax.ppermute(sent, 'fc', swap).astype(jnp.float32)]
    select_n x0 -> x1, other arithmetic: none -> 6.48 us  [to_expert_layout(): jnp.where(core == 0, jnp.stack([across, other], axis=1), jnp.stack([other...]
    convert_element_type x0 -> x2, other arithmetic: none -> 6.35 us  [to_token_layout(): within.astype(jnp.bfloat16)]
    all_gather x2, waiting for transfers between devices: 49.7 us -> 54.8 us  [to_expert_layout(): lax.all_gather(arrived.reshape(rows, feat), 'fy', axis=0, tiled=False)]
    unnamed x16 -> x26, local copies, waits for them, and re-layouts: 7.79 us -> 12.3 us
    dot_general x1, matrix products: 6.79 us -> 3.15 us  [local(): jnp.einsum('rh,hfd->frd', hidden, down_w3, preferred_element_type=jnp.flo...]
    dot_general x1, matrix products: 7.72 us -> 4.24 us  [local(): lax.dot_general(grad_rows, down_w3, (((0, 2), (1, 2)), ((), ())), preferr...]
  transfers between devices with their start and end apart: 6 -> 10, of which waited for: 4 -> 7; matrix products, arithmetic and copies ran while one was open for 19% -> 19% of each run, Pallas kernels for 0% -> 0%
where the time goes in v2:
time: 243 us; the launch traced here: 242 us
  waiting for transfers between devices  86.6 us (36%)
  matrix products  52 us (21%)
  blocking collectives  44.3 us (18%)
  local copies, waits for them, and re-layouts  15.7 us (6%)
  other arithmetic  15.1 us (6%)
  starting transfers between devices  14.6 us (6%)
  between operations  14 us (6%)
    all_gather x2, waiting for transfers between devices, to_expert_layout(): lax.all_gather(arrived.reshape(rows, feat), 'fy', axis=0, tiled=False)  54.8 us
    all_to_all x2, blocking collectives, to_expert_layout(): lax.all_to_all(place_rows(source, scaled), 'dp', split_axis=0, concat_axi...  35.7 us
    reduce_scatter x2, waiting for transfers between devices, to_token_layout(): lax.psum_scatter(within.astype(jnp.bfloat16), 'fy', scatter_dimension=0,...  14.6 us
    all_to_all x2, starting transfers between devices, to_token_layout(): lax.all_to_all(shares.reshape(dp_count, CAP, feat), 'dp', split_axis=0, c...  13.9 us
    unnamed x26, local copies, waits for them, and re-layouts  12.3 us
    ppermute x2, waiting for transfers between devices, to_token_layout(): lax.ppermute(sent, 'fc', swap).astype(jnp.float32)  9.76 us
    all_gather x1, blocking collectives, local(): lax.all_gather(prob_terms, ('fy', 'fc'), axis=0, tiled=False)  8.6 us
    dot_general x1, matrix products, local(): jnp.einsum('rh,frd->hfd', hidden, grad_rows, preferred_element_type=jnp.f...  8.46 us
  transfers between devices with their start and end apart: 10, of which 7 were waited for; matrix products, arithmetic and copies ran while one was open for 19% of the time, Pallas kernels for 0%

profile of v2, /device:TPU:0, one launch (start us, length us, event | category | flops | bytes accessed | tf_op | source)
XLA Modules:
  0.0 242.2 jit_solution(12178755977055316412)
XLA Ops:
  7.2 0.8 copy.53
  11.0 1.5 convolution_convert_fusion.3
  12.5 20.6 %all_to_all.20 = bf16[16,40,512]{2,1,0:T(8,128)(2,1)} all-to-all(bf16[16,40,512]{2,1,0:T(8,128)(2,1)S(1)} %bitcast.137), channel_id=1, replica_groups=mesh['dp'=16,'fy'=4,'fc'=2] {'dp'}, dimensions={0} | all-to-all | bytes 1310720 | tf_op jit(solution)/shard_map/all_to_all | solution.py:56
  33.6 15.1 %all_to_all.21 = bf16[16,40,512]{2,1,0:T(8,128)(2,1)} all-to-all(bf16[16,40,512]{2,1,0:T(8,128)(2,1)S(1)} %bitcast.138), channel_id=1, replica_groups=mesh['dp'=16,'fy'=4,'fc'=2] {'dp'}, dimensions={0} | all-to-all | bytes 1310720 | tf_op jit(solution)/shard_map/all_to_all | solution.py:56
  48.8 17.9 %all-gather.6.cloned.1.call-done = bf16[4,640,512]{2,1,0:T(8,128)(2,1)} async-done(((bf16[1,640,512]{2,1,0:T(8,128)(2,1)}), bf16[4,640,512]{2,1,0:T(8,128)(2,1)}) %all-gather.6.cloned.1.call-update) | async-done | bytes 2621456 | tf_op jit(solution)/shard_map/all_gather | solution.py:59
  66.6 37.0 %all-gather.4.cloned.1.call-done = bf16[4,640,512]{2,1,0:T(8,128)(2,1)} async-done(((bf16[1,640,512]{2,1,0:T(8,128)(2,1)}), bf16[4,640,512]{2,1,0:T(8,128)(2,1)}) %all-gather.4.cloned.1.call-update) | async-done | bytes 2621456 | tf_op jit(solution)/shard_map/all_gather | solution.py:59
  103.6 5.2 %collective-permute-done = bf16[4,640,512]{2,1,0:T(8,128)(2,1)} collective-permute-done((bf16[4,640,512]{2,1,0:T(8,128)(2,1)}, bf16[4,640,512]{2,1,0:T(8,128)(2,1)}, u32[]{:S(2)}, u32[]{:S(2)}) %collective-permute-start) | collective-permute-done | bytes 2621472 | tf_op jit(solution)/shard_map/ppermute | solution.py:60
  108.9 6.5 %maximum_select_fusion = (bf16[4,2,640,512]{3,2,1,0:T(8,128)(2,1)S(1)}, bf16[4,2,640,512]{3,2,1,0:T(8,128)(2,1)S(1)}) fusion(bf16[4,1,640,512]{3,2,1,0:T(8,128)(2,1)} %bitcast.9, bf16[4,1,640,512]{3,2,1,0:T(8,128)(2,1)} %bitcast.132, pred[]{:T(512)S(6)} %eq.71, bf16[4,1,640,512]{3,2,1,0:T(8,128)(2,1)} %bitcast.131, bf16[4,1,640,512]{3,2,1,0:T(8,128)(2,1)S(1)} %bitcast.133), kind=kLoop, calls=%fused_computation.1 | loop fusion | flops 15728640 | bytes 20971520 | tf_op jit(solution)/shard_map/jit(_where)/select_n | solution.py:61
  115.7 2.9 %convolution_bitcast_fusion = f32[640,512]{1,0:T(8,128)S(1)} fusion(bf16[8,640,512]{2,1,0:T(8,128)(2,1)S(1)} %bitcast.122, bf16[8,512,512]{2,1,0:T(8,128)(2,1)S(1)} %bitcast.129), kind=kOutput, calls=%fused_computation.20 | convolution fusion | flops 2684354560 | bytes 10747904 | tf_op jit(solution)/shard_map/dot_general | solution.py:87
  118.5 2.4 copy-done.2
  120.9 2.9 %convolution_bitcast_fusion.1 = f32[640,512]{1,0:T(8,128)S(1)} fusion(bf16[8,640,512]{2,1,0:T(8,128)(2,1)S(1)} %bitcast.123, bf16[8,512,512]{2,1,0:T(8,128)(2,1)S(1)} %bitcast.117), kind=kOutput, calls=%fused_computation.21 | convolution fusion | flops 2684354560 | bytes 10747904 | tf_op jit(solution)/shard_map/dot_general | solution.py:86
  123.8 4.2 %fusion.16 = (bf16[640,512,1]{1,0,2:T(8,128)(2,1)S(1)}, bf16[640,512]{1,0:T(8,128)(2,1)}, bf16[640,512,1]{1,0,2:T(8,128)(2,1)S(1)}) fusion(f32[640,512]{1,0:T(8,128)S(1)} %convolution_bitcast_fusion.1, f32[640,512]{1,0:T(8,128)S(1)} %convolution_bitcast_fusion, bf16[8,640,512]{2,1,0:T(8,128)(2,1)S(1)} %bitcast.126, bf16[64,8,8,512]{3,2,1,0:T(8,128)(2,1)S(1)} %bitcast.146), kind=kOutput, calls=%fused_computation.33 | convolution fusion | flops 2689269760 | bytes 14024704 | tf_op jit(solution)/shard_map/dot_general | solution.py:117
  128.0 3.1 %fusion.8 = bf16[640,8,512]{2,0,1:T(8,128)(2,1)S(1)} fusion(bf16[640,512,1]{1,0,2:T(8,128)(2,1)S(1)} %get-tuple-element.40, bf16[64,8,8,512]{3,2,1,0:T(8,128)(2,1)S(1)} %bitcast.147), kind=kOutput, calls=%fused_computation.13 | convolution fusion | flops 2686976000 | bytes 10092544 | tf_op jit(solution)/shard_map/rh,hfd->frd/dot_general | solution.py:91
  131.2 2.4 copy-done.3
  133.6 1.7 dynamic-slice_bitcast_fusion.1
  135.4 5.0 %collective-permute-done.1 = bf16[4,640,512]{2,1,0:T(8,128)(2,1)S(1)} collective-permute-done((bf16[4,640,512]{2,1,0:T(8,128)(2,1)}, bf16[4,640,512]{2,1,0:T(8,128)(2,1)S(1)}, u32[]{:S(2)}, u32[]{:S(2)}) %collective-permute-start.1) | collective-permute-done | bytes 2621472 | tf_op jit(solution)/shard_map/ppermute | solution.py:69
  140.4 4.0 %fusion.1 = bf16[4,640,512]{2,1,0:T(8,128)(2,1)} fusion(bf16[4,640,512]{2,1,0:T(8,128)(2,1)S(1)} %collective-permute-done.1, bf16[4,2,640,512]{3,2,1,0:T(8,128)(2,1)} %bitcast.121, s32[]{:T(128)S(6)} %select_n.57), kind=kLoop, calls=%fused_computation.6 | loop fusion | flops 5242880 | bytes 7864324 | tf_op jit(solution)/shard_map/convert_element_type | solution.py:70
  144.6 5.1 %fusion.18 = f32[640,8,512]{2,0,1:T(8,128)S(1)} fusion(bf16[8,512,512]{2,1,0:T(8,128)(2,1)} %bitcast.116, bf16[640,512]{1,0:T(8,128)(2,1)} %get-tuple-element.39), kind=kOutput, calls=%fused_computation.35 | convolution fusion | flops 2684354560 | bytes 15335424 | tf_op jit(solution)/shard_map/rh,fdh->frd/dot_general | solution.py:132
  149.7 5.6 %add_convert_fusion = bf16[640,8,512]{2,0,1:T(8,128)(2,1)S(1)} fusion(f32[640,8,512]{2,0,1:T(8,128)S(1)} %fusion.18, bf16[640,512,1]{1,0,2:T(8,128)(2,1)S(1)} %get-tuple-element.38, bf16[8,512,512]{2,1,0:T(8,128)(2,1)} %bitcast.128), kind=kOutput, calls=%fused_computation | convolution fusion | flops 2689597440 | bytes 20578304 | tf_op jit(solution)/shard_map/rh,fdh->frd/dot_general | solution.py:135
  155.7 4.8 %collective-permute-done.3 = bf16[4,640,512]{2,1,0:T(8,128)(2,1)S(1)} collective-permute-done((bf16[4,640,512]{2,1,0:T(8,128)(2,1)S(1)}, bf16[4,640,512]{2,1,0:T(8,128)(2,1)S(1)}, u32[]{:S(2)}, u32[]{:S(2)}) %collective-permute-start.3) | collective-permute-done | bytes 2621472 | tf_op jit(solution)/shard_map/ppermute | solution.py:69
  160.5 2.4 fusion
  162.9 8.5 %convolution_convert_fusion = bf16[512,8,512]{0,2,1:T(8,128)(2,1)} fusion(bf16[640,512,1]{1,0,2:T(8,128)(2,1)S(1)} %copy-done.11, bf16[8,640,512]{2,1,0:T(8,128)(2,1)} %bitcast.127), kind=kOutput, calls=%fused_computation.14 | convolution fusion | flops 2686451712 | bytes 10092544 | tf_op jit(solution)/shard_map/rh,frd->hfd/dot_general | solution.py:129
  171.4 6.4 %copy.61 = bf16[512,4096]{1,0:T(8,128)(2,1)} copy(bf16[512,4096]{0,1:T(8,128)(2,1)} %bitcast.130) | data formatting | bytes 8388608
  177.8 7.6 %convolution_convert_fusion.2 = bf16[8,512,512]{2,1,0:T(8,128)(2,1)} fusion(bf16[8,640,512]{2,1,0:T(8,128)(2,1)} %bitcast.124, bf16[640,512]{1,0:T(8,128)(2,1)S(1)} %copy-done.7), kind=kOutput, calls=%fused_computation.16 | convolution fusion | flops 2686451712 | bytes 10092544 | tf_op jit(solution)/shard_map/frd,rh->fdh/dot_general | solution.py:123
  185.3 7.0 %all-to-all-start.1 = ((bf16[16,40,512]{2,1,0:T(8,128)(2,1)}), bf16[16,40,512]{2,1,0:T(8,128)(2,1)S(1)}, u32[]{:S(2)}, u32[]{:S(2)}) async-start(bf16[16,40,512]{2,1,0:T(8,128)(2,1)} %bitcast.140), calls=%async_computation.2 | async-start | bytes 1310720 | tf_op jit(solution)/shard_map/all_to_all | solution.py:71
  192.4 7.6 %convolution_convert_fusion.1 = bf16[8,512,512]{2,1,0:T(8,128)(2,1)} fusion(bf16[8,640,512]{2,1,0:T(8,128)(2,1)} %bitcast.125, bf16[640,512,1]{1,0,2:T(8,128)(2,1)S(1)} %get-tuple-element.38), kind=kOutput, calls=%fused_computation.15 | convolution fusion | flops 2686451712 | bytes 10092544 | tf_op jit(solution)/shard_map/frd,rh->fdh/dot_general | solution.py:126
  200.0 14.6 %reduce-scatter.5.cloned.1.call-done = bf16[1,640,512]{2,1,0:T(8,128)(2,1)} async-done(((bf16[4,640,512]{2,1,0:T(8,128)(2,1)}), bf16[1,640,512]{2,1,0:T(8,128)(2,1)}) %reduce-scatter.5.cloned.1.call-update) | async-done | bytes 655376 | tf_op jit(solution)/shard_map/reduce_scatter | solution.py:70
  214.6 7.0 %all-to-all-start.3 = ((bf16[16,40,512]{2,1,0:T(8,128)(2,1)}), bf16[16,40,512]{2,1,0:T(8,128)(2,1)S(1)}, u32[]{:S(2)}, u32[]{:S(2)}) async-start(bf16[16,40,512]{2,1,0:T(8,128)(2,1)} %bitcast.141), calls=%async_computation.5 | async-start | bytes 1310720 | tf_op jit(solution)/shard_map/all_to_all | solution.py:71
  222.1 1.1 fusion.20
  223.3 8.6 %all-gather = f32[1024,2]{0,1:T(2,128)S(1)} all-gather(f32[128,2]{0,1:T(2,128)S(1)} %pad_maximum_fusion), channel_id=2, replica_groups=mesh['dp'=16,'fy'=4,'fc'=2] {'fy','fc'}, dimensions={0}, use_global_device_ids=true | all-gather | bytes 9216 | tf_op jit(solution)/shard_map/all_gather | solution.py:115
  232.4 2.0 all-to-all-done.3
  234.6 1.1 convolution_convert_fusion.5
  (59 shorter events, 5.9 us)
Async XLA Ops:
  7.2 26.0 %copy-start = (bf16[128,512]{1,0:T(8,128)(2,1)S(1)}, bf16[128,512]{1,0:T(8,128)(2,1)}, u32[]{:S(2)}) copy-start(bf16[128,512]{1,0:T(8,128)(2,1)} %param.7) | copy-start | bytes 393220
  7.2 59.5 %all-gather.6.cloned.1.call-start = ((), (), s32[]{:S(2)}) async-start(), calls=%async_computation.8 | async-start | bytes 3276800 | tf_op jit(solution)/shard_map/all_gather | solution.py:59
  33.1 70.5 %all-gather.4.cloned.1.call-start = ((), (), s32[]{:S(2)}) async-start(), calls=%async_computation.6 | async-start | bytes 3276800 | tf_op jit(solution)/shard_map/all_gather | solution.py:59
  48.7 136.6 %reduce-scatter.3.cloned.1.call-start = ((), (), s32[]{:S(2)}) async-start(), calls=%async_computation.7 | async-start | bytes 3276800 | tf_op jit(solution)/shard_map/reduce_scatter | solution.py:70
  66.6 37.0 %collective-permute-start.2 = (bf16[4,640,512]{2,1,0:T(8,128)(2,1)}, bf16[4,640,512]{2,1,0:T(8,128)(2,1)S(1)}, u32[]{:S(2)}, u32[]{:S(2)}) collective-permute-start(bf16[4,640,512]{2,1,0:T(8,128)(2,1)} %all-gather.6.cloned.1.call-done), channel_id=1, source_target_pairs={{0,1},{1,0},{2,3},{3,2},{4,5},{5,4},{6,7},{7,6},{8,9},{9,8},{10,11... | collective-permute-start | bytes 7864328 | tf_op jit(solution)/shard_map/ppermute | solution.py:60
  103.6 5.3 %collective-permute-start = (bf16[4,640,512]{2,1,0:T(8,128)(2,1)}, bf16[4,640,512]{2,1,0:T(8,128)(2,1)}, u32[]{:S(2)}, u32[]{:S(2)}) collective-permute-start(bf16[4,640,512]{2,1,0:T(8,128)(2,1)} %all-gather.4.cloned.1.call-done), channel_id=1, source_target_pairs={{0,1},{1,0},{2,3},{3,2},{4,5},{5,4},{6,7},{7,6},{8,9},{9,8},{10,11... | collective-permute-start | bytes 7864328 | tf_op jit(solution)/shard_map/ppermute | solution.py:60
  108.9 6.8 %copy-start.6 = (bf16[4096,512]{1,0:T(8,128)(2,1)S(1)}, bf16[4096,512]{1,0:T(8,128)(2,1)}, u32[]{:S(2)}) copy-start(bf16[4096,512]{1,0:T(8,128)(2,1)} %param.11) | copy-start | bytes 12582916
  115.4 3.2 %copy-start.4 = (bf16[4,2,640,512]{3,2,1,0:T(8,128)(2,1)}, bf16[4,2,640,512]{3,2,1,0:T(8,128)(2,1)S(1)}, u32[]{:S(2)}) copy-start(bf16[4,2,640,512]{3,2,1,0:T(8,128)(2,1)S(1)} %get-tuple-element.46) | copy-start | bytes 15728644
  115.4 8.4 %copy-start.5 = (bf16[4,2,640,512]{3,2,1,0:T(8,128)(2,1)}, bf16[4,2,640,512]{3,2,1,0:T(8,128)(2,1)S(1)}, u32[]{:S(2)}) copy-start(bf16[4,2,640,512]{3,2,1,0:T(8,128)(2,1)S(1)} %get-tuple-element.47) | copy-start | bytes 15728644
  115.7 5.2 %copy-start.2 = (bf16[4096,512]{1,0:T(8,128)(2,1)S(1)}, bf16[4096,512]{1,0:T(8,128)(2,1)}, u32[]{:S(2)}) copy-start(bf16[4096,512]{1,0:T(8,128)(2,1)} %param.10) | copy-start | bytes 12582916
  120.9 2.9 %copy-start.9 = (bf16[512,4096]{1,0:T(8,128)(2,1)S(1)}, bf16[512,4096]{1,0:T(8,128)(2,1)}, u32[]{:S(2)}) copy-start(bf16[512,4096]{1,0:T(8,128)(2,1)} %param.12) | copy-start | bytes 12582916
  128.0 3.2 %copy-start.10 = (bf16[640,512,1]{1,0,2:T(8,128)(2,1)}, bf16[640,512,1]{1,0,2:T(8,128)(2,1)S(1)}, u32[]{:S(2)}) copy-start(bf16[640,512,1]{1,0,2:T(8,128)(2,1)S(1)} %get-tuple-element.40) | copy-start | bytes 1966084
  131.2 2.4 copy-start.3
  135.2 5.1 %collective-permute-start.1 = (bf16[4,640,512]{2,1,0:T(8,128)(2,1)}, bf16[4,640,512]{2,1,0:T(8,128)(2,1)S(1)}, u32[]{:S(2)}, u32[]{:S(2)}) collective-permute-start(bf16[4,640,512]{2,1,0:T(8,128)(2,1)} %dynamic-slice_bitcast_fusion.1), channel_id=1, source_target_pairs={{0,1},{1,0},{2,3},{3,2},{4,5},{5,4},{6,7},{7,6},{8,9},{9,8},{10,11... | collective-permute-start | bytes 7864328 | tf_op jit(solution)/shard_map/ppermute | solution.py:69
  144.4 70.2 %reduce-scatter.5.cloned.1.call-start = ((), (), s32[]{:S(2)}) async-start(), calls=%async_computation.9 | async-start | bytes 3276800 | tf_op jit(solution)/shard_map/reduce_scatter | solution.py:70
  155.5 7.4 %copy-start.11 = (bf16[640,512,1]{1,0,2:T(8,128)(2,1)S(1)}, bf16[640,512,1]{1,0,2:T(8,128)(2,1)}, u32[]{:S(2)}) copy-start(bf16[640,512,1]{1,0,2:T(8,128)(2,1)} %copy-done.10) | copy-start | bytes 1966084
  155.5 5.0 %collective-permute-start.3 = (bf16[4,640,512]{2,1,0:T(8,128)(2,1)S(1)}, bf16[4,640,512]{2,1,0:T(8,128)(2,1)S(1)}, u32[]{:S(2)}, u32[]{:S(2)}) collective-permute-start(bf16[4,640,512]{2,1,0:T(8,128)(2,1)S(1)} %dynamic-slice_bitcast_fusion), channel_id=1, source_target_pairs={{0,1},{1,0},{2,3},{3,2},{4,5},{5,4},{6,7},{7,6},{8,9},{9,8},{10,11... | collective-permute-start | bytes 7864328 | tf_op jit(solution)/shard_map/ppermute | solution.py:69
  171.4 6.4 %copy-start.7 = (bf16[640,512]{1,0:T(8,128)(2,1)S(1)}, bf16[640,512]{1,0:T(8,128)(2,1)}, u32[]{:S(2)}) copy-start(bf16[640,512]{1,0:T(8,128)(2,1)} %get-tuple-element.39) | copy-start | bytes 1966084
  185.3 29.2 %all-to-all-start.1 = ((bf16[16,40,512]{2,1,0:T(8,128)(2,1)}), bf16[16,40,512]{2,1,0:T(8,128)(2,1)S(1)}, u32[]{:S(2)}, u32[]{:S(2)}) async-start(bf16[16,40,512]{2,1,0:T(8,128)(2,1)} %bitcast.140), calls=%async_computation.2 | async-start | bytes 1310720 | tf_op jit(solution)/shard_map/all_to_all | solution.py:71
  192.3 29.8 %copy-start.8 = (bf16[128,512]{1,0:T(8,128)(2,1)S(1)}, bf16[128,512]{1,0:T(8,128)(2,1)}, u32[]{:S(2)}) copy-start(bf16[128,512]{1,0:T(8,128)(2,1)} %param.13) | copy-start | bytes 393220
  192.3 43.4 %copy-start.1 = (bf16[128,512]{1,0:T(8,128)(2,1)S(1)}, bf16[128,512]{1,0:T(8,128)(2,1)}, u32[]{:S(2)}) copy-start(bf16[128,512]{1,0:T(8,128)(2,1)} %param.7) | copy-start | bytes 393220
  214.6 19.9 %all-to-all-start.3 = ((bf16[16,40,512]{2,1,0:T(8,128)(2,1)}), bf16[16,40,512]{2,1,0:T(8,128)(2,1)S(1)}, u32[]{:S(2)}, u32[]{:S(2)}) async-start(bf16[16,40,512]{2,1,0:T(8,128)(2,1)} %bitcast.141), calls=%async_computation.5 | async-start | bytes 1310720 | tf_op jit(solution)/shard_map/all_to_all | solution.py:71
Sparse Core Ops, SparseCore 0:
  33.3 33.3 all-gather.5
  68.3 35.2 all-gather.3
  144.5 34.0 reduce-scatter.2
  180.8 33.6 reduce-scatter.4

commit v3 on v2

--- a/solution.py
+++ b/solution.py
@@ -56,18 +56,23 @@
         arrived = lax.all_to_all(
             place_rows(source, scaled), "dp", split_axis=0, concat_axis=0, tiled=True
         )
-        across = lax.all_gather(arrived.reshape(rows, feat), "fy", axis=0, tiled=False)
-        other = lax.ppermute(across, "fc", swap)
-        joined = jnp.where(core == 0, jnp.stack([across, other], axis=1),
-                           jnp.stack([other, across], axis=1))
-        return joined.reshape(fsdp_count, rows, feat)
+        mine = arrived.reshape(1, rows, feat)
+        across = lax.all_to_all(
+            jnp.broadcast_to(mine, (chips, rows, feat)), "fy", split_axis=0, concat_axis=0, tiled=True
+        )
+        both = lax.all_to_all(
+            jnp.broadcast_to(across[:, None], (chips, cores, rows, feat)),
+            "fc", split_axis=1, concat_axis=1, tiled=True,
+        )
+        return both.reshape(fsdp_count, rows, feat)
 
     def to_token_layout(partial_value):
         blocks = partial_value.astype(jnp.bfloat16).reshape(chips, cores, rows, feat)
         kept = lax.dynamic_index_in_dim(blocks, core, axis=1, keepdims=False)
         sent = lax.dynamic_index_in_dim(blocks, 1 - core, axis=1, keepdims=False)
         within = kept.astype(jnp.float32) + lax.ppermute(sent, "fc", swap).astype(jnp.float32)
-        shares = lax.psum_scatter(within.astype(jnp.bfloat16), "fy", scatter_dimension=0, tiled=False)
+        parts = lax.all_to_all(within.astype(jnp.bfloat16), "fy", split_axis=0, concat_axis=0, tiled=True)
+        shares = jnp.sum(parts.astype(jnp.float32), axis=0).astype(jnp.bfloat16)
         returned = lax.all_to_all(
             shares.reshape(dp_count, CAP, feat),
             "dp",

time: 243 us -> 285 us (1.17)
  blocking collectives: 44.3 us -> 66.5 us
  starting transfers between devices: 14.6 us -> 36.7 us
  local copies, waits for them, and re-layouts: 15.7 us -> 30.5 us
  between operations: 14 us -> 0.98 us
  waiting for transfers between devices: 86.6 us -> 82.3 us
    all_to_all x0 -> x5, waiting for transfers between devices: none -> 81.1 us  [the longest x2 36.1 us: to_token_layout(): lax.all_to_all(within.astype(jnp.bfloat16), 'fy', split_axis=0, concat_ax...]
    all_gather x2 -> x0, waiting for transfers between devices: 54.8 us -> none  [to_expert_layout(): lax.all_gather(arrived.reshape(rows, feat), 'fy', axis=0, tiled=False)]
    all_to_all x0 -> x2, blocking collectives: none -> 42.7 us  [the longest x1 33.6 us: to_expert_layout(): lax.all_to_all(jnp.broadcast_to(mine, (chips, rows, feat)), 'fy', split_a...]
    all_to_all x0 -> x5, starting transfers between devices: none -> 25.8 us  [the longest x2 8.22 us: to_token_layout(): lax.all_to_all(within.astype(jnp.bfloat16), 'fy', split_axis=0, concat_ax...]
    all_to_all x2 -> x1, blocking collectives: 35.7 us -> 14.9 us  [to_expert_layout(): lax.all_to_all(place_rows(source, scaled), 'dp', split_axis=0, concat_axi...]
    reduce_scatter x2 -> x0, waiting for transfers between devices: 14.6 us -> none  [to_token_layout(): lax.psum_scatter(within.astype(jnp.bfloat16), 'fy', scatter_dimension=0,...]
    ppermute x2, waiting for transfers between devices: 9.76 us -> 0.01 us  [to_token_layout(): lax.ppermute(sent, 'fc', swap).astype(jnp.float32)]
    select_n x1 -> x0, other arithmetic: 6.48 us -> none  [to_expert_layout(): jnp.where(core == 0, jnp.stack([across, other], axis=1), jnp.stack([other...]
  transfers between devices with their start and end apart: 10 -> 9, of which waited for: 7 -> 5; matrix products, arithmetic and copies ran while one was open for 19% -> 22% of each run, Pallas kernels for 0% -> 0%
where the time goes in v3:
time: 285 us; the launch traced here: 283 us
  waiting for transfers between devices  82.3 us (29%)
  blocking collectives  66.5 us (23%)
  matrix products  49.2 us (17%)
  starting transfers between devices  36.7 us (13%)
  local copies, waits for them, and re-layouts  30.5 us (11%)
  other arithmetic  16.5 us (6%)
    all_to_all x2, waiting for transfers between devices, to_token_layout(): lax.all_to_all(within.astype(jnp.bfloat16), 'fy', split_axis=0, concat_ax...  36.1 us
    all_to_all x1, blocking collectives, to_expert_layout(): lax.all_to_all(jnp.broadcast_to(mine, (chips, rows, feat)), 'fy', split_a...  33.6 us
    all_to_all x1, waiting for transfers between devices, to_expert_layout(): lax.all_to_all(jnp.broadcast_to(mine, (chips, rows, feat)), 'fy', split_a...  32.5 us
    all_to_all x1, blocking collectives, to_expert_layout(): lax.all_to_all(place_rows(source, scaled), 'dp', split_axis=0, concat_axi...  14.9 us
    unnamed x28, local copies, waits for them, and re-layouts  13.1 us
    all_to_all x1, waiting for transfers between devices, to_expert_layout(): lax.all_to_all(place_rows(source, scaled), 'dp', split_axis=0, concat_axi...  12.5 us
    all_to_all x2, starting transfers between devices, to_token_layout(): lax.all_to_all(shares.reshape(dp_count, CAP, feat), 'dp', split_axis=0, c...  10.4 us
    convert_element_type x2, other arithmetic, to_token_layout(): within.astype(jnp.bfloat16)  9.6 us
  transfers between devices with their start and end apart: 9, of which 5 were waited for; matrix products, arithmetic and copies ran while one was open for 22% of the time, Pallas kernels for 0%

profile of v3, /device:TPU:0, one launch (start us, length us, event | category | flops | bytes accessed | tf_op | source)
XLA Modules:
  0.0 282.6 jit_solution(912992188694771626)
XLA Ops:
  6.7 8.0 %all-to-all-start.5 = ((bf16[16,40,512]{2,1,0:T(8,128)(2,1)}), bf16[16,40,512]{2,1,0:T(8,128)(2,1)S(1)}, u32[]{:S(2)}, u32[]{:S(2)}) async-start(bf16[16,40,512]{2,1,0:T(8,128)(2,1)} %bitcast.24), calls=%async_computation.5 | async-start | bytes 1310720 | tf_op jit(solution)/shard_map/all_to_all | solution.py:56
  15.1 12.5 %all-to-all-done.5 = bf16[16,40,512]{2,1,0:T(8,128)(2,1)S(1)} async-done(((bf16[16,40,512]{2,1,0:T(8,128)(2,1)}), bf16[16,40,512]{2,1,0:T(8,128)(2,1)S(1)}, u32[]{:S(2)}, u32[]{:S(2)}) %all-to-all-start.5) | async-done | bytes 655392 | tf_op jit(solution)/shard_map/all_to_all | solution.py:56
  27.7 14.9 %all_to_all.50 = bf16[16,40,512]{2,1,0:T(8,128)(2,1)S(1)} all-to-all(bf16[16,40,512]{2,1,0:T(8,128)(2,1)S(1)} %bitcast.126), channel_id=1, replica_groups=mesh['dp'=16,'fy'=4,'fc'=2] {'dp'}, dimensions={0} | all-to-all | bytes 1310720 | tf_op jit(solution)/shard_map/all_to_all | solution.py:56
  42.7 33.6 %all_to_all.51 = bf16[4,640,512]{2,1,0:T(8,128)(2,1)S(1)} all-to-all(bf16[4,640,512]{2,1,0:T(8,128)(2,1)S(1)} %broadcast_in_dim.62), channel_id=1, replica_groups=mesh['dp'=16,'fy'=4,'fc'=2] {'fy'}, dimensions={0} | all-to-all | bytes 5242880 | tf_op jit(solution)/shard_map/all_to_all | solution.py:60
  76.8 9.1 %all_to_all.52 = bf16[4,2,640,512]{3,2,0,1:T(8,128)(2,1)} all-to-all(bf16[4,2,640,512]{3,2,0,1:T(8,128)(2,1)S(1)} %broadcast_in_dim.63), channel_id=1, replica_groups=mesh['dp'=16,'fy'=4,'fc'=2] {'fc'}, dimensions={1} | all-to-all | bytes 10485760 | tf_op jit(solution)/shard_map/all_to_all | solution.py:63
  87.6 3.7 %all-to-all-start.1 = ((bf16[4,640,512]{2,1,0:T(8,128)(2,1)}), bf16[4,640,512]{2,1,0:T(8,128)(2,1)S(1)}, u32[]{:S(2)}, u32[]{:S(2)}) async-start(bf16[4,640,512]{2,1,0:T(8,128)(2,1)} %broadcast_in_dim.55), calls=%async_computation.1 | async-start | bytes 5242880 | tf_op jit(solution)/shard_map/all_to_all | solution.py:60
  91.2 32.5 %all-to-all-done.1 = bf16[4,640,512]{2,1,0:T(8,128)(2,1)S(1)} async-done(((bf16[4,640,512]{2,1,0:T(8,128)(2,1)}), bf16[4,640,512]{2,1,0:T(8,128)(2,1)S(1)}, u32[]{:S(2)}, u32[]{:S(2)}) %all-to-all-start.1) | async-done | bytes 2621472 | tf_op jit(solution)/shard_map/all_to_all | solution.py:60
  123.7 2.9 %broadcast_in_dim.56 = bf16[4,2,640,512]{3,2,0,1:T(8,128)(2,1)} broadcast(bf16[4,640,512]{2,1,0:T(8,128)(2,1)S(1)} %all-to-all-done.1), dimensions={0,2,3} | broadcast | bytes 7864320 | tf_op jit(solution)/shard_map/broadcast_in_dim | solution.py:64
  126.6 6.0 %all-to-all-start.2 = ((bf16[4,2,640,512]{3,2,0,1:T(8,128)(2,1)}), bf16[4,2,640,512]{3,2,0,1:T(8,128)(2,1)}, u32[]{:S(2)}, u32[]{:S(2)}) async-start(bf16[4,2,640,512]{3,2,0,1:T(8,128)(2,1)} %broadcast_in_dim.56), calls=%async_computation.2 | async-start | bytes 10485760 | tf_op jit(solution)/shard_map/all_to_all | solution.py:63
  132.6 3.2 %copy.68 = bf16[4,2,640,512]{3,2,1,0:T(8,128)(2,1)S(1)} copy(bf16[4,2,640,512]{3,2,0,1:T(8,128)(2,1)} %all_to_all.52) | data formatting | bytes 10485760 | tf_op jit(solution)/shard_map/all_to_all | solution.py:63
  138.1 2.9 %fusion.11 = f32[640,512]{1,0:T(8,128)S(1)} fusion(bf16[8,640,512]{2,1,0:T(8,128)(2,1)S(1)} %bitcast.118, bf16[64,8,8,512]{3,2,1,0:T(8,128)(2,1)S(1)} %bitcast.134), kind=kOutput, calls=%fused_computation.17 | convolution fusion | flops 2684354560 | bytes 10747904 | tf_op jit(solution)/shard_map/dot_general | solution.py:122
  141.1 3.2 %copy.66 = bf16[4,2,640,512]{3,2,1,0:T(8,128)(2,1)S(1)} copy(bf16[4,2,640,512]{3,2,0,1:T(8,128)(2,1)} %all-to-all-done.2) | data formatting | bytes 10485760 | tf_op jit(solution)/shard_map/all_to_all | solution.py:63
  144.8 2.9 %convolution_bitcast_fusion = f32[640,512]{1,0:T(8,128)S(1)} fusion(bf16[8,640,512]{2,1,0:T(8,128)(2,1)S(1)} %bitcast.114, bf16[8,512,512]{2,1,0:T(8,128)(2,1)S(1)} %bitcast.123), kind=kOutput, calls=%fused_computation.18 | convolution fusion | flops 2684354560 | bytes 10747904 | tf_op jit(solution)/shard_map/dot_general | solution.py:92
  148.3 3.5 %fusion.16 = (bf16[640,512,1]{1,0,2:T(8,128)(2,1)S(1)}, bf16[640,512]{1,0:T(8,128)(2,1)S(1)}, bf16[640,512,1]{1,0,2:T(8,128)(2,1)S(1)}) fusion(f32[640,512]{1,0:T(8,128)S(1)} %fusion.11, f32[640,512]{1,0:T(8,128)S(1)} %convolution_bitcast_fusion, bf16[8,640,512]{2,1,0:T(8,128)(2,1)S(1)} %bitcast.115, bf16[8,512,512]{2,1,0:T(8,128)(2,1)S(1)} %bitcast.110), kind=kOutput, calls=%fused_computation.31 | convolution fusion | flops 2689269760 | bytes 14024704 | tf_op jit(solution)/shard_map/dot_general | solution.py:91
  151.8 3.2 %fusion.8 = bf16[640,8,512]{2,0,1:T(8,128)(2,1)S(1)} fusion(bf16[640,512,1]{1,0,2:T(8,128)(2,1)S(1)} %get-tuple-element.46, bf16[64,8,8,512]{3,2,1,0:T(8,128)(2,1)S(1)} %bitcast.135), kind=kOutput, calls=%fused_computation.11 | convolution fusion | flops 2686976000 | bytes 10092544 | tf_op jit(solution)/shard_map/rh,hfd->frd/dot_general | solution.py:96
  157.3 2.9 %fusion.18 = f32[640,8,512]{2,0,1:T(8,128)S(1)} fusion(bf16[8,512,512]{2,1,0:T(8,128)(2,1)S(1)} %bitcast.111, bf16[640,512]{1,0:T(8,128)(2,1)S(1)} %get-tuple-element.45), kind=kOutput, calls=%fused_computation.33 | convolution fusion | flops 2684354560 | bytes 15335424 | tf_op jit(solution)/shard_map/rh,fdh->frd/dot_general | solution.py:137
  160.2 5.6 %add_convert_fusion = bf16[640,8,512]{2,0,1:T(8,128)(2,1)S(1)} fusion(f32[640,8,512]{2,0,1:T(8,128)S(1)} %fusion.18, bf16[640,512,1]{1,0,2:T(8,128)(2,1)S(1)} %get-tuple-element.44, bf16[8,512,512]{2,1,0:T(8,128)(2,1)} %bitcast.122), kind=kOutput, calls=%fused_computation | convolution fusion | flops 2689597440 | bytes 20578304 | tf_op jit(solution)/shard_map/rh,fdh->frd/dot_general | solution.py:140
  165.8 2.4 copy-done.2
  169.8 4.8 %fusion.1 = bf16[4,640,512]{2,1,0:T(8,128)(2,1)} fusion(bf16[4,640,512]{2,1,0:T(8,128)(2,1)} %collective-permute-done, bf16[4,2,640,512]{3,2,1,0:T(8,128)(2,1)} %bitcast.121, s32[]{:T(128)S(6)} %select_n.16), kind=kLoop, calls=%fused_computation.4 | loop fusion | flops 5242880 | bytes 7864324 | tf_op jit(solution)/shard_map/convert_element_type | solution.py:74
  174.6 3.7 %all-to-all-start.3 = ((bf16[4,640,512]{2,1,0:T(8,128)(2,1)}), bf16[4,640,512]{2,1,0:T(8,128)(2,1)S(1)}, u32[]{:S(2)}, u32[]{:S(2)}) async-start(bf16[4,640,512]{2,1,0:T(8,128)(2,1)} %fusion.1), calls=%async_computation.3 | async-start | bytes 5242880 | tf_op jit(solution)/shard_map/all_to_all | solution.py:74
  178.3 4.8 %fusion = bf16[4,640,512]{2,1,0:T(8,128)(2,1)} fusion(bf16[4,640,512]{2,1,0:T(8,128)(2,1)} %collective-permute-done.1, bf16[4,2,640,512]{3,2,1,0:T(8,128)(2,1)} %bitcast.109, s32[]{:T(128)S(6)} %select_n.16), kind=kLoop, calls=%fused_computation.2 | loop fusion | flops 5242880 | bytes 7864324 | tf_op jit(solution)/shard_map/convert_element_type | solution.py:74
  183.1 28.0 %all-to-all-done.3 = bf16[4,640,512]{2,1,0:T(8,128)(2,1)S(1)} async-done(((bf16[4,640,512]{2,1,0:T(8,128)(2,1)}), bf16[4,640,512]{2,1,0:T(8,128)(2,1)S(1)}, u32[]{:S(2)}, u32[]{:S(2)}) %all-to-all-start.3) | async-done | bytes 2621472 | tf_op jit(solution)/shard_map/all_to_all | solution.py:74
  211.1 4.6 %all-to-all-start.8 = ((bf16[4,640,512]{2,1,0:T(8,128)(2,1)}), bf16[4,640,512]{2,1,0:T(8,128)(2,1)}, u32[]{:S(2)}, u32[]{:S(2)}) async-start(bf16[4,640,512]{2,1,0:T(8,128)(2,1)} %fusion), calls=%async_computation.8 | async-start | bytes 5242880 | tf_op jit(solution)/shard_map/all_to_all | solution.py:74
  215.7 8.2 %convolution_convert_fusion = bf16[512,8,512]{0,2,1:T(8,128)(2,1)} fusion(bf16[640,512,1]{1,0,2:T(8,128)(2,1)} %copy-done.12, bf16[8,640,512]{2,1,0:T(8,128)(2,1)} %bitcast.119), kind=kOutput, calls=%fused_computation.12 | convolution fusion | flops 2686451712 | bytes 10092544 | tf_op jit(solution)/shard_map/rh,frd->hfd/dot_general | solution.py:134
  223.9 6.3 %copy.73 = bf16[512,4096]{1,0:T(8,128)(2,1)} copy(bf16[512,4096]{0,1:T(8,128)(2,1)} %bitcast.124) | data formatting | bytes 8388608
  230.2 8.1 %convolution_convert_fusion.2 = bf16[8,512,512]{2,1,0:T(8,128)(2,1)} fusion(bf16[8,640,512]{2,1,0:T(8,128)(2,1)} %bitcast.116, bf16[640,512]{1,0:T(8,128)(2,1)} %copy-done.8), kind=kOutput, calls=%fused_computation.14 | convolution fusion | flops 2686451712 | bytes 10092544 | tf_op jit(solution)/shard_map/frd,rh->fdh/dot_general | solution.py:128
  239.8 8.1 %all-to-all-done.8 = bf16[4,640,512]{2,1,0:T(8,128)(2,1)} async-done(((bf16[4,640,512]{2,1,0:T(8,128)(2,1)}), bf16[4,640,512]{2,1,0:T(8,128)(2,1)}, u32[]{:S(2)}, u32[]{:S(2)}) %all-to-all-start.8) | async-done | bytes 2621472 | tf_op jit(solution)/shard_map/all_to_all | solution.py:74
  247.9 4.3 %all-to-all-start.4 = ((bf16[16,40,512]{2,1,0:T(8,128)(2,1)}), bf16[16,40,512]{2,1,0:T(8,128)(2,1)S(1)}, u32[]{:S(2)}, u32[]{:S(2)}) async-start(bf16[16,40,512]{2,1,0:T(8,128)(2,1)} %bitcast.19), calls=%async_computation.4 | async-start | bytes 1310720 | tf_op jit(solution)/shard_map/all_to_all | solution.py:76
  252.1 7.5 %convolution_convert_fusion.1 = bf16[8,512,512]{2,1,0:T(8,128)(2,1)} fusion(bf16[8,640,512]{2,1,0:T(8,128)(2,1)} %bitcast.117, bf16[640,512,1]{1,0,2:T(8,128)(2,1)S(1)} %get-tuple-element.44), kind=kOutput, calls=%fused_computation.13 | convolution fusion | flops 2686451712 | bytes 10092544 | tf_op jit(solution)/shard_map/frd,rh->fdh/dot_general | solution.py:131
  259.7 3.2 %reduce_sum.84 = bf16[640,512]{1,0:T(8,128)(2,1)} reduce(bf16[4,640,512]{2,1,0:T(8,128)(2,1)} %all-to-all-done.8, bf16[]{:T(256)} %constant.32.clone.1), dimensions={0}, to_apply=%region_5.6 | reduce | flops 983040 | bytes 3276802 | tf_op jit(solution)/shard_map/reduce_sum | solution.py:75
  264.0 6.1 %all-to-all-start.9 = ((bf16[16,40,512]{2,1,0:T(8,128)(2,1)}), bf16[16,40,512]{2,1,0:T(8,128)(2,1)S(1)}, u32[]{:S(2)}, u32[]{:S(2)}) async-start(bf16[16,40,512]{2,1,0:T(8,128)(2,1)} %bitcast.35), calls=%async_computation.9 | async-start | bytes 1310720 | tf_op jit(solution)/shard_map/all_to_all | solution.py:76
  271.8 9.0 %all-gather = f32[1024,2]{0,1:T(2,128)S(1)} all-gather(f32[128,2]{0,1:T(2,128)S(1)} %pad_maximum_fusion), channel_id=2, replica_groups=mesh['dp'=16,'fy'=4,'fc'=2] {'fy','fc'}, dimensions={0}, use_global_device_ids=true | all-gather | bytes 9216 | tf_op jit(solution)/shard_map/all_gather | solution.py:120
  (63 shorter events, 22.4 us)
Async XLA Ops:
  0.6 14.1 %copy-start = (bf16[128,512]{1,0:T(8,128)(2,1)S(1)}, bf16[128,512]{1,0:T(8,128)(2,1)}, u32[]{:S(2)}) copy-start(bf16[128,512]{1,0:T(8,128)(2,1)} %param.7) | copy-start | bytes 393220
  6.7 20.9 %all-to-all-start.5 = ((bf16[16,40,512]{2,1,0:T(8,128)(2,1)}), bf16[16,40,512]{2,1,0:T(8,128)(2,1)S(1)}, u32[]{:S(2)}, u32[]{:S(2)}) async-start(bf16[16,40,512]{2,1,0:T(8,128)(2,1)} %bitcast.24), calls=%async_computation.5 | async-start | bytes 1310720 | tf_op jit(solution)/shard_map/all_to_all | solution.py:56
  87.6 36.2 %all-to-all-start.1 = ((bf16[4,640,512]{2,1,0:T(8,128)(2,1)}), bf16[4,640,512]{2,1,0:T(8,128)(2,1)S(1)}, u32[]{:S(2)}, u32[]{:S(2)}) async-start(bf16[4,640,512]{2,1,0:T(8,128)(2,1)} %broadcast_in_dim.55), calls=%async_computation.1 | async-start | bytes 5242880 | tf_op jit(solution)/shard_map/all_to_all | solution.py:60
  126.6 14.5 %all-to-all-start.2 = ((bf16[4,2,640,512]{3,2,0,1:T(8,128)(2,1)}), bf16[4,2,640,512]{3,2,0,1:T(8,128)(2,1)}, u32[]{:S(2)}, u32[]{:S(2)}) async-start(bf16[4,2,640,512]{3,2,0,1:T(8,128)(2,1)} %broadcast_in_dim.56), calls=%async_computation.2 | async-start | bytes 10485760 | tf_op jit(solution)/shard_map/all_to_all | solution.py:63
  132.6 5.6 %copy-start.10 = (bf16[512,4096]{1,0:T(8,128)(2,1)S(1)}, bf16[512,4096]{1,0:T(8,128)(2,1)}, u32[]{:S(2)}) copy-start(bf16[512,4096]{1,0:T(8,128)(2,1)} %param.12) | copy-start | bytes 12582916
  135.8 2.3 copy-start.5
  141.0 3.7 %copy-start.7 = (bf16[4096,512]{1,0:T(8,128)(2,1)S(1)}, bf16[4096,512]{1,0:T(8,128)(2,1)}, u32[]{:S(2)}) copy-start(bf16[4096,512]{1,0:T(8,128)(2,1)} %param.11) | copy-start | bytes 12582916
  144.3 3.4 %copy-start.4 = (bf16[4,2,640,512]{3,2,1,0:T(8,128)(2,1)}, bf16[4,2,640,512]{3,2,1,0:T(8,128)(2,1)S(1)}, u32[]{:S(2)}) copy-start(bf16[4,2,640,512]{3,2,1,0:T(8,128)(2,1)S(1)} %copy.66) | copy-start | bytes 15728644
  144.8 3.5 %copy-start.3 = (bf16[4096,512]{1,0:T(8,128)(2,1)S(1)}, bf16[4096,512]{1,0:T(8,128)(2,1)}, u32[]{:S(2)}) copy-start(bf16[4096,512]{1,0:T(8,128)(2,1)} %param.10) | copy-start | bytes 12582916
  148.3 3.5 %copy-start.11 = (bf16[512,4096]{1,0:T(8,128)(2,1)S(1)}, bf16[512,4096]{1,0:T(8,128)(2,1)}, u32[]{:S(2)}) copy-start(bf16[512,4096]{1,0:T(8,128)(2,1)} %param.12) | copy-start | bytes 12582916
  151.8 3.2 %copy-start.12 = (bf16[640,512,1]{1,0,2:T(8,128)(2,1)}, bf16[640,512,1]{1,0,2:T(8,128)(2,1)S(1)}, u32[]{:S(2)}) copy-start(bf16[640,512,1]{1,0,2:T(8,128)(2,1)S(1)} %get-tuple-element.46) | copy-start | bytes 1966084
  151.8 5.5 %copy-start.8 = (bf16[640,512]{1,0:T(8,128)(2,1)}, bf16[640,512]{1,0:T(8,128)(2,1)S(1)}, u32[]{:S(2)}) copy-start(bf16[640,512]{1,0:T(8,128)(2,1)S(1)} %get-tuple-element.45) | copy-start | bytes 1966084
  155.0 5.2 %copy-start.6 = (bf16[640,8,512]{2,0,1:T(8,128)(2,1)}, bf16[640,8,512]{2,0,1:T(8,128)(2,1)S(1)}, u32[]{:S(2)}) copy-start(bf16[640,8,512]{2,0,1:T(8,128)(2,1)S(1)} %fusion.8) | copy-start | bytes 15728644
  156.8 13.0 %collective-permute-start = (bf16[4,640,512]{2,1,0:T(8,128)(2,1)}, bf16[4,640,512]{2,1,0:T(8,128)(2,1)}, u32[]{:S(2)}, u32[]{:S(2)}) collective-permute-start(bf16[4,640,512]{2,1,0:T(8,128)(2,1)} %dynamic-slice_bitcast_fusion.1), channel_id=1, source_target_pairs={{0,1},{1,0},{2,3},{3,2},{4,5},{5,4},{6,7},{7,6},{8,9},{9,8},{10,11... | collective-permute-start | bytes 7864328 | tf_op jit(solution)/shard_map/ppermute | solution.py:73
  165.8 2.4 copy-start.2
  169.8 8.5 %collective-permute-start.1 = (bf16[4,640,512]{2,1,0:T(8,128)(2,1)}, bf16[4,640,512]{2,1,0:T(8,128)(2,1)}, u32[]{:S(2)}, u32[]{:S(2)}) collective-permute-start(bf16[4,640,512]{2,1,0:T(8,128)(2,1)} %dynamic-slice_bitcast_fusion), channel_id=1, source_target_pairs={{0,1},{1,0},{2,3},{3,2},{4,5},{5,4},{6,7},{7,6},{8,9},{9,8},{10,11... | collective-permute-start | bytes 7864328 | tf_op jit(solution)/shard_map/ppermute | solution.py:73
  174.6 36.5 %all-to-all-start.3 = ((bf16[4,640,512]{2,1,0:T(8,128)(2,1)}), bf16[4,640,512]{2,1,0:T(8,128)(2,1)S(1)}, u32[]{:S(2)}, u32[]{:S(2)}) async-start(bf16[4,640,512]{2,1,0:T(8,128)(2,1)} %fusion.1), calls=%async_computation.3 | async-start | bytes 5242880 | tf_op jit(solution)/shard_map/all_to_all | solution.py:74
  211.1 36.7 %all-to-all-start.8 = ((bf16[4,640,512]{2,1,0:T(8,128)(2,1)}), bf16[4,640,512]{2,1,0:T(8,128)(2,1)}, u32[]{:S(2)}, u32[]{:S(2)}) async-start(bf16[4,640,512]{2,1,0:T(8,128)(2,1)} %fusion), calls=%async_computation.8 | async-start | bytes 5242880 | tf_op jit(solution)/shard_map/all_to_all | solution.py:74
  247.9 16.1 %all-to-all-start.4 = ((bf16[16,40,512]{2,1,0:T(8,128)(2,1)}), bf16[16,40,512]{2,1,0:T(8,128)(2,1)S(1)}, u32[]{:S(2)}, u32[]{:S(2)}) async-start(bf16[16,40,512]{2,1,0:T(8,128)(2,1)} %bitcast.19), calls=%async_computation.4 | async-start | bytes 1310720 | tf_op jit(solution)/shard_map/all_to_all | solution.py:76
  259.7 11.0 %copy-start.9 = (bf16[128,512]{1,0:T(8,128)(2,1)S(1)}, bf16[128,512]{1,0:T(8,128)(2,1)}, u32[]{:S(2)}) copy-start(bf16[128,512]{1,0:T(8,128)(2,1)} %param.13) | copy-start | bytes 393220
  259.7 23.0 %copy-start.1 = (bf16[128,512]{1,0:T(8,128)(2,1)S(1)}, bf16[128,512]{1,0:T(8,128)(2,1)}, u32[]{:S(2)}) copy-start(bf16[128,512]{1,0:T(8,128)(2,1)} %param.7) | copy-start | bytes 393220
  264.0 17.4 %all-to-all-start.9 = ((bf16[16,40,512]{2,1,0:T(8,128)(2,1)}), bf16[16,40,512]{2,1,0:T(8,128)(2,1)S(1)}, u32[]{:S(2)}, u32[]{:S(2)}) async-start(bf16[16,40,512]{2,1,0:T(8,128)(2,1)} %bitcast.35), calls=%async_computation.9 | async-start | bytes 1310720 | tf_op jit(solution)/shard_map/all_to_all | solution.py:76

commit v4 on v3

--- a/solution.py
+++ b/solution.py
@@ -56,10 +56,10 @@
         arrived = lax.all_to_all(
             place_rows(source, scaled), "dp", split_axis=0, concat_axis=0, tiled=True
         )
-        mine = arrived.reshape(1, rows, feat)
-        across = lax.all_to_all(
-            jnp.broadcast_to(mine, (chips, rows, feat)), "fy", split_axis=0, concat_axis=0, tiled=True
-        )
+        across = lax.all_gather(arrived.reshape(rows, feat), "fy", axis=0, tiled=False)
+        return across
+
+    def join_cores(across):
         both = lax.all_to_all(
             jnp.broadcast_to(across[:, None], (chips, cores, rows, feat)),
             "fc", split_axis=1, concat_axis=1, tiled=True,
@@ -71,8 +71,7 @@
         kept = lax.dynamic_index_in_dim(blocks, core, axis=1, keepdims=False)
         sent = lax.dynamic_index_in_dim(blocks, 1 - core, axis=1, keepdims=False)
         within = kept.astype(jnp.float32) + lax.ppermute(sent, "fc", swap).astype(jnp.float32)
-        parts = lax.all_to_all(within.astype(jnp.bfloat16), "fy", split_axis=0, concat_axis=0, tiled=True)
-        shares = jnp.sum(parts.astype(jnp.float32), axis=0).astype(jnp.bfloat16)
+        shares = lax.psum_scatter(within.astype(jnp.bfloat16), "fy", scatter_dimension=0, tiled=False)
         returned = lax.all_to_all(
             shares.reshape(dp_count, CAP, feat),
             "dp",
@@ -87,7 +86,7 @@
     down_w3 = w_down.reshape(hid, fsdp_count, feat)
     in_dims = (((0, 2), (0, 1)), ((), ()))
 
-    expert_rows = to_expert_layout(tokens, False)
+    expert_rows = join_cores(to_expert_layout(tokens, False))
     gate_proj = lax.dot_general(expert_rows, gate_w3, in_dims, preferred_element_type=jnp.float32)
     up_proj = lax.dot_general(expert_rows, up_w3, in_dims, preferred_element_type=jnp.float32)
     sigmoid_gate = jax.nn.sigmoid(gate_proj)
@@ -96,6 +95,8 @@
     out_partial = jnp.einsum(
         "rh,hfd->frd", hidden, down_w3, preferred_element_type=jnp.float32
     )
+    grad_across = to_expert_layout(out_grad, True)
+    out_partial, grad_across = lax.optimization_barrier((out_partial, grad_across))
     out_slots = to_token_layout(out_partial)
     first_pair = jnp.dot(
         select_first.astype(jnp.float32),
@@ -118,7 +119,7 @@
         axis=1,
     )
     prob_grad = jnp.sum(lax.all_gather(prob_terms, ("fy", "fc"), axis=0, tiled=False), axis=0)
-    grad_rows = to_expert_layout(out_grad, True)
+    grad_rows = join_cores(grad_across)
     hidden_grad = lax.dot_general(grad_rows, down_w3, (((0, 2), (1, 2)), ((), ())),
                                   preferred_element_type=jnp.float32)
     gate_grad = (

time: 285 us -> 230 us (0.81)
  waiting for transfers between devices: 82.3 us -> 52.1 us
  starting transfers between devices: 36.7 us -> 14.5 us
  between operations: 0.98 us -> 14.1 us
  other arithmetic: 16.5 us -> 7.29 us
  blocking collectives: 66.5 us -> 60.5 us
  local copies, waits for them, and re-layouts: 30.5 us -> 24.6 us
  matrix products: 49.2 us -> 55 us
    all_to_all x5 -> x0, waiting for transfers between devices: 81.1 us -> none  [the longest x2 36.1 us: to_token_layout(): lax.all_to_all(within.astype(jnp.bfloat16), 'fy', split_axis=0, concat_ax...]
    all_gather x0 -> x2, waiting for transfers between devices: none -> 27 us  [to_expert_layout(): lax.all_gather(arrived.reshape(rows, feat), 'fy', axis=0, tiled=False)]
    all_to_all x2, blocking collectives: 42.7 us -> 16.2 us  [join_cores(): lax.all_to_all(jnp.broadcast_to(across[:, None], (chips, cores, rows, fea...]
    all_to_all x5 -> x0, starting transfers between devices: 25.8 us -> none  [the longest x2 8.22 us: to_token_layout(): lax.all_to_all(within.astype(jnp.bfloat16), 'fy', split_axis=0, concat_ax...]
    all_to_all x1 -> x2, blocking collectives: 14.9 us -> 35.7 us  [to_expert_layout(): lax.all_to_all(place_rows(source, scaled), 'dp', split_axis=0, concat_axi...]
    all_to_all x2, waiting for transfers between devices: 1.13 us -> 11.2 us  [to_token_layout(): lax.all_to_all(shares.reshape(dp_count, CAP, feat), 'dp', split_axis=0, c...]
    reduce_scatter x0 -> x2, waiting for transfers between devices: none -> 9.02 us  [to_token_layout(): lax.psum_scatter(within.astype(jnp.bfloat16), 'fy', scatter_dimension=0,...]
    dot_general x1, matrix products: 2.9 us -> 7.85 us  [local(): lax.dot_general(grad_rows, down_w3, (((0, 2), (1, 2)), ((), ())), preferr...]
  transfers between devices with their start and end apart: 9 -> 8, of which waited for: 5 -> 5; matrix products, arithmetic and copies ran while one was open for 22% -> 31% of each run, Pallas kernels for 0% -> 0%
where the time goes in v4:
time: 230 us; the launch traced here: 228 us
  blocking collectives  60.5 us (26%)
  matrix products  55 us (24%)
  waiting for transfers between devices  52.1 us (23%)
  local copies, waits for them, and re-layouts  24.6 us (11%)
  starting transfers between devices  14.5 us (6%)
  between operations  14.1 us (6%)
  other arithmetic  7.29 us (3%)
    all_to_all x2, blocking collectives, to_expert_layout(): lax.all_to_all(place_rows(source, scaled), 'dp', split_axis=0, concat_axi...  35.7 us
    all_gather x2, waiting for transfers between devices, to_expert_layout(): lax.all_gather(arrived.reshape(rows, feat), 'fy', axis=0, tiled=False)  27 us
    all_to_all x2, blocking collectives, join_cores(): lax.all_to_all(jnp.broadcast_to(across[:, None], (chips, cores, rows, fea...  16.2 us
    all_to_all x2, starting transfers between devices, to_token_layout(): lax.all_to_all(shares.reshape(dp_count, CAP, feat), 'dp', split_axis=0, c...  13.9 us
    unnamed x30, local copies, waits for them, and re-layouts  11.7 us
    all_to_all x2, waiting for transfers between devices, to_token_layout(): lax.all_to_all(shares.reshape(dp_count, CAP, feat), 'dp', split_axis=0, c...  11.2 us
    reduce_scatter x2, waiting for transfers between devices, to_token_layout(): lax.psum_scatter(within.astype(jnp.bfloat16), 'fy', scatter_dimension=0,...  9.02 us
    all_gather x1, blocking collectives, local(): lax.all_gather(prob_terms, ('fy', 'fc'), axis=0, tiled=False)  8.61 us
  transfers between devices with their start and end apart: 8, of which 5 were waited for; matrix products, arithmetic and copies ran while one was open for 31% of the time, Pallas kernels for 0%

profile of v4, /device:TPU:0, one launch (start us, length us, event | category | flops | bytes accessed | tf_op | source)
XLA Modules:
  0.0 228.1 jit_solution(482641025060720502)
XLA Ops:
  10.6 20.6 %all_to_all.30 = bf16[16,40,512]{2,1,0:T(8,128)(2,1)} all-to-all(bf16[16,40,512]{2,1,0:T(8,128)(2,1)S(1)} %bitcast.132), channel_id=1, replica_groups=mesh['dp'=16,'fy'=4,'fc'=2] {'dp'}, dimensions={0} | all-to-all | bytes 1310720 | tf_op jit(solution)/shard_map/all_to_all | solution.py:56
  32.1 1.5 convolution_convert_fusion.3
  33.6 15.1 %all_to_all.31 = bf16[16,40,512]{2,1,0:T(8,128)(2,1)} all-to-all(bf16[16,40,512]{2,1,0:T(8,128)(2,1)S(1)} %bitcast.133), channel_id=1, replica_groups=mesh['dp'=16,'fy'=4,'fc'=2] {'dp'}, dimensions={0} | all-to-all | bytes 1310720 | tf_op jit(solution)/shard_map/all_to_all | solution.py:56
  48.8 16.0 %all-gather.4.cloned.1.call-done = bf16[4,640,512]{2,1,0:T(8,128)(2,1)} async-done(((bf16[1,640,512]{2,1,0:T(8,128)(2,1)}), bf16[4,640,512]{2,1,0:T(8,128)(2,1)}) %all-gather.4.cloned.1.call-update) | async-done | bytes 2621456 | tf_op jit(solution)/shard_map/all_gather | solution.py:59
  64.8 2.2 broadcast_in_dim.42
  67.0 7.9 %all_to_all.32 = bf16[4,2,640,512]{3,2,0,1:T(8,128)(2,1)S(1)} all-to-all(bf16[4,2,640,512]{3,2,0,1:T(8,128)(2,1)S(1)} %broadcast_in_dim.42), channel_id=1, replica_groups=mesh['dp'=16,'fy'=4,'fc'=2] {'fc'}, dimensions={1} | all-to-all | bytes 10485760 | tf_op jit(solution)/shard_map/all_to_all | solution.py:63
  75.3 3.9 %copy-done.5 = bf16[4096,512]{1,0:T(8,128)(2,1)S(1)} copy-done((bf16[4096,512]{1,0:T(8,128)(2,1)S(1)}, bf16[4096,512]{1,0:T(8,128)(2,1)}, u32[]{:S(2)}) %copy-start.5) | copy-done | bytes 4194328
  79.2 2.9 %convolution_bitcast_fusion = f32[640,512]{1,0:T(8,128)S(1)} fusion(bf16[8,640,512]{2,1,0:T(8,128)(2,1)S(1)} %bitcast.116, bf16[8,512,512]{2,1,0:T(8,128)(2,1)S(1)} %bitcast.127), kind=kOutput, calls=%fused_computation.18 | convolution fusion | flops 2684354560 | bytes 10747904 | tf_op jit(solution)/shard_map/dot_general | solution.py:91
  82.1 2.9 %convolution_bitcast_fusion.1 = f32[640,512]{1,0:T(8,128)S(1)} fusion(bf16[8,640,512]{2,1,0:T(8,128)(2,1)S(1)} %bitcast.117, bf16[8,512,512]{2,1,0:T(8,128)(2,1)S(1)} %bitcast.112), kind=kOutput, calls=%fused_computation.19 | convolution fusion | flops 2684354560 | bytes 10747904 | tf_op jit(solution)/shard_map/dot_general | solution.py:90
  86.0 4.7 %fusion.6 = bf16[8,640,512]{2,1,0:T(8,128)(2,1)} fusion(bf16[640,512,1]{1,0,2:T(8,128)(2,1)S(1)} %fusion.15, bf16[64,8,8,512]{3,2,1,0:T(8,128)(2,1)S(1)} %bitcast.142), kind=kOutput, calls=%fused_computation.9 | convolution fusion | flops 2684354560 | bytes 10092544 | tf_op jit(solution)/shard_map/rh,hfd->frd/dot_general | solution.py:95
  90.7 11.1 %all-gather.6.cloned.1.call-done = bf16[4,640,512]{2,1,0:T(8,128)(2,1)} async-done(((bf16[1,640,512]{2,1,0:T(8,128)(2,1)}), bf16[4,640,512]{2,1,0:T(8,128)(2,1)}) %all-gather.6.cloned.1.call-update) | async-done | bytes 2621456 | tf_op jit(solution)/shard_map/all_gather | solution.py:59
  101.8 3.4 %dynamic-slice_bitcast_fusion.1 = bf16[4,640,512]{2,1,0:T(8,128)(2,1)} fusion(bf16[4,2,640,512]{3,2,1,0:T(8,128)(2,1)} %bitcast.122, s32[]{:T(128)S(6)} %select_n.19), kind=kLoop, calls=%fused_computation.16 | loop fusion | bytes 5242884 | tf_op jit(solution)/shard_map/jit(dynamic_index_in_dim)/squeeze | solution.py:72
  105.2 2.2 broadcast_in_dim.48
  107.4 8.2 %all_to_all.33 = bf16[4,2,640,512]{3,2,0,1:T(8,128)(2,1)S(1)} all-to-all(bf16[4,2,640,512]{3,2,0,1:T(8,128)(2,1)S(1)} %broadcast_in_dim.48), channel_id=1, replica_groups=mesh['dp'=16,'fy'=4,'fc'=2] {'fc'}, dimensions={1} | all-to-all | bytes 10485760 | tf_op jit(solution)/shard_map/all_to_all | solution.py:63
  115.6 2.9 %copy.56 = bf16[4,2,640,512]{3,2,1,0:T(8,128)(2,1)} copy(bf16[4,2,640,512]{3,2,0,1:T(8,128)(2,1)S(1)} %all_to_all.33) | data formatting | bytes 10485760 | tf_op jit(solution)/shard_map/all_to_all | solution.py:63
  118.6 2.4 %fusion.1 = bf16[4,640,512]{2,1,0:T(8,128)(2,1)} fusion(bf16[4,640,512]{2,1,0:T(8,128)(2,1)S(1)} %collective-permute-done, bf16[4,2,640,512]{3,2,1,0:T(8,128)(2,1)S(1)} %bitcast.125, s32[]{:T(128)S(6)} %select_n.18), kind=kLoop, calls=%fused_computation.4 | loop fusion | flops 5242880 | bytes 7864324 | tf_op jit(solution)/shard_map/convert_element_type | solution.py:74
  121.2 7.8 %fusion.16 = (bf16[640,512,1]{1,0,2:T(8,128)(2,1)S(1)}, bf16[640,512]{1,0:T(8,128)(2,1)S(1)}) fusion(f32[640,512]{1,0:T(8,128)} %copy-done.7, f32[640,512]{1,0:T(8,128)} %copy-done.6, bf16[8,640,512]{2,1,0:T(8,128)(2,1)} %bitcast.120, bf16[64,8,8,512]{3,2,1,0:T(8,128)(2,1)} %bitcast.141), kind=kOutput, calls=%fused_computation.31 | convolution fusion | flops 2688614400 | bytes 13369344 | tf_op jit(solution)/shard_map/dot_general | solution.py:123
  129.1 3.0 %fusion.18 = f32[640,8,512]{2,0,1:T(8,128)S(1)} fusion(bf16[8,512,512]{2,1,0:T(8,128)(2,1)S(1)} %bitcast.113, bf16[640,512]{1,0:T(8,128)(2,1)S(1)} %get-tuple-element.43), kind=kOutput, calls=%fused_computation.33 | convolution fusion | flops 2684354560 | bytes 15335424 | tf_op jit(solution)/shard_map/rh,fdh->frd/dot_general | solution.py:138
  132.0 5.6 %add_convert_fusion = bf16[640,8,512]{2,0,1:T(8,128)(2,1)S(1)} fusion(f32[640,8,512]{2,0,1:T(8,128)S(1)} %fusion.18, bf16[640,512,1]{1,0,2:T(8,128)(2,1)S(1)} %get-tuple-element.42, bf16[8,512,512]{2,1,0:T(8,128)(2,1)} %bitcast.126), kind=kOutput, calls=%fused_computation | convolution fusion | flops 2689597440 | bytes 20578304 | tf_op jit(solution)/shard_map/rh,fdh->frd/dot_general | solution.py:141
  138.0 4.8 %collective-permute-done.1 = bf16[4,640,512]{2,1,0:T(8,128)(2,1)S(1)} collective-permute-done((bf16[4,640,512]{2,1,0:T(8,128)(2,1)S(1)}, bf16[4,640,512]{2,1,0:T(8,128)(2,1)S(1)}, u32[]{:S(2)}, u32[]{:S(2)}) %collective-permute-start.1) | collective-permute-done | bytes 2621472 | tf_op jit(solution)/shard_map/ppermute | solution.py:73
  142.8 2.3 %fusion = bf16[4,640,512]{2,1,0:T(8,128)(2,1)} fusion(bf16[4,640,512]{2,1,0:T(8,128)(2,1)S(1)} %collective-permute-done.1, bf16[4,2,640,512]{3,2,1,0:T(8,128)(2,1)S(1)} %bitcast.111, s32[]{:T(128)S(6)} %select_n.18), kind=kLoop, calls=%fused_computation.2 | loop fusion | flops 5242880 | bytes 7864324 | tf_op jit(solution)/shard_map/convert_element_type | solution.py:74
  145.2 8.5 %convolution_convert_fusion = bf16[512,8,512]{0,2,1:T(8,128)(2,1)} fusion(bf16[640,512,1]{1,0,2:T(8,128)(2,1)S(1)} %fusion.15, bf16[8,640,512]{2,1,0:T(8,128)(2,1)} %bitcast.121), kind=kOutput, calls=%fused_computation.12 | convolution fusion | flops 2686451712 | bytes 10092544 | tf_op jit(solution)/shard_map/rh,frd->hfd/dot_general | solution.py:135
  153.6 6.3 %copy.61 = bf16[512,4096]{1,0:T(8,128)(2,1)} copy(bf16[512,4096]{0,1:T(8,128)(2,1)} %bitcast.128) | data formatting | bytes 8388608
  159.9 7.5 %convolution_convert_fusion.2 = bf16[8,512,512]{2,1,0:T(8,128)(2,1)} fusion(bf16[8,640,512]{2,1,0:T(8,128)(2,1)} %bitcast.118, bf16[640,512]{1,0:T(8,128)(2,1)S(1)} %get-tuple-element.43), kind=kOutput, calls=%fused_computation.14 | convolution fusion | flops 2686451712 | bytes 10092544 | tf_op jit(solution)/shard_map/frd,rh->fdh/dot_general | solution.py:129
  167.5 7.0 %all-to-all-start.3 = ((bf16[16,40,512]{2,1,0:T(8,128)(2,1)}), bf16[16,40,512]{2,1,0:T(8,128)(2,1)S(1)}, u32[]{:S(2)}, u32[]{:S(2)}) async-start(bf16[16,40,512]{2,1,0:T(8,128)(2,1)} %bitcast.135), calls=%async_computation.4 | async-start | bytes 1310720 | tf_op jit(solution)/shard_map/all_to_all | solution.py:75
  174.5 7.7 %convolution_convert_fusion.1 = bf16[8,512,512]{2,1,0:T(8,128)(2,1)} fusion(bf16[8,640,512]{2,1,0:T(8,128)(2,1)} %bitcast.119, bf16[640,512,1]{1,0,2:T(8,128)(2,1)S(1)} %get-tuple-element.42), kind=kOutput, calls=%fused_computation.13 | convolution fusion | flops 2686451712 | bytes 10092544 | tf_op jit(solution)/shard_map/frd,rh->fdh/dot_general | solution.py:132
  182.2 9.0 %reduce-scatter.5.cloned.1.call-done = bf16[1,640,512]{2,1,0:T(8,128)(2,1)} async-done(((bf16[4,640,512]{2,1,0:T(8,128)(2,1)}), bf16[1,640,512]{2,1,0:T(8,128)(2,1)}) %reduce-scatter.5.cloned.1.call-update) | async-done | bytes 655376 | tf_op jit(solution)/shard_map/reduce_scatter | solution.py:74
  191.2 6.9 %all-to-all-start.5 = ((bf16[16,40,512]{2,1,0:T(8,128)(2,1)}), bf16[16,40,512]{2,1,0:T(8,128)(2,1)S(1)}, u32[]{:S(2)}, u32[]{:S(2)}) async-start(bf16[16,40,512]{2,1,0:T(8,128)(2,1)} %bitcast.136), calls=%async_computation.7 | async-start | bytes 1310720 | tf_op jit(solution)/shard_map/all_to_all | solution.py:75
  198.7 1.1 fusion.20
  199.9 11.2 %all-to-all-done.5 = bf16[16,40,512]{2,1,0:T(8,128)(2,1)S(1)} async-done(((bf16[16,40,512]{2,1,0:T(8,128)(2,1)}), bf16[16,40,512]{2,1,0:T(8,128)(2,1)S(1)}, u32[]{:S(2)}, u32[]{:S(2)}) %all-to-all-start.5) | async-done | bytes 655392 | tf_op jit(solution)/shard_map/all_to_all | solution.py:75
  211.2 1.1 convolution_convert_fusion.5
  212.3 8.6 %all-gather = f32[1024,2]{0,1:T(2,128)S(1)} all-gather(f32[128,2]{0,1:T(2,128)S(1)} %pad_maximum_fusion), channel_id=2, replica_groups=mesh['dp'=16,'fy'=4,'fc'=2] {'fy','fc'}, dimensions={0}, use_global_device_ids=true | all-gather | bytes 9216 | tf_op jit(solution)/shard_map/all_gather | solution.py:121
  (66 shorter events, 7.7 us)
Async XLA Ops:
  7.2 3.0 %copy-start = (bf16[128,512]{1,0:T(8,128)(2,1)S(1)}, bf16[128,512]{1,0:T(8,128)(2,1)}, u32[]{:S(2)}) copy-start(bf16[128,512]{1,0:T(8,128)(2,1)} %param.7) | copy-start | bytes 393220
  7.2 57.6 %all-gather.4.cloned.1.call-start = ((), (), s32[]{:S(2)}) async-start(), calls=%async_computation.8 | async-start | bytes 3276800 | tf_op jit(solution)/shard_map/all_gather | solution.py:59
  31.3 70.5 %all-gather.6.cloned.1.call-start = ((), (), s32[]{:S(2)}) async-start(), calls=%async_computation.9 | async-start | bytes 3276800 | tf_op jit(solution)/shard_map/all_gather | solution.py:59
  32.1 34.9 %copy-start.9 = (f32[128]{0:T(128)}, f32[128]{0:T(128)S(1)}, u32[]{:S(2)}) copy-start(f32[128]{0:T(128)S(1)} %get-tuple-element.46) | copy-start | bytes 1540
  48.7 118.7 %reduce-scatter.3.cloned.1.call-start = ((), (), s32[]{:S(2)}) async-start(), calls=%async_computation.10 | async-start | bytes 3276800 | tf_op jit(solution)/shard_map/reduce_scatter | solution.py:74
  75.0 4.2 %copy-start.5 = (bf16[4096,512]{1,0:T(8,128)(2,1)S(1)}, bf16[4096,512]{1,0:T(8,128)(2,1)}, u32[]{:S(2)}) copy-start(bf16[4096,512]{1,0:T(8,128)(2,1)} %param.11) | copy-start | bytes 12582916
  75.3 6.8 %copy-start.4 = (bf16[4,2,640,512]{3,2,1,0:T(8,128)(2,1)}, bf16[4,2,640,512]{3,2,1,0:T(8,128)(2,1)S(1)}, u32[]{:S(2)}) copy-start(bf16[4,2,640,512]{3,2,1,0:T(8,128)(2,1)S(1)} %copy.54) | copy-start | bytes 15728644
  79.2 2.9 %copy-start.2 = (bf16[4096,512]{1,0:T(8,128)(2,1)S(1)}, bf16[4096,512]{1,0:T(8,128)(2,1)}, u32[]{:S(2)}) copy-start(bf16[4096,512]{1,0:T(8,128)(2,1)} %param.10) | copy-start | bytes 12582916
  82.0 2.9 %copy-start.6 = (f32[640,512]{1,0:T(8,128)}, f32[640,512]{1,0:T(8,128)S(1)}, u32[]{:S(2)}) copy-start(f32[640,512]{1,0:T(8,128)S(1)} %convolution_bitcast_fusion) | copy-start | bytes 3932164
  82.1 3.9 %copy-start.11 = (bf16[512,4096]{1,0:T(8,128)(2,1)S(1)}, bf16[512,4096]{1,0:T(8,128)(2,1)}, u32[]{:S(2)}) copy-start(bf16[512,4096]{1,0:T(8,128)(2,1)} %param.12) | copy-start | bytes 12582916
  85.0 1.1 copy-start.7
  105.2 13.4 %collective-permute-start = (bf16[4,640,512]{2,1,0:T(8,128)(2,1)}, bf16[4,640,512]{2,1,0:T(8,128)(2,1)S(1)}, u32[]{:S(2)}, u32[]{:S(2)}) collective-permute-start(bf16[4,640,512]{2,1,0:T(8,128)(2,1)} %dynamic-slice_bitcast_fusion.1), channel_id=1, source_target_pairs={{0,1},{1,0},{2,3},{3,2},{4,5},{5,4},{6,7},{7,6},{8,9},{9,8},{10,11... | collective-permute-start | bytes 7864328 | tf_op jit(solution)/shard_map/ppermute | solution.py:73
  107.4 11.2 %slice-start = ((s8[5242880]{0:T(1024)(128)(4,1)}), s8[4194304]{0:T(1024)(128)(4,1)S(1)}, s32[]{:S(2)}) async-start(s8[5242880]{0:T(1024)(128)(4,1)} %bitcast.123), calls=%async_computation.12 | async-start | bytes 8388608
  115.6 2.9 %slice-start.1 = ((s8[5242880]{0:T(1024)(128)(4,1)}), s8[1048576]{0:T(1024)(128)(4,1)S(1)}, s32[]{:S(2)}) async-start(s8[5242880]{0:T(1024)(128)(4,1)} %bitcast.123), calls=%async_computation.13 | async-start | bytes 2097152
  121.0 70.2 %reduce-scatter.5.cloned.1.call-start = ((), (), s32[]{:S(2)}) async-start(), calls=%async_computation.11 | async-start | bytes 3276800 | tf_op jit(solution)/shard_map/reduce_scatter | solution.py:74
  121.2 7.9 %copy-start.3 = (bf16[4096,512]{1,0:T(8,128)(2,1)S(1)}, bf16[4096,512]{1,0:T(8,128)(2,1)}, u32[]{:S(2)}) copy-start(bf16[4096,512]{1,0:T(8,128)(2,1)} %param.10) | copy-start | bytes 12582916
  137.8 5.0 %collective-permute-start.1 = (bf16[4,640,512]{2,1,0:T(8,128)(2,1)S(1)}, bf16[4,640,512]{2,1,0:T(8,128)(2,1)S(1)}, u32[]{:S(2)}, u32[]{:S(2)}) collective-permute-start(bf16[4,640,512]{2,1,0:T(8,128)(2,1)S(1)} %dynamic-slice_bitcast_fusion), channel_id=1, source_target_pairs={{0,1},{1,0},{2,3},{3,2},{4,5},{5,4},{6,7},{7,6},{8,9},{9,8},{10,11... | collective-permute-start | bytes 7864328 | tf_op jit(solution)/shard_map/ppermute | solution.py:73
  167.5 23.7 %all-to-all-start.3 = ((bf16[16,40,512]{2,1,0:T(8,128)(2,1)}), bf16[16,40,512]{2,1,0:T(8,128)(2,1)S(1)}, u32[]{:S(2)}, u32[]{:S(2)}) async-start(bf16[16,40,512]{2,1,0:T(8,128)(2,1)} %bitcast.135), calls=%async_computation.4 | async-start | bytes 1310720 | tf_op jit(solution)/shard_map/all_to_all | solution.py:75
  174.4 24.3 %copy-start.8 = (bf16[128,512]{1,0:T(8,128)(2,1)S(1)}, bf16[128,512]{1,0:T(8,128)(2,1)}, u32[]{:S(2)}) copy-start(bf16[128,512]{1,0:T(8,128)(2,1)} %param.13) | copy-start | bytes 393220
  174.4 24.3 %copy-start.10 = (f32[128]{0:T(128)S(1)}, f32[128]{0:T(128)}, u32[]{:S(2)}) copy-start(f32[128]{0:T(128)} %copy-done.9) | copy-start | bytes 1540
  174.5 47.1 %copy-start.1 = (bf16[128,512]{1,0:T(8,128)(2,1)S(1)}, bf16[128,512]{1,0:T(8,128)(2,1)}, u32[]{:S(2)}) copy-start(bf16[128,512]{1,0:T(8,128)(2,1)} %param.7) | copy-start | bytes 393220
  191.2 19.9 %all-to-all-start.5 = ((bf16[16,40,512]{2,1,0:T(8,128)(2,1)}), bf16[16,40,512]{2,1,0:T(8,128)(2,1)S(1)}, u32[]{:S(2)}, u32[]{:S(2)}) async-start(bf16[16,40,512]{2,1,0:T(8,128)(2,1)} %bitcast.136), calls=%async_computation.7 | async-start | bytes 1310720 | tf_op jit(solution)/shard_map/all_to_all | solution.py:75
Sparse Core Ops, SparseCore 0:
  31.4 33.3 all-gather.3
  66.4 35.2 all-gather.5
  121.1 34.0 reduce-scatter.2
  157.5 33.6 reduce-scatter.4

commit v5 on v4

--- a/solution.py
+++ b/solution.py
@@ -66,12 +66,17 @@
         )
         return both.reshape(fsdp_count, rows, feat)
 
-    def to_token_layout(partial_value):
+    def swap_cores(partial_value):
         blocks = partial_value.astype(jnp.bfloat16).reshape(chips, cores, rows, feat)
         kept = lax.dynamic_index_in_dim(blocks, core, axis=1, keepdims=False)
         sent = lax.dynamic_index_in_dim(blocks, 1 - core, axis=1, keepdims=False)
         within = kept.astype(jnp.float32) + lax.ppermute(sent, "fc", swap).astype(jnp.float32)
-        shares = lax.psum_scatter(within.astype(jnp.bfloat16), "fy", scatter_dimension=0, tiled=False)
+        return within.astype(jnp.bfloat16)
+
+    def scatter_chips(within):
+        return lax.psum_scatter(within, "fy", scatter_dimension=0, tiled=False)
+
+    def to_token_layout(shares):
         returned = lax.all_to_all(
             shares.reshape(dp_count, CAP, feat),
             "dp",
@@ -96,8 +101,8 @@
         "rh,hfd->frd", hidden, down_w3, preferred_element_type=jnp.float32
     )
     grad_across = to_expert_layout(out_grad, True)
-    out_partial, grad_across = lax.optimization_barrier((out_partial, grad_across))
-    out_slots = to_token_layout(out_partial)
+    out_within, grad_across = lax.optimization_barrier((swap_cores(out_partial), grad_across))
+    out_slots = to_token_layout(scatter_chips(out_within))
     first_pair = jnp.dot(
         select_first.astype(jnp.float32),
         out_slots,
@@ -141,7 +146,9 @@
     input_partial = input_partial + jnp.einsum(
         "rh,fdh->frd", up_grad, up_w3, preferred_element_type=jnp.float32
     )
-    input_slots = to_token_layout(input_partial)
+    input_shares = scatter_chips(swap_cores(input_partial))
+    prob_grad, input_shares = lax.optimization_barrier((prob_grad, input_shares))
+    input_slots = to_token_layout(input_shares)
     token_grad = jnp.dot(
         picker.astype(jnp.float32),
         input_slots,

time: 230 us -> 209 us (0.909)
  blocking collectives: 60.5 us -> 45.1 us
  matrix products: 55 us -> 49 us
  waiting for transfers between devices: 52.1 us -> 47.2 us
  local copies, waits for them, and re-layouts: 24.6 us -> 28.9 us
    all_to_all x2 -> x1, blocking collectives: 35.7 us -> 20.6 us  [to_expert_layout(): lax.all_to_all(place_rows(source, scaled), 'dp', split_axis=0, concat_axi...]
    all_gather x2, waiting for transfers between devices: 27 us -> 14.1 us  [to_expert_layout(): lax.all_gather(arrived.reshape(rows, feat), 'fy', axis=0, tiled=False)]
    all_to_all x0 -> x1, waiting for transfers between devices: none -> 11.7 us  [to_expert_layout(): lax.all_to_all(place_rows(source, scaled), 'dp', split_axis=0, concat_axi...]
    unnamed x30 -> x40, local copies, waits for them, and re-layouts: 11.7 us -> 21.3 us
    reduce_scatter x2, waiting for transfers between devices: 9.02 us -> 0.01 us  [scatter_chips(): return lax.psum_scatter(within, 'fy', scatter_dimension=0, tiled=False)]
    ppermute x2, waiting for transfers between devices: 4.77 us -> 9.66 us  [swap_cores(): lax.ppermute(sent, 'fc', swap).astype(jnp.float32)]
    dot_general x1, matrix products: 7.85 us -> 3.25 us  [local(): lax.dot_general(grad_rows, down_w3, (((0, 2), (1, 2)), ((), ())), preferr...]
    all_to_all x0 -> x1, starting transfers between devices: none -> 3.64 us  [to_expert_layout(): lax.all_to_all(place_rows(source, scaled), 'dp', split_axis=0, concat_axi...]
  transfers between devices with their start and end apart: 8 -> 9, of which waited for: 5 -> 6; matrix products, arithmetic and copies ran while one was open for 31% -> 33% of each run, Pallas kernels for 0% -> 0%
where the time goes in v5:
time: 209 us; the launch traced here: 208 us
  matrix products  49 us (23%)
  waiting for transfers between devices  47.2 us (23%)
  blocking collectives  45.1 us (22%)
  local copies, waits for them, and re-layouts  28.9 us (14%)
  starting transfers between devices  14.8 us (7%)
  between operations  14.1 us (7%)
  other arithmetic  8.97 us (4%)
    unnamed x40, local copies, waits for them, and re-layouts  21.3 us
    all_to_all x1, blocking collectives, to_expert_layout(): lax.all_to_all(place_rows(source, scaled), 'dp', split_axis=0, concat_axi...  20.6 us
    all_to_all x2, blocking collectives, join_cores(): lax.all_to_all(jnp.broadcast_to(across[:, None], (chips, cores, rows, fea...  15.9 us
    all_gather x2, waiting for transfers between devices, to_expert_layout(): lax.all_gather(arrived.reshape(rows, feat), 'fy', axis=0, tiled=False)  14.1 us
    all_to_all x2, waiting for transfers between devices, to_token_layout(): lax.all_to_all(shares.reshape(dp_count, CAP, feat), 'dp', split_axis=0, c...  11.8 us
    all_to_all x1, waiting for transfers between devices, to_expert_layout(): lax.all_to_all(place_rows(source, scaled), 'dp', split_axis=0, concat_axi...  11.7 us
    all_to_all x2, starting transfers between devices, to_token_layout(): lax.all_to_all(shares.reshape(dp_count, CAP, feat), 'dp', split_axis=0, c...  10.6 us
    ppermute x2, waiting for transfers between devices, swap_cores(): lax.ppermute(sent, 'fc', swap).astype(jnp.float32)  9.66 us
  transfers between devices with their start and end apart: 9, of which 6 were waited for; matrix products, arithmetic and copies ran while one was open for 33% of the time, Pallas kernels for 0%

profile of v5, /device:TPU:0, one launch (start us, length us, event | category | flops | bytes accessed | tf_op | source)
XLA Modules:
  0.0 208.1 jit_solution(6525536743138608088)
XLA Ops:
  10.6 20.6 %all_to_all.30 = bf16[16,40,512]{2,1,0:T(8,128)(2,1)} all-to-all(bf16[16,40,512]{2,1,0:T(8,128)(2,1)S(1)} %bitcast.131), channel_id=1, replica_groups=mesh['dp'=16,'fy'=4,'fc'=2] {'dp'}, dimensions={0} | all-to-all | bytes 1310720 | tf_op jit(solution)/shard_map/all_to_all | solution.py:56
  32.0 1.5 convolution_convert_fusion.3
  34.4 3.6 %all-to-all-start.2 = ((bf16[16,40,512]{2,1,0:T(8,128)(2,1)}), bf16[16,40,512]{2,1,0:T(8,128)(2,1)S(1)}, u32[]{:S(2)}, u32[]{:S(2)}) async-start(bf16[16,40,512]{2,1,0:T(8,128)(2,1)} %bitcast.21), calls=%async_computation.2 | async-start | bytes 1310720 | tf_op jit(solution)/shard_map/all_to_all | solution.py:56
  38.1 11.7 %all-to-all-done.2 = bf16[16,40,512]{2,1,0:T(8,128)(2,1)S(1)} async-done(((bf16[16,40,512]{2,1,0:T(8,128)(2,1)}), bf16[16,40,512]{2,1,0:T(8,128)(2,1)S(1)}, u32[]{:S(2)}, u32[]{:S(2)}) %all-to-all-start.2) | async-done | bytes 655392 | tf_op jit(solution)/shard_map/all_to_all | solution.py:56
  50.7 14.1 %all-gather.4.cloned.1.call-done = bf16[4,640,512]{2,1,0:T(8,128)(2,1)} async-done(((bf16[1,640,512]{2,1,0:T(8,128)(2,1)}), bf16[4,640,512]{2,1,0:T(8,128)(2,1)}) %all-gather.4.cloned.1.call-update) | async-done | bytes 2621456 | tf_op jit(solution)/shard_map/all_gather | solution.py:59
  64.8 2.2 %broadcast_in_dim.42 = bf16[4,2,640,512]{3,2,0,1:T(8,128)(2,1)S(1)} broadcast(bf16[4,640,512]{2,1,0:T(8,128)(2,1)} %all-gather.4.cloned.1.call-done), dimensions={0,2,3} | broadcast | bytes 7864320 | tf_op jit(solution)/shard_map/broadcast_in_dim | solution.py:64
  67.0 7.9 %all_to_all.31 = bf16[4,2,640,512]{3,2,0,1:T(8,128)(2,1)S(1)} all-to-all(bf16[4,2,640,512]{3,2,0,1:T(8,128)(2,1)S(1)} %broadcast_in_dim.42), channel_id=1, replica_groups=mesh['dp'=16,'fy'=4,'fc'=2] {'fc'}, dimensions={1} | all-to-all | bytes 10485760 | tf_op jit(solution)/shard_map/all_to_all | solution.py:63
  75.3 3.9 %copy-done.7 = bf16[4096,512]{1,0:T(8,128)(2,1)S(1)} copy-done((bf16[4096,512]{1,0:T(8,128)(2,1)S(1)}, bf16[4096,512]{1,0:T(8,128)(2,1)}, u32[]{:S(2)}) %copy-start.7) | copy-done | bytes 4194328
  79.2 2.9 %convolution_bitcast_fusion = f32[640,512]{1,0:T(8,128)S(1)} fusion(bf16[8,640,512]{2,1,0:T(8,128)(2,1)S(1)} %bitcast.117, bf16[8,512,512]{2,1,0:T(8,128)(2,1)S(1)} %bitcast.126), kind=kOutput, calls=%fused_computation.18 | convolution fusion | flops 2684354560 | bytes 10747904 | tf_op jit(solution)/shard_map/dot_general | solution.py:96
  82.1 2.9 %convolution_bitcast_fusion.1 = f32[640,512]{1,0:T(8,128)S(1)} fusion(bf16[8,640,512]{2,1,0:T(8,128)(2,1)S(1)} %bitcast.118, bf16[8,512,512]{2,1,0:T(8,128)(2,1)S(1)} %bitcast.113), kind=kOutput, calls=%fused_computation.19 | convolution fusion | flops 2684354560 | bytes 10747904 | tf_op jit(solution)/shard_map/dot_general | solution.py:95
  86.0 3.2 %fusion.8 = bf16[640,8,512]{2,0,1:T(8,128)(2,1)S(1)} fusion(bf16[640,512,1]{1,0,2:T(8,128)(2,1)S(1)} %fusion.15, bf16[64,8,8,512]{3,2,1,0:T(8,128)(2,1)S(1)} %bitcast.139), kind=kOutput, calls=%fused_computation.11 | convolution fusion | flops 2686976000 | bytes 10092544 | tf_op jit(solution)/shard_map/rh,hfd->frd/dot_general | solution.py:100
  89.2 2.3 %copy-done.6 = bf16[640,8,512]{2,0,1:T(8,128)(2,1)} copy-done((bf16[640,8,512]{2,0,1:T(8,128)(2,1)}, bf16[640,8,512]{2,0,1:T(8,128)(2,1)S(1)}, u32[]{:S(2)}) %copy-start.6) | copy-done | bytes 5242904
  91.5 1.7 dynamic-slice_bitcast_fusion.1
  93.3 5.0 %collective-permute-done = bf16[4,640,512]{2,1,0:T(8,128)(2,1)S(1)} collective-permute-done((bf16[4,640,512]{2,1,0:T(8,128)(2,1)}, bf16[4,640,512]{2,1,0:T(8,128)(2,1)S(1)}, u32[]{:S(2)}, u32[]{:S(2)}) %collective-permute-start) | collective-permute-done | bytes 2621472 | tf_op jit(solution)/shard_map/ppermute | solution.py:73
  98.3 4.0 %fusion.1 = bf16[4,640,512]{2,1,0:T(8,128)(2,1)} fusion(bf16[4,640,512]{2,1,0:T(8,128)(2,1)S(1)} %collective-permute-done, bf16[4,2,640,512]{3,2,1,0:T(8,128)(2,1)} %bitcast.124, s32[]{:T(128)S(6)} %select_n.16), kind=kLoop, calls=%fused_computation.4 | loop fusion | flops 5242880 | bytes 7864324 | tf_op jit(solution)/shard_map/convert_element_type | solution.py:74
  102.4 1.7 copy-done.9
  104.5 7.9 %all_to_all.32 = bf16[4,2,640,512]{3,2,0,1:T(8,128)(2,1)S(1)} all-to-all(bf16[4,2,640,512]{3,2,0,1:T(8,128)(2,1)S(1)} %broadcast_in_dim.48), channel_id=1, replica_groups=mesh['dp'=16,'fy'=4,'fc'=2] {'fc'}, dimensions={1} | all-to-all | bytes 10485760 | tf_op jit(solution)/shard_map/all_to_all | solution.py:63
  115.5 1.9 copy-done.18
  117.5 3.3 %fusion.16 = (bf16[640,512,1]{1,0,2:T(8,128)(2,1)S(1)}, bf16[640,512]{1,0:T(8,128)(2,1)S(1)}) fusion(f32[640,512]{1,0:T(8,128)S(1)} %copy-done.13, f32[640,512]{1,0:T(8,128)S(1)} %copy-done.11, bf16[8,640,512]{2,1,0:T(8,128)(2,1)S(1)} %bitcast.121, bf16[64,8,8,512]{3,2,1,0:T(8,128)(2,1)S(1)} %bitcast.140), kind=kOutput, calls=%fused_computation.31 | convolution fusion | flops 2688614400 | bytes 13369344 | tf_op jit(solution)/shard_map/dot_general | solution.py:128
  120.7 3.0 %fusion.18 = f32[640,8,512]{2,0,1:T(8,128)S(1)} fusion(bf16[8,512,512]{2,1,0:T(8,128)(2,1)S(1)} %bitcast.114, bf16[640,512]{1,0:T(8,128)(2,1)S(1)} %get-tuple-element.47), kind=kOutput, calls=%fused_computation.33 | convolution fusion | flops 2684354560 | bytes 15335424 | tf_op jit(solution)/shard_map/rh,fdh->frd/dot_general | solution.py:143
  123.7 5.6 %add_convert_fusion = bf16[640,8,512]{2,0,1:T(8,128)(2,1)S(1)} fusion(f32[640,8,512]{2,0,1:T(8,128)S(1)} %fusion.18, bf16[640,512,1]{1,0,2:T(8,128)(2,1)S(1)} %get-tuple-element.46, bf16[8,512,512]{2,1,0:T(8,128)(2,1)} %bitcast.125), kind=kOutput, calls=%fused_computation | convolution fusion | flops 2689597440 | bytes 20578304 | tf_op jit(solution)/shard_map/rh,fdh->frd/dot_general | solution.py:146
  129.8 4.7 %collective-permute-done.1 = bf16[4,640,512]{2,1,0:T(8,128)(2,1)S(1)} collective-permute-done((bf16[4,640,512]{2,1,0:T(8,128)(2,1)S(1)}, bf16[4,640,512]{2,1,0:T(8,128)(2,1)S(1)}, u32[]{:S(2)}, u32[]{:S(2)}) %collective-permute-start.1) | collective-permute-done | bytes 2621472 | tf_op jit(solution)/shard_map/ppermute | solution.py:73
  134.5 2.4 %fusion = bf16[4,640,512]{2,1,0:T(8,128)(2,1)} fusion(bf16[4,640,512]{2,1,0:T(8,128)(2,1)S(1)} %collective-permute-done.1, bf16[4,2,640,512]{3,2,1,0:T(8,128)(2,1)S(1)} %bitcast.112, s32[]{:T(128)S(6)} %select_n.16), kind=kLoop, calls=%fused_computation.2 | loop fusion | flops 5242880 | bytes 7864324 | tf_op jit(solution)/shard_map/convert_element_type | solution.py:74
  137.0 8.5 %convolution_convert_fusion = bf16[512,8,512]{0,2,1:T(8,128)(2,1)} fusion(bf16[640,512,1]{1,0,2:T(8,128)(2,1)S(1)} %fusion.15, bf16[8,640,512]{2,1,0:T(8,128)(2,1)} %bitcast.122), kind=kOutput, calls=%fused_computation.12 | convolution fusion | flops 2686451712 | bytes 10092544 | tf_op jit(solution)/shard_map/rh,frd->hfd/dot_general | solution.py:140
  145.4 6.4 %copy.61 = bf16[512,4096]{1,0:T(8,128)(2,1)} copy(bf16[512,4096]{0,1:T(8,128)(2,1)} %bitcast.127) | data formatting | bytes 8388608
  151.8 7.0 %all-to-all-start.3 = ((bf16[16,40,512]{2,1,0:T(8,128)(2,1)}), bf16[16,40,512]{2,1,0:T(8,128)(2,1)S(1)}, u32[]{:S(2)}, u32[]{:S(2)}) async-start(bf16[16,40,512]{2,1,0:T(8,128)(2,1)} %bitcast.133), calls=%async_computation.4 | async-start | bytes 1310720 | tf_op jit(solution)/shard_map/all_to_all | solution.py:80
  158.8 7.6 %convolution_convert_fusion.2 = bf16[8,512,512]{2,1,0:T(8,128)(2,1)} fusion(bf16[8,640,512]{2,1,0:T(8,128)(2,1)} %bitcast.119, bf16[640,512]{1,0:T(8,128)(2,1)S(1)} %get-tuple-element.47), kind=kOutput, calls=%fused_computation.14 | convolution fusion | flops 2686451712 | bytes 10092544 | tf_op jit(solution)/shard_map/frd,rh->fdh/dot_general | solution.py:134
  166.5 5.6 %all-to-all-done.3 = bf16[16,40,512]{2,1,0:T(8,128)(2,1)S(1)} async-done(((bf16[16,40,512]{2,1,0:T(8,128)(2,1)}), bf16[16,40,512]{2,1,0:T(8,128)(2,1)S(1)}, u32[]{:S(2)}, u32[]{:S(2)}) %all-to-all-start.3) | async-done | bytes 655392 | tf_op jit(solution)/shard_map/all_to_all | solution.py:80
  173.8 8.6 %all-gather = f32[1024,2]{0,1:T(2,128)S(1)} all-gather(f32[128,2]{0,1:T(2,128)S(1)} %pad_maximum_fusion), channel_id=2, replica_groups=mesh['dp'=16,'fy'=4,'fc'=2] {'fy','fc'}, dimensions={0}, use_global_device_ids=true | all-gather | bytes 9216 | tf_op jit(solution)/shard_map/all_gather | solution.py:126
  183.0 3.6 %all-to-all-start.5 = ((bf16[16,40,512]{2,1,0:T(8,128)(2,1)}), bf16[16,40,512]{2,1,0:T(8,128)(2,1)S(1)}, u32[]{:S(2)}, u32[]{:S(2)}) async-start(bf16[16,40,512]{2,1,0:T(8,128)(2,1)} %bitcast.134), calls=%async_computation.7 | async-start | bytes 1310720 | tf_op jit(solution)/shard_map/all_to_all | solution.py:80
  186.6 7.6 %convolution_convert_fusion.1 = bf16[8,512,512]{2,1,0:T(8,128)(2,1)} fusion(bf16[8,640,512]{2,1,0:T(8,128)(2,1)} %bitcast.120, bf16[640,512,1]{1,0,2:T(8,128)(2,1)S(1)} %get-tuple-element.46), kind=kOutput, calls=%fused_computation.13 | convolution fusion | flops 2686451712 | bytes 10092544 | tf_op jit(solution)/shard_map/frd,rh->fdh/dot_general | solution.py:137
  194.2 6.2 %all-to-all-done.5 = bf16[16,40,512]{2,1,0:T(8,128)(2,1)S(1)} async-done(((bf16[16,40,512]{2,1,0:T(8,128)(2,1)}), bf16[16,40,512]{2,1,0:T(8,128)(2,1)S(1)}, u32[]{:S(2)}, u32[]{:S(2)}) %all-to-all-start.5) | async-done | bytes 655392 | tf_op jit(solution)/shard_map/all_to_all | solution.py:80
  (76 shorter events, 15.2 us)
Async XLA Ops:
  7.2 3.0 %copy-start = (bf16[128,512]{1,0:T(8,128)(2,1)S(1)}, bf16[128,512]{1,0:T(8,128)(2,1)}, u32[]{:S(2)}) copy-start(bf16[128,512]{1,0:T(8,128)(2,1)} %param.7) | copy-start | bytes 393220
  7.2 57.6 %all-gather.4.cloned.1.call-start = ((), (), s32[]{:S(2)}) async-start(), calls=%async_computation.8 | async-start | bytes 3276800 | tf_op jit(solution)/shard_map/all_gather | solution.py:59
  32.0 35.0 %copy-start.15 = (f32[128]{0:T(128)}, f32[128]{0:T(128)S(1)}, u32[]{:S(2)}) copy-start(f32[128]{0:T(128)S(1)} %get-tuple-element.50) | copy-start | bytes 1540
  34.4 15.4 %all-to-all-start.2 = ((bf16[16,40,512]{2,1,0:T(8,128)(2,1)}), bf16[16,40,512]{2,1,0:T(8,128)(2,1)S(1)}, u32[]{:S(2)}, u32[]{:S(2)}) async-start(bf16[16,40,512]{2,1,0:T(8,128)(2,1)} %bitcast.21), calls=%async_computation.2 | async-start | bytes 1310720 | tf_op jit(solution)/shard_map/all_to_all | solution.py:56
  38.0 64.3 %all-gather.6.cloned.1.call-start = ((), (), s32[]{:S(2)}) async-start(), calls=%async_computation.9 | async-start | bytes 3276800 | tf_op jit(solution)/shard_map/all_gather | solution.py:59
  49.8 0.9 copy-start.8
  50.6 101.2 %reduce-scatter.3.cloned.1.call-start = ((), (), s32[]{:S(2)}) async-start(), calls=%async_computation.10 | async-start | bytes 3276800 | tf_op jit(solution)/shard_map/reduce_scatter | solution.py:77
  75.0 4.2 %copy-start.7 = (bf16[4096,512]{1,0:T(8,128)(2,1)S(1)}, bf16[4096,512]{1,0:T(8,128)(2,1)}, u32[]{:S(2)}) copy-start(bf16[4096,512]{1,0:T(8,128)(2,1)} %param.11) | copy-start | bytes 12582916
  75.3 6.7 %copy-start.4 = (bf16[4,2,640,512]{3,2,1,0:T(8,128)(2,1)}, bf16[4,2,640,512]{3,2,1,0:T(8,128)(2,1)S(1)}, u32[]{:S(2)}) copy-start(bf16[4,2,640,512]{3,2,1,0:T(8,128)(2,1)S(1)} %copy.54) | copy-start | bytes 15728644
  79.2 2.9 %copy-start.2 = (bf16[4096,512]{1,0:T(8,128)(2,1)S(1)}, bf16[4096,512]{1,0:T(8,128)(2,1)}, u32[]{:S(2)}) copy-start(bf16[4096,512]{1,0:T(8,128)(2,1)} %param.10) | copy-start | bytes 12582916
  82.0 2.9 %copy-start.10 = (f32[640,512]{1,0:T(8,128)}, f32[640,512]{1,0:T(8,128)S(1)}, u32[]{:S(2)}) copy-start(f32[640,512]{1,0:T(8,128)S(1)} %convolution_bitcast_fusion) | copy-start | bytes 3932164
  82.1 4.0 %copy-start.17 = (bf16[512,4096]{1,0:T(8,128)(2,1)S(1)}, bf16[512,4096]{1,0:T(8,128)(2,1)}, u32[]{:S(2)}) copy-start(bf16[512,4096]{1,0:T(8,128)(2,1)} %param.12) | copy-start | bytes 12582916
  85.0 1.1 copy-start.12
  89.2 2.3 %copy-start.6 = (bf16[640,8,512]{2,0,1:T(8,128)(2,1)}, bf16[640,8,512]{2,0,1:T(8,128)(2,1)S(1)}, u32[]{:S(2)}) copy-start(bf16[640,8,512]{2,0,1:T(8,128)(2,1)S(1)} %fusion.8) | copy-start | bytes 15728644
  93.2 5.1 %collective-permute-start = (bf16[4,640,512]{2,1,0:T(8,128)(2,1)}, bf16[4,640,512]{2,1,0:T(8,128)(2,1)S(1)}, u32[]{:S(2)}, u32[]{:S(2)}) collective-permute-start(bf16[4,640,512]{2,1,0:T(8,128)(2,1)} %dynamic-slice_bitcast_fusion.1), channel_id=1, source_target_pairs={{0,1},{1,0},{2,3},{3,2},{4,5},{5,4},{6,7},{7,6},{8,9},{9,8},{10,11... | collective-permute-start | bytes 7864328 | tf_op jit(solution)/shard_map/ppermute | solution.py:73
  102.3 1.7 copy-start.9
  102.3 80.6 %reduce-scatter.5.cloned.1.call-start = ((), (), s32[]{:S(2)}) async-start(), calls=%async_computation.11 | async-start | bytes 3276800 | tf_op jit(solution)/shard_map/reduce_scatter | solution.py:77
  112.4 1.7 copy-start.11
  112.4 3.1 %copy-start.13 = (f32[640,512]{1,0:T(8,128)S(1)}, f32[640,512]{1,0:T(8,128)}, u32[]{:S(2)}) copy-start(f32[640,512]{1,0:T(8,128)} %copy-done.12) | copy-start | bytes 3932164
  112.5 5.0 %copy-start.18 = (bf16[512,4096]{1,0:T(8,128)(2,1)S(1)}, bf16[512,4096]{1,0:T(8,128)(2,1)}, u32[]{:S(2)}) copy-start(bf16[512,4096]{1,0:T(8,128)(2,1)} %param.12) | copy-start | bytes 12582916
  112.8 7.9 %copy-start.5 = (bf16[4,2,640,512]{3,2,1,0:T(8,128)(2,1)}, bf16[4,2,640,512]{3,2,1,0:T(8,128)(2,1)S(1)}, u32[]{:S(2)}) copy-start(bf16[4,2,640,512]{3,2,1,0:T(8,128)(2,1)S(1)} %copy.56) | copy-start | bytes 15728644
  117.5 3.3 %copy-start.3 = (bf16[4096,512]{1,0:T(8,128)(2,1)S(1)}, bf16[4096,512]{1,0:T(8,128)(2,1)}, u32[]{:S(2)}) copy-start(bf16[4096,512]{1,0:T(8,128)(2,1)} %param.10) | copy-start | bytes 12582916
  129.5 5.0 %collective-permute-start.1 = (bf16[4,640,512]{2,1,0:T(8,128)(2,1)S(1)}, bf16[4,640,512]{2,1,0:T(8,128)(2,1)S(1)}, u32[]{:S(2)}, u32[]{:S(2)}) collective-permute-start(bf16[4,640,512]{2,1,0:T(8,128)(2,1)S(1)} %dynamic-slice_bitcast_fusion), channel_id=1, source_target_pairs={{0,1},{1,0},{2,3},{3,2},{4,5},{5,4},{6,7},{7,6},{8,9},{9,8},{10,11... | collective-permute-start | bytes 7864328 | tf_op jit(solution)/shard_map/ppermute | solution.py:73
  151.8 20.2 %all-to-all-start.3 = ((bf16[16,40,512]{2,1,0:T(8,128)(2,1)}), bf16[16,40,512]{2,1,0:T(8,128)(2,1)S(1)}, u32[]{:S(2)}, u32[]{:S(2)}) async-start(bf16[16,40,512]{2,1,0:T(8,128)(2,1)} %bitcast.133), calls=%async_computation.4 | async-start | bytes 1310720 | tf_op jit(solution)/shard_map/all_to_all | solution.py:80
  158.8 13.8 %copy-start.14 = (bf16[128,512]{1,0:T(8,128)(2,1)S(1)}, bf16[128,512]{1,0:T(8,128)(2,1)}, u32[]{:S(2)}) copy-start(bf16[128,512]{1,0:T(8,128)(2,1)} %param.13) | copy-start | bytes 393220
  158.8 13.8 %copy-start.16 = (f32[128]{0:T(128)S(1)}, f32[128]{0:T(128)}, u32[]{:S(2)}) copy-start(f32[128]{0:T(128)} %copy-done.15) | copy-start | bytes 1540
  183.0 17.4 %all-to-all-start.5 = ((bf16[16,40,512]{2,1,0:T(8,128)(2,1)}), bf16[16,40,512]{2,1,0:T(8,128)(2,1)S(1)}, u32[]{:S(2)}, u32[]{:S(2)}) async-start(bf16[16,40,512]{2,1,0:T(8,128)(2,1)} %bitcast.134), calls=%async_computation.7 | async-start | bytes 1310720 | tf_op jit(solution)/shard_map/all_to_all | solution.py:80
  186.6 15.0 %copy-start.1 = (bf16[128,512]{1,0:T(8,128)(2,1)S(1)}, bf16[128,512]{1,0:T(8,128)(2,1)}, u32[]{:S(2)}) copy-start(bf16[128,512]{1,0:T(8,128)(2,1)} %param.7) | copy-start | bytes 393220
Sparse Core Ops, SparseCore 0:
  31.4 33.3 all-gather.3
  66.4 35.2 all-gather.5
  104.8 34.0 reduce-scatter.2
  141.1 33.6 reduce-scatter.4

commit v6 on v5

--- a/solution.py
+++ b/solution.py
@@ -19,6 +19,7 @@
     hid = w_gate.shape[1]
     slot_total = E * CAP
     rows = dp_count * CAP
+    split_rows = rows // 2
     core = lax.axis_index("fc")
     swap = [(0, 1), (1, 0)]
     routing = expert_ids.reshape(-1)
@@ -56,8 +57,11 @@
         arrived = lax.all_to_all(
             place_rows(source, scaled), "dp", split_axis=0, concat_axis=0, tiled=True
         )
-        across = lax.all_gather(arrived.reshape(rows, feat), "fy", axis=0, tiled=False)
-        return across
+        flat = arrived.reshape(rows, feat)
+        first = lax.all_gather(flat[:split_rows], "fy", axis=0, tiled=False)
+        copies = jnp.broadcast_to(flat[None, split_rows:], (chips, rows - split_rows, feat))
+        second = lax.all_to_all(copies, "fy", split_axis=0, concat_axis=0, tiled=True)
+        return jnp.concatenate([first, second], axis=1)
 
     def join_cores(across):
         both = lax.all_to_all(
@@ -74,7 +78,10 @@
         return within.astype(jnp.bfloat16)
 
     def scatter_chips(within):
-        return lax.psum_scatter(within, "fy", scatter_dimension=0, tiled=False)
+        first = lax.psum_scatter(within[:, :split_rows], "fy", scatter_dimension=0, tiled=False)
+        parts = lax.all_to_all(within[:, split_rows:], "fy", split_axis=0, concat_axis=0, tiled=True)
+        second = jnp.sum(parts.astype(jnp.float32), axis=0).astype(jnp.bfloat16)
+        return jnp.concatenate([first, second], axis=0)
 
     def to_token_layout(shares):
         returned = lax.all_to_all(

time: 209 us -> 286 us (1.37)
  waiting for transfers between devices: 47.2 us -> 91.7 us
  starting transfers between devices: 14.8 us -> 30.3 us
  other arithmetic: 8.97 us -> 17.4 us
  local copies, waits for them, and re-layouts: 28.9 us -> 35.2 us
  blocking collectives: 45.1 us -> 48.3 us
    all_to_all x0 -> x4, waiting for transfers between devices: none -> 78.9 us  [the longest x2 55 us: to_expert_layout(): lax.all_to_all(copies, 'fy', split_axis=0, concat_axis=0, tiled=True)]
    all_to_all x0 -> x4, starting transfers between devices: none -> 15.3 us  [the longest x2 8 us: to_expert_layout(): lax.all_to_all(copies, 'fy', split_axis=0, concat_axis=0, tiled=True)]
    all_gather x2, waiting for transfers between devices: 14.1 us -> 0.86 us  [to_expert_layout(): first = lax.all_gather(flat[:split_rows], 'fy', axis=0, tiled=False)]
    all_to_all x1, waiting for transfers between devices: 11.7 us -> 0.01 us  [to_expert_layout(): lax.all_to_all(place_rows(source, scaled), 'dp', split_axis=0, concat_axi...]
    ppermute x2, waiting for transfers between devices: 9.66 us -> 0.01 us  [swap_cores(): lax.ppermute(sent, 'fc', swap).astype(jnp.float32)]
    concatenate x0 -> x4, other arithmetic: none -> 6.86 us  [the longest x2 3.74 us: scatter_chips(): return jnp.concatenate([first, second], axis=0)]
    slice x1 -> x5, local copies, waits for them, and re-layouts: 0.21 us -> 5.19 us  [the longest x2 3.39 us: scatter_chips(): within[:, :split_rows]]
    all_to_all x2, local copies, waits for them, and re-layouts: 0.68 us -> 3.55 us  [join_cores(): lax.all_to_all(jnp.broadcast_to(across[:, None], (chips, cores, rows, fea...]
  transfers between devices with their start and end apart: 9 -> 13, of which waited for: 6 -> 7; matrix products, arithmetic and copies ran while one was open for 33% -> 21% of each run, Pallas kernels for 0% -> 0%
where the time goes in v6:
time: 286 us; the launch traced here: 285 us
  waiting for transfers between devices  91.7 us (32%)
  blocking collectives  48.3 us (17%)
  matrix products  47.8 us (17%)
  local copies, waits for them, and re-layouts  35.2 us (12%)
  starting transfers between devices  30.3 us (11%)
  other arithmetic  17.4 us (6%)
  between operations  14.2 us (5%)
    all_to_all x2, waiting for transfers between devices, to_expert_layout(): lax.all_to_all(copies, 'fy', split_axis=0, concat_axis=0, tiled=True)  55 us
    all_to_all x2, waiting for transfers between devices, scatter_chips(): lax.all_to_all(within[:, split_rows:], 'fy', split_axis=0, concat_axis=0,...  23.9 us
    all_to_all x1, blocking collectives, to_expert_layout(): lax.all_to_all(place_rows(source, scaled), 'dp', split_axis=0, concat_axi...  20.5 us
    unnamed x42, local copies, waits for them, and re-layouts  18.5 us
    all_to_all x2, blocking collectives, join_cores(): lax.all_to_all(jnp.broadcast_to(across[:, None], (chips, cores, rows, fea...  17 us
    all_to_all x2, waiting for transfers between devices, to_token_layout(): lax.all_to_all(shares.reshape(dp_count, CAP, feat), 'dp', split_axis=0, c...  11.6 us
    all_gather x1, blocking collectives, local(): lax.all_gather(prob_terms, ('fy', 'fc'), axis=0, tiled=False)  10.7 us
    all_to_all x2, starting transfers between devices, to_token_layout(): lax.all_to_all(shares.reshape(dp_count, CAP, feat), 'dp', split_axis=0, c...  10.6 us
  transfers between devices with their start and end apart: 13, of which 7 were waited for; matrix products, arithmetic and copies ran while one was open for 21% of the time, Pallas kernels for 0%

profile of v6, /device:TPU:0, one launch (start us, length us, event | category | flops | bytes accessed | tf_op | source)
XLA Modules:
  0.0 284.8 jit_solution(8212588783007269419)
XLA Ops:
  10.6 20.5 %all_to_all.50 = bf16[16,40,512]{2,1,0:T(8,128)(2,1)S(1)} all-to-all(bf16[16,40,512]{2,1,0:T(8,128)(2,1)S(1)} %bitcast.132), channel_id=1, replica_groups=mesh['dp'=16,'fy'=4,'fc'=2] {'dp'}, dimensions={0} | all-to-all | bytes 1310720 | tf_op jit(solution)/shard_map/all_to_all | solution.py:57
  33.1 4.5 %all-to-all-start.1 = ((bf16[4,320,512]{2,1,0:T(8,128)(2,1)}), bf16[4,320,512]{2,1,0:T(8,128)(2,1)S(1)}, u32[]{:S(2)}, u32[]{:S(2)}) async-start(bf16[4,320,512]{2,1,0:T(8,128)(2,1)} %broadcast_in_dim.59), calls=%async_computation.1 | async-start | bytes 2621440 | tf_op jit(solution)/shard_map/all_to_all | solution.py:63
  38.2 26.4 %all-to-all-done.1 = bf16[4,320,512]{2,1,0:T(8,128)(2,1)S(1)} async-done(((bf16[4,320,512]{2,1,0:T(8,128)(2,1)}), bf16[4,320,512]{2,1,0:T(8,128)(2,1)S(1)}, u32[]{:S(2)}, u32[]{:S(2)}) %all-to-all-start.1) | async-done | bytes 1310752 | tf_op jit(solution)/shard_map/all_to_all | solution.py:63
  66.6 9.1 %all_to_all.51 = bf16[4,2,640,512]{3,2,0,1:T(8,128)(2,1)} all-to-all(bf16[4,2,640,512]{3,2,0,1:T(8,128)(2,1)S(1)} %broadcast_in_dim.60), channel_id=1, replica_groups=mesh['dp'=16,'fy'=4,'fc'=2] {'fc'}, dimensions={1} | all-to-all | bytes 10485760 | tf_op jit(solution)/shard_map/all_to_all | solution.py:67
  76.5 3.9 %all-to-all-start.3 = ((bf16[16,40,512]{2,1,0:T(8,128)(2,1)}), bf16[16,40,512]{2,1,0:T(8,128)(2,1)S(1)}, u32[]{:S(2)}, u32[]{:S(2)}) async-start(bf16[16,40,512]{2,1,0:T(8,128)(2,1)} %bitcast.22), calls=%async_computation.3 | async-start | bytes 1310720 | tf_op jit(solution)/shard_map/all_to_all | solution.py:57
  80.5 3.2 %copy.54 = bf16[4,2,640,512]{3,2,1,0:T(8,128)(2,1)S(1)} copy(bf16[4,2,640,512]{3,2,0,1:T(8,128)(2,1)} %all_to_all.51) | data formatting | bytes 10485760 | tf_op jit(solution)/shard_map/all_to_all | solution.py:67
  84.3 2.9 %convolution_bitcast_fusion = f32[640,512]{1,0:T(8,128)S(1)} fusion(bf16[8,640,512]{2,1,0:T(8,128)(2,1)S(1)} %bitcast.120, bf16[8,512,512]{2,1,0:T(8,128)(2,1)S(1)} %bitcast.129), kind=kOutput, calls=%fused_computation.20 | convolution fusion | flops 2684354560 | bytes 10747904 | tf_op jit(solution)/shard_map/dot_general | solution.py:103
  87.8 2.9 %convolution_bitcast_fusion.1 = f32[640,512]{1,0:T(8,128)S(1)} fusion(bf16[8,640,512]{2,1,0:T(8,128)(2,1)S(1)} %bitcast.121, bf16[8,512,512]{2,1,0:T(8,128)(2,1)S(1)} %bitcast.116), kind=kOutput, calls=%fused_computation.21 | convolution fusion | flops 2684354560 | bytes 10747904 | tf_op jit(solution)/shard_map/dot_general | solution.py:102
  91.8 3.1 %fusion.8 = bf16[640,8,512]{2,0,1:T(8,128)(2,1)S(1)} fusion(bf16[640,512,1]{1,0,2:T(8,128)(2,1)S(1)} %fusion.15, bf16[64,8,8,512]{3,2,1,0:T(8,128)(2,1)S(1)} %bitcast.144), kind=kOutput, calls=%fused_computation.11 | convolution fusion | flops 2686976000 | bytes 10092544 | tf_op jit(solution)/shard_map/rh,hfd->frd/dot_general | solution.py:107
  94.9 2.3 copy-done.8
  100.9 3.5 %all-to-all-start.4 = ((bf16[4,320,512]{2,1,0:T(8,128)(2,1)}), bf16[4,320,512]{2,1,0:T(8,128)(2,1)S(1)}, u32[]{:S(2)}, u32[]{:S(2)}) async-start(bf16[4,320,512]{2,1,0:T(8,128)(2,1)} %broadcast_in_dim.67), calls=%async_computation.4 | async-start | bytes 2621440 | tf_op jit(solution)/shard_map/all_to_all | solution.py:63
  104.5 28.6 %all-to-all-done.4 = bf16[4,320,512]{2,1,0:T(8,128)(2,1)S(1)} async-done(((bf16[4,320,512]{2,1,0:T(8,128)(2,1)}), bf16[4,320,512]{2,1,0:T(8,128)(2,1)S(1)}, u32[]{:S(2)}, u32[]{:S(2)}) %all-to-all-start.4) | async-done | bytes 1310752 | tf_op jit(solution)/shard_map/all_to_all | solution.py:63
  136.8 4.0 %fusion.1 = bf16[4,640,512]{2,1,0:T(8,128)(2,1)} fusion(bf16[4,640,512]{2,1,0:T(8,128)(2,1)} %collective-permute-done, bf16[4,2,640,512]{3,2,1,0:T(8,128)(2,1)S(1)} %bitcast.127, s32[]{:T(128)S(6)} %select_n.16), kind=kLoop, calls=%fused_computation.4 | loop fusion | flops 5242880 | bytes 7864324 | tf_op jit(solution)/shard_map/convert_element_type | solution.py:78
  141.3 7.9 %all_to_all.52 = bf16[4,2,640,512]{3,2,0,1:T(8,128)(2,1)S(1)} all-to-all(bf16[4,2,640,512]{3,2,0,1:T(8,128)(2,1)S(1)} %broadcast_in_dim.68), channel_id=1, replica_groups=mesh['dp'=16,'fy'=4,'fc'=2] {'fc'}, dimensions={1} | all-to-all | bytes 10485760 | tf_op jit(solution)/shard_map/all_to_all | solution.py:67
  150.6 3.1 %copy-done.19 = bf16[512,4096]{1,0:T(8,128)(2,1)S(1)} copy-done((bf16[512,4096]{1,0:T(8,128)(2,1)S(1)}, bf16[512,4096]{1,0:T(8,128)(2,1)}, u32[]{:S(2)}) %copy-start.19) | copy-done | bytes 4194328
  153.7 3.3 %fusion.16 = (bf16[640,512,1]{1,0,2:T(8,128)(2,1)S(1)}, bf16[640,512]{1,0:T(8,128)(2,1)S(1)}) fusion(f32[640,512]{1,0:T(8,128)S(1)} %copy-done.12, f32[640,512]{1,0:T(8,128)S(1)} %convolution_bitcast_fusion, bf16[8,640,512]{2,1,0:T(8,128)(2,1)S(1)} %bitcast.124, bf16[64,8,8,512]{3,2,1,0:T(8,128)(2,1)S(1)} %bitcast.145), kind=kOutput, calls=%fused_computation.33 | convolution fusion | flops 2688614400 | bytes 13369344 | tf_op jit(solution)/shard_map/dot_general | solution.py:135
  157.0 2.9 %fusion.18 = f32[640,8,512]{2,0,1:T(8,128)S(1)} fusion(bf16[8,512,512]{2,1,0:T(8,128)(2,1)S(1)} %bitcast.117, bf16[640,512]{1,0:T(8,128)(2,1)S(1)} %get-tuple-element.49), kind=kOutput, calls=%fused_computation.37 | convolution fusion | flops 2684354560 | bytes 15335424 | tf_op jit(solution)/shard_map/rh,fdh->frd/dot_general | solution.py:150
  159.9 5.5 %add_convert_fusion = bf16[640,8,512]{2,0,1:T(8,128)(2,1)S(1)} fusion(f32[640,8,512]{2,0,1:T(8,128)S(1)} %fusion.18, bf16[640,512,1]{1,0,2:T(8,128)(2,1)S(1)} %get-tuple-element.48, bf16[8,512,512]{2,1,0:T(8,128)(2,1)} %bitcast.128), kind=kOutput, calls=%fused_computation | convolution fusion | flops 2689597440 | bytes 20578304 | tf_op jit(solution)/shard_map/rh,fdh->frd/dot_general | solution.py:153
  170.8 3.6 %all-to-all-start.5 = ((bf16[4,320,512]{2,1,0:T(8,128)(2,1)}), bf16[4,320,512]{2,1,0:T(8,128)(2,1)S(1)}, u32[]{:S(2)}, u32[]{:S(2)}) async-start(bf16[4,320,512]{2,1,0:T(8,128)(2,1)} %get-tuple-element.51), calls=%async_computation.6 | async-start | bytes 2621440 | tf_op jit(solution)/shard_map/all_to_all | solution.py:82
  174.5 3.3 %fusion = bf16[4,640,512]{2,1,0:T(8,128)(2,1)S(1)} fusion(bf16[4,640,512]{2,1,0:T(8,128)(2,1)} %collective-permute-done.1, bf16[4,2,640,512]{3,2,1,0:T(8,128)(2,1)} %bitcast.115, s32[]{:T(128)S(6)} %select_n.16), kind=kLoop, calls=%fused_computation.2 | loop fusion | flops 5242880 | bytes 7864324 | tf_op jit(solution)/shard_map/convert_element_type | solution.py:78
  179.5 23.9 %all-to-all-done.5 = bf16[4,320,512]{2,1,0:T(8,128)(2,1)S(1)} async-done(((bf16[4,320,512]{2,1,0:T(8,128)(2,1)}), bf16[4,320,512]{2,1,0:T(8,128)(2,1)S(1)}, u32[]{:S(2)}, u32[]{:S(2)}) %all-to-all-start.5) | async-done | bytes 1310752 | tf_op jit(solution)/shard_map/all_to_all | solution.py:82
  205.8 7.0 %all-to-all-start.6 = ((bf16[16,40,512]{2,1,0:T(8,128)(2,1)}), bf16[16,40,512]{2,1,0:T(8,128)(2,1)S(1)}, u32[]{:S(2)}, u32[]{:S(2)}) async-start(bf16[16,40,512]{2,1,0:T(8,128)(2,1)} %bitcast.26), calls=%async_computation.7 | async-start | bytes 1310720 | tf_op jit(solution)/shard_map/all_to_all | solution.py:87
  212.9 7.7 %convolution_convert_fusion.2 = bf16[8,512,512]{2,1,0:T(8,128)(2,1)} fusion(bf16[8,640,512]{2,1,0:T(8,128)(2,1)} %bitcast.122, bf16[640,512]{1,0:T(8,128)(2,1)S(1)} %copy-done.14), kind=kOutput, calls=%fused_computation.14 | convolution fusion | flops 2686451712 | bytes 10092544 | tf_op jit(solution)/shard_map/frd,rh->fdh/dot_general | solution.py:141
  220.7 5.4 %all-to-all-done.6 = bf16[16,40,512]{2,1,0:T(8,128)(2,1)S(1)} async-done(((bf16[16,40,512]{2,1,0:T(8,128)(2,1)}), bf16[16,40,512]{2,1,0:T(8,128)(2,1)S(1)}, u32[]{:S(2)}, u32[]{:S(2)}) %all-to-all-start.6) | async-done | bytes 655392 | tf_op jit(solution)/shard_map/all_to_all | solution.py:87
  226.1 3.8 %all-to-all-start.8 = ((bf16[4,320,512]{2,1,0:T(8,128)(2,1)}), bf16[4,320,512]{2,1,0:T(8,128)(2,1)S(1)}, u32[]{:S(2)}, u32[]{:S(2)}) async-start(bf16[4,320,512]{2,1,0:T(8,128)(2,1)} %get-tuple-element.47), calls=%async_computation.10 | async-start | bytes 2621440 | tf_op jit(solution)/shard_map/all_to_all | solution.py:82
  229.8 8.2 %convolution_convert_fusion = bf16[512,8,512]{0,2,1:T(8,128)(2,1)} fusion(bf16[640,512,1]{1,0,2:T(8,128)(2,1)} %copy-done.15, bf16[8,640,512]{2,1,0:T(8,128)(2,1)} %bitcast.125), kind=kOutput, calls=%fused_computation.12 | convolution fusion | flops 2686451712 | bytes 10092544 | tf_op jit(solution)/shard_map/rh,frd->hfd/dot_general | solution.py:147
  238.0 6.3 %copy.61 = bf16[512,4096]{1,0:T(8,128)(2,1)} copy(bf16[512,4096]{0,1:T(8,128)(2,1)} %bitcast.130) | data formatting | bytes 8388608
  246.1 10.7 %all-gather = f32[1024,2]{0,1:T(2,128)S(1)} all-gather(f32[128,2]{0,1:T(2,128)S(1)} %pad_maximum_fusion.4), channel_id=2, replica_groups=mesh['dp'=16,'fy'=4,'fc'=2] {'fy','fc'}, dimensions={0}, use_global_device_ids=true | all-gather | bytes 9216 | tf_op jit(solution)/shard_map/all_gather | solution.py:133
  257.8 1.9 pad_maximum_fusion.3
  259.7 3.6 %all-to-all-start.9 = ((bf16[16,40,512]{2,1,0:T(8,128)(2,1)}), bf16[16,40,512]{2,1,0:T(8,128)(2,1)S(1)}, u32[]{:S(2)}, u32[]{:S(2)}) async-start(bf16[16,40,512]{2,1,0:T(8,128)(2,1)} %bitcast.41), calls=%async_computation.11 | async-start | bytes 1310720 | tf_op jit(solution)/shard_map/all_to_all | solution.py:87
  263.3 7.6 %convolution_convert_fusion.1 = bf16[8,512,512]{2,1,0:T(8,128)(2,1)} fusion(bf16[8,640,512]{2,1,0:T(8,128)(2,1)} %bitcast.123, bf16[640,512,1]{1,0,2:T(8,128)(2,1)S(1)} %get-tuple-element.48), kind=kOutput, calls=%fused_computation.13 | convolution fusion | flops 2686451712 | bytes 10092544 | tf_op jit(solution)/shard_map/frd,rh->fdh/dot_general | solution.py:144
  270.8 6.2 %all-to-all-done.9 = bf16[16,40,512]{2,1,0:T(8,128)(2,1)S(1)} async-done(((bf16[16,40,512]{2,1,0:T(8,128)(2,1)}), bf16[16,40,512]{2,1,0:T(8,128)(2,1)S(1)}, u32[]{:S(2)}, u32[]{:S(2)}) %all-to-all-start.9) | async-done | bytes 655392 | tf_op jit(solution)/shard_map/all_to_all | solution.py:87
  (98 shorter events, 33.7 us)
Async XLA Ops:
  7.2 3.0 %copy-start = (bf16[128,512]{1,0:T(8,128)(2,1)S(1)}, bf16[128,512]{1,0:T(8,128)(2,1)}, u32[]{:S(2)}) copy-start(bf16[128,512]{1,0:T(8,128)(2,1)} %param.7) | copy-start | bytes 393220
  7.2 57.4 %all-gather.4.cloned.1.call-start = ((), (), s32[]{:S(2)}) async-start(), calls=%async_computation.12 | async-start | bytes 1638400 | tf_op jit(solution)/shard_map/all_gather | solution.py:61
  10.6 27.0 %copy-start.17 = (f32[128,2]{0,1:T(2,128)S(1)}, f32[128,2]{0,1:T(2,128)}, u32[]{:S(2)}) copy-start(f32[128,2]{0,1:T(2,128)} %param.9) | copy-start | bytes 3076
  10.6 27.0 %copy-start.16 = (bf16[128,512]{1,0:T(8,128)(2,1)S(1)}, bf16[128,512]{1,0:T(8,128)(2,1)}, u32[]{:S(2)}) copy-start(bf16[128,512]{1,0:T(8,128)(2,1)} %param.13) | copy-start | bytes 393220
  33.1 31.5 %all-to-all-start.1 = ((bf16[4,320,512]{2,1,0:T(8,128)(2,1)}), bf16[4,320,512]{2,1,0:T(8,128)(2,1)S(1)}, u32[]{:S(2)}, u32[]{:S(2)}) async-start(bf16[4,320,512]{2,1,0:T(8,128)(2,1)} %broadcast_in_dim.59), calls=%async_computation.1 | async-start | bytes 2621440 | tf_op jit(solution)/shard_map/all_to_all | solution.py:63
  76.5 22.4 %all-to-all-start.3 = ((bf16[16,40,512]{2,1,0:T(8,128)(2,1)}), bf16[16,40,512]{2,1,0:T(8,128)(2,1)S(1)}, u32[]{:S(2)}, u32[]{:S(2)}) async-start(bf16[16,40,512]{2,1,0:T(8,128)(2,1)} %bitcast.22), calls=%async_computation.3 | async-start | bytes 1310720 | tf_op jit(solution)/shard_map/all_to_all | solution.py:57
  80.5 53.4 %all-gather.6.cloned.1.call-start = ((), (), s32[]{:S(2)}) async-start(), calls=%async_computation.13 | async-start | bytes 1638400 | tf_op jit(solution)/shard_map/all_gather | solution.py:61
  80.5 3.7 %copy-start.10 = (bf16[4096,512]{1,0:T(8,128)(2,1)S(1)}, bf16[4096,512]{1,0:T(8,128)(2,1)}, u32[]{:S(2)}) copy-start(bf16[4096,512]{1,0:T(8,128)(2,1)} %param.11) | copy-start | bytes 12582916
  83.8 3.4 %copy-start.6 = (bf16[4,2,640,512]{3,2,1,0:T(8,128)(2,1)}, bf16[4,2,640,512]{3,2,1,0:T(8,128)(2,1)S(1)}, u32[]{:S(2)}) copy-start(bf16[4,2,640,512]{3,2,1,0:T(8,128)(2,1)S(1)} %copy.54) | copy-start | bytes 15728644
  84.3 3.5 %copy-start.3 = (bf16[4096,512]{1,0:T(8,128)(2,1)S(1)}, bf16[4096,512]{1,0:T(8,128)(2,1)}, u32[]{:S(2)}) copy-start(bf16[4096,512]{1,0:T(8,128)(2,1)} %param.10) | copy-start | bytes 12582916
  87.8 3.9 %copy-start.18 = (bf16[512,4096]{1,0:T(8,128)(2,1)S(1)}, bf16[512,4096]{1,0:T(8,128)(2,1)}, u32[]{:S(2)}) copy-start(bf16[512,4096]{1,0:T(8,128)(2,1)} %param.12) | copy-start | bytes 12582916
  91.7 3.2 %copy-start.15 = (bf16[640,512,1]{1,0,2:T(8,128)(2,1)}, bf16[640,512,1]{1,0,2:T(8,128)(2,1)S(1)}, u32[]{:S(2)}) copy-start(bf16[640,512,1]{1,0,2:T(8,128)(2,1)S(1)} %fusion.15) | copy-start | bytes 1966084
  94.9 2.4 copy-start.8
  98.9 36.6 %collective-permute-start = (bf16[4,640,512]{2,1,0:T(8,128)(2,1)}, bf16[4,640,512]{2,1,0:T(8,128)(2,1)}, u32[]{:S(2)}, u32[]{:S(2)}) collective-permute-start(bf16[4,640,512]{2,1,0:T(8,128)(2,1)} %dynamic-slice_bitcast_fusion.1), channel_id=1, source_target_pairs={{0,1},{1,0},{2,3},{3,2},{4,5},{5,4},{6,7},{7,6},{8,9},{9,8},{10,11... | collective-permute-start | bytes 7864328 | tf_op jit(solution)/shard_map/ppermute | solution.py:77
  100.9 32.1 %all-to-all-start.4 = ((bf16[4,320,512]{2,1,0:T(8,128)(2,1)}), bf16[4,320,512]{2,1,0:T(8,128)(2,1)S(1)}, u32[]{:S(2)}, u32[]{:S(2)}) async-start(bf16[4,320,512]{2,1,0:T(8,128)(2,1)} %broadcast_in_dim.67), calls=%async_computation.4 | async-start | bytes 2621440 | tf_op jit(solution)/shard_map/all_to_all | solution.py:63
  104.5 99.5 %reduce-scatter.3.cloned.1.call-start = ((), (), s32[]{:S(2)}) async-start(), calls=%async_computation.14 | async-start | bytes 1638400 | tf_op jit(solution)/shard_map/reduce_scatter | solution.py:81
  133.9 2.9 %copy-start.9 = (bf16[640,8,512]{2,0,1:T(8,128)(2,1)S(1)}, bf16[640,8,512]{2,0,1:T(8,128)(2,1)}, u32[]{:S(2)}) copy-start(bf16[640,8,512]{2,0,1:T(8,128)(2,1)} %copy-done.8) | copy-start | bytes 15728644
  149.2 1.4 copy-start.12
  149.2 4.5 %copy-start.19 = (bf16[512,4096]{1,0:T(8,128)(2,1)S(1)}, bf16[512,4096]{1,0:T(8,128)(2,1)}, u32[]{:S(2)}) copy-start(bf16[512,4096]{1,0:T(8,128)(2,1)} %param.12) | copy-start | bytes 12582916
  149.6 7.4 %copy-start.7 = (bf16[4,2,640,512]{3,2,1,0:T(8,128)(2,1)}, bf16[4,2,640,512]{3,2,1,0:T(8,128)(2,1)S(1)}, u32[]{:S(2)}) copy-start(bf16[4,2,640,512]{3,2,1,0:T(8,128)(2,1)S(1)} %copy.56) | copy-start | bytes 15728644
  153.7 3.3 %copy-start.4 = (bf16[4096,512]{1,0:T(8,128)(2,1)S(1)}, bf16[4096,512]{1,0:T(8,128)(2,1)}, u32[]{:S(2)}) copy-start(bf16[4096,512]{1,0:T(8,128)(2,1)} %param.10) | copy-start | bytes 12582916
  157.0 2.9 %copy-start.13 = (bf16[640,512]{1,0:T(8,128)(2,1)}, bf16[640,512]{1,0:T(8,128)(2,1)S(1)}, u32[]{:S(2)}) copy-start(bf16[640,512]{1,0:T(8,128)(2,1)S(1)} %get-tuple-element.49) | copy-start | bytes 1966084
  165.5 5.3 %copy-start.2 = (bf16[640,8,512]{2,0,1:T(8,128)(2,1)}, bf16[640,8,512]{2,0,1:T(8,128)(2,1)S(1)}, u32[]{:S(2)}) copy-start(bf16[640,8,512]{2,0,1:T(8,128)(2,1)S(1)} %add_convert_fusion) | copy-start | bytes 15728644
  165.5 3.6 %copy-start.5 = (bf16[4,640,512]{2,1,0:T(8,128)(2,1)S(1)}, bf16[4,640,512]{2,1,0:T(8,128)(2,1)}, u32[]{:S(2)}) copy-start(bf16[4,640,512]{2,1,0:T(8,128)(2,1)} %fusion.1) | copy-start | bytes 7864324
  167.2 7.3 %collective-permute-start.1 = (bf16[4,640,512]{2,1,0:T(8,128)(2,1)}, bf16[4,640,512]{2,1,0:T(8,128)(2,1)}, u32[]{:S(2)}, u32[]{:S(2)}) collective-permute-start(bf16[4,640,512]{2,1,0:T(8,128)(2,1)} %dynamic-slice_bitcast_fusion), channel_id=1, source_target_pairs={{0,1},{1,0},{2,3},{3,2},{4,5},{5,4},{6,7},{7,6},{8,9},{9,8},{10,11... | collective-permute-start | bytes 7864328 | tf_op jit(solution)/shard_map/ppermute | solution.py:77
  170.8 32.6 %all-to-all-start.5 = ((bf16[4,320,512]{2,1,0:T(8,128)(2,1)}), bf16[4,320,512]{2,1,0:T(8,128)(2,1)S(1)}, u32[]{:S(2)}, u32[]{:S(2)}) async-start(bf16[4,320,512]{2,1,0:T(8,128)(2,1)} %get-tuple-element.51), calls=%async_computation.6 | async-start | bytes 2621440 | tf_op jit(solution)/shard_map/all_to_all | solution.py:82
  174.4 83.4 %reduce-scatter.5.cloned.1.call-start = ((), (), s32[]{:S(2)}) async-start(), calls=%async_computation.15 | async-start | bytes 1638400 | tf_op jit(solution)/shard_map/reduce_scatter | solution.py:81
  177.7 35.2 %copy-start.14 = (bf16[640,512]{1,0:T(8,128)(2,1)S(1)}, bf16[640,512]{1,0:T(8,128)(2,1)}, u32[]{:S(2)}) copy-start(bf16[640,512]{1,0:T(8,128)(2,1)} %copy-done.13) | copy-start | bytes 1966084
  205.8 20.2 %all-to-all-start.6 = ((bf16[16,40,512]{2,1,0:T(8,128)(2,1)}), bf16[16,40,512]{2,1,0:T(8,128)(2,1)S(1)}, u32[]{:S(2)}, u32[]{:S(2)}) async-start(bf16[16,40,512]{2,1,0:T(8,128)(2,1)} %bitcast.26), calls=%async_computation.7 | async-start | bytes 1310720 | tf_op jit(solution)/shard_map/all_to_all | solution.py:87
  226.1 31.3 %all-to-all-start.8 = ((bf16[4,320,512]{2,1,0:T(8,128)(2,1)}), bf16[4,320,512]{2,1,0:T(8,128)(2,1)S(1)}, u32[]{:S(2)}, u32[]{:S(2)}) async-start(bf16[4,320,512]{2,1,0:T(8,128)(2,1)} %get-tuple-element.47), calls=%async_computation.10 | async-start | bytes 2621440 | tf_op jit(solution)/shard_map/all_to_all | solution.py:82
  259.7 17.4 %all-to-all-start.9 = ((bf16[16,40,512]{2,1,0:T(8,128)(2,1)}), bf16[16,40,512]{2,1,0:T(8,128)(2,1)S(1)}, u32[]{:S(2)}, u32[]{:S(2)}) async-start(bf16[16,40,512]{2,1,0:T(8,128)(2,1)} %bitcast.41), calls=%async_computation.11 | async-start | bytes 1310720 | tf_op jit(solution)/shard_map/all_to_all | solution.py:87
  263.3 15.0 %copy-start.1 = (bf16[128,512]{1,0:T(8,128)(2,1)S(1)}, bf16[128,512]{1,0:T(8,128)(2,1)}, u32[]{:S(2)}) copy-start(bf16[128,512]{1,0:T(8,128)(2,1)} %param.7) | copy-start | bytes 393220
  (1 other events, 1.1 us)
Sparse Core Ops, SparseCore 0:
  32.1 31.2 all-gather.3
  99.9 34.0 all-gather.5
  171.0 32.9 reduce-scatter.2
  206.3 24.4 reduce-scatter.4

commit v7 on v5

--- a/solution.py
+++ b/solution.py
@@ -19,6 +19,10 @@
     hid = w_gate.shape[1]
     slot_total = E * CAP
     rows = dp_count * CAP
+    split_rows = rows // 2
+    chip = lax.axis_index("fy")
+    ring_up = [(i, (i + 1) % chips) for i in range(chips)]
+    ring_down = [(i, (i - 1) % chips) for i in range(chips)]
     core = lax.axis_index("fc")
     swap = [(0, 1), (1, 0)]
     routing = expert_ids.reshape(-1)
@@ -56,8 +60,13 @@
         arrived = lax.all_to_all(
             place_rows(source, scaled), "dp", split_axis=0, concat_axis=0, tiled=True
         )
-        across = lax.all_gather(arrived.reshape(rows, feat), "fy", axis=0, tiled=False)
-        return across
+        mine = arrived.reshape(rows, feat)
+        from_below = lax.ppermute(mine, "fy", ring_up)
+        from_above = lax.ppermute(mine, "fy", ring_down)
+        far = jnp.concatenate([lax.ppermute(from_below[:split_rows], "fy", ring_up),
+                               lax.ppermute(from_above[split_rows:], "fy", ring_down)], axis=0)
+        relative = jnp.stack([mine, from_below, far, from_above])
+        return jnp.take(relative, (chip - jnp.arange(chips)) % chips, axis=0)
 
     def join_cores(across):
         both = lax.all_to_all(
@@ -74,7 +83,19 @@
         return within.astype(jnp.bfloat16)
 
     def scatter_chips(within):
-        return lax.psum_scatter(within, "fy", scatter_dimension=0, tiled=False)
+        def block(offset):
+            return lax.dynamic_index_in_dim(within, (chip + offset) % chips, axis=0, keepdims=False)
+
+        far = block(2)
+        got_up = lax.ppermute(far[:split_rows], "fy", ring_up).astype(jnp.float32)
+        got_down = lax.ppermute(far[split_rows:], "fy", ring_down).astype(jnp.float32)
+        up_next = block(1).astype(jnp.float32)
+        up_next = jnp.concatenate([up_next[:split_rows] + got_up, up_next[split_rows:]], axis=0)
+        down_next = block(-1).astype(jnp.float32)
+        down_next = jnp.concatenate([down_next[:split_rows], down_next[split_rows:] + got_down], axis=0)
+        from_below = lax.ppermute(up_next.astype(jnp.bfloat16), "fy", ring_up).astype(jnp.float32)
+        from_above = lax.ppermute(down_next.astype(jnp.bfloat16), "fy", ring_down).astype(jnp.float32)
+        return (block(0).astype(jnp.float32) + from_below + from_above).astype(jnp.bfloat16)
 
     def to_token_layout(shares):
         returned = lax.all_to_all(

time: 209 us -> 260 us (1.24)
  starting transfers between devices: 14.8 us -> 51.4 us
  waiting for transfers between devices: 47.2 us -> 67.7 us
  blocking collectives: 45.1 us -> 29.9 us
  other arithmetic: 8.97 us -> 23.3 us
  between operations: 14.1 us -> 1.21 us
  local copies, waits for them, and re-layouts: 28.9 us -> 36.8 us
    ppermute x0 -> x16, waiting for transfers between devices: none -> 35.7 us  [the longest x2 12.8 us: to_expert_layout(): from_above = lax.ppermute(mine, 'fy', ring_down)]
    ppermute x0 -> x16, starting transfers between devices: none -> 25.6 us  [the longest x2 7.45 us: to_expert_layout(): lax.ppermute(from_above[split_rows:], 'fy', ring_down)]
    all_to_all x1 -> x0, blocking collectives: 20.6 us -> none  [to_expert_layout(): lax.all_to_all(place_rows(source, scaled), 'dp', split_axis=0, concat_axi...]
    all_gather x2 -> x0, waiting for transfers between devices: 14.1 us -> none  [to_expert_layout(): lax.all_gather(arrived.reshape(rows, feat), 'fy', axis=0, tiled=False)]
    all_to_all x1 -> x2, waiting for transfers between devices: 11.7 us -> 21 us  [to_expert_layout(): lax.all_to_all(place_rows(source, scaled), 'dp', split_axis=0, concat_axi...]
    all_to_all x1 -> x2, starting transfers between devices: 3.64 us -> 11.6 us  [to_expert_layout(): lax.all_to_all(place_rows(source, scaled), 'dp', split_axis=0, concat_axi...]
    another operation x2 -> x8, other arithmetic: 0.62 us -> 7.77 us  [the longest x4 4.58 us: to_expert_layout(): relative = jnp.stack([mine, from_below, far, from_above])]
    all_to_all x2, waiting for transfers between devices: 11.8 us -> 5.84 us  [to_token_layout(): lax.all_to_all(shares.reshape(dp_count, CAP, feat), 'dp', split_axis=0, c...]
  transfers between devices with their start and end apart: 9 -> 22, of which waited for: 6 -> 11; matrix products, arithmetic and copies ran while one was open for 33% -> 18% of each run, Pallas kernels for 0% -> 0%
where the time goes in v7:
time: 260 us; the launch traced here: 259 us
  waiting for transfers between devices  67.7 us (26%)
  starting transfers between devices  51.4 us (20%)
  matrix products  48.7 us (19%)
  local copies, waits for them, and re-layouts  36.8 us (14%)
  blocking collectives  29.9 us (12%)
  other arithmetic  23.3 us (9%)
    all_to_all x2, waiting for transfers between devices, to_expert_layout(): lax.all_to_all(place_rows(source, scaled), 'dp', split_axis=0, concat_axi...  21 us
    unnamed x60, local copies, waits for them, and re-layouts  19.4 us
    all_to_all x2, blocking collectives, join_cores(): lax.all_to_all(jnp.broadcast_to(across[:, None], (chips, cores, rows, fea...  15.9 us
    all_to_all x2, starting transfers between devices, to_token_layout(): lax.all_to_all(shares.reshape(dp_count, CAP, feat), 'dp', split_axis=0, c...  14 us
    all_gather x1, blocking collectives, local(): lax.all_gather(prob_terms, ('fy', 'fc'), axis=0, tiled=False)  14 us
    ppermute x2, waiting for transfers between devices, to_expert_layout(): from_above = lax.ppermute(mine, 'fy', ring_down)  12.8 us
    all_to_all x2, starting transfers between devices, to_expert_layout(): lax.all_to_all(place_rows(source, scaled), 'dp', split_axis=0, concat_axi...  11.6 us
    dot_general x1, matrix products, local(): jnp.einsum('rh,frd->hfd', hidden, grad_rows, preferred_element_type=jnp.f...  8.39 us
  transfers between devices with their start and end apart: 22, of which 11 were waited for; matrix products, arithmetic and copies ran while one was open for 18% of the time, Pallas kernels for 0%

profile of v7, /device:TPU:0, one launch (start us, length us, event | category | flops | bytes accessed | tf_op | source)
XLA Modules:
  0.0 259.0 jit_solution(12820219197671100516)
XLA Ops:
  6.7 8.0 %all-to-all-start.2 = ((bf16[16,40,512]{2,1,0:T(8,128)(2,1)}), bf16[16,40,512]{2,1,0:T(8,128)(2,1)S(1)}, u32[]{:S(2)}, u32[]{:S(2)}) async-start(bf16[16,40,512]{2,1,0:T(8,128)(2,1)} %bitcast.25), calls=%async_computation.2 | async-start | bytes 1310720 | tf_op jit(solution)/shard_map/all_to_all | solution.py:60
  15.1 12.5 %all-to-all-done.2 = bf16[16,40,512]{2,1,0:T(8,128)(2,1)S(1)} async-done(((bf16[16,40,512]{2,1,0:T(8,128)(2,1)}), bf16[16,40,512]{2,1,0:T(8,128)(2,1)S(1)}, u32[]{:S(2)}, u32[]{:S(2)}) %all-to-all-start.2) | async-done | bytes 655392 | tf_op jit(solution)/shard_map/all_to_all | solution.py:60
  28.5 3.6 %all-to-all-start = ((bf16[16,40,512]{2,1,0:T(8,128)(2,1)}), bf16[16,40,512]{2,1,0:T(8,128)(2,1)S(1)}, u32[]{:S(2)}, u32[]{:S(2)}) async-start(bf16[16,40,512]{2,1,0:T(8,128)(2,1)} %bitcast.6), calls=%async_computation | async-start | bytes 1310720 | tf_op jit(solution)/shard_map/all_to_all | solution.py:60
  32.1 3.1 %collective-permute-start.7 = (bf16[640,512]{1,0:T(8,128)(2,1)S(1)}, bf16[640,512]{1,0:T(8,128)(2,1)S(1)}, u32[]{:S(2)}, u32[]{:S(2)}) collective-permute-start(bf16[640,512]{1,0:T(8,128)(2,1)S(1)} %bitcast.182), channel_id=1, source_target_pairs={{0,6},{2,0},{4,2},{6,4},{1,7},{3,1},{5,3},{7,5},{8,14},{10,8},{12,... | collective-permute-start | bytes 1966088 | tf_op jit(solution)/shard_map/ppermute | solution.py:65
  35.2 8.5 %all-to-all-done = bf16[16,40,512]{2,1,0:T(8,128)(2,1)S(1)} async-done(((bf16[16,40,512]{2,1,0:T(8,128)(2,1)}), bf16[16,40,512]{2,1,0:T(8,128)(2,1)S(1)}, u32[]{:S(2)}, u32[]{:S(2)}) %all-to-all-start) | async-done | bytes 655392 | tf_op jit(solution)/shard_map/all_to_all | solution.py:60
  46.8 3.6 %collective-permute-done.7 = bf16[640,512]{1,0:T(8,128)(2,1)S(1)} collective-permute-done((bf16[640,512]{1,0:T(8,128)(2,1)S(1)}, bf16[640,512]{1,0:T(8,128)(2,1)S(1)}, u32[]{:S(2)}, u32[]{:S(2)}) %collective-permute-start.7) | collective-permute-done | bytes 655392 | tf_op jit(solution)/shard_map/ppermute | solution.py:65
  50.4 3.8 %collective-permute-start.8 = (bf16[320,512]{1,0:T(8,128)(2,1)S(1)}, bf16[320,512]{1,0:T(8,128)(2,1)S(1)}, u32[]{:S(2)}, u32[]{:S(2)}) collective-permute-start(bf16[320,512]{1,0:T(8,128)(2,1)S(1)} %slice.170), channel_id=1, source_target_pairs={{0,6},{2,0},{4,2},{6,4},{1,7},{3,1},{5,3},{7,5},{8,14},{10,8},{12,... | collective-permute-start | bytes 983048 | tf_op jit(solution)/shard_map/ppermute | solution.py:67
  55.3 9.1 %collective-permute-done.2 = bf16[640,512]{1,0:T(8,128)(2,1)S(1)} collective-permute-done((bf16[640,512]{1,0:T(8,128)(2,1)S(1)}, bf16[640,512]{1,0:T(8,128)(2,1)S(1)}, u32[]{:S(2)}, u32[]{:S(2)}) %collective-permute-start.2) | collective-permute-done | bytes 655392 | tf_op jit(solution)/shard_map/ppermute | solution.py:65
  65.3 3.7 %collective-permute-start.3 = (bf16[320,512]{1,0:T(8,128)(2,1)}, bf16[320,512]{1,0:T(8,128)(2,1)}, u32[]{:S(2)}, u32[]{:S(2)}) collective-permute-start(bf16[320,512]{1,0:T(8,128)(2,1)} %slice.168), channel_id=1, source_target_pairs={{0,6},{2,0},{4,2},{6,4},{1,7},{3,1},{5,3},{7,5},{8,14},{10,8},{12,... | collective-permute-start | bytes 983048 | tf_op jit(solution)/shard_map/ppermute | solution.py:67
  71.5 3.7 %collective-permute-done.6 = bf16[320,512]{1,0:T(8,128)(2,1)S(1)} collective-permute-done((bf16[320,512]{1,0:T(8,128)(2,1)S(1)}, bf16[320,512]{1,0:T(8,128)(2,1)S(1)}, u32[]{:S(2)}, u32[]{:S(2)}) %collective-permute-start.6) | collective-permute-done | bytes 327712 | tf_op jit(solution)/shard_map/ppermute | solution.py:66
  87.7 7.9 %all_to_all.30 = bf16[4,2,640,512]{3,2,0,1:T(8,128)(2,1)S(1)} all-to-all(bf16[4,2,640,512]{3,2,0,1:T(8,128)(2,1)S(1)} %broadcast_in_dim.51), channel_id=1, replica_groups=mesh['dp'=16,'fy'=4,'fc'=2] {'fc'}, dimensions={1} | all-to-all | bytes 10485760 | tf_op jit(solution)/shard_map/all_to_all | solution.py:72
  96.0 3.7 %copy-done.9 = bf16[4096,512]{1,0:T(8,128)(2,1)S(1)} copy-done((bf16[4096,512]{1,0:T(8,128)(2,1)S(1)}, bf16[4096,512]{1,0:T(8,128)(2,1)}, u32[]{:S(2)}) %copy-start.9) | copy-done | bytes 4194328
  106.6 3.1 %fusion.8 = bf16[640,8,512]{2,0,1:T(8,128)(2,1)S(1)} fusion(bf16[640,512,1]{1,0,2:T(8,128)(2,1)S(1)} %fusion.19, bf16[64,8,8,512]{3,2,1,0:T(8,128)(2,1)S(1)} %bitcast.195), kind=kOutput, calls=%fused_computation.13 | convolution fusion | flops 2686976000 | bytes 10092544 | tf_op jit(solution)/shard_map/rh,hfd->frd/dot_general | solution.py:121
  113.1 5.1 %collective-permute-done.4 = bf16[4,640,512]{2,1,0:T(8,128)(2,1)} collective-permute-done((bf16[4,640,512]{2,1,0:T(8,128)(2,1)}, bf16[4,640,512]{2,1,0:T(8,128)(2,1)}, u32[]{:S(2)}, u32[]{:S(2)}) %collective-permute-start.4) | collective-permute-done | bytes 2621472 | tf_op jit(solution)/shard_map/ppermute | solution.py:82
  118.2 4.8 %fusion.1 = bf16[4,640,512]{2,1,0:T(8,128)(2,1)} fusion(bf16[4,640,512]{2,1,0:T(8,128)(2,1)} %collective-permute-done.4, bf16[4,2,640,512]{3,2,1,0:T(8,128)(2,1)} %bitcast.175, s32[]{:T(128)S(6)} %select_n.76), kind=kLoop, calls=%fused_computation.6 | loop fusion | flops 5242880 | bytes 7864324 | tf_op jit(solution)/shard_map/convert_element_type | solution.py:83
  123.5 7.9 %all_to_all.31 = bf16[4,2,640,512]{3,2,0,1:T(8,128)(2,1)S(1)} all-to-all(bf16[4,2,640,512]{3,2,0,1:T(8,128)(2,1)S(1)} %broadcast_in_dim.57), channel_id=1, replica_groups=mesh['dp'=16,'fy'=4,'fc'=2] {'fc'}, dimensions={1} | all-to-all | bytes 10485760 | tf_op jit(solution)/shard_map/all_to_all | solution.py:72
  136.3 3.3 %fusion.20 = (bf16[640,512,1]{1,0,2:T(8,128)(2,1)S(1)}, bf16[640,512]{1,0:T(8,128)(2,1)S(1)}) fusion(f32[640,512]{1,0:T(8,128)S(1)} %copy-done.17, f32[640,512]{1,0:T(8,128)S(1)} %copy-done.15, bf16[8,640,512]{2,1,0:T(8,128)(2,1)S(1)} %bitcast.172, bf16[64,8,8,512]{3,2,1,0:T(8,128)(2,1)S(1)} %bitcast.196), kind=kOutput, calls=%fused_computation.43 | convolution fusion | flops 2688614400 | bytes 13369344 | tf_op jit(solution)/shard_map/dot_general | solution.py:149
  142.6 5.6 %add_convert_fusion = bf16[640,8,512]{2,0,1:T(8,128)(2,1)S(1)} fusion(f32[640,8,512]{2,0,1:T(8,128)S(1)} %fusion.26, bf16[640,512,1]{1,0,2:T(8,128)(2,1)S(1)} %get-tuple-element.53, bf16[8,512,512]{2,1,0:T(8,128)(2,1)} %bitcast.176), kind=kOutput, calls=%fused_computation.2 | convolution fusion | flops 2689597440 | bytes 20578304 | tf_op jit(solution)/shard_map/rh,fdh->frd/dot_general | solution.py:167
  152.8 3.2 %collective-permute-start.11 = (bf16[320,512]{1,0:T(8,128)(2,1)}, bf16[320,512]{1,0:T(8,128)(2,1)}, u32[]{:S(2)}, u32[]{:S(2)}) collective-permute-start(bf16[320,512]{1,0:T(8,128)(2,1)} %get-tuple-element.59), channel_id=1, source_target_pairs={{0,6},{2,0},{4,2},{6,4},{1,7},{3,1},{5,3},{7,5},{8,14},{10,8},{12,... | collective-permute-start | bytes 983048 | tf_op jit(solution)/shard_map/ppermute | solution.py:91
  156.0 8.3 %collective-permute-done.9 = bf16[320,512]{1,0:T(8,128)(2,1)} collective-permute-done((bf16[320,512]{1,0:T(8,128)(2,1)}, bf16[320,512]{1,0:T(8,128)(2,1)}, u32[]{:S(2)}, u32[]{:S(2)}) %collective-permute-start.9) | collective-permute-done | bytes 327712 | tf_op jit(solution)/shard_map/ppermute | solution.py:90
  169.0 7.5 %convolution_convert_fusion.2 = bf16[8,512,512]{2,1,0:T(8,128)(2,1)} fusion(bf16[8,640,512]{2,1,0:T(8,128)(2,1)} %bitcast.170, bf16[640,512]{1,0:T(8,128)(2,1)S(1)} %copy-done.23), kind=kOutput, calls=%fused_computation.16 | convolution fusion | flops 2686451712 | bytes 10092544 | tf_op jit(solution)/shard_map/frd,rh->fdh/dot_general | solution.py:155
  176.5 5.5 %collective-permute-done.12 = bf16[640,512]{1,0:T(8,128)(2,1)S(1)} collective-permute-done((bf16[640,512]{1,0:T(8,128)(2,1)S(1)}, bf16[640,512]{1,0:T(8,128)(2,1)S(1)}, u32[]{:S(2)}, u32[]{:S(2)}) %collective-permute-start.12) | collective-permute-done | bytes 655392 | tf_op jit(solution)/shard_map/ppermute | solution.py:97
  182.0 3.7 %collective-permute-done.10 = bf16[640,512]{1,0:T(8,128)(2,1)S(1)} collective-permute-done((bf16[640,512]{1,0:T(8,128)(2,1)S(1)}, bf16[640,512]{1,0:T(8,128)(2,1)S(1)}, u32[]{:S(2)}, u32[]{:S(2)}) %collective-permute-start.10) | collective-permute-done | bytes 655392 | tf_op jit(solution)/shard_map/ppermute | solution.py:96
  186.9 7.1 %all-to-all-start.3 = ((bf16[16,40,512]{2,1,0:T(8,128)(2,1)}), bf16[16,40,512]{2,1,0:T(8,128)(2,1)S(1)}, u32[]{:S(2)}, u32[]{:S(2)}) async-start(bf16[16,40,512]{2,1,0:T(8,128)(2,1)} %bitcast.186), calls=%async_computation.3 | async-start | bytes 1310720 | tf_op jit(solution)/shard_map/all_to_all | solution.py:101
  194.0 3.3 %fusion = bf16[4,640,512]{2,1,0:T(8,128)(2,1)S(1)} fusion(bf16[4,640,512]{2,1,0:T(8,128)(2,1)} %collective-permute-done.13, bf16[4,2,640,512]{3,2,1,0:T(8,128)(2,1)} %bitcast.163, s32[]{:T(128)S(6)} %select_n.76), kind=kLoop, calls=%fused_computation.4 | loop fusion | flops 5242880 | bytes 7864324 | tf_op jit(solution)/shard_map/convert_element_type | solution.py:83
  198.4 3.2 %collective-permute-start.16 = (bf16[320,512]{1,0:T(8,128)(2,1)}, bf16[320,512]{1,0:T(8,128)(2,1)}, u32[]{:S(2)}, u32[]{:S(2)}) collective-permute-start(bf16[320,512]{1,0:T(8,128)(2,1)} %get-tuple-element.51), channel_id=1, source_target_pairs={{0,6},{2,0},{4,2},{6,4},{1,7},{3,1},{5,3},{7,5},{8,14},{10,8},{12,... | collective-permute-start | bytes 983048 | tf_op jit(solution)/shard_map/ppermute | solution.py:91
  201.6 8.4 %convolution_convert_fusion = bf16[512,8,512]{0,2,1:T(8,128)(2,1)} fusion(bf16[640,512,1]{1,0,2:T(8,128)(2,1)S(1)} %copy-done.25, bf16[8,640,512]{2,1,0:T(8,128)(2,1)} %bitcast.173), kind=kOutput, calls=%fused_computation.14 | convolution fusion | flops 2686451712 | bytes 10092544 | tf_op jit(solution)/shard_map/rh,frd->hfd/dot_general | solution.py:161
  210.0 6.3 %copy.61 = bf16[512,4096]{1,0:T(8,128)(2,1)} copy(bf16[512,4096]{0,1:T(8,128)(2,1)} %bitcast.178) | data formatting | bytes 8388608
  221.7 14.0 %all-gather = f32[1024,2]{0,1:T(2,128)S(1)} all-gather(f32[128,2]{0,1:T(2,128)S(1)} %pad_maximum_fusion.6), channel_id=2, replica_groups=mesh['dp'=16,'fy'=4,'fc'=2] {'fy','fc'}, dimensions={0}, use_global_device_ids=true | all-gather | bytes 9216 | tf_op jit(solution)/shard_map/all_gather | solution.py:147
  237.3 6.9 %all-to-all-start.5 = ((bf16[16,40,512]{2,1,0:T(8,128)(2,1)}), bf16[16,40,512]{2,1,0:T(8,128)(2,1)S(1)}, u32[]{:S(2)}, u32[]{:S(2)}) async-start(bf16[16,40,512]{2,1,0:T(8,128)(2,1)} %bitcast.59), calls=%async_computation.5 | async-start | bytes 1310720 | tf_op jit(solution)/shard_map/all_to_all | solution.py:101
  244.3 7.6 %convolution_convert_fusion.1 = bf16[8,512,512]{2,1,0:T(8,128)(2,1)} fusion(bf16[8,640,512]{2,1,0:T(8,128)(2,1)} %bitcast.171, bf16[640,512,1]{1,0,2:T(8,128)(2,1)S(1)} %copy-done.21), kind=kOutput, calls=%fused_computation.15 | convolution fusion | flops 2686451712 | bytes 10092544 | tf_op jit(solution)/shard_map/frd,rh->fdh/dot_general | solution.py:158
  251.9 5.8 %all-to-all-done.5 = bf16[16,40,512]{2,1,0:T(8,128)(2,1)S(1)} async-done(((bf16[16,40,512]{2,1,0:T(8,128)(2,1)}), bf16[16,40,512]{2,1,0:T(8,128)(2,1)S(1)}, u32[]{:S(2)}, u32[]{:S(2)}) %all-to-all-start.5) | async-done | bytes 655392 | tf_op jit(solution)/shard_map/all_to_all | solution.py:101
  (141 shorter events, 65.7 us)
Async XLA Ops:
  0.6 14.1 %copy-start = (bf16[128,512]{1,0:T(8,128)(2,1)S(1)}, bf16[128,512]{1,0:T(8,128)(2,1)}, u32[]{:S(2)}) copy-start(bf16[128,512]{1,0:T(8,128)(2,1)} %param.9) | copy-start | bytes 393220
  6.7 20.9 %all-to-all-start.2 = ((bf16[16,40,512]{2,1,0:T(8,128)(2,1)}), bf16[16,40,512]{2,1,0:T(8,128)(2,1)S(1)}, u32[]{:S(2)}, u32[]{:S(2)}) async-start(bf16[16,40,512]{2,1,0:T(8,128)(2,1)} %bitcast.25), calls=%async_computation.2 | async-start | bytes 1310720 | tf_op jit(solution)/shard_map/all_to_all | solution.py:60
  27.6 47.6 %copy-start.10 = (bf16[16,40,512]{2,1,0:T(8,128)(2,1)}, bf16[16,40,512]{2,1,0:T(8,128)(2,1)S(1)}, u32[]{:S(2)}) copy-start(bf16[16,40,512]{2,1,0:T(8,128)(2,1)S(1)} %all-to-all-done.2) | copy-start | bytes 1966084
  28.5 15.2 %all-to-all-start = ((bf16[16,40,512]{2,1,0:T(8,128)(2,1)}), bf16[16,40,512]{2,1,0:T(8,128)(2,1)S(1)}, u32[]{:S(2)}, u32[]{:S(2)}) async-start(bf16[16,40,512]{2,1,0:T(8,128)(2,1)} %bitcast.6), calls=%async_computation | async-start | bytes 1310720 | tf_op jit(solution)/shard_map/all_to_all | solution.py:60
  32.1 18.3 %collective-permute-start.7 = (bf16[640,512]{1,0:T(8,128)(2,1)S(1)}, bf16[640,512]{1,0:T(8,128)(2,1)S(1)}, u32[]{:S(2)}, u32[]{:S(2)}) collective-permute-start(bf16[640,512]{1,0:T(8,128)(2,1)S(1)} %bitcast.182), channel_id=1, source_target_pairs={{0,6},{2,0},{4,2},{6,4},{1,7},{3,1},{5,3},{7,5},{8,14},{10,8},{12,... | collective-permute-start | bytes 1966088 | tf_op jit(solution)/shard_map/ppermute | solution.py:65
  35.2 19.0 %collective-permute-start.5 = (bf16[640,512]{1,0:T(8,128)(2,1)S(1)}, bf16[640,512]{1,0:T(8,128)(2,1)}, u32[]{:S(2)}, u32[]{:S(2)}) collective-permute-start(bf16[640,512]{1,0:T(8,128)(2,1)S(1)} %bitcast.183), channel_id=1, source_target_pairs={{0,2},{2,4},{4,6},{6,0},{1,3},{3,5},{5,7},{7,1},{8,10},{10,12},{12... | collective-permute-start | bytes 1966088 | tf_op jit(solution)/shard_map/ppermute | solution.py:64
  43.7 20.7 %collective-permute-start.2 = (bf16[640,512]{1,0:T(8,128)(2,1)S(1)}, bf16[640,512]{1,0:T(8,128)(2,1)S(1)}, u32[]{:S(2)}, u32[]{:S(2)}) collective-permute-start(bf16[640,512]{1,0:T(8,128)(2,1)S(1)} %bitcast.179), channel_id=1, source_target_pairs={{0,6},{2,0},{4,2},{6,4},{1,7},{3,1},{5,3},{7,5},{8,14},{10,8},{12,... | collective-permute-start | bytes 1966088 | tf_op jit(solution)/shard_map/ppermute | solution.py:65
  46.8 22.2 %collective-permute-start = (bf16[640,512]{1,0:T(8,128)(2,1)S(1)}, bf16[640,512]{1,0:T(8,128)(2,1)S(1)}, u32[]{:S(2)}, u32[]{:S(2)}) collective-permute-start(bf16[640,512]{1,0:T(8,128)(2,1)S(1)} %bitcast.180), channel_id=1, source_target_pairs={{0,2},{2,4},{4,6},{6,0},{1,3},{3,5},{5,7},{7,1},{8,10},{10,12},{12... | collective-permute-start | bytes 1966088 | tf_op jit(solution)/shard_map/ppermute | solution.py:64
  50.4 24.8 %copy-start.13 = (bf16[640,512]{1,0:T(8,128)(2,1)}, bf16[640,512]{1,0:T(8,128)(2,1)S(1)}, u32[]{:S(2)}) copy-start(bf16[640,512]{1,0:T(8,128)(2,1)S(1)} %collective-permute-done.7) | copy-start | bytes 1966084
  50.4 21.0 %collective-permute-start.8 = (bf16[320,512]{1,0:T(8,128)(2,1)S(1)}, bf16[320,512]{1,0:T(8,128)(2,1)S(1)}, u32[]{:S(2)}, u32[]{:S(2)}) collective-permute-start(bf16[320,512]{1,0:T(8,128)(2,1)S(1)} %slice.170), channel_id=1, source_target_pairs={{0,6},{2,0},{4,2},{6,4},{1,7},{3,1},{5,3},{7,5},{8,14},{10,8},{12,... | collective-permute-start | bytes 983048 | tf_op jit(solution)/shard_map/ppermute | solution.py:67
  55.2 20.0 %collective-permute-start.6 = (bf16[320,512]{1,0:T(8,128)(2,1)S(1)}, bf16[320,512]{1,0:T(8,128)(2,1)S(1)}, u32[]{:S(2)}, u32[]{:S(2)}) collective-permute-start(bf16[320,512]{1,0:T(8,128)(2,1)S(1)} %slice.169), channel_id=1, source_target_pairs={{0,2},{2,4},{4,6},{6,0},{1,3},{3,5},{5,7},{7,1},{8,10},{10,12},{12... | collective-permute-start | bytes 983048 | tf_op jit(solution)/shard_map/ppermute | solution.py:66
  64.5 10.8 %copy-start.11 = (bf16[640,512]{1,0:T(8,128)(2,1)}, bf16[640,512]{1,0:T(8,128)(2,1)S(1)}, u32[]{:S(2)}) copy-start(bf16[640,512]{1,0:T(8,128)(2,1)S(1)} %collective-permute-done.2) | copy-start | bytes 1966084
  65.3 14.0 %collective-permute-start.3 = (bf16[320,512]{1,0:T(8,128)(2,1)}, bf16[320,512]{1,0:T(8,128)(2,1)}, u32[]{:S(2)}, u32[]{:S(2)}) collective-permute-start(bf16[320,512]{1,0:T(8,128)(2,1)} %slice.168), channel_id=1, source_target_pairs={{0,6},{2,0},{4,2},{6,4},{1,7},{3,1},{5,3},{7,5},{8,14},{10,8},{12,... | collective-permute-start | bytes 983048 | tf_op jit(solution)/shard_map/ppermute | solution.py:67
  68.9 6.3 %copy-start.12 = (bf16[640,512]{1,0:T(8,128)(2,1)}, bf16[640,512]{1,0:T(8,128)(2,1)S(1)}, u32[]{:S(2)}) copy-start(bf16[640,512]{1,0:T(8,128)(2,1)S(1)} %collective-permute-done) | copy-start | bytes 1966084
  69.7 9.5 %collective-permute-start.1 = (bf16[320,512]{1,0:T(8,128)(2,1)}, bf16[320,512]{1,0:T(8,128)(2,1)}, u32[]{:S(2)}, u32[]{:S(2)}) collective-permute-start(bf16[320,512]{1,0:T(8,128)(2,1)} %slice.167), channel_id=1, source_target_pairs={{0,2},{2,4},{4,6},{6,0},{1,3},{3,5},{5,7},{7,1},{8,10},{10,12},{12... | collective-permute-start | bytes 983048 | tf_op jit(solution)/shard_map/ppermute | solution.py:66
  96.0 6.6 %copy-start.6 = (bf16[4,2,640,512]{3,2,1,0:T(8,128)(2,1)}, bf16[4,2,640,512]{3,2,1,0:T(8,128)(2,1)S(1)}, u32[]{:S(2)}) copy-start(bf16[4,2,640,512]{3,2,1,0:T(8,128)(2,1)S(1)} %copy.54) | copy-start | bytes 15728644
  113.0 5.3 %collective-permute-start.4 = (bf16[4,640,512]{2,1,0:T(8,128)(2,1)}, bf16[4,640,512]{2,1,0:T(8,128)(2,1)}, u32[]{:S(2)}, u32[]{:S(2)}) collective-permute-start(bf16[4,640,512]{2,1,0:T(8,128)(2,1)} %dynamic-slice_bitcast_fusion.1), channel_id=1, source_target_pairs={{0,1},{1,0},{2,3},{3,2},{4,5},{5,4},{6,7},{7,6},{8,9},{9,8},{10,11... | collective-permute-start | bytes 7864328 | tf_op jit(solution)/shard_map/ppermute | solution.py:82
  131.8 7.8 %copy-start.7 = (bf16[4,2,640,512]{3,2,1,0:T(8,128)(2,1)}, bf16[4,2,640,512]{3,2,1,0:T(8,128)(2,1)S(1)}, u32[]{:S(2)}) copy-start(bf16[4,2,640,512]{3,2,1,0:T(8,128)(2,1)S(1)} %copy.56) | copy-start | bytes 15728644
  151.7 42.3 %collective-permute-start.13 = (bf16[4,640,512]{2,1,0:T(8,128)(2,1)}, bf16[4,640,512]{2,1,0:T(8,128)(2,1)}, u32[]{:S(2)}, u32[]{:S(2)}) collective-permute-start(bf16[4,640,512]{2,1,0:T(8,128)(2,1)} %dynamic-slice_bitcast_fusion), channel_id=1, source_target_pairs={{0,1},{1,0},{2,3},{3,2},{4,5},{5,4},{6,7},{7,6},{8,9},{9,8},{10,11... | collective-permute-start | bytes 7864328 | tf_op jit(solution)/shard_map/ppermute | solution.py:82
  152.8 11.5 %collective-permute-start.9 = (bf16[320,512]{1,0:T(8,128)(2,1)}, bf16[320,512]{1,0:T(8,128)(2,1)}, u32[]{:S(2)}, u32[]{:S(2)}) collective-permute-start(bf16[320,512]{1,0:T(8,128)(2,1)} %get-tuple-element.57), channel_id=1, source_target_pairs={{0,2},{2,4},{4,6},{6,0},{1,3},{3,5},{5,7},{7,1},{8,10},{10,12},{12... | collective-permute-start | bytes 983048 | tf_op jit(solution)/shard_map/ppermute | solution.py:90
  152.8 11.5 %collective-permute-start.11 = (bf16[320,512]{1,0:T(8,128)(2,1)}, bf16[320,512]{1,0:T(8,128)(2,1)}, u32[]{:S(2)}, u32[]{:S(2)}) collective-permute-start(bf16[320,512]{1,0:T(8,128)(2,1)} %get-tuple-element.59), channel_id=1, source_target_pairs={{0,6},{2,0},{4,2},{6,4},{1,7},{3,1},{5,3},{7,5},{8,14},{10,8},{12,... | collective-permute-start | bytes 983048 | tf_op jit(solution)/shard_map/ppermute | solution.py:91
  156.0 12.9 %copy-start.23 = (bf16[640,512]{1,0:T(8,128)(2,1)S(1)}, bf16[640,512]{1,0:T(8,128)(2,1)}, u32[]{:S(2)}) copy-start(bf16[640,512]{1,0:T(8,128)(2,1)} %copy-done.22) | copy-start | bytes 1966084
  165.6 16.4 %collective-permute-start.12 = (bf16[640,512]{1,0:T(8,128)(2,1)S(1)}, bf16[640,512]{1,0:T(8,128)(2,1)S(1)}, u32[]{:S(2)}, u32[]{:S(2)}) collective-permute-start(bf16[640,512]{1,0:T(8,128)(2,1)S(1)} %pad_maximum_fusion.3), channel_id=1, source_target_pairs={{0,6},{2,0},{4,2},{6,4},{1,7},{3,1},{5,3},{7,5},{8,14},{10,8},{12,... | collective-permute-start | bytes 1966088 | tf_op jit(solution)/shard_map/ppermute | solution.py:97
  168.6 17.1 %collective-permute-start.10 = (bf16[640,512]{1,0:T(8,128)(2,1)S(1)}, bf16[640,512]{1,0:T(8,128)(2,1)S(1)}, u32[]{:S(2)}, u32[]{:S(2)}) collective-permute-start(bf16[640,512]{1,0:T(8,128)(2,1)S(1)} %pad_maximum_fusion.2), channel_id=1, source_target_pairs={{0,2},{2,4},{4,6},{6,0},{1,3},{3,5},{5,7},{7,1},{8,10},{10,12},{12... | collective-permute-start | bytes 1966088 | tf_op jit(solution)/shard_map/ppermute | solution.py:96
  186.9 29.5 %all-to-all-start.3 = ((bf16[16,40,512]{2,1,0:T(8,128)(2,1)}), bf16[16,40,512]{2,1,0:T(8,128)(2,1)S(1)}, u32[]{:S(2)}, u32[]{:S(2)}) async-start(bf16[16,40,512]{2,1,0:T(8,128)(2,1)} %bitcast.186), calls=%async_computation.3 | async-start | bytes 1310720 | tf_op jit(solution)/shard_map/all_to_all | solution.py:101
  198.4 18.1 %collective-permute-start.14 = (bf16[320,512]{1,0:T(8,128)(2,1)}, bf16[320,512]{1,0:T(8,128)(2,1)}, u32[]{:S(2)}, u32[]{:S(2)}) collective-permute-start(bf16[320,512]{1,0:T(8,128)(2,1)} %get-tuple-element.49), channel_id=1, source_target_pairs={{0,2},{2,4},{4,6},{6,0},{1,3},{3,5},{5,7},{7,1},{8,10},{10,12},{12... | collective-permute-start | bytes 983048 | tf_op jit(solution)/shard_map/ppermute | solution.py:90
  198.4 18.1 %collective-permute-start.16 = (bf16[320,512]{1,0:T(8,128)(2,1)}, bf16[320,512]{1,0:T(8,128)(2,1)}, u32[]{:S(2)}, u32[]{:S(2)}) collective-permute-start(bf16[320,512]{1,0:T(8,128)(2,1)} %get-tuple-element.51), channel_id=1, source_target_pairs={{0,6},{2,0},{4,2},{6,4},{1,7},{3,1},{5,3},{7,5},{8,14},{10,8},{12,... | collective-permute-start | bytes 983048 | tf_op jit(solution)/shard_map/ppermute | solution.py:91
  217.9 18.4 %collective-permute-start.17 = (bf16[640,512]{1,0:T(8,128)(2,1)S(1)}, bf16[640,512]{1,0:T(8,128)(2,1)S(1)}, u32[]{:S(2)}, u32[]{:S(2)}) collective-permute-start(bf16[640,512]{1,0:T(8,128)(2,1)S(1)} %pad_maximum_fusion.5), channel_id=1, source_target_pairs={{0,6},{2,0},{4,2},{6,4},{1,7},{3,1},{5,3},{7,5},{8,14},{10,8},{12,... | collective-permute-start | bytes 1966088 | tf_op jit(solution)/shard_map/ppermute | solution.py:97
  218.0 18.3 %collective-permute-start.15 = (bf16[640,512]{1,0:T(8,128)(2,1)S(1)}, bf16[640,512]{1,0:T(8,128)(2,1)S(1)}, u32[]{:S(2)}, u32[]{:S(2)}) collective-permute-start(bf16[640,512]{1,0:T(8,128)(2,1)S(1)} %pad_maximum_fusion.4), channel_id=1, source_target_pairs={{0,2},{2,4},{4,6},{6,0},{1,3},{3,5},{5,7},{7,1},{8,10},{10,12},{12... | collective-permute-start | bytes 1966088 | tf_op jit(solution)/shard_map/ppermute | solution.py:96
  220.5 23.7 %copy-start.21 = (bf16[640,512,1]{1,0,2:T(8,128)(2,1)S(1)}, bf16[640,512,1]{1,0,2:T(8,128)(2,1)}, u32[]{:S(2)}) copy-start(bf16[640,512,1]{1,0,2:T(8,128)(2,1)} %copy-done.20) | copy-start | bytes 1966084
  237.3 20.4 %all-to-all-start.5 = ((bf16[16,40,512]{2,1,0:T(8,128)(2,1)}), bf16[16,40,512]{2,1,0:T(8,128)(2,1)S(1)}, u32[]{:S(2)}, u32[]{:S(2)}) async-start(bf16[16,40,512]{2,1,0:T(8,128)(2,1)} %bitcast.59), calls=%async_computation.5 | async-start | bytes 1310720 | tf_op jit(solution)/shard_map/all_to_all | solution.py:101
  244.3 14.7 %copy-start.1 = (bf16[128,512]{1,0:T(8,128)(2,1)S(1)}, bf16[128,512]{1,0:T(8,128)(2,1)}, u32[]{:S(2)}) copy-start(bf16[128,512]{1,0:T(8,128)(2,1)} %param.9) | copy-start | bytes 393220
  (19 other events, 58.2 us)

commit v8 on v5

--- a/solution.py
+++ b/solution.py
@@ -138,7 +138,7 @@
         "frd,rh->fdh", expert_rows, up_grad, preferred_element_type=jnp.float32
     ).astype(jnp.bfloat16).reshape(fsdp_count * feat, hid)
     down_weight_grad = jnp.einsum(
-        "rh,frd->hfd", hidden, grad_rows, preferred_element_type=jnp.float32
+        "hr,frd->hfd", hidden.T, grad_rows, preferred_element_type=jnp.float32
     ).astype(jnp.bfloat16).reshape(hid, model)
     input_partial = jnp.einsum(
         "rh,fdh->frd", gate_grad, gate_w3, preferred_element_type=jnp.float32
@@ -147,7 +147,8 @@
         "rh,fdh->frd", up_grad, up_w3, preferred_element_type=jnp.float32
     )
     input_shares = scatter_chips(swap_cores(input_partial))
-    prob_grad, input_shares = lax.optimization_barrier((prob_grad, input_shares))
+    prob_grad, gate_weight_grad, up_weight_grad, down_weight_grad, input_shares = lax.optimization_barrier(
+        (prob_grad, gate_weight_grad, up_weight_grad, down_weight_grad, input_shares))
     input_slots = to_token_layout(input_shares)
     token_grad = jnp.dot(
         picker.astype(jnp.float32),

time: 209 us -> 208 us (level)
  matrix products: 49 us -> 46.7 us
    dot_general x1, matrix products: 7.58 us -> 5.05 us  [local(): jnp.einsum('frd,rh->fdh', expert_rows, up_grad, preferred_element_type=jn...]
    unnamed x40 -> x44, local copies, waits for them, and re-layouts: 21.3 us -> 21.3 us
  transfers between devices with their start and end apart: 9 -> 9, of which waited for: 6 -> 6; matrix products, arithmetic and copies ran while one was open for 33% -> 32% of each run, Pallas kernels for 0% -> 0%
where the time goes in v8:
time: 208 us; the launch traced here: 207 us
  waiting for transfers between devices  48.5 us (23%)
  matrix products  46.7 us (22%)
  blocking collectives  45.2 us (22%)
  local copies, waits for them, and re-layouts  28.9 us (14%)
  starting transfers between devices  14.8 us (7%)
  between operations  14.1 us (7%)
  other arithmetic  8.87 us (4%)
    unnamed x44, local copies, waits for them, and re-layouts  21.3 us
    all_to_all x1, blocking collectives, to_expert_layout(): lax.all_to_all(place_rows(source, scaled), 'dp', split_axis=0, concat_axi...  20.6 us
    all_to_all x2, blocking collectives, join_cores(): lax.all_to_all(jnp.broadcast_to(across[:, None], (chips, cores, rows, fea...  15.9 us
    all_gather x2, waiting for transfers between devices, to_expert_layout(): lax.all_gather(arrived.reshape(rows, feat), 'fy', axis=0, tiled=False)  14.1 us
    all_to_all x2, waiting for transfers between devices, to_token_layout(): lax.all_to_all(shares.reshape(dp_count, CAP, feat), 'dp', split_axis=0, c...  13 us
    all_to_all x1, waiting for transfers between devices, to_expert_layout(): lax.all_to_all(place_rows(source, scaled), 'dp', split_axis=0, concat_axi...  11.7 us
    all_to_all x2, starting transfers between devices, to_token_layout(): lax.all_to_all(shares.reshape(dp_count, CAP, feat), 'dp', split_axis=0, c...  10.5 us
    ppermute x2, waiting for transfers between devices, swap_cores(): lax.ppermute(sent, 'fc', swap).astype(jnp.float32)  9.67 us
  transfers between devices with their start and end apart: 9, of which 6 were waited for; matrix products, arithmetic and copies ran while one was open for 32% of the time, Pallas kernels for 0%

profile of v8, /device:TPU:0, one launch (start us, length us, event | category | flops | bytes accessed | tf_op | source)
XLA Modules:
  0.0 206.9 jit_solution(2024629733312966073)
XLA Ops:
  10.6 20.6 %all_to_all.30 = bf16[16,40,512]{2,1,0:T(8,128)(2,1)} all-to-all(bf16[16,40,512]{2,1,0:T(8,128)(2,1)S(1)} %bitcast.133), channel_id=1, replica_groups=mesh['dp'=16,'fy'=4,'fc'=2] {'dp'}, dimensions={0} | all-to-all | bytes 1310720 | tf_op jit(solution)/shard_map/all_to_all | solution.py:56
  32.0 1.5 convolution_convert_fusion.3
  34.4 3.6 %all-to-all-start.2 = ((bf16[16,40,512]{2,1,0:T(8,128)(2,1)}), bf16[16,40,512]{2,1,0:T(8,128)(2,1)S(1)}, u32[]{:S(2)}, u32[]{:S(2)}) async-start(bf16[16,40,512]{2,1,0:T(8,128)(2,1)} %bitcast.21), calls=%async_computation.2 | async-start | bytes 1310720 | tf_op jit(solution)/shard_map/all_to_all | solution.py:56
  38.1 11.7 %all-to-all-done.2 = bf16[16,40,512]{2,1,0:T(8,128)(2,1)S(1)} async-done(((bf16[16,40,512]{2,1,0:T(8,128)(2,1)}), bf16[16,40,512]{2,1,0:T(8,128)(2,1)S(1)}, u32[]{:S(2)}, u32[]{:S(2)}) %all-to-all-start.2) | async-done | bytes 655392 | tf_op jit(solution)/shard_map/all_to_all | solution.py:56
  50.7 14.1 %all-gather.4.cloned.1.call-done = bf16[4,640,512]{2,1,0:T(8,128)(2,1)} async-done(((bf16[1,640,512]{2,1,0:T(8,128)(2,1)}), bf16[4,640,512]{2,1,0:T(8,128)(2,1)}) %all-gather.4.cloned.1.call-update) | async-done | bytes 2621456 | tf_op jit(solution)/shard_map/all_gather | solution.py:59
  64.8 2.2 %broadcast_in_dim.42 = bf16[4,2,640,512]{3,2,0,1:T(8,128)(2,1)S(1)} broadcast(bf16[4,640,512]{2,1,0:T(8,128)(2,1)} %all-gather.4.cloned.1.call-done), dimensions={0,2,3} | broadcast | bytes 7864320 | tf_op jit(solution)/shard_map/broadcast_in_dim | solution.py:64
  67.0 7.9 %all_to_all.31 = bf16[4,2,640,512]{3,2,0,1:T(8,128)(2,1)S(1)} all-to-all(bf16[4,2,640,512]{3,2,0,1:T(8,128)(2,1)S(1)} %broadcast_in_dim.42), channel_id=1, replica_groups=mesh['dp'=16,'fy'=4,'fc'=2] {'fc'}, dimensions={1} | all-to-all | bytes 10485760 | tf_op jit(solution)/shard_map/all_to_all | solution.py:63
  75.3 3.9 %copy-done.7 = bf16[4096,512]{1,0:T(8,128)(2,1)S(1)} copy-done((bf16[4096,512]{1,0:T(8,128)(2,1)S(1)}, bf16[4096,512]{1,0:T(8,128)(2,1)}, u32[]{:S(2)}) %copy-start.7) | copy-done | bytes 4194328
  79.2 2.9 %convolution_bitcast_fusion = f32[640,512]{1,0:T(8,128)S(1)} fusion(bf16[8,640,512]{2,1,0:T(8,128)(2,1)S(1)} %bitcast.117, bf16[8,512,512]{2,1,0:T(8,128)(2,1)S(1)} %bitcast.128), kind=kOutput, calls=%fused_computation.18 | convolution fusion | flops 2684354560 | bytes 10747904 | tf_op jit(solution)/shard_map/dot_general | solution.py:96
  82.1 2.9 %convolution_bitcast_fusion.1 = f32[640,512]{1,0:T(8,128)S(1)} fusion(bf16[8,640,512]{2,1,0:T(8,128)(2,1)S(1)} %bitcast.118, bf16[8,512,512]{2,1,0:T(8,128)(2,1)S(1)} %bitcast.113), kind=kOutput, calls=%fused_computation.19 | convolution fusion | flops 2684354560 | bytes 10747904 | tf_op jit(solution)/shard_map/dot_general | solution.py:95
  86.0 3.2 %fusion.8 = bf16[640,8,512]{2,0,1:T(8,128)(2,1)S(1)} fusion(bf16[640,512,1]{1,0,2:T(8,128)(2,1)S(1)} %fusion.15, bf16[64,8,8,512]{3,2,1,0:T(8,128)(2,1)S(1)} %bitcast.141), kind=kOutput, calls=%fused_computation.11 | convolution fusion | flops 2686976000 | bytes 10092544 | tf_op jit(solution)/shard_map/rh,hfd->frd/dot_general | solution.py:100
  89.2 2.3 %copy-done.6 = bf16[640,8,512]{2,0,1:T(8,128)(2,1)} copy-done((bf16[640,8,512]{2,0,1:T(8,128)(2,1)}, bf16[640,8,512]{2,0,1:T(8,128)(2,1)S(1)}, u32[]{:S(2)}) %copy-start.6) | copy-done | bytes 5242904
  91.6 1.7 dynamic-slice_bitcast_fusion.1
  93.4 5.0 %collective-permute-done = bf16[4,640,512]{2,1,0:T(8,128)(2,1)S(1)} collective-permute-done((bf16[4,640,512]{2,1,0:T(8,128)(2,1)}, bf16[4,640,512]{2,1,0:T(8,128)(2,1)S(1)}, u32[]{:S(2)}, u32[]{:S(2)}) %collective-permute-start) | collective-permute-done | bytes 2621472 | tf_op jit(solution)/shard_map/ppermute | solution.py:73
  98.4 4.0 %fusion.1 = bf16[4,640,512]{2,1,0:T(8,128)(2,1)} fusion(bf16[4,640,512]{2,1,0:T(8,128)(2,1)S(1)} %collective-permute-done, bf16[4,2,640,512]{3,2,1,0:T(8,128)(2,1)} %bitcast.126, s32[]{:T(128)S(6)} %select_n.16), kind=kLoop, calls=%fused_computation.4 | loop fusion | flops 5242880 | bytes 7864324 | tf_op jit(solution)/shard_map/convert_element_type | solution.py:74
  102.4 1.7 copy-done.9
  104.5 7.9 %all_to_all.32 = bf16[4,2,640,512]{3,2,0,1:T(8,128)(2,1)S(1)} all-to-all(bf16[4,2,640,512]{3,2,0,1:T(8,128)(2,1)S(1)} %broadcast_in_dim.48), channel_id=1, replica_groups=mesh['dp'=16,'fy'=4,'fc'=2] {'fc'}, dimensions={1} | all-to-all | bytes 10485760 | tf_op jit(solution)/shard_map/all_to_all | solution.py:63
  115.6 1.9 copy-done.18
  117.5 3.3 %fusion.16 = (bf16[640,512,1]{1,0,2:T(8,128)(2,1)S(1)}, bf16[640,512]{1,0:T(8,128)(2,1)S(1)}) fusion(f32[640,512]{1,0:T(8,128)S(1)} %copy-done.13, f32[640,512]{1,0:T(8,128)S(1)} %copy-done.11, bf16[8,640,512]{2,1,0:T(8,128)(2,1)S(1)} %bitcast.123, bf16[64,8,8,512]{3,2,1,0:T(8,128)(2,1)S(1)} %bitcast.142), kind=kOutput, calls=%fused_computation.31 | convolution fusion | flops 2688614400 | bytes 13369344 | tf_op jit(solution)/shard_map/dot_general | solution.py:128
  120.8 3.0 %fusion.17 = f32[640,8,512]{2,0,1:T(8,128)S(1)} fusion(bf16[8,512,512]{2,1,0:T(8,128)(2,1)S(1)} %bitcast.114, bf16[640,512]{1,0:T(8,128)(2,1)S(1)} %get-tuple-element.53), kind=kOutput, calls=%fused_computation.32 | convolution fusion | flops 2684354560 | bytes 15335424 | tf_op jit(solution)/shard_map/rh,fdh->frd/dot_general | solution.py:143
  123.7 5.6 %add_convert_fusion = bf16[640,8,512]{2,0,1:T(8,128)(2,1)S(1)} fusion(f32[640,8,512]{2,0,1:T(8,128)S(1)} %fusion.17, bf16[640,512,1]{1,0,2:T(8,128)(2,1)S(1)} %get-tuple-element.52, bf16[8,512,512]{2,1,0:T(8,128)(2,1)} %bitcast.127), kind=kOutput, calls=%fused_computation | convolution fusion | flops 2689597440 | bytes 20578304 | tf_op jit(solution)/shard_map/rh,fdh->frd/dot_general | solution.py:146
  129.9 4.7 %collective-permute-done.1 = bf16[4,640,512]{2,1,0:T(8,128)(2,1)S(1)} collective-permute-done((bf16[4,640,512]{2,1,0:T(8,128)(2,1)S(1)}, bf16[4,640,512]{2,1,0:T(8,128)(2,1)S(1)}, u32[]{:S(2)}, u32[]{:S(2)}) %collective-permute-start.1) | collective-permute-done | bytes 2621472 | tf_op jit(solution)/shard_map/ppermute | solution.py:73
  134.5 2.3 %fusion = bf16[4,640,512]{2,1,0:T(8,128)(2,1)} fusion(bf16[4,640,512]{2,1,0:T(8,128)(2,1)S(1)} %collective-permute-done.1, bf16[4,2,640,512]{3,2,1,0:T(8,128)(2,1)S(1)} %bitcast.112, s32[]{:T(128)S(6)} %select_n.16), kind=kLoop, calls=%fused_computation.2 | loop fusion | flops 5242880 | bytes 7864324 | tf_op jit(solution)/shard_map/convert_element_type | solution.py:74
  136.9 8.7 %convolution_convert_fusion = bf16[512,8,512]{0,2,1:T(8,128)(2,1)} fusion(bf16[640,512,1]{1,0,2:T(8,128)(2,1)S(1)} %fusion.15, bf16[8,640,512]{2,1,0:T(8,128)(2,1)} %bitcast.124), kind=kOutput, calls=%fused_computation.12 | convolution fusion | flops 2686451712 | bytes 10092544 | tf_op jit(solution)/shard_map/hr,frd->hfd/dot_general | solution.py:140
  145.6 5.0 %convolution_convert_fusion.1 = bf16[8,512,512]{2,1,0:T(8,128)(2,1)} fusion(bf16[8,640,512]{2,1,0:T(8,128)(2,1)S(1)} %bitcast.122, bf16[640,512,1]{1,0,2:T(8,128)(2,1)S(1)} %get-tuple-element.52), kind=kOutput, calls=%fused_computation.13 | convolution fusion | flops 2686451712 | bytes 10092544 | tf_op jit(solution)/shard_map/frd,rh->fdh/dot_general | solution.py:137
  150.6 6.9 %all-to-all-start.3 = ((bf16[16,40,512]{2,1,0:T(8,128)(2,1)}), bf16[16,40,512]{2,1,0:T(8,128)(2,1)S(1)}, u32[]{:S(2)}, u32[]{:S(2)}) async-start(bf16[16,40,512]{2,1,0:T(8,128)(2,1)} %bitcast.135), calls=%async_computation.4 | async-start | bytes 1310720 | tf_op jit(solution)/shard_map/all_to_all | solution.py:80
  157.6 7.6 %convolution_convert_fusion.2 = bf16[8,512,512]{2,1,0:T(8,128)(2,1)} fusion(bf16[8,640,512]{2,1,0:T(8,128)(2,1)} %bitcast.119, bf16[640,512]{1,0:T(8,128)(2,1)S(1)} %get-tuple-element.53), kind=kOutput, calls=%fused_computation.14 | convolution fusion | flops 2686451712 | bytes 10092544 | tf_op jit(solution)/shard_map/frd,rh->fdh/dot_general | solution.py:134
  165.2 5.6 %all-to-all-done.3 = bf16[16,40,512]{2,1,0:T(8,128)(2,1)S(1)} async-done(((bf16[16,40,512]{2,1,0:T(8,128)(2,1)}), bf16[16,40,512]{2,1,0:T(8,128)(2,1)S(1)}, u32[]{:S(2)}, u32[]{:S(2)}) %all-to-all-start.3) | async-done | bytes 655392 | tf_op jit(solution)/shard_map/all_to_all | solution.py:80
  172.6 8.7 %all-gather = f32[1024,2]{0,1:T(2,128)S(1)} all-gather(f32[128,2]{0,1:T(2,128)S(1)} %pad_maximum_fusion), channel_id=2, replica_groups=mesh['dp'=16,'fy'=4,'fc'=2] {'fy','fc'}, dimensions={0}, use_global_device_ids=true | all-gather | bytes 9216 | tf_op jit(solution)/shard_map/all_gather | solution.py:126
  181.8 3.6 %all-to-all-start.5 = ((bf16[16,40,512]{2,1,0:T(8,128)(2,1)}), bf16[16,40,512]{2,1,0:T(8,128)(2,1)S(1)}, u32[]{:S(2)}, u32[]{:S(2)}) async-start(bf16[16,40,512]{2,1,0:T(8,128)(2,1)} %bitcast.136), calls=%async_computation.7 | async-start | bytes 1310720 | tf_op jit(solution)/shard_map/all_to_all | solution.py:80
  185.4 6.4 %copy.61 = bf16[512,4096]{1,0:T(8,128)(2,1)} copy(bf16[512,4096]{0,1:T(8,128)(2,1)} %bitcast.129) | data formatting | bytes 8388608
  191.8 7.4 %all-to-all-done.5 = bf16[16,40,512]{2,1,0:T(8,128)(2,1)S(1)} async-done(((bf16[16,40,512]{2,1,0:T(8,128)(2,1)}), bf16[16,40,512]{2,1,0:T(8,128)(2,1)S(1)}, u32[]{:S(2)}, u32[]{:S(2)}) %all-to-all-start.5) | async-done | bytes 655392 | tf_op jit(solution)/shard_map/all_to_all | solution.py:80
  (81 shorter events, 15.2 us)
Async XLA Ops:
  7.2 3.0 %copy-start = (bf16[128,512]{1,0:T(8,128)(2,1)S(1)}, bf16[128,512]{1,0:T(8,128)(2,1)}, u32[]{:S(2)}) copy-start(bf16[128,512]{1,0:T(8,128)(2,1)} %param.7) | copy-start | bytes 393220
  7.2 57.6 %all-gather.4.cloned.1.call-start = ((), (), s32[]{:S(2)}) async-start(), calls=%async_computation.8 | async-start | bytes 3276800 | tf_op jit(solution)/shard_map/all_gather | solution.py:59
  32.0 35.0 %copy-start.15 = (f32[128]{0:T(128)}, f32[128]{0:T(128)S(1)}, u32[]{:S(2)}) copy-start(f32[128]{0:T(128)S(1)} %get-tuple-element.56) | copy-start | bytes 1540
  34.4 15.4 %all-to-all-start.2 = ((bf16[16,40,512]{2,1,0:T(8,128)(2,1)}), bf16[16,40,512]{2,1,0:T(8,128)(2,1)S(1)}, u32[]{:S(2)}, u32[]{:S(2)}) async-start(bf16[16,40,512]{2,1,0:T(8,128)(2,1)} %bitcast.21), calls=%async_computation.2 | async-start | bytes 1310720 | tf_op jit(solution)/shard_map/all_to_all | solution.py:56
  38.0 64.3 %all-gather.6.cloned.1.call-start = ((), (), s32[]{:S(2)}) async-start(), calls=%async_computation.9 | async-start | bytes 3276800 | tf_op jit(solution)/shard_map/all_gather | solution.py:59
  49.8 0.8 copy-start.8
  50.6 100.0 %reduce-scatter.3.cloned.1.call-start = ((), (), s32[]{:S(2)}) async-start(), calls=%async_computation.10 | async-start | bytes 3276800 | tf_op jit(solution)/shard_map/reduce_scatter | solution.py:77
  75.0 4.2 %copy-start.7 = (bf16[4096,512]{1,0:T(8,128)(2,1)S(1)}, bf16[4096,512]{1,0:T(8,128)(2,1)}, u32[]{:S(2)}) copy-start(bf16[4096,512]{1,0:T(8,128)(2,1)} %param.11) | copy-start | bytes 12582916
  75.3 6.8 %copy-start.4 = (bf16[4,2,640,512]{3,2,1,0:T(8,128)(2,1)}, bf16[4,2,640,512]{3,2,1,0:T(8,128)(2,1)S(1)}, u32[]{:S(2)}) copy-start(bf16[4,2,640,512]{3,2,1,0:T(8,128)(2,1)S(1)} %copy.54) | copy-start | bytes 15728644
  79.2 2.9 %copy-start.2 = (bf16[4096,512]{1,0:T(8,128)(2,1)S(1)}, bf16[4096,512]{1,0:T(8,128)(2,1)}, u32[]{:S(2)}) copy-start(bf16[4096,512]{1,0:T(8,128)(2,1)} %param.10) | copy-start | bytes 12582916
  82.0 2.9 %copy-start.10 = (f32[640,512]{1,0:T(8,128)}, f32[640,512]{1,0:T(8,128)S(1)}, u32[]{:S(2)}) copy-start(f32[640,512]{1,0:T(8,128)S(1)} %convolution_bitcast_fusion) | copy-start | bytes 3932164
  82.1 3.9 %copy-start.17 = (bf16[512,4096]{1,0:T(8,128)(2,1)S(1)}, bf16[512,4096]{1,0:T(8,128)(2,1)}, u32[]{:S(2)}) copy-start(bf16[512,4096]{1,0:T(8,128)(2,1)} %param.12) | copy-start | bytes 12582916
  85.0 1.1 copy-start.12
  89.2 2.3 %copy-start.6 = (bf16[640,8,512]{2,0,1:T(8,128)(2,1)}, bf16[640,8,512]{2,0,1:T(8,128)(2,1)S(1)}, u32[]{:S(2)}) copy-start(bf16[640,8,512]{2,0,1:T(8,128)(2,1)S(1)} %fusion.8) | copy-start | bytes 15728644
  93.2 5.1 %collective-permute-start = (bf16[4,640,512]{2,1,0:T(8,128)(2,1)}, bf16[4,640,512]{2,1,0:T(8,128)(2,1)S(1)}, u32[]{:S(2)}, u32[]{:S(2)}) collective-permute-start(bf16[4,640,512]{2,1,0:T(8,128)(2,1)} %dynamic-slice_bitcast_fusion.1), channel_id=1, source_target_pairs={{0,1},{1,0},{2,3},{3,2},{4,5},{5,4},{6,7},{7,6},{8,9},{9,8},{10,11... | collective-permute-start | bytes 7864328 | tf_op jit(solution)/shard_map/ppermute | solution.py:73
  102.3 1.7 copy-start.9
  102.4 79.5 %reduce-scatter.5.cloned.1.call-start = ((), (), s32[]{:S(2)}) async-start(), calls=%async_computation.11 | async-start | bytes 3276800 | tf_op jit(solution)/shard_map/reduce_scatter | solution.py:77
  112.5 1.7 copy-start.11
  112.5 3.1 %copy-start.13 = (f32[640,512]{1,0:T(8,128)S(1)}, f32[640,512]{1,0:T(8,128)}, u32[]{:S(2)}) copy-start(f32[640,512]{1,0:T(8,128)} %copy-done.12) | copy-start | bytes 3932164
  112.5 5.0 %copy-start.18 = (bf16[512,4096]{1,0:T(8,128)(2,1)S(1)}, bf16[512,4096]{1,0:T(8,128)(2,1)}, u32[]{:S(2)}) copy-start(bf16[512,4096]{1,0:T(8,128)(2,1)} %param.12) | copy-start | bytes 12582916
  112.8 7.9 %copy-start.5 = (bf16[4,2,640,512]{3,2,1,0:T(8,128)(2,1)}, bf16[4,2,640,512]{3,2,1,0:T(8,128)(2,1)S(1)}, u32[]{:S(2)}) copy-start(bf16[4,2,640,512]{3,2,1,0:T(8,128)(2,1)S(1)} %copy.56) | copy-start | bytes 15728644
  117.5 3.3 %copy-start.3 = (bf16[4096,512]{1,0:T(8,128)(2,1)S(1)}, bf16[4096,512]{1,0:T(8,128)(2,1)}, u32[]{:S(2)}) copy-start(bf16[4096,512]{1,0:T(8,128)(2,1)} %param.10) | copy-start | bytes 12582916
  129.6 5.0 %collective-permute-start.1 = (bf16[4,640,512]{2,1,0:T(8,128)(2,1)S(1)}, bf16[4,640,512]{2,1,0:T(8,128)(2,1)S(1)}, u32[]{:S(2)}, u32[]{:S(2)}) collective-permute-start(bf16[4,640,512]{2,1,0:T(8,128)(2,1)S(1)} %dynamic-slice_bitcast_fusion), channel_id=1, source_target_pairs={{0,1},{1,0},{2,3},{3,2},{4,5},{5,4},{6,7},{7,6},{8,9},{9,8},{10,11... | collective-permute-start | bytes 7864328 | tf_op jit(solution)/shard_map/ppermute | solution.py:73
  136.9 8.7 %slice-start = ((s8[5242880]{0:T(1024)(128)(4,1)}), s8[1048576]{0:T(1024)(128)(4,1)S(1)}, s32[]{:S(2)}) async-start(s8[5242880]{0:T(1024)(128)(4,1)} %bitcast.120), calls=%async_computation.12 | async-start | bytes 2097152
  136.9 8.7 %slice-start.1 = ((s8[5242880]{0:T(1024)(128)(4,1)}), s8[4194304]{0:T(1024)(128)(4,1)S(1)}, s32[]{:S(2)}) async-start(s8[5242880]{0:T(1024)(128)(4,1)} %bitcast.120), calls=%async_computation.13 | async-start | bytes 8388608
  150.6 20.2 %all-to-all-start.3 = ((bf16[16,40,512]{2,1,0:T(8,128)(2,1)}), bf16[16,40,512]{2,1,0:T(8,128)(2,1)S(1)}, u32[]{:S(2)}, u32[]{:S(2)}) async-start(bf16[16,40,512]{2,1,0:T(8,128)(2,1)} %bitcast.135), calls=%async_computation.4 | async-start | bytes 1310720 | tf_op jit(solution)/shard_map/all_to_all | solution.py:80
  157.6 13.8 %copy-start.14 = (bf16[128,512]{1,0:T(8,128)(2,1)S(1)}, bf16[128,512]{1,0:T(8,128)(2,1)}, u32[]{:S(2)}) copy-start(bf16[128,512]{1,0:T(8,128)(2,1)} %param.13) | copy-start | bytes 393220
  157.6 13.8 %copy-start.16 = (f32[128]{0:T(128)S(1)}, f32[128]{0:T(128)}, u32[]{:S(2)}) copy-start(f32[128]{0:T(128)} %copy-done.15) | copy-start | bytes 1540
  181.8 17.4 %all-to-all-start.5 = ((bf16[16,40,512]{2,1,0:T(8,128)(2,1)}), bf16[16,40,512]{2,1,0:T(8,128)(2,1)S(1)}, u32[]{:S(2)}, u32[]{:S(2)}) async-start(bf16[16,40,512]{2,1,0:T(8,128)(2,1)} %bitcast.136), calls=%async_computation.7 | async-start | bytes 1310720 | tf_op jit(solution)/shard_map/all_to_all | solution.py:80
  185.4 15.0 %copy-start.1 = (bf16[128,512]{1,0:T(8,128)(2,1)S(1)}, bf16[128,512]{1,0:T(8,128)(2,1)}, u32[]{:S(2)}) copy-start(bf16[128,512]{1,0:T(8,128)(2,1)} %param.7) | copy-start | bytes 393220
Sparse Core Ops, SparseCore 0:
  31.4 33.3 all-gather.3
  66.4 35.2 all-gather.5
  104.8 34.0 reduce-scatter.2
  141.1 33.6 reduce-scatter.4

commit v9 on v8

--- a/solution.py
+++ b/solution.py
@@ -60,11 +60,12 @@
         return across
 
     def join_cores(across):
+        by_row = jnp.transpose(across, (1, 0, 2))[:, :, None, :]
         both = lax.all_to_all(
-            jnp.broadcast_to(across[:, None], (chips, cores, rows, feat)),
-            "fc", split_axis=1, concat_axis=1, tiled=True,
+            jnp.broadcast_to(by_row, (rows, chips, cores, feat)),
+            "fc", split_axis=2, concat_axis=2, tiled=True,
         )
-        return both.reshape(fsdp_count, rows, feat)
+        return both.reshape(rows, fsdp_count * feat)
 
     def swap_cores(partial_value):
         blocks = partial_value.astype(jnp.bfloat16).reshape(chips, cores, rows, feat)
@@ -89,11 +90,11 @@
     gate_w3 = w_gate.reshape(fsdp_count, feat, hid)
     up_w3 = w_up.reshape(fsdp_count, feat, hid)
     down_w3 = w_down.reshape(hid, fsdp_count, feat)
-    in_dims = (((0, 2), (0, 1)), ((), ()))
+
 
     expert_rows = join_cores(to_expert_layout(tokens, False))
-    gate_proj = lax.dot_general(expert_rows, gate_w3, in_dims, preferred_element_type=jnp.float32)
-    up_proj = lax.dot_general(expert_rows, up_w3, in_dims, preferred_element_type=jnp.float32)
+    gate_proj = jnp.dot(expert_rows, w_gate, preferred_element_type=jnp.float32)
+    up_proj = jnp.dot(expert_rows, w_up, preferred_element_type=jnp.float32)
     sigmoid_gate = jax.nn.sigmoid(gate_proj)
     activated = gate_proj * sigmoid_gate
     hidden = (activated * up_proj).astype(jnp.bfloat16)
@@ -125,21 +126,22 @@
     )
     prob_grad = jnp.sum(lax.all_gather(prob_terms, ("fy", "fc"), axis=0, tiled=False), axis=0)
     grad_rows = join_cores(grad_across)
-    hidden_grad = lax.dot_general(grad_rows, down_w3, (((0, 2), (1, 2)), ((), ())),
-                                  preferred_element_type=jnp.float32)
+    hidden_grad = lax.dot_general(grad_rows, w_down, back_dims, preferred_element_type=jnp.float32)
     gate_grad = (
         hidden_grad * up_proj * sigmoid_gate * (1.0 + gate_proj * (1.0 - sigmoid_gate))
     ).astype(jnp.bfloat16)
     up_grad = (hidden_grad * activated).astype(jnp.bfloat16)
-    gate_weight_grad = jnp.einsum(
-        "frd,rh->fdh", expert_rows, gate_grad, preferred_element_type=jnp.float32
-    ).astype(jnp.bfloat16).reshape(fsdp_count * feat, hid)
-    up_weight_grad = jnp.einsum(
-        "frd,rh->fdh", expert_rows, up_grad, preferred_element_type=jnp.float32
-    ).astype(jnp.bfloat16).reshape(fsdp_count * feat, hid)
-    down_weight_grad = jnp.einsum(
-        "hr,frd->hfd", hidden.T, grad_rows, preferred_element_type=jnp.float32
-    ).astype(jnp.bfloat16).reshape(hid, model)
+    out_slots, expert_rows, gate_grad_w, up_grad_w, grad_rows_w = lax.optimization_barrier(
+        (out_slots, expert_rows, gate_grad, up_grad, grad_rows))
+    gate_weight_grad = lax.dot_general(
+        expert_rows, gate_grad_w, contract_rows, preferred_element_type=jnp.float32
+    ).astype(jnp.bfloat16)
+    up_weight_grad = lax.dot_general(
+        expert_rows, up_grad_w, contract_rows, preferred_element_type=jnp.float32
+    ).astype(jnp.bfloat16)
+    down_weight_grad = lax.dot_general(
+        hidden, grad_rows_w, contract_rows, preferred_element_type=jnp.float32
+    ).astype(jnp.bfloat16)
     input_partial = jnp.einsum(
         "rh,fdh->frd", gate_grad, gate_w3, preferred_element_type=jnp.float32
     )

time: 208 us -> 239 us (1.15)
  blocking collectives: 45.2 us -> 85.2 us
  waiting for transfers between devices: 48.5 us -> 35.5 us
  starting transfers between devices: 14.8 us -> 4.41 us
  local copies, waits for them, and re-layouts: 28.9 us -> 38.1 us
  matrix products: 46.7 us -> 52 us
    all_to_all x2 -> x4, blocking collectives: 15.9 us -> 55.4 us  [the longest x2 37.2 us: to_token_layout(): lax.all_to_all(shares.reshape(dp_count, CAP, feat), 'dp', split_axis=0, c...]
    all_to_all x2, local copies, waits for them, and re-layouts: 0.68 us -> 19.5 us  [join_cores(): lax.all_to_all(jnp.broadcast_to(by_row, (rows, chips, cores, feat)), 'fc'...]
    unnamed x44 -> x31, local copies, waits for them, and re-layouts: 21.3 us -> 4.14 us
    all_to_all x2 -> x0, waiting for transfers between devices: 13 us -> none  [to_token_layout(): lax.all_to_all(shares.reshape(dp_count, CAP, feat), 'dp', split_axis=0, c...]
    all_to_all x2 -> x0, starting transfers between devices: 10.5 us -> none  [to_token_layout(): lax.all_to_all(shares.reshape(dp_count, CAP, feat), 'dp', split_axis=0, c...]
    transpose x0 -> x2, local copies, waits for them, and re-layouts: none -> 7.53 us  [join_cores(): by_row = jnp.transpose(across, (1, 0, 2))[:, :, None, :]]
    dot_general x6, matrix products: 30.3 us -> 35.8 us  [the longest x1 7.73 us: local(): lax.dot_general(hidden, grad_rows_w, contract_rows, preferred_element_typ...]
  transfers between devices with their start and end apart: 9 -> 7, of which waited for: 6 -> 4; matrix products, arithmetic and copies ran while one was open for 32% -> 37% of each run, Pallas kernels for 0% -> 0%
where the time goes in v9:
time: 239 us; the launch traced here: 238 us
  blocking collectives  85.2 us (36%)
  matrix products  52 us (22%)
  local copies, waits for them, and re-layouts  38.1 us (16%)
  waiting for transfers between devices  35.5 us (15%)
  between operations  14 us (6%)
  other arithmetic  8.57 us (4%)
  starting transfers between devices  4.41 us (2%)
    all_to_all x2, blocking collectives, to_token_layout(): lax.all_to_all(shares.reshape(dp_count, CAP, feat), 'dp', split_axis=0, c...  37.2 us
    all_to_all x1, blocking collectives, to_expert_layout(): lax.all_to_all(place_rows(source, scaled), 'dp', split_axis=0, concat_axi...  20.6 us
    all_to_all x2, local copies, waits for them, and re-layouts, join_cores(): lax.all_to_all(jnp.broadcast_to(by_row, (rows, chips, cores, feat)), 'fc'...  19.5 us
    all_to_all x2, blocking collectives, join_cores(): lax.all_to_all(jnp.broadcast_to(by_row, (rows, chips, cores, feat)), 'fc'...  18.2 us
    all_gather x2, waiting for transfers between devices, to_expert_layout(): lax.all_gather(arrived.reshape(rows, feat), 'fy', axis=0, tiled=False)  14.1 us
    all_to_all x1, waiting for transfers between devices, to_expert_layout(): lax.all_to_all(place_rows(source, scaled), 'dp', split_axis=0, concat_axi...  11.7 us
    ppermute x2, waiting for transfers between devices, swap_cores(): lax.ppermute(sent, 'fc', swap).astype(jnp.float32)  9.71 us
    all_gather x1, blocking collectives, local(): lax.all_gather(prob_terms, ('fy', 'fc'), axis=0, tiled=False)  9.18 us
  transfers between devices with their start and end apart: 7, of which 4 were waited for; matrix products, arithmetic and copies ran while one was open for 37% of the time, Pallas kernels for 0%

profile of v9, /device:TPU:0, one launch (start us, length us, event | category | flops | bytes accessed | tf_op | source)
XLA Modules:
  0.0 237.8 jit_solution(17807022526239269358)
XLA Ops:
  10.6 20.6 %all_to_all.30 = bf16[16,40,512]{2,1,0:T(8,128)(2,1)} all-to-all(bf16[16,40,512]{2,1,0:T(8,128)(2,1)S(1)} %bitcast.117), channel_id=1, replica_groups=mesh['dp'=16,'fy'=4,'fc'=2] {'dp'}, dimensions={0} | all-to-all | bytes 1310720 | tf_op jit(solution)/shard_map/all_to_all | solution.py:56
  32.0 1.5 convolution_convert_fusion.3
  34.4 3.6 %all-to-all-start.2 = ((bf16[16,40,512]{2,1,0:T(8,128)(2,1)}), bf16[16,40,512]{2,1,0:T(8,128)(2,1)S(1)}, u32[]{:S(2)}, u32[]{:S(2)}) async-start(bf16[16,40,512]{2,1,0:T(8,128)(2,1)} %bitcast.18), calls=%async_computation.2 | async-start | bytes 1310720 | tf_op jit(solution)/shard_map/all_to_all | solution.py:56
  38.1 11.7 %all-to-all-done.2 = bf16[16,40,512]{2,1,0:T(8,128)(2,1)S(1)} async-done(((bf16[16,40,512]{2,1,0:T(8,128)(2,1)}), bf16[16,40,512]{2,1,0:T(8,128)(2,1)S(1)}, u32[]{:S(2)}, u32[]{:S(2)}) %all-to-all-start.2) | async-done | bytes 655392 | tf_op jit(solution)/shard_map/all_to_all | solution.py:56
  50.7 14.1 %all-gather.4.cloned.1.call-done = bf16[4,640,512]{2,1,0:T(8,128)(2,1)} async-done(((bf16[1,640,512]{2,1,0:T(8,128)(2,1)}), bf16[4,640,512]{2,1,0:T(8,128)(2,1)}) %all-gather.4.cloned.1.call-update) | async-done | bytes 2621456 | tf_op jit(solution)/shard_map/all_gather | solution.py:59
  64.8 3.8 %copy.49 = bf16[640,4,512]{2,1,0:T(4,128)(2,1)S(1)} copy(bf16[640,4,512]{2,0,1:T(8,128)(2,1)} %bitcast.112) | data formatting | bytes 5242880 | tf_op jit(solution)/shard_map/transpose | solution.py:63
  68.5 1.4 broadcast_in_dim.42
  69.9 9.1 %all_to_all.31 = bf16[640,4,2,512]{3,1,0,2:T(4,128)(2,1)} all-to-all(bf16[640,4,2,512]{3,1,0,2:T(4,128)(2,1)S(1)} %broadcast_in_dim.42), channel_id=1, replica_groups=mesh['dp'=16,'fy'=4,'fc'=2] {'fc'}, dimensions={2} | all-to-all | bytes 10485760 | tf_op jit(solution)/shard_map/all_to_all | solution.py:64
  79.0 9.7 %copy.50 = bf16[640,4,2,512]{0,3,2,1:T(8,128)(2,1)} copy(bf16[640,4,2,512]{3,1,0,2:T(4,128)(2,1)} %all_to_all.31) | data formatting | bytes 10485760 | tf_op jit(solution)/shard_map/all_to_all | solution.py:64
  88.7 6.6 %fusion.38 = f32[640,512]{1,0:T(8,128)S(1)} fusion(bf16[640,4096]{0,1:T(8,128)(2,1)} %bitcast.101, bf16[4096,512]{1,0:T(8,128)(2,1)} %param.10), kind=kOutput, calls=%fused_computation.67 | convolution fusion | flops 2684354560 | bytes 10747904 | tf_op jit(solution)/shard_map/dot_general | solution.py:96
  95.3 4.0 %multiply_convert_fusion.2 = (bf16[640,512]{1,0:T(8,128)(2,1)S(1)}, f32[640,512]{1,0:T(8,128)}) fusion(f32[640,512]{1,0:T(8,128)S(1)} %fusion.38, bf16[640,4096]{0,1:T(8,128)(2,1)S(1)} %bitcast.102, bf16[4096,512]{1,0:T(8,128)(2,1)S(1)} %copy-done.5), kind=kOutput, calls=%fused_computation.18 | convolution fusion | flops 2686320640 | bytes 12713984 | tf_op jit(solution)/shard_map/dot_general | solution.py:97
  99.3 3.1 %fusion.5 = bf16[640,8,512]{2,0,1:T(8,128)(2,1)S(1)} fusion(bf16[64,8,8,512]{3,2,1,0:T(8,128)(2,1)S(1)} %bitcast.125, bf16[640,512]{1,0:T(8,128)(2,1)S(1)} %get-tuple-element.37), kind=kOutput, calls=%fused_computation.11 | convolution fusion | flops 2686976000 | bytes 10092544 | tf_op jit(solution)/shard_map/rh,hfd->frd/dot_general | solution.py:101
  102.5 2.3 copy-done.4
  104.8 1.7 dynamic-slice_bitcast_fusion.1
  106.6 5.0 %collective-permute-done = bf16[4,640,512]{2,1,0:T(8,128)(2,1)S(1)} collective-permute-done((bf16[4,640,512]{2,1,0:T(8,128)(2,1)}, bf16[4,640,512]{2,1,0:T(8,128)(2,1)S(1)}, u32[]{:S(2)}, u32[]{:S(2)}) %collective-permute-start) | collective-permute-done | bytes 2621472 | tf_op jit(solution)/shard_map/ppermute | solution.py:74
  111.6 4.0 %fusion.1 = bf16[4,640,512]{2,1,0:T(8,128)(2,1)} fusion(bf16[4,640,512]{2,1,0:T(8,128)(2,1)S(1)} %collective-permute-done, bf16[4,2,640,512]{3,2,1,0:T(8,128)(2,1)} %bitcast.110, s32[]{:T(128)S(6)} %select_n.16), kind=kLoop, calls=%fused_computation.7 | loop fusion | flops 5242880 | bytes 7864324 | tf_op jit(solution)/shard_map/convert_element_type | solution.py:75
  115.6 3.8 %copy.52 = bf16[640,4,512]{2,1,0:T(4,128)(2,1)S(1)} copy(bf16[640,4,512]{2,0,1:T(8,128)(2,1)} %bitcast.113) | data formatting | bytes 5242880 | tf_op jit(solution)/shard_map/transpose | solution.py:63
  119.4 1.4 broadcast_in_dim.48
  120.8 9.1 %all_to_all.32 = bf16[640,4,2,512]{3,1,0,2:T(4,128)(2,1)} all-to-all(bf16[640,4,2,512]{3,1,0,2:T(4,128)(2,1)S(1)} %broadcast_in_dim.48), channel_id=1, replica_groups=mesh['dp'=16,'fy'=4,'fc'=2] {'fc'}, dimensions={2} | all-to-all | bytes 10485760 | tf_op jit(solution)/shard_map/all_to_all | solution.py:64
  129.9 9.8 %copy.53 = bf16[640,4,2,512]{0,3,2,1:T(8,128)(2,1)} copy(bf16[640,4,2,512]{3,1,0,2:T(4,128)(2,1)} %all_to_all.32) | data formatting | bytes 10485760 | tf_op jit(solution)/shard_map/all_to_all | solution.py:64
  139.7 7.6 %multiply_convert_fusion = (bf16[640,512]{1,0:T(8,128)(2,1)S(1)}, bf16[640,512]{1,0:T(8,128)(2,1)S(1)}) fusion(f32[640,512]{1,0:T(8,128)S(1)} %copy-done.10, f32[640,512]{1,0:T(8,128)} %get-tuple-element.38, bf16[640,4096]{0,1:T(8,128)(2,1)} %bitcast.107, bf16[512,4096]{1,0:T(8,128)(2,1)} %param.12), kind=kOutput, calls=%fused_computation.16 | convolution fusion | flops 2688614400 | bytes 13369344 | tf_op jit(solution)/shard_map/dot_general | solution.py:129
  147.3 3.0 %fusion.10 = f32[640,8,512]{2,0,1:T(8,128)S(1)} fusion(bf16[8,512,512]{2,1,0:T(8,128)(2,1)S(1)} %bitcast.98, bf16[640,512]{1,0:T(8,128)(2,1)S(1)} %get-tuple-element.20), kind=kOutput, calls=%fused_computation.25 | convolution fusion | flops 2684354560 | bytes 15335424 | tf_op jit(solution)/shard_map/rh,fdh->frd/dot_general | solution.py:145
  150.3 5.6 %add_convert_fusion = bf16[640,8,512]{2,0,1:T(8,128)(2,1)S(1)} fusion(f32[640,8,512]{2,0,1:T(8,128)S(1)} %fusion.10, bf16[8,512,512]{2,1,0:T(8,128)(2,1)} %bitcast.111, bf16[640,512]{1,0:T(8,128)(2,1)S(1)} %get-tuple-element.21), kind=kOutput, calls=%fused_computation | convolution fusion | flops 2689597440 | bytes 20578304 | tf_op jit(solution)/shard_map/rh,fdh->frd/dot_general | solution.py:148
  156.5 4.7 %collective-permute-done.1 = bf16[4,640,512]{2,1,0:T(8,128)(2,1)S(1)} collective-permute-done((bf16[4,640,512]{2,1,0:T(8,128)(2,1)S(1)}, bf16[4,640,512]{2,1,0:T(8,128)(2,1)S(1)}, u32[]{:S(2)}, u32[]{:S(2)}) %collective-permute-start.1) | collective-permute-done | bytes 2621472 | tf_op jit(solution)/shard_map/ppermute | solution.py:74
  161.3 2.4 %fusion = bf16[4,640,512]{2,1,0:T(8,128)(2,1)} fusion(bf16[4,640,512]{2,1,0:T(8,128)(2,1)S(1)} %collective-permute-done.1, bf16[4,2,640,512]{3,2,1,0:T(8,128)(2,1)S(1)} %bitcast.97, s32[]{:T(128)S(6)} %select_n.16), kind=kLoop, calls=%fused_computation.5 | loop fusion | flops 5242880 | bytes 7864324 | tf_op jit(solution)/shard_map/convert_element_type | solution.py:75
  163.7 20.2 %all_to_all.33 = bf16[16,40,512]{2,1,0:T(8,128)(2,1)S(1)} all-to-all(bf16[16,40,512]{2,1,0:T(8,128)(2,1)} %bitcast.119), channel_id=1, replica_groups=mesh['dp'=16,'fy'=4,'fc'=2] {'dp'}, dimensions={0} | all-to-all | bytes 1310720 | tf_op jit(solution)/shard_map/all_to_all | solution.py:81
  184.5 1.1 fusion.13
  185.6 9.2 %all-gather = f32[1024,2]{0,1:T(2,128)S(1)} all-gather(f32[128,2]{0,1:T(2,128)S(1)} %pad_maximum_fusion), channel_id=2, replica_groups=mesh['dp'=16,'fy'=4,'fc'=2] {'fy','fc'}, dimensions={0}, use_global_device_ids=true | all-gather | bytes 9216 | tf_op jit(solution)/shard_map/all_gather | solution.py:127
  195.4 7.7 %convolution_convert_fusion = bf16[512,4096]{1,0:T(8,128)(2,1)} fusion(bf16[640,512]{1,0:T(8,128)(2,1)S(1)} %copy-done.12, bf16[640,4096]{0,1:T(8,128)(2,1)} %bitcast.108), kind=kOutput, calls=%fused_computation.1 | convolution fusion | flops 2686451712 | bytes 10092544 | tf_op jit(solution)/shard_map/dot_general | solution.py:142
  203.1 4.9 %convolution_convert_fusion.2 = bf16[4096,512]{1,0:T(8,128)(2,1)} fusion(bf16[640,4096]{0,1:T(8,128)(2,1)S(1)} %bitcast.105, bf16[640,512]{1,0:T(8,128)(2,1)S(1)} %get-tuple-element.20), kind=kOutput, calls=%fused_computation.3 | convolution fusion | flops 2686451712 | bytes 10092544 | tf_op jit(solution)/shard_map/dot_general | solution.py:136
  208.1 4.9 %convolution_convert_fusion.1 = bf16[4096,512]{1,0:T(8,128)(2,1)} fusion(bf16[640,4096]{0,1:T(8,128)(2,1)S(1)} %bitcast.106, bf16[640,512]{1,0:T(8,128)(2,1)S(1)} %get-tuple-element.21), kind=kOutput, calls=%fused_computation.2 | convolution fusion | flops 2686451712 | bytes 10092544 | tf_op jit(solution)/shard_map/dot_general | solution.py:139
  213.0 17.0 %all_to_all.34 = bf16[16,40,512]{2,1,0:T(8,128)(2,1)S(1)} all-to-all(bf16[16,40,512]{2,1,0:T(8,128)(2,1)} %bitcast.120), channel_id=1, replica_groups=mesh['dp'=16,'fy'=4,'fc'=2] {'dp'}, dimensions={0} | all-to-all | bytes 1310720 | tf_op jit(solution)/shard_map/all_to_all | solution.py:81
  (67 shorter events, 9.4 us)
Async XLA Ops:
  7.2 3.0 %copy-start = (bf16[128,512]{1,0:T(8,128)(2,1)S(1)}, bf16[128,512]{1,0:T(8,128)(2,1)}, u32[]{:S(2)}) copy-start(bf16[128,512]{1,0:T(8,128)(2,1)} %param.7) | copy-start | bytes 393220
  7.2 57.6 %all-gather.4.cloned.1.call-start = ((), (), s32[]{:S(2)}) async-start(), calls=%async_computation.8 | async-start | bytes 3276800 | tf_op jit(solution)/shard_map/all_gather | solution.py:59
  34.4 15.4 %all-to-all-start.2 = ((bf16[16,40,512]{2,1,0:T(8,128)(2,1)}), bf16[16,40,512]{2,1,0:T(8,128)(2,1)S(1)}, u32[]{:S(2)}, u32[]{:S(2)}) async-start(bf16[16,40,512]{2,1,0:T(8,128)(2,1)} %bitcast.18), calls=%async_computation.2 | async-start | bytes 1310720 | tf_op jit(solution)/shard_map/all_to_all | solution.py:56
  38.0 77.5 %all-gather.6.cloned.1.call-start = ((), (), s32[]{:S(2)}) async-start(), calls=%async_computation.9 | async-start | bytes 3276800 | tf_op jit(solution)/shard_map/all_gather | solution.py:59
  49.7 0.9 copy-start.6
  50.7 113.0 %reduce-scatter.3.cloned.1.call-start = ((), (), s32[]{:S(2)}) async-start(), calls=%async_computation.10 | async-start | bytes 3276800 | tf_op jit(solution)/shard_map/reduce_scatter | solution.py:78
  88.7 6.6 %copy-start.3 = (bf16[640,4,2,512]{0,3,2,1:T(8,128)(2,1)S(1)}, bf16[640,4,2,512]{0,3,2,1:T(8,128)(2,1)}, u32[]{:S(2)}) copy-start(bf16[640,4,2,512]{0,3,2,1:T(8,128)(2,1)} %copy.50) | copy-start | bytes 15728644
  88.7 6.6 %copy-start.5 = (bf16[4096,512]{1,0:T(8,128)(2,1)S(1)}, bf16[4096,512]{1,0:T(8,128)(2,1)}, u32[]{:S(2)}) copy-start(bf16[4096,512]{1,0:T(8,128)(2,1)} %param.11) | copy-start | bytes 12582916
  95.3 4.0 %copy-start.9 = (f32[640,512]{1,0:T(8,128)}, f32[640,512]{1,0:T(8,128)S(1)}, u32[]{:S(2)}) copy-start(f32[640,512]{1,0:T(8,128)S(1)} %fusion.38) | copy-start | bytes 3932164
  95.3 4.0 %copy-start.8 = (bf16[512,4096]{1,0:T(8,128)(2,1)S(1)}, bf16[512,4096]{1,0:T(8,128)(2,1)}, u32[]{:S(2)}) copy-start(bf16[512,4096]{1,0:T(8,128)(2,1)} %param.12) | copy-start | bytes 12582916
  99.3 3.2 %copy-start.11 = (bf16[640,512]{1,0:T(8,128)(2,1)}, bf16[640,512]{1,0:T(8,128)(2,1)S(1)}, u32[]{:S(2)}) copy-start(bf16[640,512]{1,0:T(8,128)(2,1)S(1)} %get-tuple-element.37) | copy-start | bytes 1966084
  102.5 2.3 copy-start.4
  106.5 5.1 %collective-permute-start = (bf16[4,640,512]{2,1,0:T(8,128)(2,1)}, bf16[4,640,512]{2,1,0:T(8,128)(2,1)S(1)}, u32[]{:S(2)}, u32[]{:S(2)}) collective-permute-start(bf16[4,640,512]{2,1,0:T(8,128)(2,1)} %dynamic-slice_bitcast_fusion.1), channel_id=1, source_target_pairs={{0,1},{1,0},{2,3},{3,2},{4,5},{5,4},{6,7},{7,6},{8,9},{9,8},{10,11... | collective-permute-start | bytes 7864328 | tf_op jit(solution)/shard_map/ppermute | solution.py:74
  119.4 93.6 %reduce-scatter.5.cloned.1.call-start = ((), (), s32[]{:S(2)}) async-start(), calls=%async_computation.11 | async-start | bytes 3276800 | tf_op jit(solution)/shard_map/reduce_scatter | solution.py:78
  129.9 9.8 %copy-start.10 = (f32[640,512]{1,0:T(8,128)S(1)}, f32[640,512]{1,0:T(8,128)}, u32[]{:S(2)}) copy-start(f32[640,512]{1,0:T(8,128)} %copy-done.9) | copy-start | bytes 3932164
  139.7 7.6 %copy-start.2 = (bf16[4096,512]{1,0:T(8,128)(2,1)S(1)}, bf16[4096,512]{1,0:T(8,128)(2,1)}, u32[]{:S(2)}) copy-start(bf16[4096,512]{1,0:T(8,128)(2,1)} %param.10) | copy-start | bytes 12582916
  156.1 5.2 %collective-permute-start.1 = (bf16[4,640,512]{2,1,0:T(8,128)(2,1)S(1)}, bf16[4,640,512]{2,1,0:T(8,128)(2,1)S(1)}, u32[]{:S(2)}, u32[]{:S(2)}) collective-permute-start(bf16[4,640,512]{2,1,0:T(8,128)(2,1)S(1)} %dynamic-slice_bitcast_fusion), channel_id=1, source_target_pairs={{0,1},{1,0},{2,3},{3,2},{4,5},{5,4},{6,7},{7,6},{8,9},{9,8},{10,11... | collective-permute-start | bytes 7864328 | tf_op jit(solution)/shard_map/ppermute | solution.py:74
  163.7 20.8 %copy-start.7 = (bf16[128,512]{1,0:T(8,128)(2,1)S(1)}, bf16[128,512]{1,0:T(8,128)(2,1)}, u32[]{:S(2)}) copy-start(bf16[128,512]{1,0:T(8,128)(2,1)} %param.13) | copy-start | bytes 393220
  163.7 31.7 %copy-start.12 = (bf16[640,512]{1,0:T(8,128)(2,1)S(1)}, bf16[640,512]{1,0:T(8,128)(2,1)}, u32[]{:S(2)}) copy-start(bf16[640,512]{1,0:T(8,128)(2,1)} %copy-done.11) | copy-start | bytes 1966084
  184.0 19.1 %slice-start = ((s8[5242880]{0:T(1024)(128)(4,1)}), s8[4194304]{0:T(1024)(128)(4,1)S(1)}, s32[]{:S(2)}) async-start(s8[5242880]{0:T(1024)(128)(4,1)} %bitcast.103), calls=%async_computation.12 | async-start | bytes 8388608
  195.4 7.7 %slice-start.1 = ((s8[5242880]{0:T(1024)(128)(4,1)}), s8[1048576]{0:T(1024)(128)(4,1)S(1)}, s32[]{:S(2)}) async-start(s8[5242880]{0:T(1024)(128)(4,1)} %bitcast.103), calls=%async_computation.13 | async-start | bytes 2097152
  208.1 23.2 %copy-start.1 = (bf16[128,512]{1,0:T(8,128)(2,1)S(1)}, bf16[128,512]{1,0:T(8,128)(2,1)}, u32[]{:S(2)}) copy-start(bf16[128,512]{1,0:T(8,128)(2,1)} %param.7) | copy-start | bytes 393220
Sparse Core Ops, SparseCore 0:
  31.4 33.3 all-gather.3
  66.4 35.2 all-gather.5
  119.5 34.0 reduce-scatter.2
  163.8 34.1 reduce-scatter.4

commit v10 on v8

--- a/solution.py
+++ b/solution.py
@@ -123,7 +123,8 @@
         [jnp.sum(first_pair * grad_local, axis=1), jnp.sum(second_pair * grad_local, axis=1)],
         axis=1,
     )
-    prob_grad = jnp.sum(lax.all_gather(prob_terms, ("fy", "fc"), axis=0, tiled=False), axis=0)
+    padded = jnp.zeros((token_count, 128), jnp.float32).at[:, :2].set(prob_terms)
+    prob_grad = lax.psum(padded, ("fy", "fc"))[:, :2]
     grad_rows = join_cores(grad_across)
     hidden_grad = lax.dot_general(grad_rows, down_w3, (((0, 2), (1, 2)), ((), ())),
                                   preferred_element_type=jnp.float32)

time: 208 us -> 282 us (1.36)
  waiting for transfers between devices: 48.5 us -> 122 us
  blocking collectives: 45.2 us -> 36.5 us
  local copies, waits for them, and re-layouts: 28.9 us -> 34.7 us
  starting transfers between devices: 14.8 us -> 18.3 us
    reduce_scatter x2, waiting for transfers between devices: 0.01 us -> 40 us  [scatter_chips(): return lax.psum_scatter(within, 'fy', scatter_dimension=0, tiled=False)]
    psum x0 -> x1, waiting for transfers between devices: none -> 32.1 us  [local(): prob_grad = lax.psum(padded, ('fy', 'fc'))[:, :2]]
    all_gather x1 -> x0, blocking collectives: 8.67 us -> none  [local(): lax.all_gather(prob_terms, ('fy', 'fc'), axis=0, tiled=False)]
    all_to_all x2, waiting for transfers between devices: 13 us -> 18.8 us  [to_token_layout(): lax.all_to_all(shares.reshape(dp_count, CAP, feat), 'dp', split_axis=0, c...]
    ppermute x2, waiting for transfers between devices: 9.67 us -> 4.99 us  [swap_cores(): lax.ppermute(sent, 'fc', swap).astype(jnp.float32)]
    all_to_all x2, starting transfers between devices: 10.5 us -> 13.9 us  [to_token_layout(): lax.all_to_all(shares.reshape(dp_count, CAP, feat), 'dp', split_axis=0, c...]
    unnamed x44 -> x54, local copies, waits for them, and re-layouts: 21.3 us -> 23.7 us
  transfers between devices with their start and end apart: 9 -> 10, of which waited for: 6 -> 8; matrix products, arithmetic and copies ran while one was open for 32% -> 24% of each run, Pallas kernels for 0% -> 0%
where the time goes in v10:
time: 282 us; the launch traced here: 281 us
  waiting for transfers between devices  122 us (43%)
  matrix products  43.9 us (16%)
  blocking collectives  36.5 us (13%)
  local copies, waits for them, and re-layouts  34.7 us (12%)
  starting transfers between devices  18.3 us (6%)
  between operations  14.2 us (5%)
  other arithmetic  11.2 us (4%)
    reduce_scatter x2, waiting for transfers between devices, scatter_chips(): return lax.psum_scatter(within, 'fy', scatter_dimension=0, tiled=False)  40 us
    psum x1, waiting for transfers between devices, local(): prob_grad = lax.psum(padded, ('fy', 'fc'))[:, :2]  32.1 us
    unnamed x54, local copies, waits for them, and re-layouts  23.7 us
    all_to_all x1, blocking collectives, to_expert_layout(): lax.all_to_all(place_rows(source, scaled), 'dp', split_axis=0, concat_axi...  20.6 us
    all_to_all x2, waiting for transfers between devices, to_token_layout(): lax.all_to_all(shares.reshape(dp_count, CAP, feat), 'dp', split_axis=0, c...  18.8 us
    all_to_all x2, blocking collectives, join_cores(): lax.all_to_all(jnp.broadcast_to(across[:, None], (chips, cores, rows, fea...  15.9 us
    all_gather x2, waiting for transfers between devices, to_expert_layout(): lax.all_gather(arrived.reshape(rows, feat), 'fy', axis=0, tiled=False)  14.1 us
    all_to_all x2, starting transfers between devices, to_token_layout(): lax.all_to_all(shares.reshape(dp_count, CAP, feat), 'dp', split_axis=0, c...  13.9 us
  transfers between devices with their start and end apart: 10, of which 8 were waited for; matrix products, arithmetic and copies ran while one was open for 24% of the time, Pallas kernels for 0%

profile of v10, /device:TPU:0, one launch (start us, length us, event | category | flops | bytes accessed | tf_op | source)
XLA Modules:
  0.0 280.6 jit_solution(17262740883432382659)
XLA Ops:
  10.6 20.6 %all_to_all.30 = bf16[16,40,512]{2,1,0:T(8,128)(2,1)} all-to-all(bf16[16,40,512]{2,1,0:T(8,128)(2,1)S(1)} %bitcast.128), channel_id=1, replica_groups=mesh['dp'=16,'fy'=4,'fc'=2] {'dp'}, dimensions={0} | all-to-all | bytes 1310720 | tf_op jit(solution)/shard_map/all_to_all | solution.py:56
  34.4 3.6 %all-to-all-start.2 = ((bf16[16,40,512]{2,1,0:T(8,128)(2,1)}), bf16[16,40,512]{2,1,0:T(8,128)(2,1)S(1)}, u32[]{:S(2)}, u32[]{:S(2)}) async-start(bf16[16,40,512]{2,1,0:T(8,128)(2,1)} %bitcast.21), calls=%async_computation.2 | async-start | bytes 1310720 | tf_op jit(solution)/shard_map/all_to_all | solution.py:56
  38.1 11.7 %all-to-all-done.2 = bf16[16,40,512]{2,1,0:T(8,128)(2,1)S(1)} async-done(((bf16[16,40,512]{2,1,0:T(8,128)(2,1)}), bf16[16,40,512]{2,1,0:T(8,128)(2,1)S(1)}, u32[]{:S(2)}, u32[]{:S(2)}) %all-to-all-start.2) | async-done | bytes 655392 | tf_op jit(solution)/shard_map/all_to_all | solution.py:56
  50.7 14.1 %all-gather.3.cloned.1.call-done = bf16[4,640,512]{2,1,0:T(8,128)(2,1)} async-done(((bf16[1,640,512]{2,1,0:T(8,128)(2,1)}), bf16[4,640,512]{2,1,0:T(8,128)(2,1)}) %all-gather.3.cloned.1.call-update) | async-done | bytes 2621456 | tf_op jit(solution)/shard_map/all_gather | solution.py:59
  64.8 2.2 broadcast_in_dim.43
  67.0 7.9 %all_to_all.31 = bf16[4,2,640,512]{3,2,0,1:T(8,128)(2,1)S(1)} all-to-all(bf16[4,2,640,512]{3,2,0,1:T(8,128)(2,1)S(1)} %broadcast_in_dim.43), channel_id=1, replica_groups=mesh['dp'=16,'fy'=4,'fc'=2] {'fc'}, dimensions={1} | all-to-all | bytes 10485760 | tf_op jit(solution)/shard_map/all_to_all | solution.py:63
  75.3 3.9 %copy-done.8 = bf16[4096,512]{1,0:T(8,128)(2,1)S(1)} copy-done((bf16[4096,512]{1,0:T(8,128)(2,1)S(1)}, bf16[4096,512]{1,0:T(8,128)(2,1)}, u32[]{:S(2)}) %copy-start.8) | copy-done | bytes 4194328
  79.2 2.9 %convolution_bitcast_fusion = f32[640,512]{1,0:T(8,128)S(1)} fusion(bf16[8,640,512]{2,1,0:T(8,128)(2,1)S(1)} %bitcast.112, bf16[8,512,512]{2,1,0:T(8,128)(2,1)S(1)} %bitcast.123), kind=kOutput, calls=%fused_computation.18 | convolution fusion | flops 2684354560 | bytes 10747904 | tf_op jit(solution)/shard_map/dot_general | solution.py:96
  82.1 2.9 %convolution_bitcast_fusion.1 = f32[640,512]{1,0:T(8,128)S(1)} fusion(bf16[8,640,512]{2,1,0:T(8,128)(2,1)S(1)} %bitcast.113, bf16[8,512,512]{2,1,0:T(8,128)(2,1)S(1)} %bitcast.108), kind=kOutput, calls=%fused_computation.19 | convolution fusion | flops 2684354560 | bytes 10747904 | tf_op jit(solution)/shard_map/dot_general | solution.py:95
  86.0 3.1 %fusion.8 = bf16[640,8,512]{2,0,1:T(8,128)(2,1)S(1)} fusion(bf16[640,512,1]{1,0,2:T(8,128)(2,1)S(1)} %fusion.15, bf16[64,8,8,512]{3,2,1,0:T(8,128)(2,1)S(1)} %bitcast.135), kind=kOutput, calls=%fused_computation.11 | convolution fusion | flops 2686976000 | bytes 10092544 | tf_op jit(solution)/shard_map/rh,hfd->frd/dot_general | solution.py:100
  89.2 2.4 copy-done.7
  93.3 5.0 %collective-permute-done = bf16[4,640,512]{2,1,0:T(8,128)(2,1)S(1)} collective-permute-done((bf16[4,640,512]{2,1,0:T(8,128)(2,1)}, bf16[4,640,512]{2,1,0:T(8,128)(2,1)S(1)}, u32[]{:S(2)}, u32[]{:S(2)}) %collective-permute-start) | collective-permute-done | bytes 2621472 | tf_op jit(solution)/shard_map/ppermute | solution.py:73
  98.3 4.0 %fusion.1 = bf16[4,640,512]{2,1,0:T(8,128)(2,1)} fusion(bf16[4,640,512]{2,1,0:T(8,128)(2,1)S(1)} %collective-permute-done, bf16[4,2,640,512]{3,2,1,0:T(8,128)(2,1)} %bitcast.121, s32[]{:T(128)S(6)} %select_n.16), kind=kLoop, calls=%fused_computation.4 | loop fusion | flops 5242880 | bytes 7864324 | tf_op jit(solution)/shard_map/convert_element_type | solution.py:74
  102.3 1.7 copy-done.10
  104.5 7.9 %all_to_all.32 = bf16[4,2,640,512]{3,2,0,1:T(8,128)(2,1)S(1)} all-to-all(bf16[4,2,640,512]{3,2,0,1:T(8,128)(2,1)S(1)} %broadcast_in_dim.49), channel_id=1, replica_groups=mesh['dp'=16,'fy'=4,'fc'=2] {'fc'}, dimensions={1} | all-to-all | bytes 10485760 | tf_op jit(solution)/shard_map/all_to_all | solution.py:63
  115.5 1.9 copy-done.23
  117.5 3.3 %fusion.16 = (bf16[640,512,1]{1,0,2:T(8,128)(2,1)S(1)}, bf16[640,512]{1,0:T(8,128)(2,1)S(1)}) fusion(f32[640,512]{1,0:T(8,128)S(1)} %copy-done.14, f32[640,512]{1,0:T(8,128)S(1)} %copy-done.12, bf16[8,640,512]{2,1,0:T(8,128)(2,1)S(1)} %bitcast.118, bf16[64,8,8,512]{3,2,1,0:T(8,128)(2,1)S(1)} %bitcast.136), kind=kOutput, calls=%fused_computation.31 | convolution fusion | flops 2688614400 | bytes 13369344 | tf_op jit(solution)/shard_map/dot_general | solution.py:129
  120.8 2.9 %fusion.17 = f32[640,8,512]{2,0,1:T(8,128)S(1)} fusion(bf16[8,512,512]{2,1,0:T(8,128)(2,1)S(1)} %bitcast.109, bf16[640,512]{1,0:T(8,128)(2,1)S(1)} %get-tuple-element.65), kind=kOutput, calls=%fused_computation.32 | convolution fusion | flops 2684354560 | bytes 15335424 | tf_op jit(solution)/shard_map/rh,fdh->frd/dot_general | solution.py:144
  123.7 5.6 %add_convert_fusion = bf16[640,8,512]{2,0,1:T(8,128)(2,1)S(1)} fusion(f32[640,8,512]{2,0,1:T(8,128)S(1)} %fusion.17, bf16[640,512,1]{1,0,2:T(8,128)(2,1)S(1)} %get-tuple-element.64, bf16[8,512,512]{2,1,0:T(8,128)(2,1)} %bitcast.122), kind=kOutput, calls=%fused_computation | convolution fusion | flops 2689597440 | bytes 20578304 | tf_op jit(solution)/shard_map/rh,fdh->frd/dot_general | solution.py:147
  129.3 2.4 copy-done.2
  133.6 5.3 %reduce-scatter.3.cloned.1.call-done = bf16[1,640,512]{2,1,0:T(8,128)(2,1)} async-done(((bf16[4,640,512]{2,1,0:T(8,128)(2,1)}), bf16[1,640,512]{2,1,0:T(8,128)(2,1)}) %reduce-scatter.3.cloned.1.call-update) | async-done | bytes 655376 | tf_op jit(solution)/shard_map/reduce_scatter | solution.py:77
  138.9 6.9 %all-to-all-start.3 = ((bf16[16,40,512]{2,1,0:T(8,128)(2,1)}), bf16[16,40,512]{2,1,0:T(8,128)(2,1)S(1)}, u32[]{:S(2)}, u32[]{:S(2)}) async-start(bf16[16,40,512]{2,1,0:T(8,128)(2,1)} %bitcast.130), calls=%async_computation.4 | async-start | bytes 1310720 | tf_op jit(solution)/shard_map/all_to_all | solution.py:80
  146.5 12.3 %all-to-all-done.3 = bf16[16,40,512]{2,1,0:T(8,128)(2,1)S(1)} async-done(((bf16[16,40,512]{2,1,0:T(8,128)(2,1)}), bf16[16,40,512]{2,1,0:T(8,128)(2,1)S(1)}, u32[]{:S(2)}, u32[]{:S(2)}) %all-to-all-start.3) | async-done | bytes 655392 | tf_op jit(solution)/shard_map/all_to_all | solution.py:80
  162.1 4.0 %fusion = bf16[4,640,512]{2,1,0:T(8,128)(2,1)} fusion(bf16[4,640,512]{2,1,0:T(8,128)(2,1)S(1)} %collective-permute-done.1, bf16[4,2,640,512]{3,2,1,0:T(8,128)(2,1)} %bitcast.107, s32[]{:T(128)S(6)} %select_n.16), kind=kLoop, calls=%fused_computation.2 | loop fusion | flops 5242880 | bytes 7864324 | tf_op jit(solution)/shard_map/convert_element_type | solution.py:74
  166.1 8.6 %convolution_convert_fusion = bf16[512,8,512]{0,2,1:T(8,128)(2,1)} fusion(bf16[640,512,1]{1,0,2:T(8,128)(2,1)S(1)} %copy-done.20, bf16[8,640,512]{2,1,0:T(8,128)(2,1)} %bitcast.119), kind=kOutput, calls=%fused_computation.12 | convolution fusion | flops 2686451712 | bytes 10092544 | tf_op jit(solution)/shard_map/hr,frd->hfd/dot_general | solution.py:141
  174.8 5.1 %convolution_convert_fusion.1 = bf16[8,512,512]{2,1,0:T(8,128)(2,1)} fusion(bf16[8,640,512]{2,1,0:T(8,128)(2,1)S(1)} %bitcast.116, bf16[640,512,1]{1,0,2:T(8,128)(2,1)S(1)} %copy-done.18), kind=kOutput, calls=%fused_computation.13 | convolution fusion | flops 2686451712 | bytes 10092544 | tf_op jit(solution)/shard_map/frd,rh->fdh/dot_general | solution.py:138
  179.9 5.0 %convolution_convert_fusion.2 = bf16[8,512,512]{2,1,0:T(8,128)(2,1)} fusion(bf16[8,640,512]{2,1,0:T(8,128)(2,1)S(1)} %bitcast.117, bf16[640,512]{1,0:T(8,128)(2,1)S(1)} %copy-done.16), kind=kOutput, calls=%fused_computation.14 | convolution fusion | flops 2686451712 | bytes 10092544 | tf_op jit(solution)/shard_map/frd,rh->fdh/dot_general | solution.py:135
  184.9 32.1 %all-reduce.3.cloned.1.call-done = f32[128,128]{0,1:T(8,128)} async-done(((f32[128,128]{0,1:T(8,128)}), f32[128,128]{0,1:T(8,128)}) %all-reduce.3.cloned.1.call-update) | async-done | bytes 65552 | tf_op jit(solution)/shard_map/psum | solution.py:127
  218.2 34.7 %reduce-scatter.5.cloned.1.call-done = bf16[1,640,512]{2,1,0:T(8,128)(2,1)} async-done(((bf16[4,640,512]{2,1,0:T(8,128)(2,1)}), bf16[1,640,512]{2,1,0:T(8,128)(2,1)}) %reduce-scatter.5.cloned.1.call-update) | async-done | bytes 655376 | tf_op jit(solution)/shard_map/reduce_scatter | solution.py:77
  252.9 6.9 %all-to-all-start.5 = ((bf16[16,40,512]{2,1,0:T(8,128)(2,1)}), bf16[16,40,512]{2,1,0:T(8,128)(2,1)S(1)}, u32[]{:S(2)}, u32[]{:S(2)}) async-start(bf16[16,40,512]{2,1,0:T(8,128)(2,1)} %bitcast.131), calls=%async_computation.7 | async-start | bytes 1310720 | tf_op jit(solution)/shard_map/all_to_all | solution.py:80
  259.9 6.4 %copy.61 = bf16[512,4096]{1,0:T(8,128)(2,1)} copy(bf16[512,4096]{0,1:T(8,128)(2,1)} %bitcast.124) | data formatting | bytes 8388608
  266.3 6.6 %all-to-all-done.5 = bf16[16,40,512]{2,1,0:T(8,128)(2,1)S(1)} async-done(((bf16[16,40,512]{2,1,0:T(8,128)(2,1)}), bf16[16,40,512]{2,1,0:T(8,128)(2,1)S(1)}, u32[]{:S(2)}, u32[]{:S(2)}) %all-to-all-start.5) | async-done | bytes 655392 | tf_op jit(solution)/shard_map/all_to_all | solution.py:80
  (95 shorter events, 22.6 us)
Async XLA Ops:
  7.2 3.0 %copy-start = (bf16[128,512]{1,0:T(8,128)(2,1)S(1)}, bf16[128,512]{1,0:T(8,128)(2,1)}, u32[]{:S(2)}) copy-start(bf16[128,512]{1,0:T(8,128)(2,1)} %param.9) | copy-start | bytes 393220
  7.2 57.6 %all-gather.3.cloned.1.call-start = ((), (), s32[]{:S(2)}) async-start(), calls=%async_computation.8 | async-start | bytes 3276800 | tf_op jit(solution)/shard_map/all_gather | solution.py:59
  34.4 15.4 %all-to-all-start.2 = ((bf16[16,40,512]{2,1,0:T(8,128)(2,1)}), bf16[16,40,512]{2,1,0:T(8,128)(2,1)S(1)}, u32[]{:S(2)}, u32[]{:S(2)}) async-start(bf16[16,40,512]{2,1,0:T(8,128)(2,1)} %bitcast.21), calls=%async_computation.2 | async-start | bytes 1310720 | tf_op jit(solution)/shard_map/all_to_all | solution.py:56
  38.0 64.3 %all-gather.5.cloned.1.call-start = ((), (), s32[]{:S(2)}) async-start(), calls=%async_computation.9 | async-start | bytes 3276800 | tf_op jit(solution)/shard_map/all_gather | solution.py:59
  50.6 88.2 %reduce-scatter.3.cloned.1.call-start = ((), (), s32[]{:S(2)}) async-start(), calls=%async_computation.10 | async-start | bytes 3276800 | tf_op jit(solution)/shard_map/reduce_scatter | solution.py:77
  75.0 4.2 %copy-start.8 = (bf16[4096,512]{1,0:T(8,128)(2,1)S(1)}, bf16[4096,512]{1,0:T(8,128)(2,1)}, u32[]{:S(2)}) copy-start(bf16[4096,512]{1,0:T(8,128)(2,1)} %param.13) | copy-start | bytes 12582916
  75.3 6.8 %copy-start.5 = (bf16[4,2,640,512]{3,2,1,0:T(8,128)(2,1)}, bf16[4,2,640,512]{3,2,1,0:T(8,128)(2,1)S(1)}, u32[]{:S(2)}) copy-start(bf16[4,2,640,512]{3,2,1,0:T(8,128)(2,1)S(1)} %copy.54) | copy-start | bytes 15728644
  79.2 2.9 %copy-start.3 = (bf16[4096,512]{1,0:T(8,128)(2,1)S(1)}, bf16[4096,512]{1,0:T(8,128)(2,1)}, u32[]{:S(2)}) copy-start(bf16[4096,512]{1,0:T(8,128)(2,1)} %param.12) | copy-start | bytes 12582916
  82.0 2.9 %copy-start.11 = (f32[640,512]{1,0:T(8,128)}, f32[640,512]{1,0:T(8,128)S(1)}, u32[]{:S(2)}) copy-start(f32[640,512]{1,0:T(8,128)S(1)} %convolution_bitcast_fusion) | copy-start | bytes 3932164
  82.1 4.0 %copy-start.22 = (bf16[512,4096]{1,0:T(8,128)(2,1)S(1)}, bf16[512,4096]{1,0:T(8,128)(2,1)}, u32[]{:S(2)}) copy-start(bf16[512,4096]{1,0:T(8,128)(2,1)} %param.14) | copy-start | bytes 12582916
  86.0 3.2 %copy-start.19 = (bf16[640,512,1]{1,0,2:T(8,128)(2,1)}, bf16[640,512,1]{1,0,2:T(8,128)(2,1)S(1)}, u32[]{:S(2)}) copy-start(bf16[640,512,1]{1,0,2:T(8,128)(2,1)S(1)} %fusion.15) | copy-start | bytes 1966084
  89.2 2.4 copy-start.7
  93.2 5.1 %collective-permute-start = (bf16[4,640,512]{2,1,0:T(8,128)(2,1)}, bf16[4,640,512]{2,1,0:T(8,128)(2,1)S(1)}, u32[]{:S(2)}, u32[]{:S(2)}) collective-permute-start(bf16[4,640,512]{2,1,0:T(8,128)(2,1)} %dynamic-slice_bitcast_fusion.1), channel_id=1, source_target_pairs={{0,1},{1,0},{2,3},{3,2},{4,5},{5,4},{6,7},{7,6},{8,9},{9,8},{10,11... | collective-permute-start | bytes 7864328 | tf_op jit(solution)/shard_map/ppermute | solution.py:73
  112.4 3.1 %copy-start.14 = (f32[640,512]{1,0:T(8,128)S(1)}, f32[640,512]{1,0:T(8,128)}, u32[]{:S(2)}) copy-start(f32[640,512]{1,0:T(8,128)} %copy-done.13) | copy-start | bytes 3932164
  112.4 5.0 %copy-start.23 = (bf16[512,4096]{1,0:T(8,128)(2,1)S(1)}, bf16[512,4096]{1,0:T(8,128)(2,1)}, u32[]{:S(2)}) copy-start(bf16[512,4096]{1,0:T(8,128)(2,1)} %param.14) | copy-start | bytes 12582916
  112.8 7.9 %copy-start.6 = (bf16[4,2,640,512]{3,2,1,0:T(8,128)(2,1)}, bf16[4,2,640,512]{3,2,1,0:T(8,128)(2,1)S(1)}, u32[]{:S(2)}) copy-start(bf16[4,2,640,512]{3,2,1,0:T(8,128)(2,1)S(1)} %copy.56) | copy-start | bytes 15728644
  117.5 3.3 %copy-start.4 = (bf16[4096,512]{1,0:T(8,128)(2,1)S(1)}, bf16[4096,512]{1,0:T(8,128)(2,1)}, u32[]{:S(2)}) copy-start(bf16[4096,512]{1,0:T(8,128)(2,1)} %param.12) | copy-start | bytes 12582916
  120.7 3.0 %copy-start.15 = (bf16[640,512]{1,0:T(8,128)(2,1)}, bf16[640,512]{1,0:T(8,128)(2,1)S(1)}, u32[]{:S(2)}) copy-start(bf16[640,512]{1,0:T(8,128)(2,1)S(1)} %get-tuple-element.65) | copy-start | bytes 1966084
  120.7 2.9 %copy-start.17 = (bf16[640,512,1]{1,0,2:T(8,128)(2,1)}, bf16[640,512,1]{1,0,2:T(8,128)(2,1)S(1)}, u32[]{:S(2)}) copy-start(bf16[640,512,1]{1,0,2:T(8,128)(2,1)S(1)} %get-tuple-element.64) | copy-start | bytes 1966084
  129.3 2.4 copy-start.2
  131.7 27.6 %copy-start.21 = (bf16[128,512]{1,0:T(8,128)(2,1)S(1)}, bf16[128,512]{1,0:T(8,128)(2,1)}, u32[]{:S(2)}) copy-start(bf16[128,512]{1,0:T(8,128)(2,1)} %param.15) | copy-start | bytes 393220
  133.4 28.7 %collective-permute-start.1 = (bf16[4,640,512]{2,1,0:T(8,128)(2,1)}, bf16[4,640,512]{2,1,0:T(8,128)(2,1)S(1)}, u32[]{:S(2)}, u32[]{:S(2)}) collective-permute-start(bf16[4,640,512]{2,1,0:T(8,128)(2,1)} %dynamic-slice_bitcast_fusion), channel_id=1, source_target_pairs={{0,1},{1,0},{2,3},{3,2},{4,5},{5,4},{6,7},{7,6},{8,9},{9,8},{10,11... | collective-permute-start | bytes 7864328 | tf_op jit(solution)/shard_map/ppermute | solution.py:73
  138.9 19.9 %all-to-all-start.3 = ((bf16[16,40,512]{2,1,0:T(8,128)(2,1)}), bf16[16,40,512]{2,1,0:T(8,128)(2,1)S(1)}, u32[]{:S(2)}, u32[]{:S(2)}) async-start(bf16[16,40,512]{2,1,0:T(8,128)(2,1)} %bitcast.130), calls=%async_computation.4 | async-start | bytes 1310720 | tf_op jit(solution)/shard_map/all_to_all | solution.py:80
  145.8 71.2 %all-reduce.3.cloned.1.call-start = ((), (), s32[]{:S(2)}) async-start(), calls=%async_computation.11 | async-start | bytes 131072 | tf_op jit(solution)/shard_map/psum | solution.py:127
  161.8 4.3 %copy-start.20 = (bf16[640,512,1]{1,0,2:T(8,128)(2,1)S(1)}, bf16[640,512,1]{1,0,2:T(8,128)(2,1)}, u32[]{:S(2)}) copy-start(bf16[640,512,1]{1,0,2:T(8,128)(2,1)} %copy-done.19) | copy-start | bytes 1966084
  161.8 91.1 %reduce-scatter.5.cloned.1.call-start = ((), (), s32[]{:S(2)}) async-start(), calls=%async_computation.12 | async-start | bytes 3276800 | tf_op jit(solution)/shard_map/reduce_scatter | solution.py:77
  166.1 8.7 %slice-start = ((s8[5242880]{0:T(1024)(128)(4,1)}), s8[1048576]{0:T(1024)(128)(4,1)S(1)}, s32[]{:S(2)}) async-start(s8[5242880]{0:T(1024)(128)(4,1)} %bitcast.114), calls=%async_computation.13 | async-start | bytes 2097152
  166.1 8.7 %slice-start.1 = ((s8[5242880]{0:T(1024)(128)(4,1)}), s8[4194304]{0:T(1024)(128)(4,1)S(1)}, s32[]{:S(2)}) async-start(s8[5242880]{0:T(1024)(128)(4,1)} %bitcast.114), calls=%async_computation.14 | async-start | bytes 8388608
  166.1 8.7 %copy-start.18 = (bf16[640,512,1]{1,0,2:T(8,128)(2,1)S(1)}, bf16[640,512,1]{1,0,2:T(8,128)(2,1)}, u32[]{:S(2)}) copy-start(bf16[640,512,1]{1,0,2:T(8,128)(2,1)} %copy-done.17) | copy-start | bytes 1966084
  174.8 5.1 %copy-start.16 = (bf16[640,512]{1,0:T(8,128)(2,1)S(1)}, bf16[640,512]{1,0:T(8,128)(2,1)}, u32[]{:S(2)}) copy-start(bf16[640,512]{1,0:T(8,128)(2,1)} %copy-done.15) | copy-start | bytes 1966084
  252.9 19.9 %all-to-all-start.5 = ((bf16[16,40,512]{2,1,0:T(8,128)(2,1)}), bf16[16,40,512]{2,1,0:T(8,128)(2,1)S(1)}, u32[]{:S(2)}, u32[]{:S(2)}) async-start(bf16[16,40,512]{2,1,0:T(8,128)(2,1)} %bitcast.131), calls=%async_computation.7 | async-start | bytes 1310720 | tf_op jit(solution)/shard_map/all_to_all | solution.py:80
  259.9 14.2 %copy-start.1 = (bf16[128,512]{1,0:T(8,128)(2,1)S(1)}, bf16[128,512]{1,0:T(8,128)(2,1)}, u32[]{:S(2)}) copy-start(bf16[128,512]{1,0:T(8,128)(2,1)} %param.9) | copy-start | bytes 393220
  (4 other events, 5.3 us)
Sparse Core Ops, SparseCore 0:
  31.4 33.3 all-gather.2
  66.4 35.2 all-gather.4
  104.8 34.0 reduce-scatter.2
  161.9 55.0 all-reduce.2
  219.9 32.9 reduce-scatter.4

commit v11 on v8

--- a/solution.py
+++ b/solution.py
@@ -131,14 +131,16 @@
         hidden_grad * up_proj * sigmoid_gate * (1.0 + gate_proj * (1.0 - sigmoid_gate))
     ).astype(jnp.bfloat16)
     up_grad = (hidden_grad * activated).astype(jnp.bfloat16)
+    out_slots, rows_w, gate_grad_w, up_grad_w, grad_rows_w, hidden_w = lax.optimization_barrier(
+        (out_slots, expert_rows, gate_grad, up_grad, grad_rows, hidden))
     gate_weight_grad = jnp.einsum(
-        "frd,rh->fdh", expert_rows, gate_grad, preferred_element_type=jnp.float32
+        "frd,rh->fdh", rows_w, gate_grad_w, preferred_element_type=jnp.float32
     ).astype(jnp.bfloat16).reshape(fsdp_count * feat, hid)
     up_weight_grad = jnp.einsum(
-        "frd,rh->fdh", expert_rows, up_grad, preferred_element_type=jnp.float32
+        "frd,rh->fdh", rows_w, up_grad_w, preferred_element_type=jnp.float32
     ).astype(jnp.bfloat16).reshape(fsdp_count * feat, hid)
     down_weight_grad = jnp.einsum(
-        "hr,frd->hfd", hidden.T, grad_rows, preferred_element_type=jnp.float32
+        "rh,frd->hfd", hidden_w, grad_rows_w, preferred_element_type=jnp.float32
     ).astype(jnp.bfloat16).reshape(hid, model)
     input_partial = jnp.einsum(
         "rh,fdh->frd", gate_grad, gate_w3, preferred_element_type=jnp.float32

time: 208 us -> 214 us (1.029)
  blocking collectives: 45.2 us -> 65.5 us
  starting transfers between devices: 14.8 us -> 7.84 us
  waiting for transfers between devices: 48.5 us -> 44.7 us
  matrix products: 46.7 us -> 44.3 us
    all_to_all x0 -> x1, blocking collectives: none -> 19.7 us  [to_token_layout(): lax.all_to_all(shares.reshape(dp_count, CAP, feat), 'dp', split_axis=0, c...]
    all_to_all x2 -> x1, starting transfers between devices: 10.5 us -> 3.6 us  [to_token_layout(): lax.all_to_all(shares.reshape(dp_count, CAP, feat), 'dp', split_axis=0, c...]
    all_to_all x2 -> x1, waiting for transfers between devices: 13 us -> 7.35 us  [to_token_layout(): lax.all_to_all(shares.reshape(dp_count, CAP, feat), 'dp', split_axis=0, c...]
    dot_general x3, matrix products: 21.3 us -> 17.9 us  [the longest x1 7.73 us: local(): jnp.einsum('frd,rh->fdh', rows_w, gate_grad_w, preferred_element_type=jnp...]
    unnamed x44 -> x46, local copies, waits for them, and re-layouts: 21.3 us -> 20.6 us
  transfers between devices with their start and end apart: 9 -> 8, of which waited for: 6 -> 6; matrix products, arithmetic and copies ran while one was open for 32% -> 30% of each run, Pallas kernels for 0% -> 0%
where the time goes in v11:
time: 214 us; the launch traced here: 213 us
  blocking collectives  65.5 us (31%)
  waiting for transfers between devices  44.7 us (21%)
  matrix products  44.3 us (21%)
  local copies, waits for them, and re-layouts  28.2 us (13%)
  between operations  14.1 us (7%)
  other arithmetic  8.62 us (4%)
  starting transfers between devices  7.84 us (4%)
    all_to_all x1, blocking collectives, to_expert_layout(): lax.all_to_all(place_rows(source, scaled), 'dp', split_axis=0, concat_axi...  20.6 us
    unnamed x46, local copies, waits for them, and re-layouts  20.6 us
    all_to_all x1, blocking collectives, to_token_layout(): lax.all_to_all(shares.reshape(dp_count, CAP, feat), 'dp', split_axis=0, c...  19.7 us
    all_to_all x2, blocking collectives, join_cores(): lax.all_to_all(jnp.broadcast_to(across[:, None], (chips, cores, rows, fea...  15.9 us
    all_gather x2, waiting for transfers between devices, to_expert_layout(): lax.all_gather(arrived.reshape(rows, feat), 'fy', axis=0, tiled=False)  14.1 us
    all_to_all x1, waiting for transfers between devices, to_expert_layout(): lax.all_to_all(place_rows(source, scaled), 'dp', split_axis=0, concat_axi...  11.7 us
    ppermute x2, waiting for transfers between devices, swap_cores(): lax.ppermute(sent, 'fc', swap).astype(jnp.float32)  9.66 us
    all_gather x1, blocking collectives, local(): lax.all_gather(prob_terms, ('fy', 'fc'), axis=0, tiled=False)  9.2 us
  transfers between devices with their start and end apart: 8, of which 6 were waited for; matrix products, arithmetic and copies ran while one was open for 30% of the time, Pallas kernels for 0%

profile of v11, /device:TPU:0, one launch (start us, length us, event | category | flops | bytes accessed | tf_op | source)
XLA Modules:
  0.0 213.1 jit_solution(13704428798113791110)
XLA Ops:
  10.6 20.6 %all_to_all.30 = bf16[16,40,512]{2,1,0:T(8,128)(2,1)} all-to-all(bf16[16,40,512]{2,1,0:T(8,128)(2,1)S(1)} %bitcast.138), channel_id=1, replica_groups=mesh['dp'=16,'fy'=4,'fc'=2] {'dp'}, dimensions={0} | all-to-all | bytes 1310720 | tf_op jit(solution)/shard_map/all_to_all | solution.py:56
  32.0 1.5 convolution_convert_fusion.3
  34.4 3.6 %all-to-all-start.2 = ((bf16[16,40,512]{2,1,0:T(8,128)(2,1)}), bf16[16,40,512]{2,1,0:T(8,128)(2,1)S(1)}, u32[]{:S(2)}, u32[]{:S(2)}) async-start(bf16[16,40,512]{2,1,0:T(8,128)(2,1)} %bitcast.21), calls=%async_computation.2 | async-start | bytes 1310720 | tf_op jit(solution)/shard_map/all_to_all | solution.py:56
  38.1 11.7 %all-to-all-done.2 = bf16[16,40,512]{2,1,0:T(8,128)(2,1)S(1)} async-done(((bf16[16,40,512]{2,1,0:T(8,128)(2,1)}), bf16[16,40,512]{2,1,0:T(8,128)(2,1)S(1)}, u32[]{:S(2)}, u32[]{:S(2)}) %all-to-all-start.2) | async-done | bytes 655392 | tf_op jit(solution)/shard_map/all_to_all | solution.py:56
  50.7 14.1 %all-gather.4.cloned.1.call-done = bf16[4,640,512]{2,1,0:T(8,128)(2,1)} async-done(((bf16[1,640,512]{2,1,0:T(8,128)(2,1)}), bf16[4,640,512]{2,1,0:T(8,128)(2,1)}) %all-gather.4.cloned.1.call-update) | async-done | bytes 2621456 | tf_op jit(solution)/shard_map/all_gather | solution.py:59
  64.8 2.2 %broadcast_in_dim.42 = bf16[4,2,640,512]{3,2,0,1:T(8,128)(2,1)S(1)} broadcast(bf16[4,640,512]{2,1,0:T(8,128)(2,1)} %all-gather.4.cloned.1.call-done), dimensions={0,2,3} | broadcast | bytes 7864320 | tf_op jit(solution)/shard_map/broadcast_in_dim | solution.py:64
  67.0 7.9 %all_to_all.31 = bf16[4,2,640,512]{3,2,0,1:T(8,128)(2,1)S(1)} all-to-all(bf16[4,2,640,512]{3,2,0,1:T(8,128)(2,1)S(1)} %broadcast_in_dim.42), channel_id=1, replica_groups=mesh['dp'=16,'fy'=4,'fc'=2] {'fc'}, dimensions={1} | all-to-all | bytes 10485760 | tf_op jit(solution)/shard_map/all_to_all | solution.py:63
  75.3 3.9 %copy-done.2 = bf16[4096,512]{1,0:T(8,128)(2,1)S(1)} copy-done((bf16[4096,512]{1,0:T(8,128)(2,1)S(1)}, bf16[4096,512]{1,0:T(8,128)(2,1)}, u32[]{:S(2)}) %copy-start.2) | copy-done | bytes 4194328
  79.2 2.9 %convolution_bitcast_fusion.1 = f32[640,512]{1,0:T(8,128)S(1)} fusion(bf16[8,640,512]{2,1,0:T(8,128)(2,1)S(1)} %bitcast.120, bf16[8,512,512]{2,1,0:T(8,128)(2,1)S(1)} %bitcast.116), kind=kOutput, calls=%fused_computation.19 | convolution fusion | flops 2684354560 | bytes 10747904 | tf_op jit(solution)/shard_map/dot_general | solution.py:95
  82.1 4.0 %multiply_convert_fusion.2 = (bf16[640,512]{1,0:T(8,128)(2,1)S(1)}, f32[640,512]{1,0:T(8,128)}) fusion(f32[640,512]{1,0:T(8,128)S(1)} %convolution_bitcast_fusion.1, bf16[8,640,512]{2,1,0:T(8,128)(2,1)S(1)} %bitcast.121, bf16[8,512,512]{2,1,0:T(8,128)(2,1)S(1)} %bitcast.133), kind=kOutput, calls=%fused_computation.24 | convolution fusion | flops 2686320640 | bytes 12713984 | tf_op jit(solution)/shard_map/dot_general | solution.py:96
  86.1 3.1 %fusion.8 = bf16[640,8,512]{2,0,1:T(8,128)(2,1)S(1)} fusion(bf16[64,8,8,512]{3,2,1,0:T(8,128)(2,1)S(1)} %bitcast.146, bf16[640,512]{1,0:T(8,128)(2,1)S(1)} %get-tuple-element.23), kind=kOutput, calls=%fused_computation.11 | convolution fusion | flops 2686976000 | bytes 10092544 | tf_op jit(solution)/shard_map/rh,hfd->frd/dot_general | solution.py:100
  89.3 2.3 %copy-done.6 = bf16[640,8,512]{2,0,1:T(8,128)(2,1)} copy-done((bf16[640,8,512]{2,0,1:T(8,128)(2,1)}, bf16[640,8,512]{2,0,1:T(8,128)(2,1)S(1)}, u32[]{:S(2)}) %copy-start.6) | copy-done | bytes 5242904
  91.6 1.7 dynamic-slice_bitcast_fusion.1
  93.4 5.0 %collective-permute-done = bf16[4,640,512]{2,1,0:T(8,128)(2,1)S(1)} collective-permute-done((bf16[4,640,512]{2,1,0:T(8,128)(2,1)}, bf16[4,640,512]{2,1,0:T(8,128)(2,1)S(1)}, u32[]{:S(2)}, u32[]{:S(2)}) %collective-permute-start) | collective-permute-done | bytes 2621472 | tf_op jit(solution)/shard_map/ppermute | solution.py:73
  98.4 4.0 %fusion.1 = bf16[4,640,512]{2,1,0:T(8,128)(2,1)} fusion(bf16[4,640,512]{2,1,0:T(8,128)(2,1)S(1)} %collective-permute-done, bf16[4,2,640,512]{3,2,1,0:T(8,128)(2,1)} %bitcast.131, s32[]{:T(128)S(6)} %select_n.16), kind=kLoop, calls=%fused_computation.4 | loop fusion | flops 5242880 | bytes 7864324 | tf_op jit(solution)/shard_map/convert_element_type | solution.py:74
  102.4 1.7 copy-done.9
  104.5 7.9 %all_to_all.32 = bf16[4,2,640,512]{3,2,0,1:T(8,128)(2,1)S(1)} all-to-all(bf16[4,2,640,512]{3,2,0,1:T(8,128)(2,1)S(1)} %broadcast_in_dim.48), channel_id=1, replica_groups=mesh['dp'=16,'fy'=4,'fc'=2] {'fc'}, dimensions={1} | all-to-all | bytes 10485760 | tf_op jit(solution)/shard_map/all_to_all | solution.py:63
  112.8 3.9 %copy-done.12 = bf16[512,4096]{1,0:T(8,128)(2,1)S(1)} copy-done((bf16[512,4096]{1,0:T(8,128)(2,1)S(1)}, bf16[512,4096]{1,0:T(8,128)(2,1)}, u32[]{:S(2)}) %copy-start.12) | copy-done | bytes 4194328
  117.5 3.3 %multiply_convert_fusion = (bf16[640,512]{1,0:T(8,128)(2,1)S(1)}, bf16[640,512]{1,0:T(8,128)(2,1)S(1)}) fusion(f32[640,512]{1,0:T(8,128)S(1)} %copy-done.16, f32[640,512]{1,0:T(8,128)S(1)} %copy-done.17, bf16[8,640,512]{2,1,0:T(8,128)(2,1)S(1)} %bitcast.126, bf16[64,8,8,512]{3,2,1,0:T(8,128)(2,1)S(1)} %bitcast.147), kind=kOutput, calls=%fused_computation.22 | convolution fusion | flops 2688614400 | bytes 13369344 | tf_op jit(solution)/shard_map/dot_general | solution.py:128
  120.8 3.0 %fusion.16 = f32[640,8,512]{2,0,1:T(8,128)S(1)} fusion(bf16[8,512,512]{2,1,0:T(8,128)(2,1)S(1)} %bitcast.117, bf16[640,512]{1,0:T(8,128)(2,1)S(1)} %get-tuple-element.21), kind=kOutput, calls=%fused_computation.31 | convolution fusion | flops 2684354560 | bytes 15335424 | tf_op jit(solution)/shard_map/rh,fdh->frd/dot_general | solution.py:145
  123.7 5.6 %add_convert_fusion = bf16[640,8,512]{2,0,1:T(8,128)(2,1)S(1)} fusion(f32[640,8,512]{2,0,1:T(8,128)S(1)} %fusion.16, bf16[8,512,512]{2,1,0:T(8,128)(2,1)} %bitcast.132, bf16[640,512]{1,0:T(8,128)(2,1)S(1)} %get-tuple-element.22), kind=kOutput, calls=%fused_computation | convolution fusion | flops 2689597440 | bytes 20578304 | tf_op jit(solution)/shard_map/rh,fdh->frd/dot_general | solution.py:148
  129.9 4.7 %collective-permute-done.1 = bf16[4,640,512]{2,1,0:T(8,128)(2,1)S(1)} collective-permute-done((bf16[4,640,512]{2,1,0:T(8,128)(2,1)S(1)}, bf16[4,640,512]{2,1,0:T(8,128)(2,1)S(1)}, u32[]{:S(2)}, u32[]{:S(2)}) %collective-permute-start.1) | collective-permute-done | bytes 2621472 | tf_op jit(solution)/shard_map/ppermute | solution.py:73
  134.5 2.4 %fusion = bf16[4,640,512]{2,1,0:T(8,128)(2,1)} fusion(bf16[4,640,512]{2,1,0:T(8,128)(2,1)S(1)} %collective-permute-done.1, bf16[4,2,640,512]{3,2,1,0:T(8,128)(2,1)S(1)} %bitcast.115, s32[]{:T(128)S(6)} %select_n.16), kind=kLoop, calls=%fused_computation.2 | loop fusion | flops 5242880 | bytes 7864324 | tf_op jit(solution)/shard_map/convert_element_type | solution.py:74
  137.0 1.9 reduce-scatter.3.cloned.1.call-done
  138.9 19.7 %all_to_all.33 = bf16[16,40,512]{2,1,0:T(8,128)(2,1)S(1)} all-to-all(bf16[16,40,512]{2,1,0:T(8,128)(2,1)} %bitcast.140), channel_id=1, replica_groups=mesh['dp'=16,'fy'=4,'fc'=2] {'dp'}, dimensions={0} | all-to-all | bytes 1310720 | tf_op jit(solution)/shard_map/all_to_all | solution.py:80
  160.3 9.2 %all-gather = f32[1024,2]{0,1:T(2,128)S(1)} all-gather(f32[128,2]{0,1:T(2,128)S(1)} %pad_maximum_fusion), channel_id=2, replica_groups=mesh['dp'=16,'fy'=4,'fc'=2] {'fy','fc'}, dimensions={0}, use_global_device_ids=true | all-gather | bytes 9216 | tf_op jit(solution)/shard_map/all_gather | solution.py:126
  170.1 7.7 %convolution_convert_fusion.2 = bf16[8,512,512]{2,1,0:T(8,128)(2,1)} fusion(bf16[8,640,512]{2,1,0:T(8,128)(2,1)} %bitcast.122, bf16[640,512]{1,0:T(8,128)(2,1)S(1)} %get-tuple-element.21), kind=kOutput, calls=%fused_computation.14 | convolution fusion | flops 2686451712 | bytes 10092544 | tf_op jit(solution)/shard_map/frd,rh->fdh/dot_general | solution.py:136
  177.9 5.1 %convolution_convert_fusion.1 = bf16[8,512,512]{2,1,0:T(8,128)(2,1)} fusion(bf16[8,640,512]{2,1,0:T(8,128)(2,1)S(1)} %bitcast.125, bf16[640,512]{1,0:T(8,128)(2,1)S(1)} %get-tuple-element.22), kind=kOutput, calls=%fused_computation.13 | convolution fusion | flops 2686451712 | bytes 10092544 | tf_op jit(solution)/shard_map/frd,rh->fdh/dot_general | solution.py:139
  183.0 5.1 %convolution_convert_fusion = bf16[512,8,512]{0,2,1:T(8,128)(2,1)} fusion(bf16[8,640,512]{2,1,0:T(8,128)(2,1)S(1)} %bitcast.129, bf16[640,512]{1,0:T(8,128)(2,1)S(1)} %copy-done.14), kind=kOutput, calls=%fused_computation.12 | convolution fusion | flops 2686451712 | bytes 10092544 | tf_op jit(solution)/shard_map/rh,frd->hfd/dot_general | solution.py:142
  188.0 3.6 %all-to-all-start.5 = ((bf16[16,40,512]{2,1,0:T(8,128)(2,1)}), bf16[16,40,512]{2,1,0:T(8,128)(2,1)S(1)}, u32[]{:S(2)}, u32[]{:S(2)}) async-start(bf16[16,40,512]{2,1,0:T(8,128)(2,1)} %bitcast.141), calls=%async_computation.7 | async-start | bytes 1310720 | tf_op jit(solution)/shard_map/all_to_all | solution.py:80
  191.6 6.4 %copy.61 = bf16[512,4096]{1,0:T(8,128)(2,1)} copy(bf16[512,4096]{0,1:T(8,128)(2,1)} %bitcast.134) | data formatting | bytes 8388608
  198.0 7.4 %all-to-all-done.5 = bf16[16,40,512]{2,1,0:T(8,128)(2,1)S(1)} async-done(((bf16[16,40,512]{2,1,0:T(8,128)(2,1)}), bf16[16,40,512]{2,1,0:T(8,128)(2,1)S(1)}, u32[]{:S(2)}, u32[]{:S(2)}) %all-to-all-start.5) | async-done | bytes 655392 | tf_op jit(solution)/shard_map/all_to_all | solution.py:80
  (82 shorter events, 12.2 us)
Async XLA Ops:
  7.2 3.0 %copy-start = (bf16[128,512]{1,0:T(8,128)(2,1)S(1)}, bf16[128,512]{1,0:T(8,128)(2,1)}, u32[]{:S(2)}) copy-start(bf16[128,512]{1,0:T(8,128)(2,1)} %param.7) | copy-start | bytes 393220
  7.2 57.6 %all-gather.4.cloned.1.call-start = ((), (), s32[]{:S(2)}) async-start(), calls=%async_computation.8 | async-start | bytes 3276800 | tf_op jit(solution)/shard_map/all_gather | solution.py:59
  34.4 15.4 %all-to-all-start.2 = ((bf16[16,40,512]{2,1,0:T(8,128)(2,1)}), bf16[16,40,512]{2,1,0:T(8,128)(2,1)S(1)}, u32[]{:S(2)}, u32[]{:S(2)}) async-start(bf16[16,40,512]{2,1,0:T(8,128)(2,1)} %bitcast.21), calls=%async_computation.2 | async-start | bytes 1310720 | tf_op jit(solution)/shard_map/all_to_all | solution.py:56
  38.0 64.3 %all-gather.6.cloned.1.call-start = ((), (), s32[]{:S(2)}) async-start(), calls=%async_computation.9 | async-start | bytes 3276800 | tf_op jit(solution)/shard_map/all_gather | solution.py:59
  49.7 0.8 copy-start.8
  50.6 88.2 %reduce-scatter.3.cloned.1.call-start = ((), (), s32[]{:S(2)}) async-start(), calls=%async_computation.10 | async-start | bytes 3276800 | tf_op jit(solution)/shard_map/reduce_scatter | solution.py:77
  75.0 4.2 %copy-start.2 = (bf16[4096,512]{1,0:T(8,128)(2,1)S(1)}, bf16[4096,512]{1,0:T(8,128)(2,1)}, u32[]{:S(2)}) copy-start(bf16[4096,512]{1,0:T(8,128)(2,1)} %param.10) | copy-start | bytes 12582916
  75.3 6.8 %copy-start.4 = (bf16[4,2,640,512]{3,2,1,0:T(8,128)(2,1)}, bf16[4,2,640,512]{3,2,1,0:T(8,128)(2,1)S(1)}, u32[]{:S(2)}) copy-start(bf16[4,2,640,512]{3,2,1,0:T(8,128)(2,1)S(1)} %copy.54) | copy-start | bytes 15728644
  79.2 2.9 %copy-start.7 = (bf16[4096,512]{1,0:T(8,128)(2,1)S(1)}, bf16[4096,512]{1,0:T(8,128)(2,1)}, u32[]{:S(2)}) copy-start(bf16[4096,512]{1,0:T(8,128)(2,1)} %param.11) | copy-start | bytes 12582916
  82.0 4.0 %copy-start.15 = (f32[640,512]{1,0:T(8,128)}, f32[640,512]{1,0:T(8,128)S(1)}, u32[]{:S(2)}) copy-start(f32[640,512]{1,0:T(8,128)S(1)} %convolution_bitcast_fusion.1) | copy-start | bytes 3932164
  82.1 4.0 %copy-start.11 = (bf16[512,4096]{1,0:T(8,128)(2,1)S(1)}, bf16[512,4096]{1,0:T(8,128)(2,1)}, u32[]{:S(2)}) copy-start(bf16[512,4096]{1,0:T(8,128)(2,1)} %param.12) | copy-start | bytes 12582916
  86.1 3.2 %copy-start.13 = (bf16[640,512]{1,0:T(8,128)(2,1)}, bf16[640,512]{1,0:T(8,128)(2,1)S(1)}, u32[]{:S(2)}) copy-start(bf16[640,512]{1,0:T(8,128)(2,1)S(1)} %get-tuple-element.23) | copy-start | bytes 1966084
  89.3 2.3 %copy-start.6 = (bf16[640,8,512]{2,0,1:T(8,128)(2,1)}, bf16[640,8,512]{2,0,1:T(8,128)(2,1)S(1)}, u32[]{:S(2)}) copy-start(bf16[640,8,512]{2,0,1:T(8,128)(2,1)S(1)} %fusion.8) | copy-start | bytes 15728644
  93.3 5.1 %collective-permute-start = (bf16[4,640,512]{2,1,0:T(8,128)(2,1)}, bf16[4,640,512]{2,1,0:T(8,128)(2,1)S(1)}, u32[]{:S(2)}, u32[]{:S(2)}) collective-permute-start(bf16[4,640,512]{2,1,0:T(8,128)(2,1)} %dynamic-slice_bitcast_fusion.1), channel_id=1, source_target_pairs={{0,1},{1,0},{2,3},{3,2},{4,5},{5,4},{6,7},{7,6},{8,9},{9,8},{10,11... | collective-permute-start | bytes 7864328 | tf_op jit(solution)/shard_map/ppermute | solution.py:73
  102.3 1.7 copy-start.9
  102.4 85.7 %reduce-scatter.5.cloned.1.call-start = ((), (), s32[]{:S(2)}) async-start(), calls=%async_computation.11 | async-start | bytes 3276800 | tf_op jit(solution)/shard_map/reduce_scatter | solution.py:77
  112.5 4.2 %copy-start.12 = (bf16[512,4096]{1,0:T(8,128)(2,1)S(1)}, bf16[512,4096]{1,0:T(8,128)(2,1)}, u32[]{:S(2)}) copy-start(bf16[512,4096]{1,0:T(8,128)(2,1)} %param.12) | copy-start | bytes 12582916
  112.5 4.6 %copy-start.16 = (f32[640,512]{1,0:T(8,128)S(1)}, f32[640,512]{1,0:T(8,128)}, u32[]{:S(2)}) copy-start(f32[640,512]{1,0:T(8,128)} %copy-done.15) | copy-start | bytes 3932164
  112.5 5.0 %copy-start.17 = (f32[640,512]{1,0:T(8,128)S(1)}, f32[640,512]{1,0:T(8,128)}, u32[]{:S(2)}) copy-start(f32[640,512]{1,0:T(8,128)} %get-tuple-element.70) | copy-start | bytes 3932164
  112.8 7.9 %copy-start.5 = (bf16[4,2,640,512]{3,2,1,0:T(8,128)(2,1)}, bf16[4,2,640,512]{3,2,1,0:T(8,128)(2,1)S(1)}, u32[]{:S(2)}) copy-start(bf16[4,2,640,512]{3,2,1,0:T(8,128)(2,1)S(1)} %copy.56) | copy-start | bytes 15728644
  117.5 3.3 %copy-start.3 = (bf16[4096,512]{1,0:T(8,128)(2,1)S(1)}, bf16[4096,512]{1,0:T(8,128)(2,1)}, u32[]{:S(2)}) copy-start(bf16[4096,512]{1,0:T(8,128)(2,1)} %param.10) | copy-start | bytes 12582916
  129.6 5.0 %collective-permute-start.1 = (bf16[4,640,512]{2,1,0:T(8,128)(2,1)S(1)}, bf16[4,640,512]{2,1,0:T(8,128)(2,1)S(1)}, u32[]{:S(2)}, u32[]{:S(2)}) collective-permute-start(bf16[4,640,512]{2,1,0:T(8,128)(2,1)S(1)} %dynamic-slice_bitcast_fusion), channel_id=1, source_target_pairs={{0,1},{1,0},{2,3},{3,2},{4,5},{5,4},{6,7},{7,6},{8,9},{9,8},{10,11... | collective-permute-start | bytes 7864328 | tf_op jit(solution)/shard_map/ppermute | solution.py:73
  137.0 22.2 %copy-start.10 = (bf16[128,512]{1,0:T(8,128)(2,1)S(1)}, bf16[128,512]{1,0:T(8,128)(2,1)}, u32[]{:S(2)}) copy-start(bf16[128,512]{1,0:T(8,128)(2,1)} %param.13) | copy-start | bytes 393220
  158.7 19.1 %slice-start = ((s8[5242880]{0:T(1024)(128)(4,1)}), s8[4194304]{0:T(1024)(128)(4,1)S(1)}, s32[]{:S(2)}) async-start(s8[5242880]{0:T(1024)(128)(4,1)} %bitcast.123), calls=%async_computation.12 | async-start | bytes 8388608
  170.1 7.7 %slice-start.1 = ((s8[5242880]{0:T(1024)(128)(4,1)}), s8[1048576]{0:T(1024)(128)(4,1)S(1)}, s32[]{:S(2)}) async-start(s8[5242880]{0:T(1024)(128)(4,1)} %bitcast.123), calls=%async_computation.13 | async-start | bytes 2097152
  170.1 12.8 %slice-start.2 = ((s8[5242880]{0:T(1024)(128)(4,1)}), s8[4194304]{0:T(1024)(128)(4,1)S(1)}, s32[]{:S(2)}) async-start(s8[5242880]{0:T(1024)(128)(4,1)} %bitcast.127), calls=%async_computation.14 | async-start | bytes 8388608
  177.9 5.1 %slice-start.3 = ((s8[5242880]{0:T(1024)(128)(4,1)}), s8[1048576]{0:T(1024)(128)(4,1)S(1)}, s32[]{:S(2)}) async-start(s8[5242880]{0:T(1024)(128)(4,1)} %bitcast.127), calls=%async_computation.15 | async-start | bytes 2097152
  177.9 5.1 %copy-start.14 = (bf16[640,512]{1,0:T(8,128)(2,1)S(1)}, bf16[640,512]{1,0:T(8,128)(2,1)}, u32[]{:S(2)}) copy-start(bf16[640,512]{1,0:T(8,128)(2,1)} %copy-done.13) | copy-start | bytes 1966084
  188.0 17.3 %all-to-all-start.5 = ((bf16[16,40,512]{2,1,0:T(8,128)(2,1)}), bf16[16,40,512]{2,1,0:T(8,128)(2,1)S(1)}, u32[]{:S(2)}, u32[]{:S(2)}) async-start(bf16[16,40,512]{2,1,0:T(8,128)(2,1)} %bitcast.141), calls=%async_computation.7 | async-start | bytes 1310720 | tf_op jit(solution)/shard_map/all_to_all | solution.py:80
  191.6 15.0 %copy-start.1 = (bf16[128,512]{1,0:T(8,128)(2,1)S(1)}, bf16[128,512]{1,0:T(8,128)(2,1)}, u32[]{:S(2)}) copy-start(bf16[128,512]{1,0:T(8,128)(2,1)} %param.7) | copy-start | bytes 393220
Sparse Core Ops, SparseCore 0:
  31.4 33.3 all-gather.3
  66.4 35.2 all-gather.5
  104.8 34.0 reduce-scatter.2
  141.1 33.7 reduce-scatter.4

commit v12 on v8

--- a/solution.py
+++ b/solution.py
@@ -134,9 +134,6 @@
     gate_weight_grad = jnp.einsum(
         "frd,rh->fdh", expert_rows, gate_grad, preferred_element_type=jnp.float32
     ).astype(jnp.bfloat16).reshape(fsdp_count * feat, hid)
-    up_weight_grad = jnp.einsum(
-        "frd,rh->fdh", expert_rows, up_grad, preferred_element_type=jnp.float32
-    ).astype(jnp.bfloat16).reshape(fsdp_count * feat, hid)
     down_weight_grad = jnp.einsum(
         "hr,frd->hfd", hidden.T, grad_rows, preferred_element_type=jnp.float32
     ).astype(jnp.bfloat16).reshape(hid, model)
@@ -147,8 +144,11 @@
         "rh,fdh->frd", up_grad, up_w3, preferred_element_type=jnp.float32
     )
     input_shares = scatter_chips(swap_cores(input_partial))
-    prob_grad, gate_weight_grad, up_weight_grad, down_weight_grad, input_shares = lax.optimization_barrier(
-        (prob_grad, gate_weight_grad, up_weight_grad, down_weight_grad, input_shares))
+    prob_grad, gate_weight_grad, down_weight_grad, input_shares, up_grad_late = lax.optimization_barrier(
+        (prob_grad, gate_weight_grad, down_weight_grad, input_shares, up_grad))
+    up_weight_grad = jnp.einsum(
+        "frd,rh->fdh", expert_rows, up_grad_late, preferred_element_type=jnp.float32
+    ).astype(jnp.bfloat16).reshape(fsdp_count * feat, hid)
     input_slots = to_token_layout(input_shares)
     token_grad = jnp.dot(
         picker.astype(jnp.float32),

time: 208 us -> 205 us (0.986)
  waiting for transfers between devices: 48.5 us -> 41.2 us
  matrix products: 46.7 us -> 48.9 us
    all_to_all x2, waiting for transfers between devices: 13 us -> 5.66 us  [to_token_layout(): lax.all_to_all(shares.reshape(dp_count, CAP, feat), 'dp', split_axis=0, c...]
    dot_general x1, matrix products: 5.05 us -> 7.56 us  [local(): jnp.einsum('frd,rh->fdh', expert_rows, up_grad_late, preferred_element_ty...]
    unnamed x44 -> x40, local copies, waits for them, and re-layouts: 21.3 us -> 21.3 us
  transfers between devices with their start and end apart: 9 -> 9, of which waited for: 6 -> 5; matrix products, arithmetic and copies ran while one was open for 32% -> 33% of each run, Pallas kernels for 0% -> 0%
where the time goes in v12:
time: 205 us; the launch traced here: 203 us
  matrix products  48.9 us (24%)
  blocking collectives  45.3 us (22%)
  waiting for transfers between devices  41.2 us (20%)
  local copies, waits for them, and re-layouts  28.8 us (14%)
  starting transfers between devices  16.2 us (8%)
  between operations  14.1 us (7%)
  other arithmetic  8.97 us (4%)
    unnamed x40, local copies, waits for them, and re-layouts  21.3 us
    all_to_all x1, blocking collectives, to_expert_layout(): lax.all_to_all(place_rows(source, scaled), 'dp', split_axis=0, concat_axi...  20.6 us
    all_to_all x2, blocking collectives, join_cores(): lax.all_to_all(jnp.broadcast_to(across[:, None], (chips, cores, rows, fea...  15.9 us
    all_gather x2, waiting for transfers between devices, to_expert_layout(): lax.all_gather(arrived.reshape(rows, feat), 'fy', axis=0, tiled=False)  14.1 us
    all_to_all x2, starting transfers between devices, to_token_layout(): lax.all_to_all(shares.reshape(dp_count, CAP, feat), 'dp', split_axis=0, c...  12 us
    all_to_all x1, waiting for transfers between devices, to_expert_layout(): lax.all_to_all(place_rows(source, scaled), 'dp', split_axis=0, concat_axi...  11.7 us
    ppermute x2, waiting for transfers between devices, swap_cores(): lax.ppermute(sent, 'fc', swap).astype(jnp.float32)  9.68 us
    all_gather x1, blocking collectives, local(): lax.all_gather(prob_terms, ('fy', 'fc'), axis=0, tiled=False)  8.78 us
  transfers between devices with their start and end apart: 9, of which 5 were waited for; matrix products, arithmetic and copies ran while one was open for 33% of the time, Pallas kernels for 0%

profile of v12, /device:TPU:0, one launch (start us, length us, event | category | flops | bytes accessed | tf_op | source)
XLA Modules:
  0.0 203.5 jit_solution(15394863380297065614)
XLA Ops:
  10.6 20.6 %all_to_all.30 = bf16[16,40,512]{2,1,0:T(8,128)(2,1)} all-to-all(bf16[16,40,512]{2,1,0:T(8,128)(2,1)S(1)} %bitcast.131), channel_id=1, replica_groups=mesh['dp'=16,'fy'=4,'fc'=2] {'dp'}, dimensions={0} | all-to-all | bytes 1310720 | tf_op jit(solution)/shard_map/all_to_all | solution.py:56
  32.0 1.5 convolution_convert_fusion.3
  34.4 3.6 %all-to-all-start.2 = ((bf16[16,40,512]{2,1,0:T(8,128)(2,1)}), bf16[16,40,512]{2,1,0:T(8,128)(2,1)S(1)}, u32[]{:S(2)}, u32[]{:S(2)}) async-start(bf16[16,40,512]{2,1,0:T(8,128)(2,1)} %bitcast.21), calls=%async_computation.2 | async-start | bytes 1310720 | tf_op jit(solution)/shard_map/all_to_all | solution.py:56
  38.1 11.7 %all-to-all-done.2 = bf16[16,40,512]{2,1,0:T(8,128)(2,1)S(1)} async-done(((bf16[16,40,512]{2,1,0:T(8,128)(2,1)}), bf16[16,40,512]{2,1,0:T(8,128)(2,1)S(1)}, u32[]{:S(2)}, u32[]{:S(2)}) %all-to-all-start.2) | async-done | bytes 655392 | tf_op jit(solution)/shard_map/all_to_all | solution.py:56
  50.7 14.1 %all-gather.4.cloned.1.call-done = bf16[4,640,512]{2,1,0:T(8,128)(2,1)} async-done(((bf16[1,640,512]{2,1,0:T(8,128)(2,1)}), bf16[4,640,512]{2,1,0:T(8,128)(2,1)}) %all-gather.4.cloned.1.call-update) | async-done | bytes 2621456 | tf_op jit(solution)/shard_map/all_gather | solution.py:59
  64.8 2.2 %broadcast_in_dim.42 = bf16[4,2,640,512]{3,2,0,1:T(8,128)(2,1)S(1)} broadcast(bf16[4,640,512]{2,1,0:T(8,128)(2,1)} %all-gather.4.cloned.1.call-done), dimensions={0,2,3} | broadcast | bytes 7864320 | tf_op jit(solution)/shard_map/broadcast_in_dim | solution.py:64
  67.0 7.9 %all_to_all.31 = bf16[4,2,640,512]{3,2,0,1:T(8,128)(2,1)S(1)} all-to-all(bf16[4,2,640,512]{3,2,0,1:T(8,128)(2,1)S(1)} %broadcast_in_dim.42), channel_id=1, replica_groups=mesh['dp'=16,'fy'=4,'fc'=2] {'fc'}, dimensions={1} | all-to-all | bytes 10485760 | tf_op jit(solution)/shard_map/all_to_all | solution.py:63
  75.3 3.9 %copy-done.7 = bf16[4096,512]{1,0:T(8,128)(2,1)S(1)} copy-done((bf16[4096,512]{1,0:T(8,128)(2,1)S(1)}, bf16[4096,512]{1,0:T(8,128)(2,1)}, u32[]{:S(2)}) %copy-start.7) | copy-done | bytes 4194328
  79.2 2.9 %convolution_bitcast_fusion = f32[640,512]{1,0:T(8,128)S(1)} fusion(bf16[8,640,512]{2,1,0:T(8,128)(2,1)S(1)} %bitcast.117, bf16[8,512,512]{2,1,0:T(8,128)(2,1)S(1)} %bitcast.126), kind=kOutput, calls=%fused_computation.18 | convolution fusion | flops 2684354560 | bytes 10747904 | tf_op jit(solution)/shard_map/dot_general | solution.py:96
  82.1 2.9 %convolution_bitcast_fusion.1 = f32[640,512]{1,0:T(8,128)S(1)} fusion(bf16[8,640,512]{2,1,0:T(8,128)(2,1)S(1)} %bitcast.118, bf16[8,512,512]{2,1,0:T(8,128)(2,1)S(1)} %bitcast.113), kind=kOutput, calls=%fused_computation.19 | convolution fusion | flops 2684354560 | bytes 10747904 | tf_op jit(solution)/shard_map/dot_general | solution.py:95
  86.0 3.2 %fusion.8 = bf16[640,8,512]{2,0,1:T(8,128)(2,1)S(1)} fusion(bf16[640,512,1]{1,0,2:T(8,128)(2,1)S(1)} %fusion.15, bf16[64,8,8,512]{3,2,1,0:T(8,128)(2,1)S(1)} %bitcast.139), kind=kOutput, calls=%fused_computation.11 | convolution fusion | flops 2686976000 | bytes 10092544 | tf_op jit(solution)/shard_map/rh,hfd->frd/dot_general | solution.py:100
  89.2 2.3 %copy-done.6 = bf16[640,8,512]{2,0,1:T(8,128)(2,1)} copy-done((bf16[640,8,512]{2,0,1:T(8,128)(2,1)}, bf16[640,8,512]{2,0,1:T(8,128)(2,1)S(1)}, u32[]{:S(2)}) %copy-start.6) | copy-done | bytes 5242904
  91.6 1.7 dynamic-slice_bitcast_fusion.1
  93.3 5.0 %collective-permute-done = bf16[4,640,512]{2,1,0:T(8,128)(2,1)S(1)} collective-permute-done((bf16[4,640,512]{2,1,0:T(8,128)(2,1)}, bf16[4,640,512]{2,1,0:T(8,128)(2,1)S(1)}, u32[]{:S(2)}, u32[]{:S(2)}) %collective-permute-start) | collective-permute-done | bytes 2621472 | tf_op jit(solution)/shard_map/ppermute | solution.py:73
  98.3 4.0 %fusion.1 = bf16[4,640,512]{2,1,0:T(8,128)(2,1)} fusion(bf16[4,640,512]{2,1,0:T(8,128)(2,1)S(1)} %collective-permute-done, bf16[4,2,640,512]{3,2,1,0:T(8,128)(2,1)} %bitcast.124, s32[]{:T(128)S(6)} %select_n.16), kind=kLoop, calls=%fused_computation.4 | loop fusion | flops 5242880 | bytes 7864324 | tf_op jit(solution)/shard_map/convert_element_type | solution.py:74
  102.4 1.7 copy-done.9
  104.5 7.9 %all_to_all.32 = bf16[4,2,640,512]{3,2,0,1:T(8,128)(2,1)S(1)} all-to-all(bf16[4,2,640,512]{3,2,0,1:T(8,128)(2,1)S(1)} %broadcast_in_dim.48), channel_id=1, replica_groups=mesh['dp'=16,'fy'=4,'fc'=2] {'fc'}, dimensions={1} | all-to-all | bytes 10485760 | tf_op jit(solution)/shard_map/all_to_all | solution.py:63
  114.1 1.4 copy-done.13
  115.6 1.9 copy-done.18
  117.5 3.3 %multiply_convert_fusion = (bf16[640,512]{1,0:T(8,128)(2,1)S(1)}, bf16[640,512]{1,0:T(8,128)(2,1)S(1)}) fusion(f32[640,512]{1,0:T(8,128)S(1)} %copy-done.13, f32[640,512]{1,0:T(8,128)S(1)} %copy-done.11, bf16[8,640,512]{2,1,0:T(8,128)(2,1)S(1)} %bitcast.121, bf16[64,8,8,512]{3,2,1,0:T(8,128)(2,1)S(1)} %bitcast.140), kind=kOutput, calls=%fused_computation.22 | convolution fusion | flops 2688614400 | bytes 13369344 | tf_op jit(solution)/shard_map/dot_general | solution.py:128
  120.8 3.0 %fusion.18 = f32[640,8,512]{2,0,1:T(8,128)S(1)} fusion(bf16[8,512,512]{2,1,0:T(8,128)(2,1)S(1)} %bitcast.114, bf16[640,512]{1,0:T(8,128)(2,1)S(1)} %get-tuple-element.53), kind=kOutput, calls=%fused_computation.33 | convolution fusion | flops 2684354560 | bytes 15335424 | tf_op jit(solution)/shard_map/rh,fdh->frd/dot_general | solution.py:140
  123.7 5.6 %add_convert_fusion = bf16[640,8,512]{2,0,1:T(8,128)(2,1)S(1)} fusion(f32[640,8,512]{2,0,1:T(8,128)S(1)} %fusion.18, bf16[8,512,512]{2,1,0:T(8,128)(2,1)} %bitcast.125, bf16[640,512]{1,0:T(8,128)(2,1)S(1)} %get-tuple-element.18), kind=kOutput, calls=%fused_computation | convolution fusion | flops 2689597440 | bytes 20578304 | tf_op jit(solution)/shard_map/rh,fdh->frd/dot_general | solution.py:143
  129.8 4.7 %collective-permute-done.1 = bf16[4,640,512]{2,1,0:T(8,128)(2,1)S(1)} collective-permute-done((bf16[4,640,512]{2,1,0:T(8,128)(2,1)S(1)}, bf16[4,640,512]{2,1,0:T(8,128)(2,1)S(1)}, u32[]{:S(2)}, u32[]{:S(2)}) %collective-permute-start.1) | collective-permute-done | bytes 2621472 | tf_op jit(solution)/shard_map/ppermute | solution.py:73
  134.5 2.4 %fusion = bf16[4,640,512]{2,1,0:T(8,128)(2,1)} fusion(bf16[4,640,512]{2,1,0:T(8,128)(2,1)S(1)} %collective-permute-done.1, bf16[4,2,640,512]{3,2,1,0:T(8,128)(2,1)S(1)} %bitcast.112, s32[]{:T(128)S(6)} %select_n.16), kind=kLoop, calls=%fused_computation.2 | loop fusion | flops 5242880 | bytes 7864324 | tf_op jit(solution)/shard_map/convert_element_type | solution.py:74
  137.0 8.5 %convolution_convert_fusion.1 = bf16[512,8,512]{0,2,1:T(8,128)(2,1)} fusion(bf16[640,512,1]{1,0,2:T(8,128)(2,1)S(1)} %fusion.15, bf16[8,640,512]{2,1,0:T(8,128)(2,1)} %bitcast.122), kind=kOutput, calls=%fused_computation.13 | convolution fusion | flops 2686451712 | bytes 10092544 | tf_op jit(solution)/shard_map/hr,frd->hfd/dot_general | solution.py:137
  145.4 6.9 %all-to-all-start.3 = ((bf16[16,40,512]{2,1,0:T(8,128)(2,1)}), bf16[16,40,512]{2,1,0:T(8,128)(2,1)S(1)}, u32[]{:S(2)}, u32[]{:S(2)}) async-start(bf16[16,40,512]{2,1,0:T(8,128)(2,1)} %bitcast.133), calls=%async_computation.4 | async-start | bytes 1310720 | tf_op jit(solution)/shard_map/all_to_all | solution.py:80
  152.4 7.6 %convolution_convert_fusion.2 = bf16[8,512,512]{2,1,0:T(8,128)(2,1)} fusion(bf16[8,640,512]{2,1,0:T(8,128)(2,1)} %bitcast.119, bf16[640,512]{1,0:T(8,128)(2,1)S(1)} %get-tuple-element.53), kind=kOutput, calls=%fused_computation.14 | convolution fusion | flops 2686451712 | bytes 10092544 | tf_op jit(solution)/shard_map/frd,rh->fdh/dot_general | solution.py:134
  160.0 5.7 %all-to-all-done.3 = bf16[16,40,512]{2,1,0:T(8,128)(2,1)S(1)} async-done(((bf16[16,40,512]{2,1,0:T(8,128)(2,1)}), bf16[16,40,512]{2,1,0:T(8,128)(2,1)S(1)}, u32[]{:S(2)}, u32[]{:S(2)}) %all-to-all-start.3) | async-done | bytes 655392 | tf_op jit(solution)/shard_map/all_to_all | solution.py:80
  167.4 8.8 %all-gather = f32[1024,2]{0,1:T(2,128)S(1)} all-gather(f32[128,2]{0,1:T(2,128)S(1)} %pad_maximum_fusion), channel_id=2, replica_groups=mesh['dp'=16,'fy'=4,'fc'=2] {'fy','fc'}, dimensions={0}, use_global_device_ids=true | all-gather | bytes 9216 | tf_op jit(solution)/shard_map/all_gather | solution.py:126
  176.7 5.1 %all-to-all-start.5 = ((bf16[16,40,512]{2,1,0:T(8,128)(2,1)}), bf16[16,40,512]{2,1,0:T(8,128)(2,1)S(1)}, u32[]{:S(2)}, u32[]{:S(2)}) async-start(bf16[16,40,512]{2,1,0:T(8,128)(2,1)} %bitcast.134), calls=%async_computation.7 | async-start | bytes 1310720 | tf_op jit(solution)/shard_map/all_to_all | solution.py:80
  181.8 6.3 %copy.61 = bf16[512,4096]{1,0:T(8,128)(2,1)} copy(bf16[512,4096]{0,1:T(8,128)(2,1)} %bitcast.127) | data formatting | bytes 8388608
  188.2 7.6 %convolution_convert_fusion = bf16[8,512,512]{2,1,0:T(8,128)(2,1)} fusion(bf16[8,640,512]{2,1,0:T(8,128)(2,1)} %bitcast.120, bf16[640,512]{1,0:T(8,128)(2,1)S(1)} %get-tuple-element.18), kind=kOutput, calls=%fused_computation.12 | convolution fusion | flops 2686451712 | bytes 10092544 | tf_op jit(solution)/shard_map/frd,rh->fdh/dot_general | solution.py:149
  (76 shorter events, 13.8 us)
Async XLA Ops:
  7.2 3.0 %copy-start = (bf16[128,512]{1,0:T(8,128)(2,1)S(1)}, bf16[128,512]{1,0:T(8,128)(2,1)}, u32[]{:S(2)}) copy-start(bf16[128,512]{1,0:T(8,128)(2,1)} %param.7) | copy-start | bytes 393220
  7.2 57.6 %all-gather.4.cloned.1.call-start = ((), (), s32[]{:S(2)}) async-start(), calls=%async_computation.8 | async-start | bytes 3276800 | tf_op jit(solution)/shard_map/all_gather | solution.py:59
  32.0 35.0 %copy-start.15 = (f32[128]{0:T(128)}, f32[128]{0:T(128)S(1)}, u32[]{:S(2)}) copy-start(f32[128]{0:T(128)S(1)} %get-tuple-element.56) | copy-start | bytes 1540
  34.4 15.4 %all-to-all-start.2 = ((bf16[16,40,512]{2,1,0:T(8,128)(2,1)}), bf16[16,40,512]{2,1,0:T(8,128)(2,1)S(1)}, u32[]{:S(2)}, u32[]{:S(2)}) async-start(bf16[16,40,512]{2,1,0:T(8,128)(2,1)} %bitcast.21), calls=%async_computation.2 | async-start | bytes 1310720 | tf_op jit(solution)/shard_map/all_to_all | solution.py:56
  38.0 64.3 %all-gather.6.cloned.1.call-start = ((), (), s32[]{:S(2)}) async-start(), calls=%async_computation.9 | async-start | bytes 3276800 | tf_op jit(solution)/shard_map/all_gather | solution.py:59
  49.8 0.9 copy-start.8
  50.6 94.8 %reduce-scatter.3.cloned.1.call-start = ((), (), s32[]{:S(2)}) async-start(), calls=%async_computation.10 | async-start | bytes 3276800 | tf_op jit(solution)/shard_map/reduce_scatter | solution.py:77
  75.0 4.2 %copy-start.7 = (bf16[4096,512]{1,0:T(8,128)(2,1)S(1)}, bf16[4096,512]{1,0:T(8,128)(2,1)}, u32[]{:S(2)}) copy-start(bf16[4096,512]{1,0:T(8,128)(2,1)} %param.11) | copy-start | bytes 12582916
  75.3 6.8 %copy-start.4 = (bf16[4,2,640,512]{3,2,1,0:T(8,128)(2,1)}, bf16[4,2,640,512]{3,2,1,0:T(8,128)(2,1)S(1)}, u32[]{:S(2)}) copy-start(bf16[4,2,640,512]{3,2,1,0:T(8,128)(2,1)S(1)} %copy.54) | copy-start | bytes 15728644
  79.2 2.9 %copy-start.2 = (bf16[4096,512]{1,0:T(8,128)(2,1)S(1)}, bf16[4096,512]{1,0:T(8,128)(2,1)}, u32[]{:S(2)}) copy-start(bf16[4096,512]{1,0:T(8,128)(2,1)} %param.10) | copy-start | bytes 12582916
  82.0 2.9 %copy-start.10 = (f32[640,512]{1,0:T(8,128)}, f32[640,512]{1,0:T(8,128)S(1)}, u32[]{:S(2)}) copy-start(f32[640,512]{1,0:T(8,128)S(1)} %convolution_bitcast_fusion) | copy-start | bytes 3932164
  82.1 3.9 %copy-start.17 = (bf16[512,4096]{1,0:T(8,128)(2,1)S(1)}, bf16[512,4096]{1,0:T(8,128)(2,1)}, u32[]{:S(2)}) copy-start(bf16[512,4096]{1,0:T(8,128)(2,1)} %param.12) | copy-start | bytes 12582916
  85.0 1.1 copy-start.12
  89.2 2.3 %copy-start.6 = (bf16[640,8,512]{2,0,1:T(8,128)(2,1)}, bf16[640,8,512]{2,0,1:T(8,128)(2,1)S(1)}, u32[]{:S(2)}) copy-start(bf16[640,8,512]{2,0,1:T(8,128)(2,1)S(1)} %fusion.8) | copy-start | bytes 15728644
  93.2 5.1 %collective-permute-start = (bf16[4,640,512]{2,1,0:T(8,128)(2,1)}, bf16[4,640,512]{2,1,0:T(8,128)(2,1)S(1)}, u32[]{:S(2)}, u32[]{:S(2)}) collective-permute-start(bf16[4,640,512]{2,1,0:T(8,128)(2,1)} %dynamic-slice_bitcast_fusion.1), channel_id=1, source_target_pairs={{0,1},{1,0},{2,3},{3,2},{4,5},{5,4},{6,7},{7,6},{8,9},{9,8},{10,11... | collective-permute-start | bytes 7864328 | tf_op jit(solution)/shard_map/ppermute | solution.py:73
  102.3 1.7 copy-start.9
  102.3 74.4 %reduce-scatter.5.cloned.1.call-start = ((), (), s32[]{:S(2)}) async-start(), calls=%async_computation.11 | async-start | bytes 3276800 | tf_op jit(solution)/shard_map/reduce_scatter | solution.py:77
  112.5 1.7 copy-start.11
  112.5 3.1 %copy-start.13 = (f32[640,512]{1,0:T(8,128)S(1)}, f32[640,512]{1,0:T(8,128)}, u32[]{:S(2)}) copy-start(f32[640,512]{1,0:T(8,128)} %copy-done.12) | copy-start | bytes 3932164
  112.5 5.0 %copy-start.18 = (bf16[512,4096]{1,0:T(8,128)(2,1)S(1)}, bf16[512,4096]{1,0:T(8,128)(2,1)}, u32[]{:S(2)}) copy-start(bf16[512,4096]{1,0:T(8,128)(2,1)} %param.12) | copy-start | bytes 12582916
  112.8 7.9 %copy-start.5 = (bf16[4,2,640,512]{3,2,1,0:T(8,128)(2,1)}, bf16[4,2,640,512]{3,2,1,0:T(8,128)(2,1)S(1)}, u32[]{:S(2)}) copy-start(bf16[4,2,640,512]{3,2,1,0:T(8,128)(2,1)S(1)} %copy.56) | copy-start | bytes 15728644
  117.5 3.3 %copy-start.3 = (bf16[4096,512]{1,0:T(8,128)(2,1)S(1)}, bf16[4096,512]{1,0:T(8,128)(2,1)}, u32[]{:S(2)}) copy-start(bf16[4096,512]{1,0:T(8,128)(2,1)} %param.10) | copy-start | bytes 12582916
  129.5 5.0 %collective-permute-start.1 = (bf16[4,640,512]{2,1,0:T(8,128)(2,1)S(1)}, bf16[4,640,512]{2,1,0:T(8,128)(2,1)S(1)}, u32[]{:S(2)}, u32[]{:S(2)}) collective-permute-start(bf16[4,640,512]{2,1,0:T(8,128)(2,1)S(1)} %dynamic-slice_bitcast_fusion), channel_id=1, source_target_pairs={{0,1},{1,0},{2,3},{3,2},{4,5},{5,4},{6,7},{7,6},{8,9},{9,8},{10,11... | collective-permute-start | bytes 7864328 | tf_op jit(solution)/shard_map/ppermute | solution.py:73
  145.4 20.2 %all-to-all-start.3 = ((bf16[16,40,512]{2,1,0:T(8,128)(2,1)}), bf16[16,40,512]{2,1,0:T(8,128)(2,1)S(1)}, u32[]{:S(2)}, u32[]{:S(2)}) async-start(bf16[16,40,512]{2,1,0:T(8,128)(2,1)} %bitcast.133), calls=%async_computation.4 | async-start | bytes 1310720 | tf_op jit(solution)/shard_map/all_to_all | solution.py:80
  152.4 13.8 %copy-start.14 = (bf16[128,512]{1,0:T(8,128)(2,1)S(1)}, bf16[128,512]{1,0:T(8,128)(2,1)}, u32[]{:S(2)}) copy-start(bf16[128,512]{1,0:T(8,128)(2,1)} %param.13) | copy-start | bytes 393220
  152.4 13.8 %copy-start.16 = (f32[128]{0:T(128)S(1)}, f32[128]{0:T(128)}, u32[]{:S(2)}) copy-start(f32[128]{0:T(128)} %copy-done.15) | copy-start | bytes 1540
  176.7 19.0 %all-to-all-start.5 = ((bf16[16,40,512]{2,1,0:T(8,128)(2,1)}), bf16[16,40,512]{2,1,0:T(8,128)(2,1)S(1)}, u32[]{:S(2)}, u32[]{:S(2)}) async-start(bf16[16,40,512]{2,1,0:T(8,128)(2,1)} %bitcast.134), calls=%async_computation.7 | async-start | bytes 1310720 | tf_op jit(solution)/shard_map/all_to_all | solution.py:80
  188.2 8.8 %copy-start.1 = (bf16[128,512]{1,0:T(8,128)(2,1)S(1)}, bf16[128,512]{1,0:T(8,128)(2,1)}, u32[]{:S(2)}) copy-start(bf16[128,512]{1,0:T(8,128)(2,1)} %param.7) | copy-start | bytes 393220
Sparse Core Ops, SparseCore 0:
  31.4 33.3 all-gather.3
  66.4 35.2 all-gather.5
  104.8 34.0 reduce-scatter.2
  141.1 33.6 reduce-scatter.4

commit v13 on v12

--- a/solution.py
+++ b/solution.py
@@ -123,7 +123,8 @@
         [jnp.sum(first_pair * grad_local, axis=1), jnp.sum(second_pair * grad_local, axis=1)],
         axis=1,
     )
-    prob_grad = jnp.sum(lax.all_gather(prob_terms, ("fy", "fc"), axis=0, tiled=False), axis=0)
+    pair_terms = prob_terms + lax.ppermute(prob_terms, "fc", swap)
+    prob_grad = jnp.sum(lax.all_gather(pair_terms, "fy", axis=0, tiled=False), axis=0)
     grad_rows = join_cores(grad_across)
     hidden_grad = lax.dot_general(grad_rows, down_w3, (((0, 2), (1, 2)), ((), ())),
                                   preferred_element_type=jnp.float32)

time: 205 us -> 205 us (level)
  transfers between devices with their start and end apart: 9 -> 10, of which waited for: 5 -> 6; matrix products, arithmetic and copies ran while one was open for 33% -> 33% of each run, Pallas kernels for 0% -> 0%
where the time goes in v13:
time: 205 us; the launch traced here: 203 us
  matrix products  48.9 us (24%)
  blocking collectives  44.3 us (22%)
  waiting for transfers between devices  41.9 us (20%)
  local copies, waits for them, and re-layouts  28.9 us (14%)
  starting transfers between devices  16.5 us (8%)
  between operations  14.1 us (7%)
  other arithmetic  8.97 us (4%)
    unnamed x40, local copies, waits for them, and re-layouts  21.3 us
    all_to_all x1, blocking collectives, to_expert_layout(): lax.all_to_all(place_rows(source, scaled), 'dp', split_axis=0, concat_axi...  20.6 us
    all_to_all x2, blocking collectives, join_cores(): lax.all_to_all(jnp.broadcast_to(across[:, None], (chips, cores, rows, fea...  15.9 us
    all_gather x2, waiting for transfers between devices, to_expert_layout(): lax.all_gather(arrived.reshape(rows, feat), 'fy', axis=0, tiled=False)  14.1 us
    all_to_all x2, starting transfers between devices, to_token_layout(): lax.all_to_all(shares.reshape(dp_count, CAP, feat), 'dp', split_axis=0, c...  12 us
    all_to_all x1, waiting for transfers between devices, to_expert_layout(): lax.all_to_all(place_rows(source, scaled), 'dp', split_axis=0, concat_axi...  11.7 us
    ppermute x2, waiting for transfers between devices, swap_cores(): lax.ppermute(sent, 'fc', swap).astype(jnp.float32)  9.68 us
    dot_general x1, matrix products, local(): jnp.einsum('hr,frd->hfd', hidden.T, grad_rows, preferred_element_type=jnp...  8.45 us
  transfers between devices with their start and end apart: 10, of which 6 were waited for; matrix products, arithmetic and copies ran while one was open for 33% of the time, Pallas kernels for 0%

profile of v13, /device:TPU:0, one launch (start us, length us, event | category | flops | bytes accessed | tf_op | source)
XLA Modules:
  0.0 203.5 jit_solution(859466465584878263)
XLA Ops:
  10.6 20.6 %all_to_all.30 = bf16[16,40,512]{2,1,0:T(8,128)(2,1)} all-to-all(bf16[16,40,512]{2,1,0:T(8,128)(2,1)S(1)} %bitcast.128), channel_id=1, replica_groups=mesh['dp'=16,'fy'=4,'fc'=2] {'dp'}, dimensions={0} | all-to-all | bytes 1310720 | tf_op jit(solution)/shard_map/all_to_all | solution.py:56
  32.0 1.5 convolution_convert_fusion.3
  34.4 3.6 %all-to-all-start.2 = ((bf16[16,40,512]{2,1,0:T(8,128)(2,1)}), bf16[16,40,512]{2,1,0:T(8,128)(2,1)S(1)}, u32[]{:S(2)}, u32[]{:S(2)}) async-start(bf16[16,40,512]{2,1,0:T(8,128)(2,1)} %bitcast.21), calls=%async_computation.2 | async-start | bytes 1310720 | tf_op jit(solution)/shard_map/all_to_all | solution.py:56
  38.1 11.7 %all-to-all-done.2 = bf16[16,40,512]{2,1,0:T(8,128)(2,1)S(1)} async-done(((bf16[16,40,512]{2,1,0:T(8,128)(2,1)}), bf16[16,40,512]{2,1,0:T(8,128)(2,1)S(1)}, u32[]{:S(2)}, u32[]{:S(2)}) %all-to-all-start.2) | async-done | bytes 655392 | tf_op jit(solution)/shard_map/all_to_all | solution.py:56
  50.7 14.1 %all-gather.4.cloned.1.call-done = bf16[4,640,512]{2,1,0:T(8,128)(2,1)} async-done(((bf16[1,640,512]{2,1,0:T(8,128)(2,1)}), bf16[4,640,512]{2,1,0:T(8,128)(2,1)}) %all-gather.4.cloned.1.call-update) | async-done | bytes 2621456 | tf_op jit(solution)/shard_map/all_gather | solution.py:59
  64.8 2.2 %broadcast_in_dim.42 = bf16[4,2,640,512]{3,2,0,1:T(8,128)(2,1)S(1)} broadcast(bf16[4,640,512]{2,1,0:T(8,128)(2,1)} %all-gather.4.cloned.1.call-done), dimensions={0,2,3} | broadcast | bytes 7864320 | tf_op jit(solution)/shard_map/broadcast_in_dim | solution.py:64
  67.0 7.9 %all_to_all.31 = bf16[4,2,640,512]{3,2,0,1:T(8,128)(2,1)S(1)} all-to-all(bf16[4,2,640,512]{3,2,0,1:T(8,128)(2,1)S(1)} %broadcast_in_dim.42), channel_id=1, replica_groups=mesh['dp'=16,'fy'=4,'fc'=2] {'fc'}, dimensions={1} | all-to-all | bytes 10485760 | tf_op jit(solution)/shard_map/all_to_all | solution.py:63
  75.3 3.9 %copy-done.7 = bf16[4096,512]{1,0:T(8,128)(2,1)S(1)} copy-done((bf16[4096,512]{1,0:T(8,128)(2,1)S(1)}, bf16[4096,512]{1,0:T(8,128)(2,1)}, u32[]{:S(2)}) %copy-start.7) | copy-done | bytes 4194328
  79.2 2.9 %convolution_bitcast_fusion = f32[640,512]{1,0:T(8,128)S(1)} fusion(bf16[8,640,512]{2,1,0:T(8,128)(2,1)S(1)} %bitcast.114, bf16[8,512,512]{2,1,0:T(8,128)(2,1)S(1)} %bitcast.123), kind=kOutput, calls=%fused_computation.18 | convolution fusion | flops 2684354560 | bytes 10747904 | tf_op jit(solution)/shard_map/dot_general | solution.py:96
  82.1 2.9 %convolution_bitcast_fusion.1 = f32[640,512]{1,0:T(8,128)S(1)} fusion(bf16[8,640,512]{2,1,0:T(8,128)(2,1)S(1)} %bitcast.115, bf16[8,512,512]{2,1,0:T(8,128)(2,1)S(1)} %bitcast.110), kind=kOutput, calls=%fused_computation.19 | convolution fusion | flops 2684354560 | bytes 10747904 | tf_op jit(solution)/shard_map/dot_general | solution.py:95
  86.0 3.2 %fusion.8 = bf16[640,8,512]{2,0,1:T(8,128)(2,1)S(1)} fusion(bf16[640,512,1]{1,0,2:T(8,128)(2,1)S(1)} %fusion.15, bf16[64,8,8,512]{3,2,1,0:T(8,128)(2,1)S(1)} %bitcast.137), kind=kOutput, calls=%fused_computation.11 | convolution fusion | flops 2686976000 | bytes 10092544 | tf_op jit(solution)/shard_map/rh,hfd->frd/dot_general | solution.py:100
  89.2 2.3 %copy-done.6 = bf16[640,8,512]{2,0,1:T(8,128)(2,1)} copy-done((bf16[640,8,512]{2,0,1:T(8,128)(2,1)}, bf16[640,8,512]{2,0,1:T(8,128)(2,1)S(1)}, u32[]{:S(2)}) %copy-start.6) | copy-done | bytes 5242904
  91.6 1.7 dynamic-slice_bitcast_fusion.1
  93.4 5.0 %collective-permute-done = bf16[4,640,512]{2,1,0:T(8,128)(2,1)S(1)} collective-permute-done((bf16[4,640,512]{2,1,0:T(8,128)(2,1)}, bf16[4,640,512]{2,1,0:T(8,128)(2,1)S(1)}, u32[]{:S(2)}, u32[]{:S(2)}) %collective-permute-start) | collective-permute-done | bytes 2621472 | tf_op jit(solution)/shard_map/ppermute | solution.py:73
  98.4 4.0 %fusion.1 = bf16[4,640,512]{2,1,0:T(8,128)(2,1)} fusion(bf16[4,640,512]{2,1,0:T(8,128)(2,1)S(1)} %collective-permute-done, bf16[4,2,640,512]{3,2,1,0:T(8,128)(2,1)} %bitcast.121, s32[]{:T(128)S(6)} %select_n.16), kind=kLoop, calls=%fused_computation.4 | loop fusion | flops 5242880 | bytes 7864324 | tf_op jit(solution)/shard_map/convert_element_type | solution.py:74
  102.4 1.7 copy-done.9
  104.5 7.9 %all_to_all.32 = bf16[4,2,640,512]{3,2,0,1:T(8,128)(2,1)S(1)} all-to-all(bf16[4,2,640,512]{3,2,0,1:T(8,128)(2,1)S(1)} %broadcast_in_dim.48), channel_id=1, replica_groups=mesh['dp'=16,'fy'=4,'fc'=2] {'fc'}, dimensions={1} | all-to-all | bytes 10485760 | tf_op jit(solution)/shard_map/all_to_all | solution.py:63
  115.6 1.9 copy-done.18
  117.5 3.3 %multiply_convert_fusion = (bf16[640,512]{1,0:T(8,128)(2,1)S(1)}, bf16[640,512]{1,0:T(8,128)(2,1)S(1)}) fusion(f32[640,512]{1,0:T(8,128)S(1)} %copy-done.13, f32[640,512]{1,0:T(8,128)S(1)} %copy-done.11, bf16[8,640,512]{2,1,0:T(8,128)(2,1)S(1)} %bitcast.118, bf16[64,8,8,512]{3,2,1,0:T(8,128)(2,1)S(1)} %bitcast.138), kind=kOutput, calls=%fused_computation.22 | convolution fusion | flops 2688614400 | bytes 13369344 | tf_op jit(solution)/shard_map/dot_general | solution.py:129
  120.8 3.0 %fusion.18 = f32[640,8,512]{2,0,1:T(8,128)S(1)} fusion(bf16[8,512,512]{2,1,0:T(8,128)(2,1)S(1)} %bitcast.111, bf16[640,512]{1,0:T(8,128)(2,1)S(1)} %get-tuple-element.53), kind=kOutput, calls=%fused_computation.33 | convolution fusion | flops 2684354560 | bytes 15335424 | tf_op jit(solution)/shard_map/rh,fdh->frd/dot_general | solution.py:141
  123.7 5.6 %add_convert_fusion = bf16[640,8,512]{2,0,1:T(8,128)(2,1)S(1)} fusion(f32[640,8,512]{2,0,1:T(8,128)S(1)} %fusion.18, bf16[8,512,512]{2,1,0:T(8,128)(2,1)} %bitcast.122, bf16[640,512]{1,0:T(8,128)(2,1)S(1)} %get-tuple-element.18), kind=kOutput, calls=%fused_computation | convolution fusion | flops 2689597440 | bytes 20578304 | tf_op jit(solution)/shard_map/rh,fdh->frd/dot_general | solution.py:144
  129.9 4.7 %collective-permute-done.2 = bf16[4,640,512]{2,1,0:T(8,128)(2,1)S(1)} collective-permute-done((bf16[4,640,512]{2,1,0:T(8,128)(2,1)S(1)}, bf16[4,640,512]{2,1,0:T(8,128)(2,1)S(1)}, u32[]{:S(2)}, u32[]{:S(2)}) %collective-permute-start.2) | collective-permute-done | bytes 2621472 | tf_op jit(solution)/shard_map/ppermute | solution.py:73
  134.5 2.4 %fusion = bf16[4,640,512]{2,1,0:T(8,128)(2,1)} fusion(bf16[4,640,512]{2,1,0:T(8,128)(2,1)S(1)} %collective-permute-done.2, bf16[4,2,640,512]{3,2,1,0:T(8,128)(2,1)S(1)} %bitcast.109, s32[]{:T(128)S(6)} %select_n.16), kind=kLoop, calls=%fused_computation.2 | loop fusion | flops 5242880 | bytes 7864324 | tf_op jit(solution)/shard_map/convert_element_type | solution.py:74
  137.0 1.9 reduce-scatter.3.cloned.1.call-done
  138.9 6.9 %all-to-all-start.3 = ((bf16[16,40,512]{2,1,0:T(8,128)(2,1)}), bf16[16,40,512]{2,1,0:T(8,128)(2,1)S(1)}, u32[]{:S(2)}, u32[]{:S(2)}) async-start(bf16[16,40,512]{2,1,0:T(8,128)(2,1)} %bitcast.131), calls=%async_computation.4 | async-start | bytes 1310720 | tf_op jit(solution)/shard_map/all_to_all | solution.py:80
  145.8 8.4 %convolution_convert_fusion.1 = bf16[512,8,512]{0,2,1:T(8,128)(2,1)} fusion(bf16[640,512,1]{1,0,2:T(8,128)(2,1)S(1)} %fusion.15, bf16[8,640,512]{2,1,0:T(8,128)(2,1)} %bitcast.119), kind=kOutput, calls=%fused_computation.13 | convolution fusion | flops 2686451712 | bytes 10092544 | tf_op jit(solution)/shard_map/hr,frd->hfd/dot_general | solution.py:138
  154.3 4.5 %all-to-all-done.3 = bf16[16,40,512]{2,1,0:T(8,128)(2,1)S(1)} async-done(((bf16[16,40,512]{2,1,0:T(8,128)(2,1)}), bf16[16,40,512]{2,1,0:T(8,128)(2,1)S(1)}, u32[]{:S(2)}, u32[]{:S(2)}) %all-to-all-start.3) | async-done | bytes 655392 | tf_op jit(solution)/shard_map/all_to_all | solution.py:80
  160.8 7.6 %convolution_convert_fusion.2 = bf16[8,512,512]{2,1,0:T(8,128)(2,1)} fusion(bf16[8,640,512]{2,1,0:T(8,128)(2,1)} %bitcast.116, bf16[640,512]{1,0:T(8,128)(2,1)S(1)} %get-tuple-element.53), kind=kOutput, calls=%fused_computation.14 | convolution fusion | flops 2686451712 | bytes 10092544 | tf_op jit(solution)/shard_map/frd,rh->fdh/dot_general | solution.py:135
  168.4 7.8 %all-gather = f32[512,2]{0,1:T(2,128)S(1)} all-gather(f32[128,2]{0,1:T(2,128)S(1)} %fusion.46), channel_id=2, replica_groups=mesh['dp'=16,'fy'=4,'fc'=2] {'fy'}, dimensions={0}, use_global_device_ids=true | all-gather | bytes 5120 | tf_op jit(solution)/shard_map/all_gather | solution.py:127
  176.8 5.0 %all-to-all-start.5 = ((bf16[16,40,512]{2,1,0:T(8,128)(2,1)}), bf16[16,40,512]{2,1,0:T(8,128)(2,1)S(1)}, u32[]{:S(2)}, u32[]{:S(2)}) async-start(bf16[16,40,512]{2,1,0:T(8,128)(2,1)} %bitcast.130), calls=%async_computation.7 | async-start | bytes 1310720 | tf_op jit(solution)/shard_map/all_to_all | solution.py:80
  181.8 6.3 %copy.61 = bf16[512,4096]{1,0:T(8,128)(2,1)} copy(bf16[512,4096]{0,1:T(8,128)(2,1)} %bitcast.124) | data formatting | bytes 8388608
  188.2 7.6 %convolution_convert_fusion = bf16[8,512,512]{2,1,0:T(8,128)(2,1)} fusion(bf16[8,640,512]{2,1,0:T(8,128)(2,1)} %bitcast.117, bf16[640,512]{1,0:T(8,128)(2,1)S(1)} %get-tuple-element.18), kind=kOutput, calls=%fused_computation.12 | convolution fusion | flops 2686451712 | bytes 10092544 | tf_op jit(solution)/shard_map/frd,rh->fdh/dot_general | solution.py:150
  (80 shorter events, 15.5 us)
Async XLA Ops:
  7.2 3.0 %copy-start = (bf16[128,512]{1,0:T(8,128)(2,1)S(1)}, bf16[128,512]{1,0:T(8,128)(2,1)}, u32[]{:S(2)}) copy-start(bf16[128,512]{1,0:T(8,128)(2,1)} %param.7) | copy-start | bytes 393220
  7.2 57.6 %all-gather.4.cloned.1.call-start = ((), (), s32[]{:S(2)}) async-start(), calls=%async_computation.8 | async-start | bytes 3276800 | tf_op jit(solution)/shard_map/all_gather | solution.py:59
  32.0 35.0 %copy-start.15 = (f32[128]{0:T(128)}, f32[128]{0:T(128)S(1)}, u32[]{:S(2)}) copy-start(f32[128]{0:T(128)S(1)} %get-tuple-element.56) | copy-start | bytes 1540
  34.4 15.4 %all-to-all-start.2 = ((bf16[16,40,512]{2,1,0:T(8,128)(2,1)}), bf16[16,40,512]{2,1,0:T(8,128)(2,1)S(1)}, u32[]{:S(2)}, u32[]{:S(2)}) async-start(bf16[16,40,512]{2,1,0:T(8,128)(2,1)} %bitcast.21), calls=%async_computation.2 | async-start | bytes 1310720 | tf_op jit(solution)/shard_map/all_to_all | solution.py:56
  38.0 64.3 %all-gather.6.cloned.1.call-start = ((), (), s32[]{:S(2)}) async-start(), calls=%async_computation.9 | async-start | bytes 3276800 | tf_op jit(solution)/shard_map/all_gather | solution.py:59
  49.8 0.8 copy-start.8
  50.6 88.2 %reduce-scatter.3.cloned.1.call-start = ((), (), s32[]{:S(2)}) async-start(), calls=%async_computation.10 | async-start | bytes 3276800 | tf_op jit(solution)/shard_map/reduce_scatter | solution.py:77
  75.0 4.2 %copy-start.7 = (bf16[4096,512]{1,0:T(8,128)(2,1)S(1)}, bf16[4096,512]{1,0:T(8,128)(2,1)}, u32[]{:S(2)}) copy-start(bf16[4096,512]{1,0:T(8,128)(2,1)} %param.11) | copy-start | bytes 12582916
  75.3 6.8 %copy-start.4 = (bf16[4,2,640,512]{3,2,1,0:T(8,128)(2,1)}, bf16[4,2,640,512]{3,2,1,0:T(8,128)(2,1)S(1)}, u32[]{:S(2)}) copy-start(bf16[4,2,640,512]{3,2,1,0:T(8,128)(2,1)S(1)} %copy.54) | copy-start | bytes 15728644
  79.2 2.9 %copy-start.2 = (bf16[4096,512]{1,0:T(8,128)(2,1)S(1)}, bf16[4096,512]{1,0:T(8,128)(2,1)}, u32[]{:S(2)}) copy-start(bf16[4096,512]{1,0:T(8,128)(2,1)} %param.10) | copy-start | bytes 12582916
  82.0 2.9 %copy-start.10 = (f32[640,512]{1,0:T(8,128)}, f32[640,512]{1,0:T(8,128)S(1)}, u32[]{:S(2)}) copy-start(f32[640,512]{1,0:T(8,128)S(1)} %convolution_bitcast_fusion) | copy-start | bytes 3932164
  82.1 3.9 %copy-start.17 = (bf16[512,4096]{1,0:T(8,128)(2,1)S(1)}, bf16[512,4096]{1,0:T(8,128)(2,1)}, u32[]{:S(2)}) copy-start(bf16[512,4096]{1,0:T(8,128)(2,1)} %param.12) | copy-start | bytes 12582916
  85.0 1.1 copy-start.12
  89.2 2.3 %copy-start.6 = (bf16[640,8,512]{2,0,1:T(8,128)(2,1)}, bf16[640,8,512]{2,0,1:T(8,128)(2,1)S(1)}, u32[]{:S(2)}) copy-start(bf16[640,8,512]{2,0,1:T(8,128)(2,1)S(1)} %fusion.8) | copy-start | bytes 15728644
  93.2 5.1 %collective-permute-start = (bf16[4,640,512]{2,1,0:T(8,128)(2,1)}, bf16[4,640,512]{2,1,0:T(8,128)(2,1)S(1)}, u32[]{:S(2)}, u32[]{:S(2)}) collective-permute-start(bf16[4,640,512]{2,1,0:T(8,128)(2,1)} %dynamic-slice_bitcast_fusion.1), channel_id=1, source_target_pairs={{0,1},{1,0},{2,3},{3,2},{4,5},{5,4},{6,7},{7,6},{8,9},{9,8},{10,11... | collective-permute-start | bytes 7864328 | tf_op jit(solution)/shard_map/ppermute | solution.py:73
  102.3 1.7 copy-start.9
  102.4 74.4 %reduce-scatter.5.cloned.1.call-start = ((), (), s32[]{:S(2)}) async-start(), calls=%async_computation.11 | async-start | bytes 3276800 | tf_op jit(solution)/shard_map/reduce_scatter | solution.py:77
  112.5 1.7 copy-start.11
  112.5 3.1 %copy-start.13 = (f32[640,512]{1,0:T(8,128)S(1)}, f32[640,512]{1,0:T(8,128)}, u32[]{:S(2)}) copy-start(f32[640,512]{1,0:T(8,128)} %copy-done.12) | copy-start | bytes 3932164
  112.5 5.0 %copy-start.18 = (bf16[512,4096]{1,0:T(8,128)(2,1)S(1)}, bf16[512,4096]{1,0:T(8,128)(2,1)}, u32[]{:S(2)}) copy-start(bf16[512,4096]{1,0:T(8,128)(2,1)} %param.12) | copy-start | bytes 12582916
  112.8 7.9 %copy-start.5 = (bf16[4,2,640,512]{3,2,1,0:T(8,128)(2,1)}, bf16[4,2,640,512]{3,2,1,0:T(8,128)(2,1)S(1)}, u32[]{:S(2)}) copy-start(bf16[4,2,640,512]{3,2,1,0:T(8,128)(2,1)S(1)} %copy.56) | copy-start | bytes 15728644
  117.5 3.3 %copy-start.3 = (bf16[4096,512]{1,0:T(8,128)(2,1)S(1)}, bf16[4096,512]{1,0:T(8,128)(2,1)}, u32[]{:S(2)}) copy-start(bf16[4096,512]{1,0:T(8,128)(2,1)} %param.10) | copy-start | bytes 12582916
  129.6 5.0 %collective-permute-start.2 = (bf16[4,640,512]{2,1,0:T(8,128)(2,1)S(1)}, bf16[4,640,512]{2,1,0:T(8,128)(2,1)S(1)}, u32[]{:S(2)}, u32[]{:S(2)}) collective-permute-start(bf16[4,640,512]{2,1,0:T(8,128)(2,1)S(1)} %dynamic-slice_bitcast_fusion), channel_id=1, source_target_pairs={{0,1},{1,0},{2,3},{3,2},{4,5},{5,4},{6,7},{7,6},{8,9},{9,8},{10,11... | collective-permute-start | bytes 7864328 | tf_op jit(solution)/shard_map/ppermute | solution.py:73
  138.9 19.9 %all-to-all-start.3 = ((bf16[16,40,512]{2,1,0:T(8,128)(2,1)}), bf16[16,40,512]{2,1,0:T(8,128)(2,1)S(1)}, u32[]{:S(2)}, u32[]{:S(2)}) async-start(bf16[16,40,512]{2,1,0:T(8,128)(2,1)} %bitcast.131), calls=%async_computation.4 | async-start | bytes 1310720 | tf_op jit(solution)/shard_map/all_to_all | solution.py:80
  145.8 13.5 %copy-start.14 = (bf16[128,512]{1,0:T(8,128)(2,1)S(1)}, bf16[128,512]{1,0:T(8,128)(2,1)}, u32[]{:S(2)}) copy-start(bf16[128,512]{1,0:T(8,128)(2,1)} %param.13) | copy-start | bytes 393220
  145.8 13.5 %copy-start.16 = (f32[128]{0:T(128)S(1)}, f32[128]{0:T(128)}, u32[]{:S(2)}) copy-start(f32[128]{0:T(128)} %copy-done.15) | copy-start | bytes 1540
  160.5 7.9 %collective-permute-start.1 = (f32[128,2]{0,1:T(2,128)S(1)}, f32[128,2]{0,1:T(2,128)S(1)}, u32[]{:S(2)}, u32[]{:S(2)}) collective-permute-start(f32[128,2]{0,1:T(2,128)S(1)} %pad_maximum_fusion), channel_id=1, source_target_pairs={{0,1},{1,0},{2,3},{3,2},{4,5},{5,4},{6,7},{7,6},{8,9},{9,8},{10,11... | collective-permute-start | bytes 3080 | tf_op jit(solution)/shard_map/ppermute | solution.py:126
  176.8 18.9 %all-to-all-start.5 = ((bf16[16,40,512]{2,1,0:T(8,128)(2,1)}), bf16[16,40,512]{2,1,0:T(8,128)(2,1)S(1)}, u32[]{:S(2)}, u32[]{:S(2)}) async-start(bf16[16,40,512]{2,1,0:T(8,128)(2,1)} %bitcast.130), calls=%async_computation.7 | async-start | bytes 1310720 | tf_op jit(solution)/shard_map/all_to_all | solution.py:80
  188.2 8.8 %copy-start.1 = (bf16[128,512]{1,0:T(8,128)(2,1)S(1)}, bf16[128,512]{1,0:T(8,128)(2,1)}, u32[]{:S(2)}) copy-start(bf16[128,512]{1,0:T(8,128)(2,1)} %param.7) | copy-start | bytes 393220
Sparse Core Ops, SparseCore 0:
  31.4 33.3 all-gather.3
  66.4 35.2 all-gather.5
  104.8 34.0 reduce-scatter.2
  141.1 33.6 reduce-scatter.4

commit v14 on v13

--- a/solution.py
+++ b/solution.py
@@ -23,7 +23,10 @@
     swap = [(0, 1), (1, 0)]
     routing = expert_ids.reshape(-1)
     onehot = (routing[:, None] == jnp.arange(E, dtype=jnp.int32)[None, :]).astype(jnp.int32)
-    position = jnp.sum((jnp.cumsum(onehot, axis=0) - onehot) * onehot, axis=1)
+    pair_index = jnp.arange(routing.shape[0], dtype=jnp.int32)
+    earlier = (pair_index[:, None] > pair_index[None, :]).astype(jnp.bfloat16)
+    before = jnp.dot(earlier, onehot.astype(jnp.bfloat16), preferred_element_type=jnp.float32)
+    position = jnp.sum(before * onehot.astype(jnp.float32), axis=1).astype(jnp.int32)
     slot_of = (routing * CAP + position).reshape(token_count, 2)
     slot_index = jnp.arange(slot_total, dtype=jnp.int32)
     select_first = slot_of[:, 0:1] == slot_index[None, :]

time: 205 us -> 204 us (level)
  transfers between devices with their start and end apart: 10 -> 10, of which waited for: 6 -> 6; matrix products, arithmetic and copies ran while one was open for 33% -> 34% of each run, Pallas kernels for 0% -> 0%
where the time goes in v14:
time: 204 us; the launch traced here: 203 us
  matrix products  49.1 us (24%)
  blocking collectives  44.3 us (22%)
  waiting for transfers between devices  41.8 us (20%)
  local copies, waits for them, and re-layouts  28.5 us (14%)
  starting transfers between devices  16.5 us (8%)
  between operations  14.1 us (7%)
  other arithmetic  8.29 us (4%)
    unnamed x40, local copies, waits for them, and re-layouts  21.3 us
    all_to_all x1, blocking collectives, to_expert_layout(): lax.all_to_all(place_rows(source, scaled), 'dp', split_axis=0, concat_axi...  20.6 us
    all_to_all x2, blocking collectives, join_cores(): lax.all_to_all(jnp.broadcast_to(across[:, None], (chips, cores, rows, fea...  15.9 us
    all_gather x2, waiting for transfers between devices, to_expert_layout(): lax.all_gather(arrived.reshape(rows, feat), 'fy', axis=0, tiled=False)  14.1 us
    all_to_all x2, starting transfers between devices, to_token_layout(): lax.all_to_all(shares.reshape(dp_count, CAP, feat), 'dp', split_axis=0, c...  12 us
    all_to_all x1, waiting for transfers between devices, to_expert_layout(): lax.all_to_all(place_rows(source, scaled), 'dp', split_axis=0, concat_axi...  11.7 us
    ppermute x2, waiting for transfers between devices, swap_cores(): lax.ppermute(sent, 'fc', swap).astype(jnp.float32)  9.67 us
    dot_general x1, matrix products, local(): jnp.einsum('hr,frd->hfd', hidden.T, grad_rows, preferred_element_type=jnp...  8.45 us
  transfers between devices with their start and end apart: 10, of which 6 were waited for; matrix products, arithmetic and copies ran while one was open for 34% of the time, Pallas kernels for 0%

profile of v14, /device:TPU:0, one launch (start us, length us, event | category | flops | bytes accessed | tf_op | source)
XLA Modules:
  0.0 202.6 jit_solution(5982294670945165384)
XLA Ops:
  9.7 20.6 %all_to_all.30 = bf16[16,40,512]{2,1,0:T(8,128)(2,1)} all-to-all(bf16[16,40,512]{2,1,0:T(8,128)(2,1)S(1)} %bitcast.120), channel_id=1, replica_groups=mesh['dp'=16,'fy'=4,'fc'=2] {'dp'}, dimensions={0} | all-to-all | bytes 1310720 | tf_op jit(solution)/shard_map/all_to_all | solution.py:59
  31.1 1.5 convolution_convert_fusion.3
  33.5 3.6 %all-to-all-start.2 = ((bf16[16,40,512]{2,1,0:T(8,128)(2,1)}), bf16[16,40,512]{2,1,0:T(8,128)(2,1)S(1)}, u32[]{:S(2)}, u32[]{:S(2)}) async-start(bf16[16,40,512]{2,1,0:T(8,128)(2,1)} %bitcast.19), calls=%async_computation.2 | async-start | bytes 1310720 | tf_op jit(solution)/shard_map/all_to_all | solution.py:59
  37.2 11.7 %all-to-all-done.2 = bf16[16,40,512]{2,1,0:T(8,128)(2,1)S(1)} async-done(((bf16[16,40,512]{2,1,0:T(8,128)(2,1)}), bf16[16,40,512]{2,1,0:T(8,128)(2,1)S(1)}, u32[]{:S(2)}, u32[]{:S(2)}) %all-to-all-start.2) | async-done | bytes 655392 | tf_op jit(solution)/shard_map/all_to_all | solution.py:59
  49.8 14.1 %all-gather.4.cloned.1.call-done = bf16[4,640,512]{2,1,0:T(8,128)(2,1)} async-done(((bf16[1,640,512]{2,1,0:T(8,128)(2,1)}), bf16[4,640,512]{2,1,0:T(8,128)(2,1)}) %all-gather.4.cloned.1.call-update) | async-done | bytes 2621456 | tf_op jit(solution)/shard_map/all_gather | solution.py:62
  63.9 2.2 %broadcast_in_dim.44 = bf16[4,2,640,512]{3,2,0,1:T(8,128)(2,1)S(1)} broadcast(bf16[4,640,512]{2,1,0:T(8,128)(2,1)} %all-gather.4.cloned.1.call-done), dimensions={0,2,3} | broadcast | bytes 7864320 | tf_op jit(solution)/shard_map/broadcast_in_dim | solution.py:67
  66.1 7.9 %all_to_all.31 = bf16[4,2,640,512]{3,2,0,1:T(8,128)(2,1)S(1)} all-to-all(bf16[4,2,640,512]{3,2,0,1:T(8,128)(2,1)S(1)} %broadcast_in_dim.44), channel_id=1, replica_groups=mesh['dp'=16,'fy'=4,'fc'=2] {'fc'}, dimensions={1} | all-to-all | bytes 10485760 | tf_op jit(solution)/shard_map/all_to_all | solution.py:66
  74.4 3.9 %copy-done.7 = bf16[4096,512]{1,0:T(8,128)(2,1)S(1)} copy-done((bf16[4096,512]{1,0:T(8,128)(2,1)S(1)}, bf16[4096,512]{1,0:T(8,128)(2,1)}, u32[]{:S(2)}) %copy-start.7) | copy-done | bytes 4194328
  78.3 2.9 %convolution_bitcast_fusion = f32[640,512]{1,0:T(8,128)S(1)} fusion(bf16[8,640,512]{2,1,0:T(8,128)(2,1)S(1)} %bitcast.106, bf16[8,512,512]{2,1,0:T(8,128)(2,1)S(1)} %bitcast.115), kind=kOutput, calls=%fused_computation.18 | convolution fusion | flops 2684354560 | bytes 10747904 | tf_op jit(solution)/shard_map/dot_general | solution.py:99
  81.2 2.9 %convolution_bitcast_fusion.1 = f32[640,512]{1,0:T(8,128)S(1)} fusion(bf16[8,640,512]{2,1,0:T(8,128)(2,1)S(1)} %bitcast.107, bf16[8,512,512]{2,1,0:T(8,128)(2,1)S(1)} %bitcast.102), kind=kOutput, calls=%fused_computation.19 | convolution fusion | flops 2684354560 | bytes 10747904 | tf_op jit(solution)/shard_map/dot_general | solution.py:98
  85.1 3.2 %fusion.8 = bf16[640,8,512]{2,0,1:T(8,128)(2,1)S(1)} fusion(bf16[640,512,1]{1,0,2:T(8,128)(2,1)S(1)} %fusion.16, bf16[64,8,8,512]{3,2,1,0:T(8,128)(2,1)S(1)} %bitcast.129), kind=kOutput, calls=%fused_computation.11 | convolution fusion | flops 2686976000 | bytes 10092544 | tf_op jit(solution)/shard_map/rh,hfd->frd/dot_general | solution.py:103
  88.3 2.3 %copy-done.6 = bf16[640,8,512]{2,0,1:T(8,128)(2,1)} copy-done((bf16[640,8,512]{2,0,1:T(8,128)(2,1)}, bf16[640,8,512]{2,0,1:T(8,128)(2,1)S(1)}, u32[]{:S(2)}) %copy-start.6) | copy-done | bytes 5242904
  90.7 1.7 dynamic-slice_bitcast_fusion.1
  92.5 5.0 %collective-permute-done = bf16[4,640,512]{2,1,0:T(8,128)(2,1)S(1)} collective-permute-done((bf16[4,640,512]{2,1,0:T(8,128)(2,1)}, bf16[4,640,512]{2,1,0:T(8,128)(2,1)S(1)}, u32[]{:S(2)}, u32[]{:S(2)}) %collective-permute-start) | collective-permute-done | bytes 2621472 | tf_op jit(solution)/shard_map/ppermute | solution.py:76
  97.5 4.0 %fusion.1 = bf16[4,640,512]{2,1,0:T(8,128)(2,1)} fusion(bf16[4,640,512]{2,1,0:T(8,128)(2,1)S(1)} %collective-permute-done, bf16[4,2,640,512]{3,2,1,0:T(8,128)(2,1)} %bitcast.113, s32[]{:T(128)S(6)} %select_n.16), kind=kLoop, calls=%fused_computation.4 | loop fusion | flops 5242880 | bytes 7864324 | tf_op jit(solution)/shard_map/convert_element_type | solution.py:77
  101.5 1.7 copy-done.9
  103.6 7.9 %all_to_all.32 = bf16[4,2,640,512]{3,2,0,1:T(8,128)(2,1)S(1)} all-to-all(bf16[4,2,640,512]{3,2,0,1:T(8,128)(2,1)S(1)} %broadcast_in_dim.50), channel_id=1, replica_groups=mesh['dp'=16,'fy'=4,'fc'=2] {'fc'}, dimensions={1} | all-to-all | bytes 10485760 | tf_op jit(solution)/shard_map/all_to_all | solution.py:66
  114.7 1.9 copy-done.18
  116.6 3.3 %multiply_convert_fusion = (bf16[640,512]{1,0:T(8,128)(2,1)S(1)}, bf16[640,512]{1,0:T(8,128)(2,1)S(1)}) fusion(f32[640,512]{1,0:T(8,128)S(1)} %copy-done.13, f32[640,512]{1,0:T(8,128)S(1)} %copy-done.11, bf16[8,640,512]{2,1,0:T(8,128)(2,1)S(1)} %bitcast.110, bf16[64,8,8,512]{3,2,1,0:T(8,128)(2,1)S(1)} %bitcast.130), kind=kOutput, calls=%fused_computation.22 | convolution fusion | flops 2688614400 | bytes 13369344 | tf_op jit(solution)/shard_map/dot_general | solution.py:132
  119.9 3.0 %fusion.19 = f32[640,8,512]{2,0,1:T(8,128)S(1)} fusion(bf16[8,512,512]{2,1,0:T(8,128)(2,1)S(1)} %bitcast.103, bf16[640,512]{1,0:T(8,128)(2,1)S(1)} %get-tuple-element.53), kind=kOutput, calls=%fused_computation.35 | convolution fusion | flops 2684354560 | bytes 15335424 | tf_op jit(solution)/shard_map/rh,fdh->frd/dot_general | solution.py:144
  122.9 5.6 %add_convert_fusion = bf16[640,8,512]{2,0,1:T(8,128)(2,1)S(1)} fusion(f32[640,8,512]{2,0,1:T(8,128)S(1)} %fusion.19, bf16[8,512,512]{2,1,0:T(8,128)(2,1)} %bitcast.114, bf16[640,512]{1,0:T(8,128)(2,1)S(1)} %get-tuple-element.18), kind=kOutput, calls=%fused_computation | convolution fusion | flops 2689597440 | bytes 20578304 | tf_op jit(solution)/shard_map/rh,fdh->frd/dot_general | solution.py:147
  129.0 4.7 %collective-permute-done.2 = bf16[4,640,512]{2,1,0:T(8,128)(2,1)S(1)} collective-permute-done((bf16[4,640,512]{2,1,0:T(8,128)(2,1)S(1)}, bf16[4,640,512]{2,1,0:T(8,128)(2,1)S(1)}, u32[]{:S(2)}, u32[]{:S(2)}) %collective-permute-start.2) | collective-permute-done | bytes 2621472 | tf_op jit(solution)/shard_map/ppermute | solution.py:76
  133.7 2.4 %fusion = bf16[4,640,512]{2,1,0:T(8,128)(2,1)} fusion(bf16[4,640,512]{2,1,0:T(8,128)(2,1)S(1)} %collective-permute-done.2, bf16[4,2,640,512]{3,2,1,0:T(8,128)(2,1)S(1)} %bitcast.101, s32[]{:T(128)S(6)} %select_n.16), kind=kLoop, calls=%fused_computation.2 | loop fusion | flops 5242880 | bytes 7864324 | tf_op jit(solution)/shard_map/convert_element_type | solution.py:77
  136.1 1.9 reduce-scatter.3.cloned.1.call-done
  138.0 6.9 %all-to-all-start.3 = ((bf16[16,40,512]{2,1,0:T(8,128)(2,1)}), bf16[16,40,512]{2,1,0:T(8,128)(2,1)S(1)}, u32[]{:S(2)}, u32[]{:S(2)}) async-start(bf16[16,40,512]{2,1,0:T(8,128)(2,1)} %bitcast.123), calls=%async_computation.4 | async-start | bytes 1310720 | tf_op jit(solution)/shard_map/all_to_all | solution.py:83
  145.0 8.4 %convolution_convert_fusion.1 = bf16[512,8,512]{0,2,1:T(8,128)(2,1)} fusion(bf16[640,512,1]{1,0,2:T(8,128)(2,1)S(1)} %fusion.16, bf16[8,640,512]{2,1,0:T(8,128)(2,1)} %bitcast.111), kind=kOutput, calls=%fused_computation.13 | convolution fusion | flops 2686451712 | bytes 10092544 | tf_op jit(solution)/shard_map/hr,frd->hfd/dot_general | solution.py:141
  153.4 4.5 %all-to-all-done.3 = bf16[16,40,512]{2,1,0:T(8,128)(2,1)S(1)} async-done(((bf16[16,40,512]{2,1,0:T(8,128)(2,1)}), bf16[16,40,512]{2,1,0:T(8,128)(2,1)S(1)}, u32[]{:S(2)}, u32[]{:S(2)}) %all-to-all-start.3) | async-done | bytes 655392 | tf_op jit(solution)/shard_map/all_to_all | solution.py:83
  159.9 7.6 %convolution_convert_fusion.2 = bf16[8,512,512]{2,1,0:T(8,128)(2,1)} fusion(bf16[8,640,512]{2,1,0:T(8,128)(2,1)} %bitcast.108, bf16[640,512]{1,0:T(8,128)(2,1)S(1)} %get-tuple-element.53), kind=kOutput, calls=%fused_computation.14 | convolution fusion | flops 2686451712 | bytes 10092544 | tf_op jit(solution)/shard_map/frd,rh->fdh/dot_general | solution.py:138
  167.5 7.8 %all-gather = f32[512,2]{0,1:T(2,128)S(1)} all-gather(f32[128,2]{0,1:T(2,128)S(1)} %fusion.45), channel_id=2, replica_groups=mesh['dp'=16,'fy'=4,'fc'=2] {'fy'}, dimensions={0}, use_global_device_ids=true | all-gather | bytes 5120 | tf_op jit(solution)/shard_map/all_gather | solution.py:130
  175.9 5.0 %all-to-all-start.5 = ((bf16[16,40,512]{2,1,0:T(8,128)(2,1)}), bf16[16,40,512]{2,1,0:T(8,128)(2,1)S(1)}, u32[]{:S(2)}, u32[]{:S(2)}) async-start(bf16[16,40,512]{2,1,0:T(8,128)(2,1)} %bitcast.122), calls=%async_computation.7 | async-start | bytes 1310720 | tf_op jit(solution)/shard_map/all_to_all | solution.py:83
  180.9 6.3 %copy.57 = bf16[512,4096]{1,0:T(8,128)(2,1)} copy(bf16[512,4096]{0,1:T(8,128)(2,1)} %bitcast.116) | data formatting | bytes 8388608
  187.3 7.6 %convolution_convert_fusion = bf16[8,512,512]{2,1,0:T(8,128)(2,1)} fusion(bf16[8,640,512]{2,1,0:T(8,128)(2,1)} %bitcast.109, bf16[640,512]{1,0:T(8,128)(2,1)S(1)} %get-tuple-element.18), kind=kOutput, calls=%fused_computation.12 | convolution fusion | flops 2686451712 | bytes 10092544 | tf_op jit(solution)/shard_map/frd,rh->fdh/dot_general | solution.py:153
  (75 shorter events, 14.7 us)
Async XLA Ops:
  7.2 2.2 %copy-start = (bf16[128,512]{1,0:T(8,128)(2,1)S(1)}, bf16[128,512]{1,0:T(8,128)(2,1)}, u32[]{:S(2)}) copy-start(bf16[128,512]{1,0:T(8,128)(2,1)} %param.7) | copy-start | bytes 393220
  7.2 56.7 %all-gather.4.cloned.1.call-start = ((), (), s32[]{:S(2)}) async-start(), calls=%async_computation.8 | async-start | bytes 3276800 | tf_op jit(solution)/shard_map/all_gather | solution.py:62
  31.1 35.0 %copy-start.15 = (f32[128]{0:T(128)}, f32[128]{0:T(128)S(1)}, u32[]{:S(2)}) copy-start(f32[128]{0:T(128)S(1)} %get-tuple-element.56) | copy-start | bytes 1540
  33.5 15.4 %all-to-all-start.2 = ((bf16[16,40,512]{2,1,0:T(8,128)(2,1)}), bf16[16,40,512]{2,1,0:T(8,128)(2,1)S(1)}, u32[]{:S(2)}, u32[]{:S(2)}) async-start(bf16[16,40,512]{2,1,0:T(8,128)(2,1)} %bitcast.19), calls=%async_computation.2 | async-start | bytes 1310720 | tf_op jit(solution)/shard_map/all_to_all | solution.py:59
  37.2 64.3 %all-gather.6.cloned.1.call-start = ((), (), s32[]{:S(2)}) async-start(), calls=%async_computation.9 | async-start | bytes 3276800 | tf_op jit(solution)/shard_map/all_gather | solution.py:62
  48.9 0.8 copy-start.8
  49.7 88.2 %reduce-scatter.3.cloned.1.call-start = ((), (), s32[]{:S(2)}) async-start(), calls=%async_computation.10 | async-start | bytes 3276800 | tf_op jit(solution)/shard_map/reduce_scatter | solution.py:80
  74.1 4.2 %copy-start.7 = (bf16[4096,512]{1,0:T(8,128)(2,1)S(1)}, bf16[4096,512]{1,0:T(8,128)(2,1)}, u32[]{:S(2)}) copy-start(bf16[4096,512]{1,0:T(8,128)(2,1)} %param.11) | copy-start | bytes 12582916
  74.4 6.8 %copy-start.4 = (bf16[4,2,640,512]{3,2,1,0:T(8,128)(2,1)}, bf16[4,2,640,512]{3,2,1,0:T(8,128)(2,1)S(1)}, u32[]{:S(2)}) copy-start(bf16[4,2,640,512]{3,2,1,0:T(8,128)(2,1)S(1)} %copy.50) | copy-start | bytes 15728644
  78.3 2.9 %copy-start.2 = (bf16[4096,512]{1,0:T(8,128)(2,1)S(1)}, bf16[4096,512]{1,0:T(8,128)(2,1)}, u32[]{:S(2)}) copy-start(bf16[4096,512]{1,0:T(8,128)(2,1)} %param.10) | copy-start | bytes 12582916
  81.2 2.9 %copy-start.10 = (f32[640,512]{1,0:T(8,128)}, f32[640,512]{1,0:T(8,128)S(1)}, u32[]{:S(2)}) copy-start(f32[640,512]{1,0:T(8,128)S(1)} %convolution_bitcast_fusion) | copy-start | bytes 3932164
  81.2 4.0 %copy-start.17 = (bf16[512,4096]{1,0:T(8,128)(2,1)S(1)}, bf16[512,4096]{1,0:T(8,128)(2,1)}, u32[]{:S(2)}) copy-start(bf16[512,4096]{1,0:T(8,128)(2,1)} %param.12) | copy-start | bytes 12582916
  84.1 1.1 copy-start.12
  88.3 2.4 %copy-start.6 = (bf16[640,8,512]{2,0,1:T(8,128)(2,1)}, bf16[640,8,512]{2,0,1:T(8,128)(2,1)S(1)}, u32[]{:S(2)}) copy-start(bf16[640,8,512]{2,0,1:T(8,128)(2,1)S(1)} %fusion.8) | copy-start | bytes 15728644
  92.4 5.1 %collective-permute-start = (bf16[4,640,512]{2,1,0:T(8,128)(2,1)}, bf16[4,640,512]{2,1,0:T(8,128)(2,1)S(1)}, u32[]{:S(2)}, u32[]{:S(2)}) collective-permute-start(bf16[4,640,512]{2,1,0:T(8,128)(2,1)} %dynamic-slice_bitcast_fusion.1), channel_id=1, source_target_pairs={{0,1},{1,0},{2,3},{3,2},{4,5},{5,4},{6,7},{7,6},{8,9},{9,8},{10,11... | collective-permute-start | bytes 7864328 | tf_op jit(solution)/shard_map/ppermute | solution.py:76
  101.5 1.7 copy-start.9
  101.5 74.4 %reduce-scatter.5.cloned.1.call-start = ((), (), s32[]{:S(2)}) async-start(), calls=%async_computation.11 | async-start | bytes 3276800 | tf_op jit(solution)/shard_map/reduce_scatter | solution.py:80
  111.6 1.7 copy-start.11
  111.6 3.1 %copy-start.13 = (f32[640,512]{1,0:T(8,128)S(1)}, f32[640,512]{1,0:T(8,128)}, u32[]{:S(2)}) copy-start(f32[640,512]{1,0:T(8,128)} %copy-done.12) | copy-start | bytes 3932164
  111.6 5.0 %copy-start.18 = (bf16[512,4096]{1,0:T(8,128)(2,1)S(1)}, bf16[512,4096]{1,0:T(8,128)(2,1)}, u32[]{:S(2)}) copy-start(bf16[512,4096]{1,0:T(8,128)(2,1)} %param.12) | copy-start | bytes 12582916
  111.9 7.9 %copy-start.5 = (bf16[4,2,640,512]{3,2,1,0:T(8,128)(2,1)}, bf16[4,2,640,512]{3,2,1,0:T(8,128)(2,1)S(1)}, u32[]{:S(2)}) copy-start(bf16[4,2,640,512]{3,2,1,0:T(8,128)(2,1)S(1)} %copy.52) | copy-start | bytes 15728644
  116.6 3.3 %copy-start.3 = (bf16[4096,512]{1,0:T(8,128)(2,1)S(1)}, bf16[4096,512]{1,0:T(8,128)(2,1)}, u32[]{:S(2)}) copy-start(bf16[4096,512]{1,0:T(8,128)(2,1)} %param.10) | copy-start | bytes 12582916
  128.7 5.0 %collective-permute-start.2 = (bf16[4,640,512]{2,1,0:T(8,128)(2,1)S(1)}, bf16[4,640,512]{2,1,0:T(8,128)(2,1)S(1)}, u32[]{:S(2)}, u32[]{:S(2)}) collective-permute-start(bf16[4,640,512]{2,1,0:T(8,128)(2,1)S(1)} %dynamic-slice_bitcast_fusion), channel_id=1, source_target_pairs={{0,1},{1,0},{2,3},{3,2},{4,5},{5,4},{6,7},{7,6},{8,9},{9,8},{10,11... | collective-permute-start | bytes 7864328 | tf_op jit(solution)/shard_map/ppermute | solution.py:76
  138.0 19.9 %all-to-all-start.3 = ((bf16[16,40,512]{2,1,0:T(8,128)(2,1)}), bf16[16,40,512]{2,1,0:T(8,128)(2,1)S(1)}, u32[]{:S(2)}, u32[]{:S(2)}) async-start(bf16[16,40,512]{2,1,0:T(8,128)(2,1)} %bitcast.123), calls=%async_computation.4 | async-start | bytes 1310720 | tf_op jit(solution)/shard_map/all_to_all | solution.py:83
  144.9 13.5 %copy-start.14 = (bf16[128,512]{1,0:T(8,128)(2,1)S(1)}, bf16[128,512]{1,0:T(8,128)(2,1)}, u32[]{:S(2)}) copy-start(bf16[128,512]{1,0:T(8,128)(2,1)} %param.13) | copy-start | bytes 393220
  144.9 13.5 %copy-start.16 = (f32[128]{0:T(128)S(1)}, f32[128]{0:T(128)}, u32[]{:S(2)}) copy-start(f32[128]{0:T(128)} %copy-done.15) | copy-start | bytes 1540
  159.6 7.9 %collective-permute-start.1 = (f32[128,2]{0,1:T(2,128)S(1)}, f32[128,2]{0,1:T(2,128)S(1)}, u32[]{:S(2)}, u32[]{:S(2)}) collective-permute-start(f32[128,2]{0,1:T(2,128)S(1)} %pad_maximum_fusion), channel_id=1, source_target_pairs={{0,1},{1,0},{2,3},{3,2},{4,5},{5,4},{6,7},{7,6},{8,9},{9,8},{10,11... | collective-permute-start | bytes 3080 | tf_op jit(solution)/shard_map/ppermute | solution.py:129
  175.9 18.9 %all-to-all-start.5 = ((bf16[16,40,512]{2,1,0:T(8,128)(2,1)}), bf16[16,40,512]{2,1,0:T(8,128)(2,1)S(1)}, u32[]{:S(2)}, u32[]{:S(2)}) async-start(bf16[16,40,512]{2,1,0:T(8,128)(2,1)} %bitcast.122), calls=%async_computation.7 | async-start | bytes 1310720 | tf_op jit(solution)/shard_map/all_to_all | solution.py:83
  187.3 8.8 %copy-start.1 = (bf16[128,512]{1,0:T(8,128)(2,1)S(1)}, bf16[128,512]{1,0:T(8,128)(2,1)}, u32[]{:S(2)}) copy-start(bf16[128,512]{1,0:T(8,128)(2,1)} %param.7) | copy-start | bytes 393220
Sparse Core Ops, SparseCore 0:
  30.5 33.3 all-gather.3
  65.6 35.2 all-gather.5
  103.9 34.0 reduce-scatter.2
  140.2 33.6 reduce-scatter.4

commit v15 on v14

--- a/solution.py
+++ b/solution.py
@@ -135,9 +135,12 @@
         hidden_grad * up_proj * sigmoid_gate * (1.0 + gate_proj * (1.0 - sigmoid_gate))
     ).astype(jnp.bfloat16)
     up_grad = (hidden_grad * activated).astype(jnp.bfloat16)
-    gate_weight_grad = jnp.einsum(
-        "frd,rh->fdh", expert_rows, gate_grad, preferred_element_type=jnp.float32
-    ).astype(jnp.bfloat16).reshape(fsdp_count * feat, hid)
+    both_grads = jnp.einsum(
+        "frd,rh->fdh", expert_rows, jnp.concatenate([gate_grad, up_grad], axis=1),
+        preferred_element_type=jnp.float32,
+    ).astype(jnp.bfloat16).reshape(fsdp_count * feat, 2 * hid)
+    gate_weight_grad = both_grads[:, :hid]
+    up_weight_grad = both_grads[:, hid:]
     down_weight_grad = jnp.einsum(
         "hr,frd->hfd", hidden.T, grad_rows, preferred_element_type=jnp.float32
     ).astype(jnp.bfloat16).reshape(hid, model)
@@ -148,11 +151,8 @@
         "rh,fdh->frd", up_grad, up_w3, preferred_element_type=jnp.float32
     )
     input_shares = scatter_chips(swap_cores(input_partial))
-    prob_grad, gate_weight_grad, down_weight_grad, input_shares, up_grad_late = lax.optimization_barrier(
-        (prob_grad, gate_weight_grad, down_weight_grad, input_shares, up_grad))
-    up_weight_grad = jnp.einsum(
-        "frd,rh->fdh", expert_rows, up_grad_late, preferred_element_type=jnp.float32
-    ).astype(jnp.bfloat16).reshape(fsdp_count * feat, hid)
+    prob_grad, gate_weight_grad, up_weight_grad, down_weight_grad, input_shares = lax.optimization_barrier(
+        (prob_grad, gate_weight_grad, up_weight_grad, down_weight_grad, input_shares))
     input_slots = to_token_layout(input_shares)
     token_grad = jnp.dot(
         picker.astype(jnp.float32),

time: 204 us -> 212 us (1.039)
  waiting for transfers between devices: 41.8 us -> 48.1 us
  local copies, waits for them, and re-layouts: 28.5 us -> 33.8 us
    all_to_all x2, waiting for transfers between devices: 4.48 us -> 12.7 us  [to_token_layout(): lax.all_to_all(shares.reshape(dp_count, CAP, feat), 'dp', split_axis=0, c...]
    slice x0 -> x1, local copies, waits for them, and re-layouts: none -> 5.93 us  [local(): up_weight_grad = both_grads[:, hid:]]
    dot_general x2 -> x1, matrix products: 15.2 us -> 12.5 us  [local(): jnp.einsum('frd,rh->fdh', expert_rows, jnp.concatenate([gate_grad, up_gra...]
where the time goes in v15:
time: 212 us
  waiting for transfers between devices  48.1 us (23%)
  matrix products  47.9 us (23%)
  blocking collectives  44.2 us (21%)
  local copies, waits for them, and re-layouts  33.8 us (16%)
  starting transfers between devices  15.2 us (7%)
  between operations  14.1 us (7%)
  other arithmetic  8.21 us (4%)
    unnamed x40, local copies, waits for them, and re-layouts  20.6 us
    all_to_all x1, blocking collectives, to_expert_layout(): lax.all_to_all(place_rows(source, scaled), 'dp', split_axis=0, concat_axi...  20.6 us
    all_to_all x2, blocking collectives, join_cores(): lax.all_to_all(jnp.broadcast_to(across[:, None], (chips, cores, rows, fea...  15.9 us
    all_gather x2, waiting for transfers between devices, to_expert_layout(): lax.all_gather(arrived.reshape(rows, feat), 'fy', axis=0, tiled=False)  14.1 us
    all_to_all x2, waiting for transfers between devices, to_token_layout(): lax.all_to_all(shares.reshape(dp_count, CAP, feat), 'dp', split_axis=0, c...  12.7 us
    dot_general x1, matrix products, local(): jnp.einsum('frd,rh->fdh', expert_rows, jnp.concatenate([gate_grad, up_gra...  12.5 us
    all_to_all x1, waiting for transfers between devices, to_expert_layout(): lax.all_to_all(place_rows(source, scaled), 'dp', split_axis=0, concat_axi...  11.7 us
    all_to_all x2, starting transfers between devices, to_token_layout(): lax.all_to_all(shares.reshape(dp_count, CAP, feat), 'dp', split_axis=0, c...  10.6 us
  transfers between devices with their start and end apart: 10, of which 6 were waited for; matrix products, arithmetic and copies ran while one was open for 34% of the time, Pallas kernels for 0%

profile of v15, /device:TPU:0, one launch (start us, length us, event | category | flops | bytes accessed | tf_op | source)
XLA Modules:
  0.0 211.5 jit_solution(11806354082536947233)
XLA Ops:
  9.7 20.6 %all_to_all.30 = bf16[16,40,512]{2,1,0:T(8,128)(2,1)} all-to-all(bf16[16,40,512]{2,1,0:T(8,128)(2,1)S(1)} %bitcast.117), channel_id=1, replica_groups=mesh['dp'=16,'fy'=4,'fc'=2] {'dp'}, dimensions={0} | all-to-all | bytes 1310720 | tf_op jit(solution)/shard_map/all_to_all | solution.py:59
  33.5 3.6 %all-to-all-start.2 = ((bf16[16,40,512]{2,1,0:T(8,128)(2,1)}), bf16[16,40,512]{2,1,0:T(8,128)(2,1)S(1)}, u32[]{:S(2)}, u32[]{:S(2)}) async-start(bf16[16,40,512]{2,1,0:T(8,128)(2,1)} %bitcast.19), calls=%async_computation.2 | async-start | bytes 1310720 | tf_op jit(solution)/shard_map/all_to_all | solution.py:59
  37.2 11.7 %all-to-all-done.2 = bf16[16,40,512]{2,1,0:T(8,128)(2,1)S(1)} async-done(((bf16[16,40,512]{2,1,0:T(8,128)(2,1)}), bf16[16,40,512]{2,1,0:T(8,128)(2,1)S(1)}, u32[]{:S(2)}, u32[]{:S(2)}) %all-to-all-start.2) | async-done | bytes 655392 | tf_op jit(solution)/shard_map/all_to_all | solution.py:59
  49.8 14.1 %all-gather.4.cloned.1.call-done = bf16[4,640,512]{2,1,0:T(8,128)(2,1)} async-done(((bf16[1,640,512]{2,1,0:T(8,128)(2,1)}), bf16[4,640,512]{2,1,0:T(8,128)(2,1)}) %all-gather.4.cloned.1.call-update) | async-done | bytes 2621456 | tf_op jit(solution)/shard_map/all_gather | solution.py:62
  63.9 2.2 %broadcast_in_dim.44 = bf16[4,2,640,512]{3,2,0,1:T(8,128)(2,1)S(1)} broadcast(bf16[4,640,512]{2,1,0:T(8,128)(2,1)} %all-gather.4.cloned.1.call-done), dimensions={0,2,3} | broadcast | bytes 7864320 | tf_op jit(solution)/shard_map/broadcast_in_dim | solution.py:67
  66.1 7.9 %all_to_all.31 = bf16[4,2,640,512]{3,2,0,1:T(8,128)(2,1)S(1)} all-to-all(bf16[4,2,640,512]{3,2,0,1:T(8,128)(2,1)S(1)} %broadcast_in_dim.44), channel_id=1, replica_groups=mesh['dp'=16,'fy'=4,'fc'=2] {'fc'}, dimensions={1} | all-to-all | bytes 10485760 | tf_op jit(solution)/shard_map/all_to_all | solution.py:66
  74.4 3.9 %copy-done.7 = bf16[4096,512]{1,0:T(8,128)(2,1)S(1)} copy-done((bf16[4096,512]{1,0:T(8,128)(2,1)S(1)}, bf16[4096,512]{1,0:T(8,128)(2,1)}, u32[]{:S(2)}) %copy-start.7) | copy-done | bytes 4194328
  78.3 3.5 %convolution_bitcast_fusion = f32[640,512]{0,1:T(8,128)S(1)} fusion(bf16[8,640,512]{2,1,0:T(8,128)(2,1)S(1)} %bitcast.104, bf16[8,512,512]{2,1,0:T(8,128)(2,1)S(1)} %bitcast.112), kind=kOutput, calls=%fused_computation.17 | convolution fusion | flops 2684354560 | bytes 10747904 | tf_op jit(solution)/shard_map/dot_general | solution.py:99
  81.8 3.5 %convolution_bitcast_fusion.1 = f32[640,512]{0,1:T(8,128)S(1)} fusion(bf16[8,640,512]{2,1,0:T(8,128)(2,1)S(1)} %bitcast.105, bf16[8,512,512]{2,1,0:T(8,128)(2,1)S(1)} %bitcast.99), kind=kOutput, calls=%fused_computation.18 | convolution fusion | flops 2684354560 | bytes 10747904 | tf_op jit(solution)/shard_map/dot_general | solution.py:98
  85.7 3.2 %fusion.8 = bf16[640,8,512]{2,0,1:T(8,128)(2,1)S(1)} fusion(bf16[640,512,1]{0,1,2:T(8,128)(2,1)S(1)} %fusion.18, bf16[64,8,8,512]{3,2,1,0:T(8,128)(2,1)S(1)} %bitcast.126), kind=kOutput, calls=%fused_computation.12 | convolution fusion | flops 2686976000 | bytes 10092544 | tf_op jit(solution)/shard_map/rh,hfd->frd/dot_general | solution.py:103
  88.9 2.3 %copy-done.6 = bf16[640,8,512]{2,0,1:T(8,128)(2,1)} copy-done((bf16[640,8,512]{2,0,1:T(8,128)(2,1)}, bf16[640,8,512]{2,0,1:T(8,128)(2,1)S(1)}, u32[]{:S(2)}) %copy-start.6) | copy-done | bytes 5242904
  91.2 1.7 dynamic-slice_bitcast_fusion.1
  93.1 4.9 %collective-permute-done = bf16[4,640,512]{2,1,0:T(8,128)(2,1)S(1)} collective-permute-done((bf16[4,640,512]{2,1,0:T(8,128)(2,1)}, bf16[4,640,512]{2,1,0:T(8,128)(2,1)S(1)}, u32[]{:S(2)}, u32[]{:S(2)}) %collective-permute-start) | collective-permute-done | bytes 2621472 | tf_op jit(solution)/shard_map/ppermute | solution.py:76
  98.0 4.0 %fusion.1 = bf16[4,640,512]{2,1,0:T(8,128)(2,1)} fusion(bf16[4,640,512]{2,1,0:T(8,128)(2,1)S(1)} %collective-permute-done, bf16[4,2,640,512]{3,2,1,0:T(8,128)(2,1)} %bitcast.110, s32[]{:T(128)S(6)} %select_n.16), kind=kLoop, calls=%fused_computation.5 | loop fusion | flops 5242880 | bytes 7864324 | tf_op jit(solution)/shard_map/convert_element_type | solution.py:77
  102.1 1.7 copy-done.9
  104.2 7.9 %all_to_all.32 = bf16[4,2,640,512]{3,2,0,1:T(8,128)(2,1)S(1)} all-to-all(bf16[4,2,640,512]{3,2,0,1:T(8,128)(2,1)S(1)} %broadcast_in_dim.50), channel_id=1, replica_groups=mesh['dp'=16,'fy'=4,'fc'=2] {'fc'}, dimensions={1} | all-to-all | bytes 10485760 | tf_op jit(solution)/shard_map/all_to_all | solution.py:66
  112.5 1.6 copy-done.11
  115.5 1.7 copy-done.18
  117.2 3.7 %multiply_convert_fusion.1 = (bf16[640,512]{0,1:T(8,128)(2,1)S(1)}, bf16[640,512]{0,1:T(8,128)(2,1)S(1)}) fusion(f32[640,512]{0,1:T(8,128)S(1)} %copy-done.13, f32[640,512]{0,1:T(8,128)S(1)} %copy-done.11, bf16[8,640,512]{2,1,0:T(8,128)(2,1)S(1)} %bitcast.107, bf16[64,8,8,512]{3,2,1,0:T(8,128)(2,1)S(1)} %bitcast.127), kind=kOutput, calls=%fused_computation.25 | convolution fusion | flops 2688614400 | bytes 13369344 | tf_op jit(solution)/shard_map/dot_general | solution.py:132
  120.9 3.0 %fusion.20 = f32[640,8,512]{2,0,1:T(8,128)S(1)} fusion(bf16[8,512,512]{2,1,0:T(8,128)(2,1)S(1)} %bitcast.100, bf16[640,512]{0,1:T(8,128)(2,1)S(1)} %get-tuple-element.54), kind=kOutput, calls=%fused_computation.36 | convolution fusion | flops 2684354560 | bytes 15335424 | tf_op jit(solution)/shard_map/rh,fdh->frd/dot_general | solution.py:147
  123.8 5.3 %add_convert_fusion = bf16[640,8,512]{2,0,1:T(8,128)(2,1)S(1)} fusion(f32[640,8,512]{2,0,1:T(8,128)S(1)} %fusion.20, bf16[8,512,512]{2,1,0:T(8,128)(2,1)} %bitcast.111, bf16[640,512]{0,1:T(8,128)(2,1)S(1)} %get-tuple-element.55), kind=kOutput, calls=%fused_computation | convolution fusion | flops 2689597440 | bytes 20578304 | tf_op jit(solution)/shard_map/rh,fdh->frd/dot_general | solution.py:150
  129.9 4.7 %collective-permute-done.2 = bf16[4,640,512]{2,1,0:T(8,128)(2,1)S(1)} collective-permute-done((bf16[4,640,512]{2,1,0:T(8,128)(2,1)S(1)}, bf16[4,640,512]{2,1,0:T(8,128)(2,1)S(1)}, u32[]{:S(2)}, u32[]{:S(2)}) %collective-permute-start.2) | collective-permute-done | bytes 2621472 | tf_op jit(solution)/shard_map/ppermute | solution.py:76
  134.6 2.4 %fusion = bf16[4,640,512]{2,1,0:T(8,128)(2,1)} fusion(bf16[4,640,512]{2,1,0:T(8,128)(2,1)S(1)} %collective-permute-done.2, bf16[4,2,640,512]{3,2,1,0:T(8,128)(2,1)S(1)} %bitcast.98, s32[]{:T(128)S(6)} %select_n.16), kind=kLoop, calls=%fused_computation.3 | loop fusion | flops 5242880 | bytes 7864324 | tf_op jit(solution)/shard_map/convert_element_type | solution.py:77
  137.0 12.5 %convolution_convert_fusion = bf16[8,512,1024]{2,1,0:T(8,128)(2,1)} fusion(bf16[8,640,512]{2,1,0:T(8,128)(2,1)} %bitcast.106, bf16[640,512]{0,1:T(8,128)(2,1)S(1)} %get-tuple-element.55, bf16[640,512]{0,1:T(8,128)(2,1)S(1)} %get-tuple-element.54), kind=kOutput, calls=%fused_computation.1 | convolution fusion | flops 5375524864 | bytes 14942208 | tf_op jit(solution)/shard_map/frd,rh->fdh/dot_general | solution.py:138
  149.5 7.0 %all-to-all-start.3 = ((bf16[16,40,512]{2,1,0:T(8,128)(2,1)}), bf16[16,40,512]{2,1,0:T(8,128)(2,1)S(1)}, u32[]{:S(2)}, u32[]{:S(2)}) async-start(bf16[16,40,512]{2,1,0:T(8,128)(2,1)} %bitcast.120), calls=%async_computation.4 | async-start | bytes 1310720 | tf_op jit(solution)/shard_map/all_to_all | solution.py:83
  156.5 5.9 %fusion.47 = (bf16[4096,512]{1,0:T(8,128)(2,1)}, bf16[4096,512]{1,0:T(8,128)(2,1)}) fusion(bf16[4096,1024]{1,0:T(8,128)(2,1)} %bitcast.101), kind=kLoop, calls=%fused_computation.76 | loop fusion | bytes 16777216 | tf_op jit(solution)/shard_map/slice | solution.py:143
  162.4 7.3 %all-to-all-done.3 = bf16[16,40,512]{2,1,0:T(8,128)(2,1)S(1)} async-done(((bf16[16,40,512]{2,1,0:T(8,128)(2,1)}), bf16[16,40,512]{2,1,0:T(8,128)(2,1)S(1)}, u32[]{:S(2)}, u32[]{:S(2)}) %all-to-all-start.3) | async-done | bytes 655392 | tf_op jit(solution)/shard_map/all_to_all | solution.py:83
  171.6 8.6 %convolution_convert_fusion.1 = bf16[512,8,512]{0,2,1:T(8,128)(2,1)} fusion(bf16[640,512,1]{0,1,2:T(8,128)(2,1)S(1)} %fusion.18, bf16[8,640,512]{2,1,0:T(8,128)(2,1)} %bitcast.108), kind=kOutput, calls=%fused_computation.13 | convolution fusion | flops 2686451712 | bytes 10092544 | tf_op jit(solution)/shard_map/hr,frd->hfd/dot_general | solution.py:144
  180.1 7.7 %all-gather = f32[512,2]{0,1:T(2,128)S(1)} all-gather(f32[128,2]{0,1:T(2,128)S(1)} %fusion.46), channel_id=2, replica_groups=mesh['dp'=16,'fy'=4,'fc'=2] {'fy'}, dimensions={0}, use_global_device_ids=true | all-gather | bytes 5120 | tf_op jit(solution)/shard_map/all_gather | solution.py:130
  188.4 3.6 %all-to-all-start.5 = ((bf16[16,40,512]{2,1,0:T(8,128)(2,1)}), bf16[16,40,512]{2,1,0:T(8,128)(2,1)S(1)}, u32[]{:S(2)}, u32[]{:S(2)}) async-start(bf16[16,40,512]{2,1,0:T(8,128)(2,1)} %bitcast.119), calls=%async_computation.7 | async-start | bytes 1310720 | tf_op jit(solution)/shard_map/all_to_all | solution.py:83
  192.0 6.4 %copy.87 = bf16[512,4096]{1,0:T(8,128)(2,1)} copy(bf16[512,4096]{0,1:T(8,128)(2,1)} %bitcast.113) | data formatting | bytes 8388608
  198.4 5.4 %all-to-all-done.5 = bf16[16,40,512]{2,1,0:T(8,128)(2,1)S(1)} async-done(((bf16[16,40,512]{2,1,0:T(8,128)(2,1)}), bf16[16,40,512]{2,1,0:T(8,128)(2,1)S(1)}, u32[]{:S(2)}, u32[]{:S(2)}) %all-to-all-start.5) | async-done | bytes 655392 | tf_op jit(solution)/shard_map/all_to_all | solution.py:83
  (75 shorter events, 14.2 us)
Async XLA Ops:
  7.2 2.2 %copy-start = (bf16[128,512]{1,0:T(8,128)(2,1)S(1)}, bf16[128,512]{1,0:T(8,128)(2,1)}, u32[]{:S(2)}) copy-start(bf16[128,512]{1,0:T(8,128)(2,1)} %param.7) | copy-start | bytes 393220
  7.2 56.7 %all-gather.4.cloned.1.call-start = ((), (), s32[]{:S(2)}) async-start(), calls=%async_computation.8 | async-start | bytes 3276800 | tf_op jit(solution)/shard_map/all_gather | solution.py:62
  31.1 35.0 %copy-start.15 = (f32[128]{0:T(128)}, f32[128]{0:T(128)S(1)}, u32[]{:S(2)}) copy-start(f32[128]{0:T(128)S(1)} %get-tuple-element.58) | copy-start | bytes 1540
  33.5 15.4 %all-to-all-start.2 = ((bf16[16,40,512]{2,1,0:T(8,128)(2,1)}), bf16[16,40,512]{2,1,0:T(8,128)(2,1)S(1)}, u32[]{:S(2)}, u32[]{:S(2)}) async-start(bf16[16,40,512]{2,1,0:T(8,128)(2,1)} %bitcast.19), calls=%async_computation.2 | async-start | bytes 1310720 | tf_op jit(solution)/shard_map/all_to_all | solution.py:59
  37.2 64.8 %all-gather.6.cloned.1.call-start = ((), (), s32[]{:S(2)}) async-start(), calls=%async_computation.9 | async-start | bytes 3276800 | tf_op jit(solution)/shard_map/all_gather | solution.py:62
  48.9 0.8 copy-start.8
  49.7 99.8 %reduce-scatter.3.cloned.1.call-start = ((), (), s32[]{:S(2)}) async-start(), calls=%async_computation.10 | async-start | bytes 3276800 | tf_op jit(solution)/shard_map/reduce_scatter | solution.py:80
  74.1 4.2 %copy-start.7 = (bf16[4096,512]{1,0:T(8,128)(2,1)S(1)}, bf16[4096,512]{1,0:T(8,128)(2,1)}, u32[]{:S(2)}) copy-start(bf16[4096,512]{1,0:T(8,128)(2,1)} %param.11) | copy-start | bytes 12582916
  74.4 7.3 %copy-start.4 = (bf16[4,2,640,512]{3,2,1,0:T(8,128)(2,1)}, bf16[4,2,640,512]{3,2,1,0:T(8,128)(2,1)S(1)}, u32[]{:S(2)}) copy-start(bf16[4,2,640,512]{3,2,1,0:T(8,128)(2,1)S(1)} %copy.74) | copy-start | bytes 15728644
  78.3 3.5 %copy-start.2 = (bf16[4096,512]{1,0:T(8,128)(2,1)S(1)}, bf16[4096,512]{1,0:T(8,128)(2,1)}, u32[]{:S(2)}) copy-start(bf16[4096,512]{1,0:T(8,128)(2,1)} %param.10) | copy-start | bytes 12582916
  81.8 3.5 %copy-start.10 = (f32[640,512]{0,1:T(8,128)}, f32[640,512]{0,1:T(8,128)S(1)}, u32[]{:S(2)}) copy-start(f32[640,512]{0,1:T(8,128)S(1)} %convolution_bitcast_fusion) | copy-start | bytes 3932164
  81.8 3.9 %copy-start.17 = (bf16[512,4096]{1,0:T(8,128)(2,1)S(1)}, bf16[512,4096]{1,0:T(8,128)(2,1)}, u32[]{:S(2)}) copy-start(bf16[512,4096]{1,0:T(8,128)(2,1)} %param.12) | copy-start | bytes 12582916
  85.3 3.6 %copy-start.12 = (f32[640,512]{0,1:T(8,128)}, f32[640,512]{0,1:T(8,128)S(1)}, u32[]{:S(2)}) copy-start(f32[640,512]{0,1:T(8,128)S(1)} %convolution_bitcast_fusion.1) | copy-start | bytes 3932164
  88.9 2.3 %copy-start.6 = (bf16[640,8,512]{2,0,1:T(8,128)(2,1)}, bf16[640,8,512]{2,0,1:T(8,128)(2,1)S(1)}, u32[]{:S(2)}) copy-start(bf16[640,8,512]{2,0,1:T(8,128)(2,1)S(1)} %fusion.8) | copy-start | bytes 15728644
  92.9 5.1 %collective-permute-start = (bf16[4,640,512]{2,1,0:T(8,128)(2,1)}, bf16[4,640,512]{2,1,0:T(8,128)(2,1)S(1)}, u32[]{:S(2)}, u32[]{:S(2)}) collective-permute-start(bf16[4,640,512]{2,1,0:T(8,128)(2,1)} %dynamic-slice_bitcast_fusion.1), channel_id=1, source_target_pairs={{0,1},{1,0},{2,3},{3,2},{4,5},{5,4},{6,7},{7,6},{8,9},{9,8},{10,11... | collective-permute-start | bytes 7864328 | tf_op jit(solution)/shard_map/ppermute | solution.py:76
  102.0 1.7 copy-start.9
  102.0 86.4 %reduce-scatter.5.cloned.1.call-start = ((), (), s32[]{:S(2)}) async-start(), calls=%async_computation.11 | async-start | bytes 3276800 | tf_op jit(solution)/shard_map/reduce_scatter | solution.py:80
  112.1 2.0 copy-start.11
  112.1 3.4 %copy-start.13 = (f32[640,512]{0,1:T(8,128)S(1)}, f32[640,512]{0,1:T(8,128)}, u32[]{:S(2)}) copy-start(f32[640,512]{0,1:T(8,128)} %copy-done.12) | copy-start | bytes 3932164
  112.1 5.1 %copy-start.18 = (bf16[512,4096]{1,0:T(8,128)(2,1)S(1)}, bf16[512,4096]{1,0:T(8,128)(2,1)}, u32[]{:S(2)}) copy-start(bf16[512,4096]{1,0:T(8,128)(2,1)} %param.12) | copy-start | bytes 12582916
  112.5 8.4 %copy-start.5 = (bf16[4,2,640,512]{3,2,1,0:T(8,128)(2,1)}, bf16[4,2,640,512]{3,2,1,0:T(8,128)(2,1)S(1)}, u32[]{:S(2)}) copy-start(bf16[4,2,640,512]{3,2,1,0:T(8,128)(2,1)S(1)} %copy.79) | copy-start | bytes 15728644
  117.2 3.7 %copy-start.3 = (bf16[4096,512]{1,0:T(8,128)(2,1)S(1)}, bf16[4096,512]{1,0:T(8,128)(2,1)}, u32[]{:S(2)}) copy-start(bf16[4096,512]{1,0:T(8,128)(2,1)} %param.10) | copy-start | bytes 12582916
  129.3 5.2 %collective-permute-start.2 = (bf16[4,640,512]{2,1,0:T(8,128)(2,1)S(1)}, bf16[4,640,512]{2,1,0:T(8,128)(2,1)S(1)}, u32[]{:S(2)}, u32[]{:S(2)}) collective-permute-start(bf16[4,640,512]{2,1,0:T(8,128)(2,1)S(1)} %dynamic-slice_bitcast_fusion), channel_id=1, source_target_pairs={{0,1},{1,0},{2,3},{3,2},{4,5},{5,4},{6,7},{7,6},{8,9},{9,8},{10,11... | collective-permute-start | bytes 7864328 | tf_op jit(solution)/shard_map/ppermute | solution.py:76
  149.5 20.3 %all-to-all-start.3 = ((bf16[16,40,512]{2,1,0:T(8,128)(2,1)}), bf16[16,40,512]{2,1,0:T(8,128)(2,1)S(1)}, u32[]{:S(2)}, u32[]{:S(2)}) async-start(bf16[16,40,512]{2,1,0:T(8,128)(2,1)} %bitcast.120), calls=%async_computation.4 | async-start | bytes 1310720 | tf_op jit(solution)/shard_map/all_to_all | solution.py:83
  156.5 13.9 %copy-start.14 = (bf16[128,512]{1,0:T(8,128)(2,1)S(1)}, bf16[128,512]{1,0:T(8,128)(2,1)}, u32[]{:S(2)}) copy-start(bf16[128,512]{1,0:T(8,128)(2,1)} %param.13) | copy-start | bytes 393220
  156.5 13.9 %copy-start.16 = (f32[128]{0:T(128)S(1)}, f32[128]{0:T(128)}, u32[]{:S(2)}) copy-start(f32[128]{0:T(128)} %copy-done.15) | copy-start | bytes 1540
  171.5 8.7 %collective-permute-start.1 = (f32[128,2]{0,1:T(2,128)S(1)}, f32[128,2]{0,1:T(2,128)S(1)}, u32[]{:S(2)}, u32[]{:S(2)}) collective-permute-start(f32[128,2]{0,1:T(2,128)S(1)} %pad_maximum_fusion), channel_id=1, source_target_pairs={{0,1},{1,0},{2,3},{3,2},{4,5},{5,4},{6,7},{7,6},{8,9},{9,8},{10,11... | collective-permute-start | bytes 3080 | tf_op jit(solution)/shard_map/ppermute | solution.py:129
  188.4 15.3 %all-to-all-start.5 = ((bf16[16,40,512]{2,1,0:T(8,128)(2,1)}), bf16[16,40,512]{2,1,0:T(8,128)(2,1)S(1)}, u32[]{:S(2)}, u32[]{:S(2)}) async-start(bf16[16,40,512]{2,1,0:T(8,128)(2,1)} %bitcast.119), calls=%async_computation.7 | async-start | bytes 1310720 | tf_op jit(solution)/shard_map/all_to_all | solution.py:83
  192.0 13.0 %copy-start.1 = (bf16[128,512]{1,0:T(8,128)(2,1)S(1)}, bf16[128,512]{1,0:T(8,128)(2,1)}, u32[]{:S(2)}) copy-start(bf16[128,512]{1,0:T(8,128)(2,1)} %param.7) | copy-start | bytes 393220
Sparse Core Ops, SparseCore 0:
  30.5 33.3 all-gather.3
  65.6 35.2 all-gather.5
  103.9 34.0 reduce-scatter.2
  140.2 33.6 reduce-scatter.4

commit v16 on v14

--- a/solution.py
+++ b/solution.py
@@ -106,18 +106,8 @@
     grad_across = to_expert_layout(out_grad, True)
     out_within, grad_across = lax.optimization_barrier((swap_cores(out_partial), grad_across))
     out_slots = to_token_layout(scatter_chips(out_within))
-    first_pair = jnp.dot(
-        select_first.astype(jnp.float32),
-        out_slots,
-        precision=lax.Precision.HIGHEST,
-        preferred_element_type=jnp.float32,
-    )
-    second_pair = jnp.dot(
-        select_second.astype(jnp.float32),
-        out_slots,
-        precision=lax.Precision.HIGHEST,
-        preferred_element_type=jnp.float32,
-    )
+    first_pair = jnp.take(out_slots, slot_of[:, 0], axis=0, mode="clip")
+    second_pair = jnp.take(out_slots, slot_of[:, 1], axis=0, mode="clip")
     mixed = (route_probs[:, 0:1] * first_pair + route_probs[:, 1:2] * second_pair).astype(
         jnp.bfloat16
     )
@@ -154,12 +144,8 @@
         "frd,rh->fdh", expert_rows, up_grad_late, preferred_element_type=jnp.float32
     ).astype(jnp.bfloat16).reshape(fsdp_count * feat, hid)
     input_slots = to_token_layout(input_shares)
-    token_grad = jnp.dot(
-        picker.astype(jnp.float32),
-        input_slots,
-        precision=lax.Precision.HIGHEST,
-        preferred_element_type=jnp.float32,
-    ).astype(jnp.bfloat16)
+    token_grad = (jnp.take(input_slots, slot_of[:, 0], axis=0, mode="clip")
+                  + jnp.take(input_slots, slot_of[:, 1], axis=0, mode="clip")).astype(jnp.bfloat16)
     return (mixed, token_grad, prob_grad, gate_weight_grad, up_weight_grad, down_weight_grad)
 
 

time: 204 us -> 205 us (level)
  local copies, waits for them, and re-layouts: 28.5 us -> 31.5 us
  matrix products: 49.1 us -> 46.4 us
    gather x0 -> x4, local copies, waits for them, and re-layouts: none -> 3.03 us  [the longest x1 0.76 us: local(): second_pair = jnp.take(out_slots, slot_of[:, 1], axis=0, mode='clip')]
    dot_general x3 -> x0, matrix products: 2.72 us -> none  [the longest x1 1.14 us: local(): jnp.dot(select_first.astype(jnp.float32), out_slots, precision=lax.Precis...]
where the time goes in v16:
time: 205 us; the launch traced here: 204 us
  matrix products  46.4 us (23%)
  blocking collectives  44.3 us (22%)
  waiting for transfers between devices  41.9 us (20%)
  local copies, waits for them, and re-layouts  31.5 us (15%)
  starting transfers between devices  15.7 us (8%)
  between operations  14.1 us (7%)
  other arithmetic  9.83 us (5%)
    unnamed x40, local copies, waits for them, and re-layouts  21.3 us
    all_to_all x1, blocking collectives, to_expert_layout(): lax.all_to_all(place_rows(source, scaled), 'dp', split_axis=0, concat_axi...  20.6 us
    all_to_all x2, blocking collectives, join_cores(): lax.all_to_all(jnp.broadcast_to(across[:, None], (chips, cores, rows, fea...  15.9 us
    all_gather x2, waiting for transfers between devices, to_expert_layout(): lax.all_gather(arrived.reshape(rows, feat), 'fy', axis=0, tiled=False)  14.1 us
    all_to_all x1, waiting for transfers between devices, to_expert_layout(): lax.all_to_all(place_rows(source, scaled), 'dp', split_axis=0, concat_axi...  11.7 us
    all_to_all x2, starting transfers between devices, to_token_layout(): lax.all_to_all(shares.reshape(dp_count, CAP, feat), 'dp', split_axis=0, c...  11.4 us
    ppermute x2, waiting for transfers between devices, swap_cores(): lax.ppermute(sent, 'fc', swap).astype(jnp.float32)  9.68 us
    dot_general x1, matrix products, local(): jnp.einsum('hr,frd->hfd', hidden.T, grad_rows, preferred_element_type=jnp...  8.41 us
  transfers between devices with their start and end apart: 10, of which 6 were waited for; matrix products, arithmetic and copies ran while one was open for 34% of the time, Pallas kernels for 0%

profile of v16, /device:TPU:0, one launch (start us, length us, event | category | flops | bytes accessed | tf_op | source)
XLA Modules:
  0.0 203.7 jit_solution(11138676409846630844)
XLA Ops:
  9.7 20.6 %all_to_all.30 = bf16[16,40,512]{2,1,0:T(8,128)(2,1)} all-to-all(bf16[16,40,512]{2,1,0:T(8,128)(2,1)S(1)} %bitcast.118), channel_id=1, replica_groups=mesh['dp'=16,'fy'=4,'fc'=2] {'dp'}, dimensions={0} | all-to-all | bytes 1310720 | tf_op jit(solution)/shard_map/all_to_all | solution.py:59
  31.1 1.5 convolution_convert_fusion.3
  33.5 3.6 %all-to-all-start.2 = ((bf16[16,40,512]{2,1,0:T(8,128)(2,1)}), bf16[16,40,512]{2,1,0:T(8,128)(2,1)S(1)}, u32[]{:S(2)}, u32[]{:S(2)}) async-start(bf16[16,40,512]{2,1,0:T(8,128)(2,1)} %bitcast.19), calls=%async_computation.2 | async-start | bytes 1310720 | tf_op jit(solution)/shard_map/all_to_all | solution.py:59
  37.2 11.7 %all-to-all-done.2 = bf16[16,40,512]{2,1,0:T(8,128)(2,1)S(1)} async-done(((bf16[16,40,512]{2,1,0:T(8,128)(2,1)}), bf16[16,40,512]{2,1,0:T(8,128)(2,1)S(1)}, u32[]{:S(2)}, u32[]{:S(2)}) %all-to-all-start.2) | async-done | bytes 655392 | tf_op jit(solution)/shard_map/all_to_all | solution.py:59
  49.8 14.1 %all-gather.4.cloned.1.call-done = bf16[4,640,512]{2,1,0:T(8,128)(2,1)} async-done(((bf16[1,640,512]{2,1,0:T(8,128)(2,1)}), bf16[4,640,512]{2,1,0:T(8,128)(2,1)}) %all-gather.4.cloned.1.call-update) | async-done | bytes 2621456 | tf_op jit(solution)/shard_map/all_gather | solution.py:62
  63.9 2.2 %broadcast_in_dim.49 = bf16[4,2,640,512]{3,2,0,1:T(8,128)(2,1)S(1)} broadcast(bf16[4,640,512]{2,1,0:T(8,128)(2,1)} %all-gather.4.cloned.1.call-done), dimensions={0,2,3} | broadcast | bytes 7864320 | tf_op jit(solution)/shard_map/broadcast_in_dim | solution.py:67
  66.1 7.9 %all_to_all.31 = bf16[4,2,640,512]{3,2,0,1:T(8,128)(2,1)S(1)} all-to-all(bf16[4,2,640,512]{3,2,0,1:T(8,128)(2,1)S(1)} %broadcast_in_dim.49), channel_id=1, replica_groups=mesh['dp'=16,'fy'=4,'fc'=2] {'fc'}, dimensions={1} | all-to-all | bytes 10485760 | tf_op jit(solution)/shard_map/all_to_all | solution.py:66
  74.4 3.9 %copy-done.7 = bf16[4096,512]{1,0:T(8,128)(2,1)S(1)} copy-done((bf16[4096,512]{1,0:T(8,128)(2,1)S(1)}, bf16[4096,512]{1,0:T(8,128)(2,1)}, u32[]{:S(2)}) %copy-start.7) | copy-done | bytes 4194328
  78.3 2.9 %convolution_bitcast_fusion = f32[640,512]{1,0:T(8,128)S(1)} fusion(bf16[8,640,512]{2,1,0:T(8,128)(2,1)S(1)} %bitcast.105, bf16[8,512,512]{2,1,0:T(8,128)(2,1)S(1)} %bitcast.114), kind=kOutput, calls=%fused_computation.22 | convolution fusion | flops 2684354560 | bytes 10747904 | tf_op jit(solution)/shard_map/dot_general | solution.py:99
  81.2 2.9 %convolution_bitcast_fusion.1 = f32[640,512]{1,0:T(8,128)S(1)} fusion(bf16[8,640,512]{2,1,0:T(8,128)(2,1)S(1)} %bitcast.106, bf16[8,512,512]{2,1,0:T(8,128)(2,1)S(1)} %bitcast.103), kind=kOutput, calls=%fused_computation.23 | convolution fusion | flops 2684354560 | bytes 10747904 | tf_op jit(solution)/shard_map/dot_general | solution.py:98
  85.1 3.2 %fusion.8 = bf16[640,8,512]{2,0,1:T(8,128)(2,1)S(1)} fusion(bf16[640,512,1]{1,0,2:T(8,128)(2,1)S(1)} %fusion.16, bf16[64,8,8,512]{3,2,1,0:T(8,128)(2,1)S(1)} %bitcast.127), kind=kOutput, calls=%fused_computation.15 | convolution fusion | flops 2686976000 | bytes 10092544 | tf_op jit(solution)/shard_map/rh,hfd->frd/dot_general | solution.py:103
  88.3 2.4 %copy-done.6 = bf16[640,8,512]{2,0,1:T(8,128)(2,1)} copy-done((bf16[640,8,512]{2,0,1:T(8,128)(2,1)}, bf16[640,8,512]{2,0,1:T(8,128)(2,1)S(1)}, u32[]{:S(2)}) %copy-start.6) | copy-done | bytes 5242904
  90.7 1.7 dynamic-slice_bitcast_fusion.1
  92.5 5.0 %collective-permute-done = bf16[4,640,512]{2,1,0:T(8,128)(2,1)S(1)} collective-permute-done((bf16[4,640,512]{2,1,0:T(8,128)(2,1)}, bf16[4,640,512]{2,1,0:T(8,128)(2,1)S(1)}, u32[]{:S(2)}, u32[]{:S(2)}) %collective-permute-start) | collective-permute-done | bytes 2621472 | tf_op jit(solution)/shard_map/ppermute | solution.py:76
  97.5 4.0 %fusion.1 = bf16[4,640,512]{2,1,0:T(8,128)(2,1)} fusion(bf16[4,640,512]{2,1,0:T(8,128)(2,1)S(1)} %collective-permute-done, bf16[4,2,640,512]{3,2,1,0:T(8,128)(2,1)} %bitcast.112, s32[]{:T(128)S(6)} %select_n.16), kind=kLoop, calls=%fused_computation.8 | loop fusion | flops 5242880 | bytes 7864324 | tf_op jit(solution)/shard_map/convert_element_type | solution.py:77
  101.5 1.7 copy-done.9
  103.7 7.9 %all_to_all.32 = bf16[4,2,640,512]{3,2,0,1:T(8,128)(2,1)S(1)} all-to-all(bf16[4,2,640,512]{3,2,0,1:T(8,128)(2,1)S(1)} %broadcast_in_dim.55), channel_id=1, replica_groups=mesh['dp'=16,'fy'=4,'fc'=2] {'fc'}, dimensions={1} | all-to-all | bytes 10485760 | tf_op jit(solution)/shard_map/all_to_all | solution.py:66
  114.8 1.8 copy-done.18
  116.6 3.3 %multiply_convert_fusion = (bf16[640,512]{1,0:T(8,128)(2,1)S(1)}, bf16[640,512]{1,0:T(8,128)(2,1)S(1)}) fusion(f32[640,512]{1,0:T(8,128)S(1)} %copy-done.13, f32[640,512]{1,0:T(8,128)S(1)} %copy-done.11, bf16[8,640,512]{2,1,0:T(8,128)(2,1)S(1)} %bitcast.109, bf16[64,8,8,512]{3,2,1,0:T(8,128)(2,1)S(1)} %bitcast.128), kind=kOutput, calls=%fused_computation.26 | convolution fusion | flops 2688614400 | bytes 13369344 | tf_op jit(solution)/shard_map/dot_general | solution.py:122
  119.9 3.0 %fusion.19 = f32[640,8,512]{2,0,1:T(8,128)S(1)} fusion(bf16[8,512,512]{2,1,0:T(8,128)(2,1)S(1)} %bitcast.104, bf16[640,512]{1,0:T(8,128)(2,1)S(1)} %get-tuple-element.53), kind=kOutput, calls=%fused_computation.38 | convolution fusion | flops 2684354560 | bytes 15335424 | tf_op jit(solution)/shard_map/rh,fdh->frd/dot_general | solution.py:134
  122.9 5.6 %add_convert_fusion = bf16[640,8,512]{2,0,1:T(8,128)(2,1)S(1)} fusion(f32[640,8,512]{2,0,1:T(8,128)S(1)} %fusion.19, bf16[8,512,512]{2,1,0:T(8,128)(2,1)} %bitcast.113, bf16[640,512]{1,0:T(8,128)(2,1)S(1)} %get-tuple-element.18), kind=kOutput, calls=%fused_computation.4 | convolution fusion | flops 2689597440 | bytes 20578304 | tf_op jit(solution)/shard_map/rh,fdh->frd/dot_general | solution.py:137
  129.0 4.7 %collective-permute-done.2 = bf16[4,640,512]{2,1,0:T(8,128)(2,1)S(1)} collective-permute-done((bf16[4,640,512]{2,1,0:T(8,128)(2,1)S(1)}, bf16[4,640,512]{2,1,0:T(8,128)(2,1)S(1)}, u32[]{:S(2)}, u32[]{:S(2)}) %collective-permute-start.2) | collective-permute-done | bytes 2621472 | tf_op jit(solution)/shard_map/ppermute | solution.py:76
  133.7 2.4 %fusion = bf16[4,640,512]{2,1,0:T(8,128)(2,1)} fusion(bf16[4,640,512]{2,1,0:T(8,128)(2,1)S(1)} %collective-permute-done.2, bf16[4,2,640,512]{3,2,1,0:T(8,128)(2,1)S(1)} %bitcast.102, s32[]{:T(128)S(6)} %select_n.16), kind=kLoop, calls=%fused_computation.6 | loop fusion | flops 5242880 | bytes 7864324 | tf_op jit(solution)/shard_map/convert_element_type | solution.py:77
  136.2 1.8 reduce-scatter.3.cloned.1.call-done
  138.0 6.9 %all-to-all-start.3 = ((bf16[16,40,512]{2,1,0:T(8,128)(2,1)}), bf16[16,40,512]{2,1,0:T(8,128)(2,1)S(1)}, u32[]{:S(2)}, u32[]{:S(2)}) async-start(bf16[16,40,512]{2,1,0:T(8,128)(2,1)} %bitcast.121), calls=%async_computation.4 | async-start | bytes 1310720 | tf_op jit(solution)/shard_map/all_to_all | solution.py:83
  144.9 8.4 %convolution_convert_fusion.1 = bf16[512,8,512]{0,2,1:T(8,128)(2,1)} fusion(bf16[640,512,1]{1,0,2:T(8,128)(2,1)S(1)} %fusion.16, bf16[8,640,512]{2,1,0:T(8,128)(2,1)} %bitcast.110), kind=kOutput, calls=%fused_computation.17 | convolution fusion | flops 2686451712 | bytes 10092544 | tf_op jit(solution)/shard_map/hr,frd->hfd/dot_general | solution.py:131
  153.4 4.5 %all-to-all-done.3 = bf16[16,40,512]{2,1,0:T(8,128)(2,1)S(1)} async-done(((bf16[16,40,512]{2,1,0:T(8,128)(2,1)}), bf16[16,40,512]{2,1,0:T(8,128)(2,1)S(1)}, u32[]{:S(2)}, u32[]{:S(2)}) %all-to-all-start.3) | async-done | bytes 655392 | tf_op jit(solution)/shard_map/all_to_all | solution.py:83
  160.5 7.6 %convolution_convert_fusion.2 = bf16[8,512,512]{2,1,0:T(8,128)(2,1)} fusion(bf16[8,640,512]{2,1,0:T(8,128)(2,1)} %bitcast.107, bf16[640,512]{1,0:T(8,128)(2,1)S(1)} %get-tuple-element.53), kind=kOutput, calls=%fused_computation.18 | convolution fusion | flops 2686451712 | bytes 10092544 | tf_op jit(solution)/shard_map/frd,rh->fdh/dot_general | solution.py:128
  168.1 7.8 %all-gather = f32[512,2]{0,1:T(2,128)S(1)} all-gather(f32[128,2]{0,1:T(2,128)S(1)} %fusion.38), channel_id=2, replica_groups=mesh['dp'=16,'fy'=4,'fc'=2] {'fy'}, dimensions={0}, use_global_device_ids=true | all-gather | bytes 5120 | tf_op jit(solution)/shard_map/all_gather | solution.py:120
  176.5 4.5 %all-to-all-start.5 = ((bf16[16,40,512]{2,1,0:T(8,128)(2,1)}), bf16[16,40,512]{2,1,0:T(8,128)(2,1)S(1)}, u32[]{:S(2)}, u32[]{:S(2)}) async-start(bf16[16,40,512]{2,1,0:T(8,128)(2,1)} %bitcast.120), calls=%async_computation.7 | async-start | bytes 1310720 | tf_op jit(solution)/shard_map/all_to_all | solution.py:83
  180.9 6.3 %copy.57 = bf16[512,4096]{1,0:T(8,128)(2,1)} copy(bf16[512,4096]{0,1:T(8,128)(2,1)} %bitcast.115) | data formatting | bytes 8388608
  187.3 7.6 %convolution_convert_fusion = bf16[8,512,512]{2,1,0:T(8,128)(2,1)} fusion(bf16[8,640,512]{2,1,0:T(8,128)(2,1)} %bitcast.108, bf16[640,512]{1,0:T(8,128)(2,1)S(1)} %get-tuple-element.18), kind=kOutput, calls=%fused_computation.16 | convolution fusion | flops 2686451712 | bytes 10092544 | tf_op jit(solution)/shard_map/frd,rh->fdh/dot_general | solution.py:143
  (79 shorter events, 16.3 us)
Async XLA Ops:
  7.2 2.2 %copy-start = (bf16[128,512]{1,0:T(8,128)(2,1)S(1)}, bf16[128,512]{1,0:T(8,128)(2,1)}, u32[]{:S(2)}) copy-start(bf16[128,512]{1,0:T(8,128)(2,1)} %param.7) | copy-start | bytes 393220
  7.2 56.7 %all-gather.4.cloned.1.call-start = ((), (), s32[]{:S(2)}) async-start(), calls=%async_computation.8 | async-start | bytes 3276800 | tf_op jit(solution)/shard_map/all_gather | solution.py:62
  31.1 35.0 %copy-start.15 = (f32[128]{0:T(128)}, f32[128]{0:T(128)S(1)}, u32[]{:S(2)}) copy-start(f32[128]{0:T(128)S(1)} %get-tuple-element.56) | copy-start | bytes 1540
  33.5 15.4 %all-to-all-start.2 = ((bf16[16,40,512]{2,1,0:T(8,128)(2,1)}), bf16[16,40,512]{2,1,0:T(8,128)(2,1)S(1)}, u32[]{:S(2)}, u32[]{:S(2)}) async-start(bf16[16,40,512]{2,1,0:T(8,128)(2,1)} %bitcast.19), calls=%async_computation.2 | async-start | bytes 1310720 | tf_op jit(solution)/shard_map/all_to_all | solution.py:59
  37.2 64.3 %all-gather.6.cloned.1.call-start = ((), (), s32[]{:S(2)}) async-start(), calls=%async_computation.9 | async-start | bytes 3276800 | tf_op jit(solution)/shard_map/all_gather | solution.py:62
  48.9 0.8 copy-start.8
  49.7 88.2 %reduce-scatter.3.cloned.1.call-start = ((), (), s32[]{:S(2)}) async-start(), calls=%async_computation.10 | async-start | bytes 3276800 | tf_op jit(solution)/shard_map/reduce_scatter | solution.py:80
  74.1 4.2 %copy-start.7 = (bf16[4096,512]{1,0:T(8,128)(2,1)S(1)}, bf16[4096,512]{1,0:T(8,128)(2,1)}, u32[]{:S(2)}) copy-start(bf16[4096,512]{1,0:T(8,128)(2,1)} %param.11) | copy-start | bytes 12582916
  74.4 6.8 %copy-start.4 = (bf16[4,2,640,512]{3,2,1,0:T(8,128)(2,1)}, bf16[4,2,640,512]{3,2,1,0:T(8,128)(2,1)S(1)}, u32[]{:S(2)}) copy-start(bf16[4,2,640,512]{3,2,1,0:T(8,128)(2,1)S(1)} %copy.50) | copy-start | bytes 15728644
  78.3 2.9 %copy-start.2 = (bf16[4096,512]{1,0:T(8,128)(2,1)S(1)}, bf16[4096,512]{1,0:T(8,128)(2,1)}, u32[]{:S(2)}) copy-start(bf16[4096,512]{1,0:T(8,128)(2,1)} %param.10) | copy-start | bytes 12582916
  81.2 2.9 %copy-start.10 = (f32[640,512]{1,0:T(8,128)}, f32[640,512]{1,0:T(8,128)S(1)}, u32[]{:S(2)}) copy-start(f32[640,512]{1,0:T(8,128)S(1)} %convolution_bitcast_fusion) | copy-start | bytes 3932164
  81.2 4.0 %copy-start.17 = (bf16[512,4096]{1,0:T(8,128)(2,1)S(1)}, bf16[512,4096]{1,0:T(8,128)(2,1)}, u32[]{:S(2)}) copy-start(bf16[512,4096]{1,0:T(8,128)(2,1)} %param.12) | copy-start | bytes 12582916
  84.1 1.1 copy-start.12
  88.3 2.4 %copy-start.6 = (bf16[640,8,512]{2,0,1:T(8,128)(2,1)}, bf16[640,8,512]{2,0,1:T(8,128)(2,1)S(1)}, u32[]{:S(2)}) copy-start(bf16[640,8,512]{2,0,1:T(8,128)(2,1)S(1)} %fusion.8) | copy-start | bytes 15728644
  92.4 5.1 %collective-permute-start = (bf16[4,640,512]{2,1,0:T(8,128)(2,1)}, bf16[4,640,512]{2,1,0:T(8,128)(2,1)S(1)}, u32[]{:S(2)}, u32[]{:S(2)}) collective-permute-start(bf16[4,640,512]{2,1,0:T(8,128)(2,1)} %dynamic-slice_bitcast_fusion.1), channel_id=1, source_target_pairs={{0,1},{1,0},{2,3},{3,2},{4,5},{5,4},{6,7},{7,6},{8,9},{9,8},{10,11... | collective-permute-start | bytes 7864328 | tf_op jit(solution)/shard_map/ppermute | solution.py:76
  101.5 1.7 copy-start.9
  101.5 75.0 %reduce-scatter.5.cloned.1.call-start = ((), (), s32[]{:S(2)}) async-start(), calls=%async_computation.11 | async-start | bytes 3276800 | tf_op jit(solution)/shard_map/reduce_scatter | solution.py:80
  111.6 1.7 copy-start.11
  111.6 3.2 %copy-start.13 = (f32[640,512]{1,0:T(8,128)S(1)}, f32[640,512]{1,0:T(8,128)}, u32[]{:S(2)}) copy-start(f32[640,512]{1,0:T(8,128)} %copy-done.12) | copy-start | bytes 3932164
  111.6 5.0 %copy-start.18 = (bf16[512,4096]{1,0:T(8,128)(2,1)S(1)}, bf16[512,4096]{1,0:T(8,128)(2,1)}, u32[]{:S(2)}) copy-start(bf16[512,4096]{1,0:T(8,128)(2,1)} %param.12) | copy-start | bytes 12582916
  112.0 7.9 %copy-start.5 = (bf16[4,2,640,512]{3,2,1,0:T(8,128)(2,1)}, bf16[4,2,640,512]{3,2,1,0:T(8,128)(2,1)S(1)}, u32[]{:S(2)}) copy-start(bf16[4,2,640,512]{3,2,1,0:T(8,128)(2,1)S(1)} %copy.52) | copy-start | bytes 15728644
  116.6 3.3 %copy-start.3 = (bf16[4096,512]{1,0:T(8,128)(2,1)S(1)}, bf16[4096,512]{1,0:T(8,128)(2,1)}, u32[]{:S(2)}) copy-start(bf16[4096,512]{1,0:T(8,128)(2,1)} %param.10) | copy-start | bytes 12582916
  128.7 5.0 %collective-permute-start.2 = (bf16[4,640,512]{2,1,0:T(8,128)(2,1)S(1)}, bf16[4,640,512]{2,1,0:T(8,128)(2,1)S(1)}, u32[]{:S(2)}, u32[]{:S(2)}) collective-permute-start(bf16[4,640,512]{2,1,0:T(8,128)(2,1)S(1)} %dynamic-slice_bitcast_fusion), channel_id=1, source_target_pairs={{0,1},{1,0},{2,3},{3,2},{4,5},{5,4},{6,7},{7,6},{8,9},{9,8},{10,11... | collective-permute-start | bytes 7864328 | tf_op jit(solution)/shard_map/ppermute | solution.py:76
  138.0 19.9 %all-to-all-start.3 = ((bf16[16,40,512]{2,1,0:T(8,128)(2,1)}), bf16[16,40,512]{2,1,0:T(8,128)(2,1)S(1)}, u32[]{:S(2)}, u32[]{:S(2)}) async-start(bf16[16,40,512]{2,1,0:T(8,128)(2,1)} %bitcast.121), calls=%async_computation.4 | async-start | bytes 1310720 | tf_op jit(solution)/shard_map/all_to_all | solution.py:83
  153.3 6.2 %copy-start.14 = (bf16[128,512]{1,0:T(8,128)(2,1)S(1)}, bf16[128,512]{1,0:T(8,128)(2,1)}, u32[]{:S(2)}) copy-start(bf16[128,512]{1,0:T(8,128)(2,1)} %param.13) | copy-start | bytes 393220
  153.4 6.2 %copy-start.16 = (f32[128]{0:T(128)S(1)}, f32[128]{0:T(128)}, u32[]{:S(2)}) copy-start(f32[128]{0:T(128)} %copy-done.15) | copy-start | bytes 1540
  160.4 7.7 %collective-permute-start.1 = (f32[128,2]{0,1:T(2,128)S(1)}, f32[128,2]{0,1:T(2,128)S(1)}, u32[]{:S(2)}, u32[]{:S(2)}) collective-permute-start(f32[128,2]{0,1:T(2,128)S(1)} %pad_maximum_fusion), channel_id=1, source_target_pairs={{0,1},{1,0},{2,3},{3,2},{4,5},{5,4},{6,7},{7,6},{8,9},{9,8},{10,11... | collective-permute-start | bytes 3080 | tf_op jit(solution)/shard_map/ppermute | solution.py:119
  176.5 18.4 %all-to-all-start.5 = ((bf16[16,40,512]{2,1,0:T(8,128)(2,1)}), bf16[16,40,512]{2,1,0:T(8,128)(2,1)S(1)}, u32[]{:S(2)}, u32[]{:S(2)}) async-start(bf16[16,40,512]{2,1,0:T(8,128)(2,1)} %bitcast.120), calls=%async_computation.7 | async-start | bytes 1310720 | tf_op jit(solution)/shard_map/all_to_all | solution.py:83
  187.3 9.9 %copy-start.1 = (bf16[128,512]{1,0:T(8,128)(2,1)S(1)}, bf16[128,512]{1,0:T(8,128)(2,1)}, u32[]{:S(2)}) copy-start(bf16[128,512]{1,0:T(8,128)(2,1)} %param.7) | copy-start | bytes 393220
Sparse Core Ops, SparseCore 0:
  30.5 33.3 all-gather.3
  65.6 35.2 all-gather.5
  103.9 34.0 reduce-scatter.2
  140.2 33.6 reduce-scatter.4
